TPU v7x, 32 devices: a whole 2x2x4 slice. The times are simulated.
32 devices in a mesh: groups: 2 (over y), rows: 8 (over z, x), heads: 2 (over core).
Axes of the slice: x: 2, y: 2, z: 4, core: 2. Of those that a mesh axis runs over, the one named last changes fastest.
Arguments:
- residual_in: bfloat16 [128, 8192], P(('groups', 'rows'), 'heads'), parts along dimension 0, may hold values from -6 to 6
- query: bfloat16 [128, 8192], P(('groups', 'rows'), 'heads'), parts along dimension 0, may hold values from -120 to 120
- key_cache: bfloat16 [128, 4, 32, 128], P(('groups', 'rows'), 'heads'), parts along dimension 0, may hold values from -4 to 4
- value_cache: bfloat16 [128, 4, 32, 128], P(('groups', 'rows'), 'heads'), parts along dimension 0, may hold values from -5 to 5
- key_new: bfloat16 [128, 4, 128], P(('groups', 'rows'), 'heads'), parts along dimension 0, may hold values from -4 to 4
- value_new: bfloat16 [128, 4, 128], P(('groups', 'rows'), 'heads'), parts along dimension 0, may hold values from -5 to 5
- lengths: int32 [128], P(('groups', 'rows')), parts along dimension 0, may hold values from 2 to 32, as said below
- norm_gain: bfloat16 [8192], replicated, may hold values from 0.3984375 to 1.59375
- hot_gate: bfloat16 [128, 8192], P('heads'), may hold values from -0.0625 to 0.0625
- hot_up: bfloat16 [128, 8192], P('heads'), may hold values from -0.0625 to 0.0625
- hot_down: bfloat16 [128, 8192], P('heads'), may hold values from -0.5 to 0.5
- cold_gate: bfloat16 [512, 8192], P(('rows', 'heads')), may hold values from -0.0625 to 0.0625
- cold_up: bfloat16 [512, 8192], P(('rows', 'heads')), may hold values from -0.0625 to 0.0625
- cold_down: bfloat16 [512, 8192], P(('rows', 'heads')), may hold values from -0.5 to 0.5
- active: int32 [128, 4], P(('groups', 'rows')), parts along dimension 0, may hold values from 0 to 1, as said below
Outputs:
- residual_out: bfloat16 [128, 8192], P(('groups', 'rows'), 'heads'), parts along dimension 0
There are 2 independent parts, one for each index of `groups`. A program takes and returns all parts, laid end to end along the dimension named above; an argument that names none is the same for every part. Nothing has to cross between parts.
Inputs may be any that keep to these rules, and one draw needn't show every extreme that they name: `lengths`: every request has at least two filled slots, and some request has all 32. `active`: 0 or 1; among the 8 requests of one index of rows at most 2 are active on any one cold block, and exactly 2 on some.
All inputs are finite; a program needn't handle non-finite values.
Results may differ from a plain program's by a relative error of at most 0.0085.
Values may be sent and summed in bfloat16 or wider, within the bound.
No kernel may reach another device: no remote copies, remote signals or barrier semaphores. Data moves between devices by JAX's collectives and lax.ppermute only.
A program may use at most 64 MiB of HBM per device.

v0:
```python
import jax
import jax.numpy as jnp
from jax import lax
from jax.sharding import PartitionSpec as P

HD = 128
D = 8192
CAP = 2


def partner(block, axis, bit):
    count = lax.axis_size(axis)
    route = []
    for low in range(count):
        high = low | 1 << bit
        if high != low and high < count:
            route += [(low, high), (high, low)]
    return lax.ppermute(block, axis, route)


def attention_rows(query, key_cache, value_cache, key_new, value_new, lengths):
    count = key_cache.shape[0]
    kv_local = key_cache.shape[1]
    scale_factor = 1.0 / HD**0.5
    queries = query.reshape(count, kv_local, -1, HD)
    scores = (
        jnp.einsum("rgjd,rgpd->rgjp", queries, key_cache, preferred_element_type=jnp.float32)
        * scale_factor
    )
    own_score = (
        jnp.einsum("rgjd,rgd->rgj", queries, key_new, preferred_element_type=jnp.float32)
        * scale_factor
    )
    visible = (jnp.arange(key_cache.shape[2], dtype=jnp.int32)[None, :] < lengths[:, None])[
        :, None, None, :
    ]
    scores = jnp.where(visible, scores, -1e30)
    highest = jnp.maximum(jnp.max(scores, axis=-1), own_score)
    expons = jnp.where(visible, jnp.exp(scores - highest[..., None]), 0.0)
    own_expon = jnp.exp(own_score - highest)
    totals = jnp.sum(expons, axis=-1) + own_expon
    weights = (expons / totals[..., None]).astype(jnp.bfloat16)
    own_weight = (own_expon / totals).astype(jnp.bfloat16)
    blended = jnp.einsum(
        "rgjp,rgpd->rgjd", weights, value_cache, preferred_element_type=jnp.float32
    )
    blended = (
        blended
        + own_weight.astype(jnp.float32)[..., None] * value_new.astype(jnp.float32)[:, :, None, :]
    )
    return blended.reshape(count, -1)


def swiglu_rows(normed, gate_rows, up_rows, down_rows):
    gate = jnp.einsum("rd,nd->rn", normed, gate_rows, preferred_element_type=jnp.float32)
    upper = jnp.einsum("rd,nd->rn", normed, up_rows, preferred_element_type=jnp.float32)
    hidden = (jax.nn.silu(gate) * upper).astype(jnp.bfloat16)
    return jnp.dot(hidden, down_rows, preferred_element_type=jnp.float32)


def collect_rows(selector, returned):
    return lax.dot_general(
        selector,
        returned,
        (((0,), (0,)), ((), ())),
        precision=lax.Precision.HIGHEST,
        preferred_element_type=jnp.float32,
    )


def local(
    residual_in,
    query,
    key_cache,
    value_cache,
    key_new,
    value_new,
    lengths,
    norm_gain,
    hot_gate,
    hot_up,
    hot_down,
    cold_gate,
    cold_up,
    cold_down,
    active,
):
    attended = attention_rows(query, key_cache, value_cache, key_new, value_new, lengths)
    stream = (residual_in.astype(jnp.float32) + attended).astype(jnp.bfloat16)
    half_width = stream.shape[1]
    myself = lax.axis_index("heads")
    local_wide = stream.astype(jnp.float32)
    square_total = lax.psum(jnp.sum(local_wide * local_wide, axis=-1), "heads")
    gain_half = lax.dynamic_slice_in_dim(norm_gain, myself * half_width, half_width)
    scaled = (
        local_wide * lax.rsqrt(square_total / D + 1e-05)[:, None] * gain_half.astype(jnp.float32)
    )
    normed = lax.all_gather(scaled.astype(jnp.bfloat16), "heads", axis=1, tiled=True)
    hot_part = swiglu_rows(normed, hot_gate, hot_up, hot_down)
    owner_count = lax.axis_size("rows")
    block_count = active.shape[1]
    request_count = active.shape[0]
    by_block = jnp.transpose(active)
    earlier = jnp.cumsum(by_block, axis=1) - by_block
    slot_ids = jnp.arange(CAP, dtype=jnp.int32)[None, :, None]
    slot_table = by_block[:, None, :] * (earlier[:, None, :] == slot_ids).astype(jnp.int32)
    selector = jnp.repeat(slot_table, owner_count // block_count, axis=0).reshape(
        owner_count * CAP, request_count
    )
    outgoing = jnp.dot(
        selector.astype(jnp.bfloat16), normed, preferred_element_type=jnp.float32
    ).astype(jnp.bfloat16)
    incoming = lax.all_to_all(outgoing, "rows", split_axis=0, concat_axis=0, tiled=True)
    cold_part = swiglu_rows(incoming, cold_gate, cold_up, cold_down)
    selector_wide = selector.astype(jnp.float32)
    kept = lax.dynamic_slice_in_dim(cold_part, myself * half_width, half_width, 1)
    given = lax.dynamic_slice_in_dim(cold_part, (1 - myself) * half_width, half_width, 1)
    owner_sum = kept + partner(given, "heads", 0)
    returned = lax.all_to_all(owner_sum, "rows", split_axis=0, concat_axis=0, tiled=True)
    cold_sum = collect_rows(selector_wide, returned)
    hot_total = lax.psum_scatter(hot_part, "heads", scatter_dimension=1, tiled=True)
    result = stream.astype(jnp.float32) + hot_total + cold_sum
    return result.astype(jnp.bfloat16)


def solution(mesh):
    return jax.shard_map(
        local,
        mesh=mesh,
        in_specs=(
            P(("groups", "rows"), "heads"),
            P(("groups", "rows"), "heads"),
            P(("groups", "rows"), "heads", None, None),
            P(("groups", "rows"), "heads", None, None),
            P(("groups", "rows"), "heads", None),
            P(("groups", "rows"), "heads", None),
            P(("groups", "rows")),
            P(),
            P("heads", None),
            P("heads", None),
            P("heads", None),
            P(("rows", "heads"), None),
            P(("rows", "heads"), None),
            P(("rows", "heads"), None),
            P(("groups", "rows"), None),
        ),
        out_specs=P(("groups", "rows"), "heads"),
        check_vma=False,
    )
```

profile of v0, /device:TPU:0, one launch (start us, length us, event | category | flops | bytes accessed | tf_op | source)
XLA Modules:
  0.0 60.0 jit_solution(12461291125525763739)
XLA Ops:
  6.5 0.0 copy-start
  6.5 0.0 copy-start.10
  6.5 0.0 copy-start.4
  6.5 0.7 %copy-done.10 = s32[8]{0:T(128)S(1)} copy-done((s32[8]{0:T(128)S(1)}, s32[8]{0:T(128)}, u32[]{:S(2)}) %copy-start.10) | copy-done | bytes 56
  7.3 0.1 iota_compare_fusion
  7.4 1.0 %fusion.15 = f32[8,2,1,16]{3,2,1,0:T(1,128)S(1)} fusion(bf16[8,2,16,128]{3,0,2,1:T(8,128)(2,1)} %bitcast.32, bf16[8,2,128,1]{2,1,0,3:T(2,128)(2,1)} %bitcast.40), kind=kOutput, calls=%fused_computation.28 | convolution fusion | flops 65536 | bytes 70656 | tf_op jit(solution)/shard_map/rgjd,rgd->rgj/dot_general | solution.py:31
  8.3 0.0 copy-done.4
  8.4 1.2 %fusion.39 = (f32[8,2,16]{2,1,0:T(2,128)S(1)}, f32[8,2,16,32]{3,2,1,0:T(8,128)S(1)}) fusion(bf16[8,2,32,128]{3,2,1,0:T(8,128)(2,1)} %param.17, bf16[8,2,16,128]{3,0,2,1:T(8,128)(2,1)S(1)} %bitcast.33, pred[8,32]{1,0:T(8,128)(4,1)S(1)} %iota_compare_fusion), kind=kOutput, calls=%fused_computation.60 | convolution fusion | flops 2121472 | bytes 230656 | tf_op jit(solution)/shard_map/rgjd,rgpd->rgjp/dot_general | solution.py:27
  9.5 0.0 copy-start.9
  9.6 0.2 fusion.10
  9.8 0.0 copy-start.8
  9.8 0.7 %copy-done.8 = bf16[8,2,128]{2,1,0:T(2,128)(2,1)S(1)} copy-done((bf16[8,2,128]{2,1,0:T(2,128)(2,1)S(1)}, bf16[8,2,128]{2,1,0:T(2,128)(2,1)}, u32[]{:S(2)}) %copy-start.8) | copy-done | bytes 4120
  10.5 0.0 copy-done.9
  10.5 0.0 copy-start.5
  10.5 0.0 copy-start.6
  10.5 0.3 convolution_add_fusion.1
  10.8 0.0 copy-start.7
  10.8 0.5 copy-done.5
  11.3 0.0 copy-start.2
  11.3 0.2 fusion.6
  11.5 2.7 %psum.7 = f32[8]{0:T(128)S(1)} all-reduce(f32[8]{0:T(128)S(1)} %get-tuple-element.5), channel_id=1, replica_groups=mesh['groups'=2,'rows'=8,'heads'=2] {'heads'}, use_global_device_ids=true, to_apply=%region_3.4 | all-reduce | flops 8 | bytes 64 | tf_op jit(solution)/shard_map/psum | solution.py:93
  14.2 0.0 copy-done.7
  14.3 0.1 fusion.8
  14.3 1.9 %all_gather.3 = bf16[8,8192]{1,0:T(8,128)(2,1)S(1)} all-gather(bf16[8,4096]{1,0:T(8,128)(2,1)S(1)} %fusion.8), channel_id=1, replica_groups=mesh['groups'=2,'rows'=8,'heads'=2] {'heads'}, dimensions={1}, use_global_device_ids=true | all-gather | bytes 196608 | tf_op jit(solution)/shard_map/all_gather | solution.py:98
  16.2 0.0 copy-done.6
  16.2 0.2 reduce_window_sum.11
  16.5 0.2 convolution_convert_fusion
  16.7 0.9 %all_to_all.16 = bf16[8,2,8192]{2,1,0:T(2,128)(2,1)} reshape(bf16[16,8192]{1,0:T(8,128)(2,1)S(1)} %convolution_convert_fusion) | data formatting | bytes 524288 | tf_op jit(solution)/shard_map/all_to_all | solution.py:113
  17.5 7.1 %all-to-all-start = ((bf16[8,2,8192]{2,1,0:T(2,128)(2,1)}), bf16[8,2,8192]{2,1,0:T(2,128)(2,1)S(1)}, u32[]{:S(2)}, u32[]{:S(2)}) async-start(bf16[8,2,8192]{2,1,0:T(2,128)(2,1)} %all_to_all.16), calls=%async_computation.1 | async-start | bytes 524288 | tf_op jit(solution)/shard_map/all_to_all | solution.py:113
  24.7 0.0 reduce-scatter.2.cloned.1.call-start
  24.7 0.0 copy-done.2
  24.7 0.4 fusion.40
  25.1 0.0 copy-start.3
  25.1 8.8 %all-to-all-done = bf16[8,2,8192]{2,1,0:T(2,128)(2,1)S(1)} async-done(((bf16[8,2,8192]{2,1,0:T(2,128)(2,1)}), bf16[8,2,8192]{2,1,0:T(2,128)(2,1)S(1)}, u32[]{:S(2)}, u32[]{:S(2)}) %all-to-all-start) | async-done | bytes 262176 | tf_op jit(solution)/shard_map/all_to_all | solution.py:113
  33.9 0.1 all_to_all.18
  34.0 0.0 copy-done.3
  34.0 0.2 fusion.41
  34.3 0.0 copy-start.1
  34.3 1.9 %fusion.3 = f32[16,8192]{1,0:T(8,128)S(1)} fusion(bf16[32,8192]{1,0:T(8,128)(2,1)} %param.28, bf16[16,8192]{1,0:T(8,128)(2,1)S(1)} %all_to_all.18, bf16[32,8192]{1,0:T(8,128)(2,1)} %param.27, f32[16,32]{1,0:T(8,128)S(1)} %fusion.41), kind=kOutput, calls=%fused_computation.8 | convolution fusion | flops 16780288 | bytes 1837056 | tf_op jit(solution)/shard_map/dot_general | solution.py:58
  36.2 0.1 collective-permute-start
  36.3 0.0 copy-done
  36.3 0.0 copy-done.1
  36.3 1.6 %fusion.5 = f32[8,8192]{1,0:T(8,128)} fusion(bf16[64,8192]{1,0:T(8,128)(2,1)S(1)} %copy-done, bf16[8,8192]{1,0:T(8,128)(2,1)S(1)} %all_gather.3, bf16[64,8192]{1,0:T(8,128)(2,1)S(1)} %copy-done.1, f32[8,64]{1,0:T(8,128)S(1)} %fusion.40), kind=kOutput, calls=%fused_computation.11 | convolution fusion | flops 16780288 | bytes 2492416 | tf_op jit(solution)/shard_map/dot_general | solution.py:58
  37.9 0.0 reduce-scatter.2.cloned.1.call-update
  37.9 0.0 collective-permute-done
  38.0 0.2 all_to_all.19
  38.1 12.9 %all_to_all.24 = f32[8,2,4096]{2,1,0:T(2,128)S(1)} all-to-all(f32[8,2,4096]{2,1,0:T(2,128)S(1)} %all_to_all.19), channel_id=1, replica_groups=mesh['groups'=2,'rows'=8,'heads'=2] {'rows'}, dimensions={0} | all-to-all | bytes 524288 | tf_op jit(solution)/shard_map/all_to_all | solution.py:119
  51.1 0.2 all_to_all.21
  51.3 0.0 reduce-scatter.2.cloned.1.call-done
  51.3 1.9 %fusion = bf16[8,4096]{1,0:T(8,128)(2,1)} fusion(f32[16,8]{1,0:T(8,128)S(1)} %bitcast.34, f32[16,4096]{1,0:T(8,128)S(1)} %all_to_all.21, f32[8,4096]{1,0:T(8,128)} %reduce-scatter.2.cloned.1.call-done, bf16[8,4096]{1,0:T(8,128)(2,1)S(1)} %get-tuple-element.6), kind=kOutput, calls=%fused_computation.2 | convolution fusion | flops 6422528 | bytes 524800 | tf_op jit(solution)/shard_map/dot_general | solution.py:62
  (11 shorter events, 0.1 us)
Async XLA Ops:
  6.5 29.8 %copy-start = (bf16[64,8192]{1,0:T(8,128)(2,1)S(1)}, bf16[64,8192]{1,0:T(8,128)(2,1)}, u32[]{:S(2)}) copy-start(bf16[64,8192]{1,0:T(8,128)(2,1)} %param.25) | copy-start | bytes 3145732
  6.5 0.7 %copy-start.10 = (s32[8]{0:T(128)S(1)}, s32[8]{0:T(128)}, u32[]{:S(2)}) copy-start(s32[8]{0:T(128)} %param.21) | copy-start | bytes 100
  6.5 1.8 %copy-start.4 = (bf16[8,4096]{1,0:T(8,128)(2,1)S(1)}, bf16[8,4096]{1,0:T(8,128)(2,1)}, u32[]{:S(2)}) copy-start(bf16[8,4096]{1,0:T(8,128)(2,1)} %param.16) | copy-start | bytes 196612
  9.5 1.0 %copy-start.9 = (bf16[8,2,32,128]{3,2,1,0:T(8,128)(2,1)S(1)}, bf16[8,2,32,128]{3,2,1,0:T(8,128)(2,1)}, u32[]{:S(2)}) copy-start(bf16[8,2,32,128]{3,2,1,0:T(8,128)(2,1)} %param.18) | copy-start | bytes 393220
  9.8 0.7 %copy-start.8 = (bf16[8,2,128]{2,1,0:T(2,128)(2,1)S(1)}, bf16[8,2,128]{2,1,0:T(2,128)(2,1)}, u32[]{:S(2)}) copy-start(bf16[8,2,128]{2,1,0:T(2,128)(2,1)} %param.20) | copy-start | bytes 12292
  10.5 0.8 %copy-start.5 = (bf16[8,4096]{1,0:T(8,128)(2,1)S(1)}, bf16[8,4096]{1,0:T(8,128)(2,1)}, u32[]{:S(2)}) copy-start(bf16[8,4096]{1,0:T(8,128)(2,1)} %param.15) | copy-start | bytes 196612
  10.5 5.8 %copy-start.6 = (s32[8,4]{0,1:T(4,128)S(1)}, s32[8,4]{0,1:T(4,128)}, u32[]{:S(2)}) copy-start(s32[8,4]{0,1:T(4,128)} %param.29) | copy-start | bytes 388
  10.8 3.5 %copy-start.7 = (bf16[8192]{0:T(1024)(128)(2,1)S(1)}, bf16[8192]{0:T(1024)(128)(2,1)}, u32[]{:S(2)}) copy-start(bf16[8192]{0:T(1024)(128)(2,1)} %param.22) | copy-start | bytes 49156
  11.3 13.4 %copy-start.2 = (bf16[64,8192]{1,0:T(8,128)(2,1)S(1)}, bf16[64,8192]{1,0:T(8,128)(2,1)}, u32[]{:S(2)}) copy-start(bf16[64,8192]{1,0:T(8,128)(2,1)} %param.23) | copy-start | bytes 3145732
  17.5 16.4 %all-to-all-start = ((bf16[8,2,8192]{2,1,0:T(2,128)(2,1)}), bf16[8,2,8192]{2,1,0:T(2,128)(2,1)S(1)}, u32[]{:S(2)}, u32[]{:S(2)}) async-start(bf16[8,2,8192]{2,1,0:T(2,128)(2,1)} %all_to_all.16), calls=%async_computation.1 | async-start | bytes 524288 | tf_op jit(solution)/shard_map/all_to_all | solution.py:113
  24.7 26.6 %reduce-scatter.2.cloned.1.call-start = ((), (), s32[]{:S(2)}) async-start(), calls=%async_computation.3 | async-start | bytes 393216 | tf_op jit(solution)/shard_map/reduce_scatter | solution.py:121
  25.1 8.9 %copy-start.3 = (bf16[32,8192]{1,0:T(8,128)(2,1)S(1)}, bf16[32,8192]{1,0:T(8,128)(2,1)}, u32[]{:S(2)}) copy-start(bf16[32,8192]{1,0:T(8,128)(2,1)} %param.26) | copy-start | bytes 1572868
  34.3 2.0 %copy-start.1 = (bf16[64,8192]{1,0:T(8,128)(2,1)S(1)}, bf16[64,8192]{1,0:T(8,128)(2,1)}, u32[]{:S(2)}) copy-start(bf16[64,8192]{1,0:T(8,128)(2,1)} %param.24) | copy-start | bytes 3145732
  36.2 1.7 %collective-permute-start = (f32[16,4096]{1,0:T(8,128)S(1)}, f32[16,4096]{1,0:T(8,128)S(1)}, u32[]{:S(2)}, u32[]{:S(2)}) collective-permute-start(f32[16,4096]{1,0:T(8,128)S(1)} %constant_dynamic-slice_fusion), channel_id=1, source_target_pairs={{0,1},{1,0},{2,3},{3,2},{4,5},{5,4},{6,7},{7,6},{8,9},{9,8},{10,11... | collective-permute-start | bytes 786440 | tf_op jit(solution)/shard_map/ppermute | solution.py:18
Sparse Core Ops, SparseCore 0:
  38.0 6.8 reduce-scatter.1
where the time goes:
time: 60.5 us; the launch traced here: 60 us
  blocking collectives  17.6 us (29%)
  between operations  13.6 us (22%)
  waiting for transfers between devices  8.86 us (15%)
  matrix products  8.55 us (14%)
  starting transfers between devices  7.24 us (12%)
  local copies, waits for them, and re-layouts  3.34 us (6%)
  other arithmetic  0.85 us (1%)
    all_to_all x1, blocking collectives, local(): lax.all_to_all(owner_sum, 'rows', split_axis=0, concat_axis=0, tiled=True)  12.9 us
    all_to_all x1, waiting for transfers between devices, local(): lax.all_to_all(outgoing, 'rows', split_axis=0, concat_axis=0, tiled=True)  8.82 us
    all_to_all x1, starting transfers between devices, local(): lax.all_to_all(outgoing, 'rows', split_axis=0, concat_axis=0, tiled=True)  7.14 us
    dot_general x2, matrix products, swiglu_rows(): return jnp.dot(hidden, down_rows, preferred_element_type=jnp.float32)  3.46 us
    psum x1, blocking collectives, local(): square_total = lax.psum(jnp.sum(local_wide * local_wide, axis=-1), 'heads')  2.71 us
    unnamed x22, local copies, waits for them, and re-layouts  1.98 us
    all_gather x1, blocking collectives, local(): lax.all_gather(scaled.astype(jnp.bfloat16), 'heads', axis=1, tiled=True)  1.9 us
    dot_general x1, matrix products, collect_rows(): lax.dot_general(selector, returned, (((0,), (0,)), ((), ())), precision=l...  1.86 us
  transfers between devices with their start and end apart: 3, of which 1 were waited for; matrix products, arithmetic and copies ran while one was open for 3% of the time, Pallas kernels for 0%

commit v1 on v0

--- a/solution.py
+++ b/solution.py
@@ -16,6 +16,13 @@
         if high != low and high < count:
             route += [(low, high), (high, low)]
     return lax.ppermute(block, axis, route)
+
+
+def join_halves(half, myself):
+    other = partner(half, "heads", 0)
+    low_first = jnp.concatenate([half, other], axis=1)
+    high_first = jnp.concatenate([other, half], axis=1)
+    return jnp.where(myself == 0, low_first, high_first)
 
 
 def attention_rows(query, key_cache, value_cache, key_new, value_new, lengths):
@@ -90,12 +97,13 @@
     half_width = stream.shape[1]
     myself = lax.axis_index("heads")
     local_wide = stream.astype(jnp.float32)
-    square_total = lax.psum(jnp.sum(local_wide * local_wide, axis=-1), "heads")
+    square_part = jnp.sum(local_wide * local_wide, axis=-1)
+    square_total = square_part + partner(square_part, "heads", 0)
     gain_half = lax.dynamic_slice_in_dim(norm_gain, myself * half_width, half_width)
     scaled = (
         local_wide * lax.rsqrt(square_total / D + 1e-05)[:, None] * gain_half.astype(jnp.float32)
     )
-    normed = lax.all_gather(scaled.astype(jnp.bfloat16), "heads", axis=1, tiled=True)
+    normed = join_halves(scaled.astype(jnp.bfloat16), myself)
     hot_part = swiglu_rows(normed, hot_gate, hot_up, hot_down)
     owner_count = lax.axis_size("rows")
     block_count = active.shape[1]
@@ -118,7 +126,9 @@
     owner_sum = kept + partner(given, "heads", 0)
     returned = lax.all_to_all(owner_sum, "rows", split_axis=0, concat_axis=0, tiled=True)
     cold_sum = collect_rows(selector_wide, returned)
-    hot_total = lax.psum_scatter(hot_part, "heads", scatter_dimension=1, tiled=True)
+    hot_kept = lax.dynamic_slice_in_dim(hot_part, myself * half_width, half_width, 1)
+    hot_given = lax.dynamic_slice_in_dim(hot_part, (1 - myself) * half_width, half_width, 1)
+    hot_total = hot_kept + partner(hot_given, "heads", 0)
     result = stream.astype(jnp.float32) + hot_total + cold_sum
     return result.astype(jnp.bfloat16)
 

time: 60.5 us -> 45.6 us (0.75)
  blocking collectives: 17.6 us -> 0 us
  between operations: 13.6 us -> 0.19 us
  waiting for transfers between devices: 8.86 us -> 20.4 us
  starting transfers between devices: 7.24 us -> 11.7 us
  other arithmetic: 0.85 us -> 2.53 us
  matrix products: 8.55 us -> 6.98 us
    all_to_all x1 -> x0, blocking collectives: 12.9 us -> none  [local(): lax.all_to_all(owner_sum, 'rows', split_axis=0, concat_axis=0, tiled=True)]
    all_to_all x0 -> x1, waiting for transfers between devices: none -> 9.17 us  [local(): lax.all_to_all(owner_sum, 'rows', split_axis=0, concat_axis=0, tiled=True)]
    all_to_all x0 -> x1, starting transfers between devices: none -> 3.59 us  [local(): lax.all_to_all(owner_sum, 'rows', split_axis=0, concat_axis=0, tiled=True)]
    psum x1 -> x0, blocking collectives: 2.71 us -> none  [local(): square_total = lax.psum(jnp.sum(local_wide * local_wide, axis=-1), 'heads')]
    ppermute x1 -> x4, waiting for transfers between devices: 0.01 us -> 2.3 us  [partner(): return lax.ppermute(block, axis, route)]
    all_gather x1 -> x0, blocking collectives: 1.9 us -> none  [local(): lax.all_gather(scaled.astype(jnp.bfloat16), 'heads', axis=1, tiled=True)]
    ppermute x1 -> x4, starting transfers between devices: 0.07 us -> 1.02 us  [partner(): return lax.ppermute(block, axis, route)]
    add x1, other arithmetic: 0.03 us -> 0.98 us  [local(): owner_sum = kept + partner(given, 'heads', 0)]
  transfers between devices with their start and end apart: 3 -> 6, of which waited for: 1 -> 5; matrix products, arithmetic and copies ran while one was open for 3% -> 3% of each run, Pallas kernels for 0% -> 0%
where the time goes in v1:
time: 45.6 us; the launch traced here: 45.1 us
  waiting for transfers between devices  20.4 us (45%)
  starting transfers between devices  11.7 us (26%)
  matrix products  6.98 us (15%)
  local copies, waits for them, and re-layouts  3.33 us (7%)
  other arithmetic  2.53 us (6%)
    all_to_all x1, waiting for transfers between devices, local(): lax.all_to_all(owner_sum, 'rows', split_axis=0, concat_axis=0, tiled=True)  9.17 us
    all_to_all x1, waiting for transfers between devices, local(): lax.all_to_all(outgoing, 'rows', split_axis=0, concat_axis=0, tiled=True)  8.91 us
    all_to_all x1, starting transfers between devices, local(): lax.all_to_all(outgoing, 'rows', split_axis=0, concat_axis=0, tiled=True)  7.1 us
    all_to_all x1, starting transfers between devices, local(): lax.all_to_all(owner_sum, 'rows', split_axis=0, concat_axis=0, tiled=True)  3.59 us
    dot_general x2, matrix products, swiglu_rows(): return jnp.dot(hidden, down_rows, preferred_element_type=jnp.float32)  2.78 us
    ppermute x4, waiting for transfers between devices, partner(): return lax.ppermute(block, axis, route)  2.3 us
    unnamed x20, local copies, waits for them, and re-layouts  1.24 us
    dot_general x1, matrix products, attention_rows(): jnp.einsum('rgjd,rgpd->rgjp', queries, key_cache, preferred_element_type=...  1.17 us
  transfers between devices with their start and end apart: 6, of which 5 were waited for; matrix products, arithmetic and copies ran while one was open for 3% of the time, Pallas kernels for 0%

profile of v1, /device:TPU:0, one launch (start us, length us, event | category | flops | bytes accessed | tf_op | source)
XLA Modules:
  0.0 45.1 jit_solution(7972570449464875627)
XLA Ops:
  0.0 0.0 copy-start
  0.0 0.0 copy-start.4
  0.0 0.8 %iota_compare_fusion = pred[8,32]{1,0:T(8,128)(4,1)S(1)} fusion(s32[8]{0:T(128)} %param.21), kind=kLoop, calls=%fused_computation.44 | loop fusion | flops 256 | bytes 288 | tf_op jit(solution)/shard_map/lt | solution.py:41
  0.8 1.0 %fusion.14 = f32[8,2,1,16]{3,2,1,0:T(1,128)S(1)} fusion(bf16[8,2,16,128]{3,0,2,1:T(8,128)(2,1)} %bitcast.29, bf16[8,2,128,1]{2,1,0,3:T(2,128)(2,1)} %bitcast.37), kind=kOutput, calls=%fused_computation.26 | convolution fusion | flops 65536 | bytes 70656 | tf_op jit(solution)/shard_map/rgjd,rgd->rgj/dot_general | solution.py:38
  1.8 0.0 copy-done.4
  1.8 1.2 %fusion.36 = (f32[8,2,16]{2,1,0:T(2,128)S(1)}, f32[8,2,16,32]{3,2,1,0:T(8,128)S(1)}) fusion(bf16[8,2,32,128]{3,2,1,0:T(8,128)(2,1)} %param.17, bf16[8,2,16,128]{3,0,2,1:T(8,128)(2,1)S(1)} %bitcast.30, pred[8,32]{1,0:T(8,128)(4,1)S(1)} %iota_compare_fusion), kind=kOutput, calls=%fused_computation.58 | convolution fusion | flops 2121472 | bytes 230656 | tf_op jit(solution)/shard_map/rgjd,rgpd->rgjp/dot_general | solution.py:34
  3.0 0.0 copy-start.9
  3.0 0.2 fusion.9
  3.3 0.0 copy-start.8
  3.3 0.7 %copy-done.8 = bf16[8,2,128]{2,1,0:T(2,128)(2,1)S(1)} copy-done((bf16[8,2,128]{2,1,0:T(2,128)(2,1)S(1)}, bf16[8,2,128]{2,1,0:T(2,128)(2,1)}, u32[]{:S(2)}) %copy-start.8) | copy-done | bytes 4120
  4.0 0.0 copy-done.9
  4.0 0.0 copy-start.5
  4.0 0.0 copy-start.6
  4.0 0.3 convolution_add_fusion
  4.2 0.0 copy-start.7
  4.2 0.5 %copy-done.5 = bf16[8,4096]{1,0:T(8,128)(2,1)S(1)} copy-done((bf16[8,4096]{1,0:T(8,128)(2,1)S(1)}, bf16[8,4096]{1,0:T(8,128)(2,1)}, u32[]{:S(2)}) %copy-start.5) | copy-done | bytes 65560
  4.8 0.0 copy-start.1
  4.8 0.2 fusion.3
  5.0 0.5 %collective-permute-start = (f32[8]{0:T(128)S(1)}, f32[8]{0:T(128)S(1)}, u32[]{:S(2)}, u32[]{:S(2)}) collective-permute-start(f32[8]{0:T(128)S(1)} %get-tuple-element.5), channel_id=1, source_target_pairs={{0,1},{1,0},{2,3},{3,2},{4,5},{5,4},{6,7},{7,6},{8,9},{9,8},{10,11... | collective-permute-start | bytes 104 | tf_op jit(solution)/shard_map/ppermute | solution.py:18
  5.5 0.0 copy-done.6
  5.5 0.2 reduce_window_sum.11
  5.7 0.0 copy-done.7
  5.7 0.6 %collective-permute-done = f32[8]{0:T(128)S(1)} collective-permute-done((f32[8]{0:T(128)S(1)}, f32[8]{0:T(128)S(1)}, u32[]{:S(2)}, u32[]{:S(2)}) %collective-permute-start) | collective-permute-done | bytes 64 | tf_op jit(solution)/shard_map/ppermute | solution.py:18
  6.3 0.1 fusion.5
  6.4 0.4 collective-permute-start.1
  6.8 0.9 %collective-permute-done.1 = bf16[8,4096]{1,0:T(8,128)(2,1)S(1)} collective-permute-done((bf16[8,4096]{1,0:T(8,128)(2,1)S(1)}, bf16[8,4096]{1,0:T(8,128)(2,1)S(1)}, u32[]{:S(2)}, u32[]{:S(2)}) %collective-permute-start.1) | collective-permute-done | bytes 65568 | tf_op jit(solution)/shard_map/ppermute | solution.py:18
  7.7 0.2 convolution_convert_fusion
  8.0 0.9 %all_to_all.16 = bf16[8,2,8192]{2,1,0:T(2,128)(2,1)} reshape(bf16[16,8192]{1,0:T(8,128)(2,1)S(1)} %convolution_convert_fusion) | data formatting | bytes 524288 | tf_op jit(solution)/shard_map/all_to_all | solution.py:121
  8.9 7.1 %all-to-all-start = ((bf16[8,2,8192]{2,1,0:T(2,128)(2,1)}), bf16[8,2,8192]{2,1,0:T(2,128)(2,1)S(1)}, u32[]{:S(2)}, u32[]{:S(2)}) async-start(bf16[8,2,8192]{2,1,0:T(2,128)(2,1)} %all_to_all.16), calls=%async_computation | async-start | bytes 524288 | tf_op jit(solution)/shard_map/all_to_all | solution.py:121
  16.0 0.0 copy-done.1
  16.0 0.4 fusion.33
  16.3 0.0 copy-start.3
  16.3 8.9 %all-to-all-done = bf16[8,2,8192]{2,1,0:T(2,128)(2,1)S(1)} async-done(((bf16[8,2,8192]{2,1,0:T(2,128)(2,1)}), bf16[8,2,8192]{2,1,0:T(2,128)(2,1)S(1)}, u32[]{:S(2)}, u32[]{:S(2)}) %all-to-all-start) | async-done | bytes 262176 | tf_op jit(solution)/shard_map/all_to_all | solution.py:121
  25.3 0.1 all_to_all.18
  25.4 0.0 copy-done.3
  25.4 0.2 fusion.37
  25.6 0.0 copy-start.2
  25.6 1.9 %fusion.2 = f32[16,8192]{1,0:T(8,128)S(1)} fusion(bf16[32,8192]{1,0:T(8,128)(2,1)} %param.28, bf16[16,8192]{1,0:T(8,128)(2,1)S(1)} %all_to_all.18, bf16[32,8192]{1,0:T(8,128)(2,1)} %param.27, f32[16,32]{1,0:T(8,128)S(1)} %fusion.37), kind=kOutput, calls=%fused_computation.6 | convolution fusion | flops 16780288 | bytes 1837056 | tf_op jit(solution)/shard_map/dot_general | solution.py:65
  27.5 0.1 collective-permute-start.3
  27.6 0.0 copy-done
  27.6 0.0 copy-done.2
  27.6 0.9 %fusion.27 = f32[8,8192]{1,0:T(8,128)S(1)} fusion(bf16[64,8192]{1,0:T(8,128)(2,1)S(1)} %copy-done, f32[8,64]{1,0:T(8,128)S(1)} %fusion.33, bf16[64,8192]{1,0:T(8,128)(2,1)S(1)} %copy-done.2, bf16[8,4096]{1,0:T(8,128)(2,1)S(1)} %collective-permute-done.1, bf16[8,4096]{1,0:T(8,128)(2,1)S(1)} %fusion.5, pred[]{:T(512)S(6)} %eq.16), kind=kOutput, calls=%fused_computation.46 | convolution fusion | flops 17370112 | bytes 2492417 | tf_op jit(solution)/shard_map/dot_general | solution.py:65
  28.5 0.7 %collective-permute-done.3 = f32[16,4096]{1,0:T(8,128)} collective-permute-done((f32[16,4096]{1,0:T(8,128)S(1)}, f32[16,4096]{1,0:T(8,128)}, u32[]{:S(2)}, u32[]{:S(2)}) %collective-permute-start.3) | collective-permute-done | bytes 262176 | tf_op jit(solution)/shard_map/ppermute | solution.py:18
  29.3 1.0 %dynamic-slice_add_fusion = f32[16,4096]{1,0:T(8,128)S(1)} fusion(f32[16,4096]{1,0:T(8,128)} %collective-permute-done.3, f32[16,8192]{1,0:T(8,128)S(1)} %fusion.2, s32[]{:T(128)S(6)} %select_n.27), kind=kLoop, calls=%fused_computation.7 | loop fusion | flops 65536 | bytes 786436 | tf_op jit(solution)/shard_map/add | solution.py:126
  30.2 0.9 %all_to_all.19 = f32[8,2,4096]{2,1,0:T(2,128)} reshape(f32[16,4096]{1,0:T(8,128)S(1)} %dynamic-slice_add_fusion) | data formatting | bytes 524288 | tf_op jit(solution)/shard_map/all_to_all | solution.py:127
  31.1 3.6 %all-to-all-start.1 = ((f32[8,2,4096]{2,1,0:T(2,128)}), f32[8,2,4096]{2,1,0:T(2,128)S(1)}, u32[]{:S(2)}, u32[]{:S(2)}) async-start(f32[8,2,4096]{2,1,0:T(2,128)} %all_to_all.19), calls=%async_computation.1 | async-start | bytes 524288 | tf_op jit(solution)/shard_map/all_to_all | solution.py:127
  34.7 0.1 collective-permute-start.2
  34.8 9.2 %all-to-all-done.1 = f32[8,2,4096]{2,1,0:T(2,128)S(1)} async-done(((f32[8,2,4096]{2,1,0:T(2,128)}), f32[8,2,4096]{2,1,0:T(2,128)S(1)}, u32[]{:S(2)}, u32[]{:S(2)}) %all-to-all-start.1) | async-done | bytes 262176 | tf_op jit(solution)/shard_map/all_to_all | solution.py:127
  44.0 0.2 all_to_all.21
  44.1 0.0 collective-permute-done.2
  44.2 1.0 %fusion.7 = bf16[8,4096]{1,0:T(8,128)(2,1)} fusion(bf16[8,4096]{1,0:T(8,128)(2,1)S(1)} %get-tuple-element.6, f32[8,4096]{1,0:T(8,128)S(1)} %collective-permute-done.2, f32[8,8192]{1,0:T(8,128)S(1)} %fusion.27, s32[]{:T(128)S(6)} %select_n.27, f32[16,8]{1,0:T(8,128)S(1)} %bitcast.31, f32[16,4096]{1,0:T(8,128)S(1)} %all_to_all.21), kind=kOutput, calls=%fused_computation.15 | convolution fusion | flops 6455296 | bytes 655876 | tf_op jit(solution)/shard_map/dot_general | solution.py:69
  (11 shorter events, 0.1 us)
Async XLA Ops:
  0.0 27.6 %copy-start = (bf16[64,8192]{1,0:T(8,128)(2,1)S(1)}, bf16[64,8192]{1,0:T(8,128)(2,1)}, u32[]{:S(2)}) copy-start(bf16[64,8192]{1,0:T(8,128)(2,1)} %param.25) | copy-start | bytes 3145732
  0.0 1.8 %copy-start.4 = (bf16[8,4096]{1,0:T(8,128)(2,1)S(1)}, bf16[8,4096]{1,0:T(8,128)(2,1)}, u32[]{:S(2)}) copy-start(bf16[8,4096]{1,0:T(8,128)(2,1)} %param.16) | copy-start | bytes 196612
  3.0 1.0 %copy-start.9 = (bf16[8,2,32,128]{3,2,1,0:T(8,128)(2,1)S(1)}, bf16[8,2,32,128]{3,2,1,0:T(8,128)(2,1)}, u32[]{:S(2)}) copy-start(bf16[8,2,32,128]{3,2,1,0:T(8,128)(2,1)} %param.18) | copy-start | bytes 393220
  3.3 0.7 %copy-start.8 = (bf16[8,2,128]{2,1,0:T(2,128)(2,1)S(1)}, bf16[8,2,128]{2,1,0:T(2,128)(2,1)}, u32[]{:S(2)}) copy-start(bf16[8,2,128]{2,1,0:T(2,128)(2,1)} %param.20) | copy-start | bytes 12292
  4.0 0.8 %copy-start.5 = (bf16[8,4096]{1,0:T(8,128)(2,1)S(1)}, bf16[8,4096]{1,0:T(8,128)(2,1)}, u32[]{:S(2)}) copy-start(bf16[8,4096]{1,0:T(8,128)(2,1)} %param.15) | copy-start | bytes 196612
  4.0 1.5 %copy-start.6 = (s32[8,4]{0,1:T(4,128)S(1)}, s32[8,4]{0,1:T(4,128)}, u32[]{:S(2)}) copy-start(s32[8,4]{0,1:T(4,128)} %param.29) | copy-start | bytes 388
  4.2 1.5 %copy-start.7 = (bf16[8192]{0:T(1024)(128)(2,1)S(1)}, bf16[8192]{0:T(1024)(128)(2,1)}, u32[]{:S(2)}) copy-start(bf16[8192]{0:T(1024)(128)(2,1)} %param.22) | copy-start | bytes 49156
  4.8 11.2 %copy-start.1 = (bf16[64,8192]{1,0:T(8,128)(2,1)S(1)}, bf16[64,8192]{1,0:T(8,128)(2,1)}, u32[]{:S(2)}) copy-start(bf16[64,8192]{1,0:T(8,128)(2,1)} %param.24) | copy-start | bytes 3145732
  5.0 1.3 %collective-permute-start = (f32[8]{0:T(128)S(1)}, f32[8]{0:T(128)S(1)}, u32[]{:S(2)}, u32[]{:S(2)}) collective-permute-start(f32[8]{0:T(128)S(1)} %get-tuple-element.5), channel_id=1, source_target_pairs={{0,1},{1,0},{2,3},{3,2},{4,5},{5,4},{6,7},{7,6},{8,9},{9,8},{10,11... | collective-permute-start | bytes 104 | tf_op jit(solution)/shard_map/ppermute | solution.py:18
  6.4 1.3 %collective-permute-start.1 = (bf16[8,4096]{1,0:T(8,128)(2,1)S(1)}, bf16[8,4096]{1,0:T(8,128)(2,1)S(1)}, u32[]{:S(2)}, u32[]{:S(2)}) collective-permute-start(bf16[8,4096]{1,0:T(8,128)(2,1)S(1)} %fusion.5), channel_id=1, source_target_pairs={{0,1},{1,0},{2,3},{3,2},{4,5},{5,4},{6,7},{7,6},{8,9},{9,8},{10,11... | collective-permute-start | bytes 196616 | tf_op jit(solution)/shard_map/ppermute | solution.py:18
  8.9 16.4 %all-to-all-start = ((bf16[8,2,8192]{2,1,0:T(2,128)(2,1)}), bf16[8,2,8192]{2,1,0:T(2,128)(2,1)S(1)}, u32[]{:S(2)}, u32[]{:S(2)}) async-start(bf16[8,2,8192]{2,1,0:T(2,128)(2,1)} %all_to_all.16), calls=%async_computation | async-start | bytes 524288 | tf_op jit(solution)/shard_map/all_to_all | solution.py:121
  16.3 9.0 %copy-start.3 = (bf16[32,8192]{1,0:T(8,128)(2,1)S(1)}, bf16[32,8192]{1,0:T(8,128)(2,1)}, u32[]{:S(2)}) copy-start(bf16[32,8192]{1,0:T(8,128)(2,1)} %param.26) | copy-start | bytes 1572868
  25.6 2.0 %copy-start.2 = (bf16[64,8192]{1,0:T(8,128)(2,1)S(1)}, bf16[64,8192]{1,0:T(8,128)(2,1)}, u32[]{:S(2)}) copy-start(bf16[64,8192]{1,0:T(8,128)(2,1)} %param.23) | copy-start | bytes 3145732
  27.5 1.7 %collective-permute-start.3 = (f32[16,4096]{1,0:T(8,128)S(1)}, f32[16,4096]{1,0:T(8,128)}, u32[]{:S(2)}, u32[]{:S(2)}) collective-permute-start(f32[16,4096]{1,0:T(8,128)S(1)} %constant_dynamic-slice_fusion), channel_id=1, source_target_pairs={{0,1},{1,0},{2,3},{3,2},{4,5},{5,4},{6,7},{7,6},{8,9},{9,8},{10,11... | collective-permute-start | bytes 786440 | tf_op jit(solution)/shard_map/ppermute | solution.py:18
  31.1 12.9 %all-to-all-start.1 = ((f32[8,2,4096]{2,1,0:T(2,128)}), f32[8,2,4096]{2,1,0:T(2,128)S(1)}, u32[]{:S(2)}, u32[]{:S(2)}) async-start(f32[8,2,4096]{2,1,0:T(2,128)} %all_to_all.19), calls=%async_computation.1 | async-start | bytes 524288 | tf_op jit(solution)/shard_map/all_to_all | solution.py:127
  34.7 9.4 %collective-permute-start.2 = (f32[8,4096]{1,0:T(8,128)S(1)}, f32[8,4096]{1,0:T(8,128)S(1)}, u32[]{:S(2)}, u32[]{:S(2)}) collective-permute-start(f32[8,4096]{1,0:T(8,128)S(1)} %constant_dynamic-slice_fusion.1), channel_id=1, source_target_pairs={{0,1},{1,0},{2,3},{3,2},{4,5},{5,4},{6,7},{7,6},{8,9},{9,8},{10,11... | collective-permute-start | bytes 393224 | tf_op jit(solution)/shard_map/ppermute | solution.py:18

commit v2 on v1

--- a/solution.py
+++ b/solution.py
@@ -116,16 +116,19 @@
         owner_count * CAP, request_count
     )
     outgoing = jnp.dot(
-        selector.astype(jnp.bfloat16), normed, preferred_element_type=jnp.float32
+        selector.astype(jnp.bfloat16), scaled.astype(jnp.bfloat16), preferred_element_type=jnp.float32
     ).astype(jnp.bfloat16)
-    incoming = lax.all_to_all(outgoing, "rows", split_axis=0, concat_axis=0, tiled=True)
+    incoming_half = lax.all_to_all(outgoing, "rows", split_axis=0, concat_axis=0, tiled=True)
+    incoming = join_halves(incoming_half, myself)
     cold_part = swiglu_rows(incoming, cold_gate, cold_up, cold_down)
     selector_wide = selector.astype(jnp.float32)
     kept = lax.dynamic_slice_in_dim(cold_part, myself * half_width, half_width, 1)
     given = lax.dynamic_slice_in_dim(cold_part, (1 - myself) * half_width, half_width, 1)
     owner_sum = kept + partner(given, "heads", 0)
-    returned = lax.all_to_all(owner_sum, "rows", split_axis=0, concat_axis=0, tiled=True)
-    cold_sum = collect_rows(selector_wide, returned)
+    returned = lax.all_to_all(
+        owner_sum.astype(jnp.bfloat16), "rows", split_axis=0, concat_axis=0, tiled=True
+    )
+    cold_sum = collect_rows(selector_wide, returned.astype(jnp.float32))
     hot_kept = lax.dynamic_slice_in_dim(hot_part, myself * half_width, half_width, 1)
     hot_given = lax.dynamic_slice_in_dim(hot_part, (1 - myself) * half_width, half_width, 1)
     hot_total = hot_kept + partner(hot_given, "heads", 0)

time: 45.6 us -> 41.6 us (0.912)
  waiting for transfers between devices: 20.4 us -> 16 us
    all_to_all x1, waiting for transfers between devices: 9.17 us -> 7.27 us  [local(): lax.all_to_all(owner_sum.astype(jnp.bfloat16), 'rows', split_axis=0, conc...]
    all_to_all x1, waiting for transfers between devices: 8.91 us -> 7.34 us  [local(): lax.all_to_all(outgoing, 'rows', split_axis=0, concat_axis=0, tiled=True)]
    add x1 -> x0, other arithmetic: 0.98 us -> none  [local(): owner_sum = kept + partner(given, 'heads', 0)]
    convert_element_type x0 -> x1, other arithmetic: none -> 0.98 us  [local(): owner_sum.astype(jnp.bfloat16)]
    ppermute x4 -> x5, waiting for transfers between devices: 2.3 us -> 1.38 us  [partner(): return lax.ppermute(block, axis, route)]
    unnamed x20 -> x26, local copies, waits for them, and re-layouts: 1.24 us -> 1.92 us
    ppermute x4 -> x5, starting transfers between devices: 1.02 us -> 1.53 us  [partner(): return lax.ppermute(block, axis, route)]
  transfers between devices with their start and end apart: 6 -> 7, of which waited for: 5 -> 5; matrix products, arithmetic and copies ran while one was open for 3% -> 4% of each run, Pallas kernels for 0% -> 0%
where the time goes in v2:
time: 41.6 us; the launch traced here: 41.1 us
  waiting for transfers between devices  16 us (38%)
  starting transfers between devices  12 us (29%)
  matrix products  6.7 us (16%)
  local copies, waits for them, and re-layouts  3.59 us (9%)
  other arithmetic  2.54 us (6%)
    all_to_all x1, waiting for transfers between devices, local(): lax.all_to_all(outgoing, 'rows', split_axis=0, concat_axis=0, tiled=True)  7.34 us
    all_to_all x1, waiting for transfers between devices, local(): lax.all_to_all(owner_sum.astype(jnp.bfloat16), 'rows', split_axis=0, conc...  7.27 us
    all_to_all x1, starting transfers between devices, local(): lax.all_to_all(outgoing, 'rows', split_axis=0, concat_axis=0, tiled=True)  7.1 us
    all_to_all x1, starting transfers between devices, local(): lax.all_to_all(owner_sum.astype(jnp.bfloat16), 'rows', split_axis=0, conc...  3.37 us
    dot_general x2, matrix products, swiglu_rows(): return jnp.dot(hidden, down_rows, preferred_element_type=jnp.float32)  2.61 us
    unnamed x26, local copies, waits for them, and re-layouts  1.92 us
    ppermute x5, starting transfers between devices, partner(): return lax.ppermute(block, axis, route)  1.53 us
    ppermute x5, waiting for transfers between devices, partner(): return lax.ppermute(block, axis, route)  1.38 us
  transfers between devices with their start and end apart: 7, of which 5 were waited for; matrix products, arithmetic and copies ran while one was open for 4% of the time, Pallas kernels for 0%

profile of v2, /device:TPU:0, one launch (start us, length us, event | category | flops | bytes accessed | tf_op | source)
XLA Modules:
  0.0 41.1 jit_solution(6939378674509843968)
XLA Ops:
  0.0 0.0 copy-start
  0.0 0.0 copy-start.6
  0.0 0.8 %iota_compare_fusion = pred[8,32]{1,0:T(8,128)(4,1)S(1)} fusion(s32[8]{0:T(128)} %param.21), kind=kLoop, calls=%fused_computation.43 | loop fusion | flops 256 | bytes 288 | tf_op jit(solution)/shard_map/lt | solution.py:41
  0.8 1.0 %fusion.12 = f32[8,2,1,16]{3,2,1,0:T(1,128)S(1)} fusion(bf16[8,2,16,128]{3,0,2,1:T(8,128)(2,1)} %bitcast.28, bf16[8,2,128,1]{2,1,0,3:T(2,128)(2,1)} %bitcast.36), kind=kOutput, calls=%fused_computation.24 | convolution fusion | flops 65536 | bytes 70656 | tf_op jit(solution)/shard_map/rgjd,rgd->rgj/dot_general | solution.py:38
  1.8 0.0 copy-done.6
  1.8 1.2 %fusion.38 = (f32[8,2,16]{2,1,0:T(2,128)S(1)}, f32[8,2,16,32]{3,2,1,0:T(8,128)S(1)}) fusion(bf16[8,2,32,128]{3,2,1,0:T(8,128)(2,1)} %param.17, bf16[8,2,16,128]{3,0,2,1:T(8,128)(2,1)S(1)} %bitcast.29, pred[8,32]{1,0:T(8,128)(4,1)S(1)} %iota_compare_fusion), kind=kOutput, calls=%fused_computation.59 | convolution fusion | flops 2121472 | bytes 230656 | tf_op jit(solution)/shard_map/rgjd,rgpd->rgjp/dot_general | solution.py:34
  3.0 0.0 copy-start.12
  3.0 0.2 fusion.7
  3.3 0.0 copy-start.10
  3.3 0.7 %copy-done.10 = bf16[8,2,128]{2,1,0:T(2,128)(2,1)S(1)} copy-done((bf16[8,2,128]{2,1,0:T(2,128)(2,1)S(1)}, bf16[8,2,128]{2,1,0:T(2,128)(2,1)}, u32[]{:S(2)}) %copy-start.10) | copy-done | bytes 4120
  4.0 0.0 copy-done.12
  4.0 0.0 copy-start.7
  4.0 0.0 copy-start.8
  4.0 0.0 copy-start.9
  4.0 0.3 convolution_add_fusion
  4.2 0.0 copy-start.1
  4.3 0.5 %copy-done.7 = bf16[8,4096]{1,0:T(8,128)(2,1)S(1)} copy-done((bf16[8,4096]{1,0:T(8,128)(2,1)S(1)}, bf16[8,4096]{1,0:T(8,128)(2,1)}, u32[]{:S(2)}) %copy-start.7) | copy-done | bytes 65560
  4.8 0.2 fusion.1
  5.0 0.5 %collective-permute-start = (f32[8]{0:T(128)S(1)}, f32[8]{0:T(128)S(1)}, u32[]{:S(2)}, u32[]{:S(2)}) collective-permute-start(f32[8]{0:T(128)S(1)} %get-tuple-element.5), channel_id=1, source_target_pairs={{0,1},{1,0},{2,3},{3,2},{4,5},{5,4},{6,7},{7,6},{8,9},{9,8},{10,11... | collective-permute-start | bytes 104 | tf_op jit(solution)/shard_map/ppermute | solution.py:18
  5.5 0.0 copy-done.8
  5.5 0.2 reduce_window_sum.11
  5.7 0.0 copy-done.9
  5.7 0.6 %collective-permute-done = f32[8]{0:T(128)S(1)} collective-permute-done((f32[8]{0:T(128)S(1)}, f32[8]{0:T(128)S(1)}, u32[]{:S(2)}, u32[]{:S(2)}) %collective-permute-start) | collective-permute-done | bytes 64 | tf_op jit(solution)/shard_map/ppermute | solution.py:18
  6.3 0.1 fusion.3
  6.4 0.2 convolution_convert_fusion
  6.6 0.8 %all_to_all.16 = bf16[8,2,4096]{2,1,0:T(2,128)(2,1)} reshape(bf16[16,4096]{1,0:T(8,128)(2,1)S(1)} %convolution_convert_fusion) | data formatting | bytes 262144 | tf_op jit(solution)/shard_map/all_to_all | solution.py:121
  7.4 7.1 %all-to-all-start = ((bf16[8,2,4096]{2,1,0:T(2,128)(2,1)}), bf16[8,2,4096]{2,1,0:T(2,128)(2,1)S(1)}, u32[]{:S(2)}, u32[]{:S(2)}) async-start(bf16[8,2,4096]{2,1,0:T(2,128)(2,1)} %all_to_all.16), calls=%async_computation | async-start | bytes 262144 | tf_op jit(solution)/shard_map/all_to_all | solution.py:121
  14.5 0.0 collective-permute-start.1
  14.5 7.3 %all-to-all-done = bf16[8,2,4096]{2,1,0:T(2,128)(2,1)S(1)} async-done(((bf16[8,2,4096]{2,1,0:T(2,128)(2,1)}), bf16[8,2,4096]{2,1,0:T(2,128)(2,1)S(1)}, u32[]{:S(2)}, u32[]{:S(2)}) %all-to-all-start) | async-done | bytes 131104 | tf_op jit(solution)/shard_map/all_to_all | solution.py:121
  21.8 0.1 all_to_all.18
  21.9 0.0 copy-start.11
  21.9 0.1 collective-permute-start.3
  22.0 0.0 collective-permute-done.1
  22.0 0.0 copy-done.1
  22.0 0.0 copy-start.4
  22.0 0.4 fusion.17
  22.4 0.2 copy-done.4
  22.6 0.0 copy-start.3
  22.6 0.7 %collective-permute-done.3 = bf16[16,4096]{1,0:T(8,128)(2,1)S(1)} collective-permute-done((bf16[16,4096]{1,0:T(8,128)(2,1)S(1)}, bf16[16,4096]{1,0:T(8,128)(2,1)S(1)}, u32[]{:S(2)}, u32[]{:S(2)}) %collective-permute-start.3) | collective-permute-done | bytes 131104 | tf_op jit(solution)/shard_map/ppermute | solution.py:18
  23.3 0.0 copy-done.11
  23.3 0.2 fusion.15
  23.5 0.1 copy-done.3
  23.7 0.0 copy-start.2
  23.7 1.7 %fusion.20 = f32[16,8192]{1,0:T(8,128)S(1)} fusion(bf16[32,8192]{1,0:T(8,128)(2,1)S(1)} %copy-done.3, f32[16,32]{1,0:T(8,128)S(1)} %fusion.15, bf16[32,8192]{1,0:T(8,128)(2,1)} %param.26, bf16[16,4096]{1,0:T(8,128)(2,1)S(1)} %collective-permute-done.3, bf16[16,4096]{1,0:T(8,128)(2,1)S(1)} %all_to_all.18, pred[]{:T(512)S(6)} %eq.8), kind=kOutput, calls=%fused_computation.38 | convolution fusion | flops 17959936 | bytes 1837057 | tf_op jit(solution)/shard_map/dot_general | solution.py:65
  25.4 0.0 copy-start.5
  25.5 0.5 %collective-permute-start.4 = (f32[16,4096]{1,0:T(8,128)S(1)}, f32[16,4096]{1,0:T(8,128)}, u32[]{:S(2)}, u32[]{:S(2)}) collective-permute-start(f32[16,4096]{1,0:T(8,128)S(1)} %constant_dynamic-slice_fusion), channel_id=1, source_target_pairs={{0,1},{1,0},{2,3},{3,2},{4,5},{5,4},{6,7},{7,6},{8,9},{9,8},{10,11... | collective-permute-start | bytes 786440 | tf_op jit(solution)/shard_map/ppermute | solution.py:18
  26.0 0.0 copy-done
  26.0 0.0 copy-done.2
  26.0 0.3 copy-done.5
  26.3 0.9 %fusion.25 = f32[8,8192]{1,0:T(8,128)S(1)} fusion(bf16[64,8192]{1,0:T(8,128)(2,1)S(1)} %copy-done, f32[8,64]{1,0:T(8,128)S(1)} %fusion.17, bf16[64,8192]{1,0:T(8,128)(2,1)S(1)} %copy-done.2, bf16[8,4096]{1,0:T(8,128)(2,1)S(1)} %copy-done.5, bf16[8,4096]{1,0:T(8,128)(2,1)S(1)} %fusion.3, pred[]{:T(512)S(6)} %eq.8), kind=kOutput, calls=%fused_computation.45 | convolution fusion | flops 17370112 | bytes 2492417 | tf_op jit(solution)/shard_map/dot_general | solution.py:65
  27.2 0.1 collective-permute-done.4
  27.3 1.0 %add_convert_fusion = bf16[16,4096]{1,0:T(8,128)(2,1)S(1)} fusion(f32[16,4096]{1,0:T(8,128)} %collective-permute-done.4, f32[16,8192]{1,0:T(8,128)S(1)} %fusion.20, s32[]{:T(128)S(6)} %select_n.35), kind=kLoop, calls=%fused_computation.5 | loop fusion | flops 131072 | bytes 655364 | tf_op jit(solution)/shard_map/convert_element_type | solution.py:129
  28.2 0.8 %all_to_all.19 = bf16[8,2,4096]{2,1,0:T(2,128)(2,1)} reshape(bf16[16,4096]{1,0:T(8,128)(2,1)S(1)} %add_convert_fusion) | data formatting | bytes 262144 | tf_op jit(solution)/shard_map/all_to_all | solution.py:128
  29.0 3.4 %all-to-all-start.1 = ((bf16[8,2,4096]{2,1,0:T(2,128)(2,1)}), bf16[8,2,4096]{2,1,0:T(2,128)(2,1)S(1)}, u32[]{:S(2)}, u32[]{:S(2)}) async-start(bf16[8,2,4096]{2,1,0:T(2,128)(2,1)} %all_to_all.19), calls=%async_computation.1 | async-start | bytes 262144 | tf_op jit(solution)/shard_map/all_to_all | solution.py:128
  32.4 0.4 %collective-permute-start.2 = (f32[8,4096]{1,0:T(8,128)S(1)}, f32[8,4096]{1,0:T(8,128)S(1)}, u32[]{:S(2)}, u32[]{:S(2)}) collective-permute-start(f32[8,4096]{1,0:T(8,128)S(1)} %constant_dynamic-slice_fusion.1), channel_id=1, source_target_pairs={{0,1},{1,0},{2,3},{3,2},{4,5},{5,4},{6,7},{7,6},{8,9},{9,8},{10,11... | collective-permute-start | bytes 393224 | tf_op jit(solution)/shard_map/ppermute | solution.py:18
  32.8 7.3 %all-to-all-done.1 = bf16[8,2,4096]{2,1,0:T(2,128)(2,1)S(1)} async-done(((bf16[8,2,4096]{2,1,0:T(2,128)(2,1)}), bf16[8,2,4096]{2,1,0:T(2,128)(2,1)S(1)}, u32[]{:S(2)}, u32[]{:S(2)}) %all-to-all-start.1) | async-done | bytes 131104 | tf_op jit(solution)/shard_map/all_to_all | solution.py:128
  40.1 0.1 all_to_all.21
  40.2 0.0 collective-permute-done.2
  40.2 0.9 %fusion.5 = bf16[8,4096]{1,0:T(8,128)(2,1)} fusion(bf16[8,4096]{1,0:T(8,128)(2,1)S(1)} %get-tuple-element.6, f32[8,4096]{1,0:T(8,128)S(1)} %collective-permute-done.2, f32[8,8192]{1,0:T(8,128)S(1)} %fusion.25, s32[]{:T(128)S(6)} %select_n.35, f32[16,8]{1,0:T(8,128)S(1)} %bitcast.30, bf16[16,4096]{1,0:T(8,128)(2,1)S(1)} %all_to_all.21), kind=kOutput, calls=%fused_computation.13 | convolution fusion | flops 6455296 | bytes 524804 | tf_op jit(solution)/shard_map/dot_general | solution.py:69
  (11 shorter events, 0.1 us)
Async XLA Ops:
  0.0 26.0 %copy-start = (bf16[64,8192]{1,0:T(8,128)(2,1)S(1)}, bf16[64,8192]{1,0:T(8,128)(2,1)}, u32[]{:S(2)}) copy-start(bf16[64,8192]{1,0:T(8,128)(2,1)} %param.25) | copy-start | bytes 3145732
  0.0 1.8 %copy-start.6 = (bf16[8,4096]{1,0:T(8,128)(2,1)S(1)}, bf16[8,4096]{1,0:T(8,128)(2,1)}, u32[]{:S(2)}) copy-start(bf16[8,4096]{1,0:T(8,128)(2,1)} %param.16) | copy-start | bytes 196612
  3.0 1.0 %copy-start.12 = (bf16[8,2,32,128]{3,2,1,0:T(8,128)(2,1)S(1)}, bf16[8,2,32,128]{3,2,1,0:T(8,128)(2,1)}, u32[]{:S(2)}) copy-start(bf16[8,2,32,128]{3,2,1,0:T(8,128)(2,1)} %param.18) | copy-start | bytes 393220
  3.3 0.7 %copy-start.10 = (bf16[8,2,128]{2,1,0:T(2,128)(2,1)S(1)}, bf16[8,2,128]{2,1,0:T(2,128)(2,1)}, u32[]{:S(2)}) copy-start(bf16[8,2,128]{2,1,0:T(2,128)(2,1)} %param.20) | copy-start | bytes 12292
  4.0 0.8 %copy-start.7 = (bf16[8,4096]{1,0:T(8,128)(2,1)S(1)}, bf16[8,4096]{1,0:T(8,128)(2,1)}, u32[]{:S(2)}) copy-start(bf16[8,4096]{1,0:T(8,128)(2,1)} %param.15) | copy-start | bytes 196612
  4.0 1.5 %copy-start.8 = (s32[8,4]{0,1:T(4,128)S(1)}, s32[8,4]{0,1:T(4,128)}, u32[]{:S(2)}) copy-start(s32[8,4]{0,1:T(4,128)} %param.29) | copy-start | bytes 388
  4.0 1.7 %copy-start.9 = (bf16[8192]{0:T(1024)(128)(2,1)S(1)}, bf16[8192]{0:T(1024)(128)(2,1)}, u32[]{:S(2)}) copy-start(bf16[8192]{0:T(1024)(128)(2,1)} %param.22) | copy-start | bytes 49156
  4.2 17.7 %copy-start.1 = (bf16[64,8192]{1,0:T(8,128)(2,1)S(1)}, bf16[64,8192]{1,0:T(8,128)(2,1)}, u32[]{:S(2)}) copy-start(bf16[64,8192]{1,0:T(8,128)(2,1)} %param.24) | copy-start | bytes 3145732
  5.0 1.3 %collective-permute-start = (f32[8]{0:T(128)S(1)}, f32[8]{0:T(128)S(1)}, u32[]{:S(2)}, u32[]{:S(2)}) collective-permute-start(f32[8]{0:T(128)S(1)} %get-tuple-element.5), channel_id=1, source_target_pairs={{0,1},{1,0},{2,3},{3,2},{4,5},{5,4},{6,7},{7,6},{8,9},{9,8},{10,11... | collective-permute-start | bytes 104 | tf_op jit(solution)/shard_map/ppermute | solution.py:18
  7.4 14.5 %all-to-all-start = ((bf16[8,2,4096]{2,1,0:T(2,128)(2,1)}), bf16[8,2,4096]{2,1,0:T(2,128)(2,1)S(1)}, u32[]{:S(2)}, u32[]{:S(2)}) async-start(bf16[8,2,4096]{2,1,0:T(2,128)(2,1)} %all_to_all.16), calls=%async_computation | async-start | bytes 262144 | tf_op jit(solution)/shard_map/all_to_all | solution.py:121
  14.5 7.5 %collective-permute-start.1 = (bf16[8,4096]{1,0:T(8,128)(2,1)S(1)}, bf16[8,4096]{1,0:T(8,128)(2,1)S(1)}, u32[]{:S(2)}, u32[]{:S(2)}) collective-permute-start(bf16[8,4096]{1,0:T(8,128)(2,1)S(1)} %fusion.3), channel_id=1, source_target_pairs={{0,1},{1,0},{2,3},{3,2},{4,5},{5,4},{6,7},{7,6},{8,9},{9,8},{10,11... | collective-permute-start | bytes 196616 | tf_op jit(solution)/shard_map/ppermute | solution.py:18
  21.9 1.4 %copy-start.11 = (bf16[32,8192]{1,0:T(8,128)(2,1)S(1)}, bf16[32,8192]{1,0:T(8,128)(2,1)}, u32[]{:S(2)}) copy-start(bf16[32,8192]{1,0:T(8,128)(2,1)} %param.27) | copy-start | bytes 1572868
  21.9 1.4 %collective-permute-start.3 = (bf16[16,4096]{1,0:T(8,128)(2,1)S(1)}, bf16[16,4096]{1,0:T(8,128)(2,1)S(1)}, u32[]{:S(2)}, u32[]{:S(2)}) collective-permute-start(bf16[16,4096]{1,0:T(8,128)(2,1)S(1)} %all_to_all.18), channel_id=1, source_target_pairs={{0,1},{1,0},{2,3},{3,2},{4,5},{5,4},{6,7},{7,6},{8,9},{9,8},{10,11... | collective-permute-start | bytes 393224 | tf_op jit(solution)/shard_map/ppermute | solution.py:18
  22.0 0.6 %copy-start.4 = (bf16[8,4096]{1,0:T(8,128)(2,1)}, bf16[8,4096]{1,0:T(8,128)(2,1)S(1)}, u32[]{:S(2)}) copy-start(bf16[8,4096]{1,0:T(8,128)(2,1)S(1)} %collective-permute-done.1) | copy-start | bytes 196612
  22.6 1.1 %copy-start.3 = (bf16[32,8192]{1,0:T(8,128)(2,1)S(1)}, bf16[32,8192]{1,0:T(8,128)(2,1)}, u32[]{:S(2)}) copy-start(bf16[32,8192]{1,0:T(8,128)(2,1)} %param.28) | copy-start | bytes 1572868
  23.7 2.3 %copy-start.2 = (bf16[64,8192]{1,0:T(8,128)(2,1)S(1)}, bf16[64,8192]{1,0:T(8,128)(2,1)}, u32[]{:S(2)}) copy-start(bf16[64,8192]{1,0:T(8,128)(2,1)} %param.23) | copy-start | bytes 3145732
  25.4 0.8 %copy-start.5 = (bf16[8,4096]{1,0:T(8,128)(2,1)S(1)}, bf16[8,4096]{1,0:T(8,128)(2,1)}, u32[]{:S(2)}) copy-start(bf16[8,4096]{1,0:T(8,128)(2,1)} %copy-done.4) | copy-start | bytes 196612
  25.5 1.8 %collective-permute-start.4 = (f32[16,4096]{1,0:T(8,128)S(1)}, f32[16,4096]{1,0:T(8,128)}, u32[]{:S(2)}, u32[]{:S(2)}) collective-permute-start(f32[16,4096]{1,0:T(8,128)S(1)} %constant_dynamic-slice_fusion), channel_id=1, source_target_pairs={{0,1},{1,0},{2,3},{3,2},{4,5},{5,4},{6,7},{7,6},{8,9},{9,8},{10,11... | collective-permute-start | bytes 786440 | tf_op jit(solution)/shard_map/ppermute | solution.py:18
  29.0 11.1 %all-to-all-start.1 = ((bf16[8,2,4096]{2,1,0:T(2,128)(2,1)}), bf16[8,2,4096]{2,1,0:T(2,128)(2,1)S(1)}, u32[]{:S(2)}, u32[]{:S(2)}) async-start(bf16[8,2,4096]{2,1,0:T(2,128)(2,1)} %all_to_all.19), calls=%async_computation.1 | async-start | bytes 262144 | tf_op jit(solution)/shard_map/all_to_all | solution.py:128
  32.4 7.8 %collective-permute-start.2 = (f32[8,4096]{1,0:T(8,128)S(1)}, f32[8,4096]{1,0:T(8,128)S(1)}, u32[]{:S(2)}, u32[]{:S(2)}) collective-permute-start(f32[8,4096]{1,0:T(8,128)S(1)} %constant_dynamic-slice_fusion.1), channel_id=1, source_target_pairs={{0,1},{1,0},{2,3},{3,2},{4,5},{5,4},{6,7},{7,6},{8,9},{9,8},{10,11... | collective-permute-start | bytes 393224 | tf_op jit(solution)/shard_map/ppermute | solution.py:18

commit v3 on v2

--- a/solution.py
+++ b/solution.py
@@ -65,6 +65,18 @@
     return jnp.dot(hidden, down_rows, preferred_element_type=jnp.float32)
 
 
+def swiglu_halves(normed, gate_rows, up_rows, down_rows, myself):
+    gate = jnp.einsum("rd,nd->rn", normed, gate_rows, preferred_element_type=jnp.float32)
+    upper = jnp.einsum("rd,nd->rn", normed, up_rows, preferred_element_type=jnp.float32)
+    hidden = (jax.nn.silu(gate) * upper).astype(jnp.bfloat16)
+    half_width = down_rows.shape[1] // 2
+    down_given = lax.dynamic_slice_in_dim(down_rows, (1 - myself) * half_width, half_width, 1)
+    down_kept = lax.dynamic_slice_in_dim(down_rows, myself * half_width, half_width, 1)
+    given = jnp.dot(hidden, down_given, preferred_element_type=jnp.float32)
+    kept = jnp.dot(hidden, down_kept, preferred_element_type=jnp.float32)
+    return kept, given
+
+
 def collect_rows(selector, returned):
     return lax.dot_general(
         selector,
@@ -104,7 +116,6 @@
         local_wide * lax.rsqrt(square_total / D + 1e-05)[:, None] * gain_half.astype(jnp.float32)
     )
     normed = join_halves(scaled.astype(jnp.bfloat16), myself)
-    hot_part = swiglu_rows(normed, hot_gate, hot_up, hot_down)
     owner_count = lax.axis_size("rows")
     block_count = active.shape[1]
     request_count = active.shape[0]
@@ -112,26 +123,28 @@
     earlier = jnp.cumsum(by_block, axis=1) - by_block
     slot_ids = jnp.arange(CAP, dtype=jnp.int32)[None, :, None]
     slot_table = by_block[:, None, :] * (earlier[:, None, :] == slot_ids).astype(jnp.int32)
-    selector = jnp.repeat(slot_table, owner_count // block_count, axis=0).reshape(
-        owner_count * CAP, request_count
-    )
-    outgoing = jnp.dot(
-        selector.astype(jnp.bfloat16), scaled.astype(jnp.bfloat16), preferred_element_type=jnp.float32
+    selector3 = jnp.repeat(slot_table, owner_count // block_count, axis=0)
+    selector = selector3.reshape(owner_count * CAP, request_count)
+    outgoing = jnp.einsum(
+        "ocr,rd->ocd",
+        selector3.astype(jnp.bfloat16),
+        scaled.astype(jnp.bfloat16),
+        preferred_element_type=jnp.float32,
     ).astype(jnp.bfloat16)
     incoming_half = lax.all_to_all(outgoing, "rows", split_axis=0, concat_axis=0, tiled=True)
-    incoming = join_halves(incoming_half, myself)
-    cold_part = swiglu_rows(incoming, cold_gate, cold_up, cold_down)
-    selector_wide = selector.astype(jnp.float32)
-    kept = lax.dynamic_slice_in_dim(cold_part, myself * half_width, half_width, 1)
-    given = lax.dynamic_slice_in_dim(cold_part, (1 - myself) * half_width, half_width, 1)
-    owner_sum = kept + partner(given, "heads", 0)
+    incoming = join_halves(incoming_half.reshape(owner_count * CAP, -1), myself)
+    kept, given = swiglu_halves(incoming, cold_gate, cold_up, cold_down, myself)
+    owner_sum = (kept + partner(given, "heads", 0)).astype(jnp.bfloat16)
+    normed_late, owner_sum = lax.optimization_barrier((normed, owner_sum))
     returned = lax.all_to_all(
-        owner_sum.astype(jnp.bfloat16), "rows", split_axis=0, concat_axis=0, tiled=True
+        owner_sum.reshape(owner_count, CAP, -1), "rows", split_axis=0, concat_axis=0, tiled=True
     )
-    cold_sum = collect_rows(selector_wide, returned.astype(jnp.float32))
-    hot_kept = lax.dynamic_slice_in_dim(hot_part, myself * half_width, half_width, 1)
-    hot_given = lax.dynamic_slice_in_dim(hot_part, (1 - myself) * half_width, half_width, 1)
+    hot_kept, hot_given = swiglu_halves(normed_late, hot_gate, hot_up, hot_down, myself)
     hot_total = hot_kept + partner(hot_given, "heads", 0)
+    cold_sum = collect_rows(
+        selector.astype(jnp.float32),
+        returned.reshape(owner_count * CAP, -1).astype(jnp.float32),
+    )
     result = stream.astype(jnp.float32) + hot_total + cold_sum
     return result.astype(jnp.bfloat16)
 

time: 41.6 us -> 39.1 us (0.940)
  blocking collectives: 0 us -> 14.3 us
  waiting for transfers between devices: 16 us -> 8.52 us
  starting transfers between devices: 12 us -> 4.84 us
  matrix products: 6.7 us -> 5.45 us
  other arithmetic: 2.54 us -> 1.59 us
    all_to_all x0 -> x1, blocking collectives: none -> 14.3 us  [local(): lax.all_to_all(outgoing, 'rows', split_axis=0, concat_axis=0, tiled=True)]
    all_to_all x2 -> x1, waiting for transfers between devices: 14.6 us -> 6.34 us  [local(): lax.all_to_all(owner_sum.reshape(owner_count, CAP, -1), 'rows', split_axi...]
    all_to_all x2 -> x1, starting transfers between devices: 10.5 us -> 3.37 us  [local(): lax.all_to_all(owner_sum.reshape(owner_count, CAP, -1), 'rows', split_axi...]
    all_to_all x4 -> x0, local copies, waits for them, and re-layouts: 1.61 us -> none  [the longest x2 0.81 us: local(): lax.all_to_all(outgoing, 'rows', split_axis=0, concat_axis=0, tiled=True)]
    convert_element_type x2 -> x1, other arithmetic: 0.99 us -> 0.01 us  [local(): selector3.astype(jnp.bfloat16)]
    reshape x0 -> x3, local copies, waits for them, and re-layouts: none -> 0.84 us  [the longest x1 0.74 us: local(): owner_sum.reshape(owner_count, CAP, -1)]
    unnamed x26 -> x24, local copies, waits for them, and re-layouts: 1.92 us -> 2.74 us
    ppermute x5, waiting for transfers between devices: 1.38 us -> 2.18 us  [partner(): return lax.ppermute(block, axis, route)]
  transfers between devices with their start and end apart: 7 -> 6, of which waited for: 5 -> 3; matrix products, arithmetic and copies ran while one was open for 4% -> 6% of each run, Pallas kernels for 0% -> 0%
where the time goes in v3:
time: 39.1 us; the launch traced here: 38.6 us
  blocking collectives  14.3 us (37%)
  waiting for transfers between devices  8.52 us (22%)
  matrix products  5.45 us (14%)
  starting transfers between devices  4.84 us (12%)
  local copies, waits for them, and re-layouts  3.73 us (10%)
  other arithmetic  1.59 us (4%)
    all_to_all x1, blocking collectives, local(): lax.all_to_all(outgoing, 'rows', split_axis=0, concat_axis=0, tiled=True)  14.3 us
    all_to_all x1, waiting for transfers between devices, local(): lax.all_to_all(owner_sum.reshape(owner_count, CAP, -1), 'rows', split_axi...  6.34 us
    all_to_all x1, starting transfers between devices, local(): lax.all_to_all(owner_sum.reshape(owner_count, CAP, -1), 'rows', split_axi...  3.37 us
    unnamed x24, local copies, waits for them, and re-layouts  2.74 us
    ppermute x5, waiting for transfers between devices, partner(): return lax.ppermute(block, axis, route)  2.18 us
    ppermute x5, starting transfers between devices, partner(): return lax.ppermute(block, axis, route)  1.47 us
    dot_general x1, matrix products, attention_rows(): jnp.einsum('rgjd,rgpd->rgjp', queries, key_cache, preferred_element_type=...  1.17 us
    dot_general x2, matrix products, swiglu_halves(): kept = jnp.dot(hidden, down_kept, preferred_element_type=jnp.float32)  0.99 us
  transfers between devices with their start and end apart: 6, of which 3 were waited for; matrix products, arithmetic and copies ran while one was open for 6% of the time, Pallas kernels for 0%

profile of v3, /device:TPU:0, one launch (start us, length us, event | category | flops | bytes accessed | tf_op | source)
XLA Modules:
  0.0 38.6 jit_solution(11669067823365061986)
XLA Ops:
  0.0 0.0 copy-start
  0.0 0.0 copy-start.4
  0.0 0.8 %iota_compare_fusion = pred[8,32]{1,0:T(8,128)(4,1)S(1)} fusion(s32[8]{0:T(128)} %param.21), kind=kLoop, calls=%fused_computation.49 | loop fusion | flops 256 | bytes 288 | tf_op jit(solution)/shard_map/lt | solution.py:41
  0.8 1.0 %fusion.22 = f32[8,2,1,16]{3,2,1,0:T(1,128)S(1)} fusion(bf16[8,2,16,128]{3,0,2,1:T(8,128)(2,1)} %bitcast.34, bf16[8,2,128,1]{2,1,0,3:T(2,128)(2,1)} %bitcast.42), kind=kOutput, calls=%fused_computation.35 | convolution fusion | flops 65536 | bytes 70656 | tf_op jit(solution)/shard_map/rgjd,rgd->rgj/dot_general | solution.py:38
  1.8 0.0 copy-done.4
  1.8 1.2 %fusion.40 = (f32[8,2,16]{2,1,0:T(2,128)S(1)}, f32[8,2,16,32]{3,2,1,0:T(8,128)S(1)}) fusion(bf16[8,2,32,128]{3,2,1,0:T(8,128)(2,1)} %param.17, bf16[8,2,16,128]{3,0,2,1:T(8,128)(2,1)S(1)} %bitcast.35, pred[8,32]{1,0:T(8,128)(4,1)S(1)} %iota_compare_fusion), kind=kOutput, calls=%fused_computation.61 | convolution fusion | flops 2121472 | bytes 230656 | tf_op jit(solution)/shard_map/rgjd,rgpd->rgjp/dot_general | solution.py:34
  3.0 0.0 copy-start.11
  3.0 0.2 fusion.16
  3.3 0.0 copy-start.8
  3.3 0.7 %copy-done.8 = bf16[8,2,128]{2,1,0:T(2,128)(2,1)S(1)} copy-done((bf16[8,2,128]{2,1,0:T(2,128)(2,1)S(1)}, bf16[8,2,128]{2,1,0:T(2,128)(2,1)}, u32[]{:S(2)}) %copy-start.8) | copy-done | bytes 4120
  4.0 0.0 copy-done.11
  4.0 0.0 copy-start.5
  4.0 0.3 convolution_add_fusion.2
  4.2 0.6 %copy-done.5 = bf16[8,4096]{1,0:T(8,128)(2,1)S(1)} copy-done((bf16[8,4096]{1,0:T(8,128)(2,1)S(1)}, bf16[8,4096]{1,0:T(8,128)(2,1)}, u32[]{:S(2)}) %copy-start.5) | copy-done | bytes 65560
  4.8 0.2 fusion.12
  5.0 0.5 %collective-permute-start = (f32[8]{0:T(128)S(1)}, f32[8]{0:T(128)S(1)}, u32[]{:S(2)}, u32[]{:S(2)}) collective-permute-start(f32[8]{0:T(128)S(1)} %get-tuple-element.9), channel_id=1, source_target_pairs={{0,1},{1,0},{2,3},{3,2},{4,5},{5,4},{6,7},{7,6},{8,9},{9,8},{10,11... | collective-permute-start | bytes 104 | tf_op jit(solution)/shard_map/ppermute | solution.py:18
  5.5 0.0 copy-start.6
  5.5 0.0 copy-start.7
  5.5 0.7 %copy-done.6 = s32[8,4]{0,1:T(4,128)S(1)} copy-done((s32[8,4]{0,1:T(4,128)S(1)}, s32[8,4]{0,1:T(4,128)}, u32[]{:S(2)}) %copy-start.6) | copy-done | bytes 152
  6.2 0.2 reduce_window_sum.11
  6.4 0.0 copy-done.7
  6.4 0.0 collective-permute-done
  6.4 0.1 fusion.14
  6.5 0.0 copy-start.9
  6.6 0.2 convolution_convert_fusion
  6.7 0.1 copy.23
  6.9 14.3 %all_to_all.10 = bf16[8,2,4096]{2,1,0:T(2,128)(2,1)S(1)} all-to-all(bf16[8,2,4096]{2,1,0:T(2,128)(2,1)S(1)} %copy.23), channel_id=1, replica_groups=mesh['groups'=2,'rows'=8,'heads'=2] {'rows'}, dimensions={0} | all-to-all | bytes 262144 | tf_op jit(solution)/shard_map/all_to_all | solution.py:134
  21.1 0.1 reshape.45
  21.2 0.1 collective-permute-start.2
  21.3 0.0 copy-start.10
  21.3 0.5 %collective-permute-start.1 = (bf16[8,4096]{1,0:T(8,128)(2,1)S(1)}, bf16[8,4096]{1,0:T(8,128)(2,1)S(1)}, u32[]{:S(2)}, u32[]{:S(2)}) collective-permute-start(bf16[8,4096]{1,0:T(8,128)(2,1)S(1)} %fusion.14), channel_id=1, source_target_pairs={{0,1},{1,0},{2,3},{3,2},{4,5},{5,4},{6,7},{7,6},{8,9},{9,8},{10,11... | collective-permute-start | bytes 196616 | tf_op jit(solution)/shard_map/ppermute | solution.py:18
  21.7 0.8 %collective-permute-done.2 = bf16[16,4096]{1,0:T(8,128)(2,1)S(1)} collective-permute-done((bf16[16,4096]{1,0:T(8,128)(2,1)S(1)}, bf16[16,4096]{1,0:T(8,128)(2,1)S(1)}, u32[]{:S(2)}, u32[]{:S(2)}) %collective-permute-start.2) | collective-permute-done | bytes 131104 | tf_op jit(solution)/shard_map/ppermute | solution.py:18
  22.6 0.0 copy-done.9
  22.6 0.2 fusion.26
  22.8 0.0 copy-done.10
  22.8 0.0 copy-start.3
  22.8 0.3 multiply_convert_fusion
  23.1 0.8 %copy-done.3 = bf16[32,8192]{1,0:T(8,128)(2,1)S(1)} copy-done((bf16[32,8192]{1,0:T(8,128)(2,1)S(1)}, bf16[32,8192]{1,0:T(8,128)(2,1)}, u32[]{:S(2)}) %copy-start.3) | copy-done | bytes 524312
  23.9 0.0 copy-start.1
  23.9 0.2 fusion.9
  24.1 0.2 collective-permute-start.3
  24.3 0.0 collective-permute-done.1
  24.3 0.0 copy-start.2
  24.3 1.3 %collective-permute-done.3 = f32[16,4096]{1,0:T(8,128)S(1)} collective-permute-done((f32[16,4096]{1,0:T(8,128)S(1)}, f32[16,4096]{1,0:T(8,128)S(1)}, u32[]{:S(2)}, u32[]{:S(2)}) %collective-permute-start.3) | collective-permute-done | bytes 262176 | tf_op jit(solution)/shard_map/ppermute | solution.py:18
  25.7 0.2 fusion
  25.8 0.7 %reshape.46 = bf16[8,2,4096]{2,1,0:T(2,128)(2,1)} reshape(bf16[16,4096]{1,0:T(8,128)(2,1)S(1)} %fusion) | data formatting | bytes 262144 | tf_op jit(solution)/shard_map/reshape | solution.py:140
  26.6 3.4 %all-to-all-start.1 = ((bf16[8,2,4096]{2,1,0:T(2,128)(2,1)}), bf16[8,2,4096]{2,1,0:T(2,128)(2,1)S(1)}, u32[]{:S(2)}, u32[]{:S(2)}) async-start(bf16[8,2,4096]{2,1,0:T(2,128)(2,1)} %reshape.46), calls=%async_computation.1 | async-start | bytes 262144 | tf_op jit(solution)/shard_map/all_to_all | solution.py:139
  30.0 0.0 copy-done.1
  30.0 0.4 fusion.41
  30.3 0.0 copy-done.2
  30.3 0.4 %fusion.5 = bf16[8,64]{1,0:T(8,128)(2,1)S(1)} fusion(bf16[8,8192]{1,0:T(8,128)(2,1)S(1)} %maximum_select_fusion.1, bf16[64,8192]{1,0:T(8,128)(2,1)S(1)} %copy-done.2, f32[8,64]{1,0:T(8,128)S(1)} %fusion.41), kind=kOutput, calls=%fused_computation.11 | convolution fusion | flops 8391680 | bytes 1182720 | tf_op jit(solution)/shard_map/rd,nd->rn/dot_general | solution.py:70
  30.7 0.0 copy-done
  30.7 0.2 fusion.6
  30.9 0.2 collective-permute-start.4
  31.1 6.3 %all-to-all-done.1 = bf16[8,2,4096]{2,1,0:T(2,128)(2,1)S(1)} async-done(((bf16[8,2,4096]{2,1,0:T(2,128)(2,1)}), bf16[8,2,4096]{2,1,0:T(2,128)(2,1)S(1)}, u32[]{:S(2)}, u32[]{:S(2)}) %all-to-all-start.1) | async-done | bytes 131104 | tf_op jit(solution)/shard_map/all_to_all | solution.py:139
  37.5 0.1 reshape.47
  37.5 0.3 fusion.42
  37.8 0.0 collective-permute-done.4
  37.8 0.8 %fusion.3 = bf16[8,4096]{1,0:T(8,128)(2,1)} fusion(f32[8,4096]{1,0:T(8,128)S(1)} %fusion.42, f32[8,4096]{1,0:T(8,128)S(1)} %collective-permute-done.4, bf16[8,64]{1,0:T(8,128)(2,1)S(1)} %fusion.5, bf16[64,8192]{1,0:T(8,128)(2,1)S(1)} %copy-done, s32[]{:T(128)S(6)} %select_n.35, bf16[8,4096]{1,0:T(8,128)(2,1)S(1)} %get-tuple-element.10), kind=kOutput, calls=%fused_computation.6 | convolution fusion | flops 4358144 | bytes 919556 | tf_op jit(solution)/shard_map/dot_general | solution.py:76
  (11 shorter events, 0.1 us)
Async XLA Ops:
  0.0 30.7 %copy-start = (bf16[64,8192]{1,0:T(8,128)(2,1)S(1)}, bf16[64,8192]{1,0:T(8,128)(2,1)}, u32[]{:S(2)}) copy-start(bf16[64,8192]{1,0:T(8,128)(2,1)} %param.25) | copy-start | bytes 3145732
  0.0 1.8 %copy-start.4 = (bf16[8,4096]{1,0:T(8,128)(2,1)S(1)}, bf16[8,4096]{1,0:T(8,128)(2,1)}, u32[]{:S(2)}) copy-start(bf16[8,4096]{1,0:T(8,128)(2,1)} %param.16) | copy-start | bytes 196612
  3.0 1.0 %copy-start.11 = (bf16[8,2,32,128]{3,2,1,0:T(8,128)(2,1)S(1)}, bf16[8,2,32,128]{3,2,1,0:T(8,128)(2,1)}, u32[]{:S(2)}) copy-start(bf16[8,2,32,128]{3,2,1,0:T(8,128)(2,1)} %param.18) | copy-start | bytes 393220
  3.3 0.7 %copy-start.8 = (bf16[8,2,128]{2,1,0:T(2,128)(2,1)S(1)}, bf16[8,2,128]{2,1,0:T(2,128)(2,1)}, u32[]{:S(2)}) copy-start(bf16[8,2,128]{2,1,0:T(2,128)(2,1)} %param.20) | copy-start | bytes 12292
  4.0 0.8 %copy-start.5 = (bf16[8,4096]{1,0:T(8,128)(2,1)S(1)}, bf16[8,4096]{1,0:T(8,128)(2,1)}, u32[]{:S(2)}) copy-start(bf16[8,4096]{1,0:T(8,128)(2,1)} %param.15) | copy-start | bytes 196612
  5.0 1.4 %collective-permute-start = (f32[8]{0:T(128)S(1)}, f32[8]{0:T(128)S(1)}, u32[]{:S(2)}, u32[]{:S(2)}) collective-permute-start(f32[8]{0:T(128)S(1)} %get-tuple-element.9), channel_id=1, source_target_pairs={{0,1},{1,0},{2,3},{3,2},{4,5},{5,4},{6,7},{7,6},{8,9},{9,8},{10,11... | collective-permute-start | bytes 104 | tf_op jit(solution)/shard_map/ppermute | solution.py:18
  5.5 0.7 %copy-start.6 = (s32[8,4]{0,1:T(4,128)S(1)}, s32[8,4]{0,1:T(4,128)}, u32[]{:S(2)}) copy-start(s32[8,4]{0,1:T(4,128)} %param.29) | copy-start | bytes 388
  5.5 0.9 %copy-start.7 = (bf16[8192]{0:T(1024)(128)(2,1)S(1)}, bf16[8192]{0:T(1024)(128)(2,1)}, u32[]{:S(2)}) copy-start(bf16[8192]{0:T(1024)(128)(2,1)} %param.22) | copy-start | bytes 49156
  6.5 16.1 %copy-start.9 = (bf16[32,8192]{1,0:T(8,128)(2,1)S(1)}, bf16[32,8192]{1,0:T(8,128)(2,1)}, u32[]{:S(2)}) copy-start(bf16[32,8192]{1,0:T(8,128)(2,1)} %param.26) | copy-start | bytes 1572868
  21.2 1.4 %collective-permute-start.2 = (bf16[16,4096]{1,0:T(8,128)(2,1)S(1)}, bf16[16,4096]{1,0:T(8,128)(2,1)S(1)}, u32[]{:S(2)}, u32[]{:S(2)}) collective-permute-start(bf16[16,4096]{1,0:T(8,128)(2,1)S(1)} %reshape.45), channel_id=1, source_target_pairs={{0,1},{1,0},{2,3},{3,2},{4,5},{5,4},{6,7},{7,6},{8,9},{9,8},{10,11... | collective-permute-start | bytes 393224 | tf_op jit(solution)/shard_map/ppermute | solution.py:18
  21.3 1.6 %copy-start.10 = (bf16[32,8192]{1,0:T(8,128)(2,1)S(1)}, bf16[32,8192]{1,0:T(8,128)(2,1)}, u32[]{:S(2)}) copy-start(bf16[32,8192]{1,0:T(8,128)(2,1)} %param.27) | copy-start | bytes 1572868
  21.3 3.0 %collective-permute-start.1 = (bf16[8,4096]{1,0:T(8,128)(2,1)S(1)}, bf16[8,4096]{1,0:T(8,128)(2,1)S(1)}, u32[]{:S(2)}, u32[]{:S(2)}) collective-permute-start(bf16[8,4096]{1,0:T(8,128)(2,1)S(1)} %fusion.14), channel_id=1, source_target_pairs={{0,1},{1,0},{2,3},{3,2},{4,5},{5,4},{6,7},{7,6},{8,9},{9,8},{10,11... | collective-permute-start | bytes 196616 | tf_op jit(solution)/shard_map/ppermute | solution.py:18
  22.8 1.1 %copy-start.3 = (bf16[32,8192]{1,0:T(8,128)(2,1)S(1)}, bf16[32,8192]{1,0:T(8,128)(2,1)}, u32[]{:S(2)}) copy-start(bf16[32,8192]{1,0:T(8,128)(2,1)} %param.28) | copy-start | bytes 1572868
  23.9 6.1 %copy-start.1 = (bf16[64,8192]{1,0:T(8,128)(2,1)S(1)}, bf16[64,8192]{1,0:T(8,128)(2,1)}, u32[]{:S(2)}) copy-start(bf16[64,8192]{1,0:T(8,128)(2,1)} %param.23) | copy-start | bytes 3145732
  24.1 1.6 %collective-permute-start.3 = (f32[16,4096]{1,0:T(8,128)S(1)}, f32[16,4096]{1,0:T(8,128)S(1)}, u32[]{:S(2)}, u32[]{:S(2)}) collective-permute-start(f32[16,4096]{1,0:T(8,128)S(1)} %fusion.9), channel_id=1, source_target_pairs={{0,1},{1,0},{2,3},{3,2},{4,5},{5,4},{6,7},{7,6},{8,9},{9,8},{10,11... | collective-permute-start | bytes 786440 | tf_op jit(solution)/shard_map/ppermute | solution.py:18
  24.3 6.0 %copy-start.2 = (bf16[64,8192]{1,0:T(8,128)(2,1)S(1)}, bf16[64,8192]{1,0:T(8,128)(2,1)}, u32[]{:S(2)}) copy-start(bf16[64,8192]{1,0:T(8,128)(2,1)} %param.24) | copy-start | bytes 3145732
  26.6 10.9 %all-to-all-start.1 = ((bf16[8,2,4096]{2,1,0:T(2,128)(2,1)}), bf16[8,2,4096]{2,1,0:T(2,128)(2,1)S(1)}, u32[]{:S(2)}, u32[]{:S(2)}) async-start(bf16[8,2,4096]{2,1,0:T(2,128)(2,1)} %reshape.46), calls=%async_computation.1 | async-start | bytes 262144 | tf_op jit(solution)/shard_map/all_to_all | solution.py:139
  30.9 6.9 %collective-permute-start.4 = (f32[8,4096]{1,0:T(8,128)S(1)}, f32[8,4096]{1,0:T(8,128)S(1)}, u32[]{:S(2)}, u32[]{:S(2)}) collective-permute-start(f32[8,4096]{1,0:T(8,128)S(1)} %fusion.6), channel_id=1, source_target_pairs={{0,1},{1,0},{2,3},{3,2},{4,5},{5,4},{6,7},{7,6},{8,9},{9,8},{10,11... | collective-permute-start | bytes 393224 | tf_op jit(solution)/shard_map/ppermute | solution.py:18

commit v4 on v3

--- a/solution.py
+++ b/solution.py
@@ -28,32 +28,24 @@
 def attention_rows(query, key_cache, value_cache, key_new, value_new, lengths):
     count = key_cache.shape[0]
     kv_local = key_cache.shape[1]
+    slots = key_cache.shape[2]
     scale_factor = 1.0 / HD**0.5
     queries = query.reshape(count, kv_local, -1, HD)
+    keys_all = jnp.concatenate([key_cache, key_new[:, :, None, :]], axis=2)
+    values_all = jnp.concatenate([value_cache, value_new[:, :, None, :]], axis=2)
     scores = (
-        jnp.einsum("rgjd,rgpd->rgjp", queries, key_cache, preferred_element_type=jnp.float32)
+        jnp.einsum("rgjd,rgpd->rgjp", queries, keys_all, preferred_element_type=jnp.float32)
         * scale_factor
     )
-    own_score = (
-        jnp.einsum("rgjd,rgd->rgj", queries, key_new, preferred_element_type=jnp.float32)
-        * scale_factor
-    )
-    visible = (jnp.arange(key_cache.shape[2], dtype=jnp.int32)[None, :] < lengths[:, None])[
-        :, None, None, :
-    ]
+    positions = jnp.arange(slots + 1, dtype=jnp.int32)[None, :]
+    visible = ((positions < lengths[:, None]) | (positions == slots))[:, None, None, :]
     scores = jnp.where(visible, scores, -1e30)
-    highest = jnp.maximum(jnp.max(scores, axis=-1), own_score)
+    highest = jnp.max(scores, axis=-1)
     expons = jnp.where(visible, jnp.exp(scores - highest[..., None]), 0.0)
-    own_expon = jnp.exp(own_score - highest)
-    totals = jnp.sum(expons, axis=-1) + own_expon
+    totals = jnp.sum(expons, axis=-1)
     weights = (expons / totals[..., None]).astype(jnp.bfloat16)
-    own_weight = (own_expon / totals).astype(jnp.bfloat16)
     blended = jnp.einsum(
-        "rgjp,rgpd->rgjd", weights, value_cache, preferred_element_type=jnp.float32
-    )
-    blended = (
-        blended
-        + own_weight.astype(jnp.float32)[..., None] * value_new.astype(jnp.float32)[:, :, None, :]
+        "rgjp,rgpd->rgjd", weights, values_all, preferred_element_type=jnp.float32
     )
     return blended.reshape(count, -1)
 
@@ -65,15 +57,16 @@
     return jnp.dot(hidden, down_rows, preferred_element_type=jnp.float32)
 
 
-def swiglu_halves(normed, gate_rows, up_rows, down_rows, myself):
+def swiglu_halves(normed, gate_rows, up_rows, down_rows, myself, rows_shape):
     gate = jnp.einsum("rd,nd->rn", normed, gate_rows, preferred_element_type=jnp.float32)
     upper = jnp.einsum("rd,nd->rn", normed, up_rows, preferred_element_type=jnp.float32)
     hidden = (jax.nn.silu(gate) * upper).astype(jnp.bfloat16)
+    hidden = hidden.reshape(rows_shape + hidden.shape[-1:])
     half_width = down_rows.shape[1] // 2
     down_given = lax.dynamic_slice_in_dim(down_rows, (1 - myself) * half_width, half_width, 1)
     down_kept = lax.dynamic_slice_in_dim(down_rows, myself * half_width, half_width, 1)
-    given = jnp.dot(hidden, down_given, preferred_element_type=jnp.float32)
-    kept = jnp.dot(hidden, down_kept, preferred_element_type=jnp.float32)
+    given = jnp.einsum("...n,nd->...d", hidden, down_given, preferred_element_type=jnp.float32)
+    kept = jnp.einsum("...n,nd->...d", hidden, down_kept, preferred_element_type=jnp.float32)
     return kept, given
 
 
@@ -133,13 +126,15 @@
     ).astype(jnp.bfloat16)
     incoming_half = lax.all_to_all(outgoing, "rows", split_axis=0, concat_axis=0, tiled=True)
     incoming = join_halves(incoming_half.reshape(owner_count * CAP, -1), myself)
-    kept, given = swiglu_halves(incoming, cold_gate, cold_up, cold_down, myself)
+    kept, given = swiglu_halves(
+        incoming, cold_gate, cold_up, cold_down, myself, (owner_count, CAP)
+    )
     owner_sum = (kept + partner(given, "heads", 0)).astype(jnp.bfloat16)
     normed_late, owner_sum = lax.optimization_barrier((normed, owner_sum))
-    returned = lax.all_to_all(
-        owner_sum.reshape(owner_count, CAP, -1), "rows", split_axis=0, concat_axis=0, tiled=True
+    returned = lax.all_to_all(owner_sum, "rows", split_axis=0, concat_axis=0, tiled=True)
+    hot_kept, hot_given = swiglu_halves(
+        normed_late, hot_gate, hot_up, hot_down, myself, (request_count,)
     )
-    hot_kept, hot_given = swiglu_halves(normed_late, hot_gate, hot_up, hot_down, myself)
     hot_total = hot_kept + partner(hot_given, "heads", 0)
     cold_sum = collect_rows(
         selector.astype(jnp.float32),

time: 39.1 us -> 38.1 us (0.974)
  other arithmetic: 1.59 us -> 0.6 us
  local copies, waits for them, and re-layouts: 3.73 us -> 4.33 us
  matrix products: 5.45 us -> 4.87 us
    dot_general x7 -> x5, matrix products: 3.76 us -> 1.85 us  [the longest x2 0.99 us: swiglu_halves(): jnp.einsum('...n,nd->...d', hidden, down_kept, preferred_element_type=jnp...]
    sub x0 -> x1, matrix products: none -> 1.33 us  [attention_rows(): expons = jnp.where(visible, jnp.exp(scores - highest[..., None]), 0.0)]
    lt x1 -> x0, other arithmetic: 0.82 us -> none  [attention_rows(): jnp.arange(key_cache.shape[2], dtype=jnp.int32)[None, :] < lengths[:, None]]
    broadcast_in_dim x0 -> x2, local copies, waits for them, and re-layouts: none -> 0.8 us  [the longest x1 0.79 us: attention_rows(): keys_all = jnp.concatenate([key_cache, key_new[:, :, None, :]], axis=2)]
    optimization_barrier x0 -> x1, local copies, waits for them, and re-layouts: none -> 0.79 us  [local(): normed_late, owner_sum = lax.optimization_barrier((normed, owner_sum))]
    reshape x1 -> x0, local copies, waits for them, and re-layouts: 0.74 us -> none  [local(): owner_sum.reshape(owner_count, CAP, -1)]
    unnamed x24 -> x28, local copies, waits for them, and re-layouts: 2.74 us -> 2.48 us
where the time goes in v4:
time: 38.1 us; the launch traced here: 37.7 us
  blocking collectives  14.3 us (38%)
  waiting for transfers between devices  8.52 us (22%)
  matrix products  4.87 us (13%)
  starting transfers between devices  4.84 us (13%)
  local copies, waits for them, and re-layouts  4.33 us (11%)
  other arithmetic  0.6 us (2%)
    all_to_all x1, blocking collectives, local(): lax.all_to_all(outgoing, 'rows', split_axis=0, concat_axis=0, tiled=True)  14.3 us
    all_to_all x1, waiting for transfers between devices, local(): lax.all_to_all(owner_sum, 'rows', split_axis=0, concat_axis=0, tiled=True)  6.34 us
    all_to_all x1, starting transfers between devices, local(): lax.all_to_all(owner_sum, 'rows', split_axis=0, concat_axis=0, tiled=True)  3.37 us
    unnamed x28, local copies, waits for them, and re-layouts  2.48 us
    ppermute x5, waiting for transfers between devices, partner(): return lax.ppermute(block, axis, route)  2.18 us
    ppermute x5, starting transfers between devices, partner(): return lax.ppermute(block, axis, route)  1.47 us
    sub x1, matrix products, attention_rows(): expons = jnp.where(visible, jnp.exp(scores - highest[..., None]), 0.0)  1.33 us
    dot_general x2, matrix products, swiglu_halves(): jnp.einsum('...n,nd->...d', hidden, down_kept, preferred_element_type=jnp...  0.99 us
  transfers between devices with their start and end apart: 6, of which 3 were waited for; matrix products, arithmetic and copies ran while one was open for 6% of the time, Pallas kernels for 0%

profile of v4, /device:TPU:0, one launch (start us, length us, event | category | flops | bytes accessed | tf_op | source)
XLA Modules:
  0.0 37.7 jit_solution(2953822603705123156)
XLA Ops:
  0.0 0.0 copy-start
  0.0 0.0 copy-start.7
  0.0 0.8 %copy.31 = bf16[8,2,1,128]{3,2,1,0:T(2,128)(2,1)S(1)} copy(bf16[8,2,1,128]{3,1,0,2:T(2,128)(2,1)} %bitcast.54) | data formatting | bytes 8192 | tf_op jit(solution)/shard_map/broadcast_in_dim | solution.py:34
  0.8 0.0 copy-done.7
  0.8 0.0 copy-start.8
  0.8 0.6 %copy-done.8 = s32[8]{0:T(128)S(1)} copy-done((s32[8]{0:T(128)S(1)}, s32[8]{0:T(128)}, u32[]{:S(2)}) %copy-start.8) | copy-done | bytes 56
  1.5 0.1 fusion.49
  1.5 0.0 copy-start.11
  1.5 0.0 copy-start.12
  1.5 0.0 copy-start.13
  1.6 1.3 %fusion.78 = f32[8,2,16]{2,1,0:T(2,128)S(1)} fusion(bf16[8,2,1,128]{3,2,1,0:T(2,128)(2,1)S(1)} %copy.31, bf16[8,2,32,128]{3,2,1,0:T(8,128)(2,1)} %param.17, bf16[8,2,16,128]{3,0,2,1:T(8,128)(2,1)} %bitcast.56, pred[8,33]{1,0:T(8,128)(4,1)S(1)} %fusion.49), kind=kOutput, calls=%fused_computation.74 | convolution fusion | flops 2475296 | bytes 201992 | tf_op jit(solution)/shard_map/sub | solution.py:44
  2.9 0.0 copy-done.11
  2.9 0.0 copy-done.12
  2.9 0.0 copy-done.13
  2.9 0.0 copy-start.4
  2.9 0.5 %fusion.22 = f32[8,2,16,128]{3,2,1,0:T(8,128)S(1)} fusion(bf16[8,2,1,128]{3,2,1,0:T(2,128)(2,1)S(1)} %copy.34, bf16[8,2,32,128]{3,2,1,0:T(8,128)(2,1)S(1)} %copy-done.11, f32[8,2,16]{2,1,0:T(2,128)S(1)} %fusion.78, pred[8,33]{1,0:T(8,128)(4,1)S(1)} %fusion.49, bf16[8,2,1,128]{3,2,1,0:T(2,128)(2,1)S(1)} %copy.31, bf16[8,2,32,128]{3,2,1,0:T(8,128)(2,1)S(1)} %copy-done.12, ...), kind=kOutput, calls=%fused_computation.30 | convolution fusion | flops 4917024 | bytes 468232 | tf_op jit(solution)/shard_map/rgjp,rgpd->rgjd/dot_general | solution.py:47
  3.4 0.3 copy-done.4
  3.8 0.2 fusion.26
  4.0 0.5 %collective-permute-start = (f32[8]{0:T(128)S(1)}, f32[8]{0:T(128)S(1)}, u32[]{:S(2)}, u32[]{:S(2)}) collective-permute-start(f32[8]{0:T(128)S(1)} %get-tuple-element.9), channel_id=1, source_target_pairs={{0,1},{1,0},{2,3},{3,2},{4,5},{5,4},{6,7},{7,6},{8,9},{9,8},{10,11... | collective-permute-start | bytes 104 | tf_op jit(solution)/shard_map/ppermute | solution.py:18
  4.5 0.0 copy-start.5
  4.5 0.0 copy-start.6
  4.5 0.7 %copy-done.5 = s32[8,4]{0,1:T(4,128)S(1)} copy-done((s32[8,4]{0,1:T(4,128)S(1)}, s32[8,4]{0,1:T(4,128)}, u32[]{:S(2)}) %copy-start.5) | copy-done | bytes 152
  5.2 0.2 reduce_window_sum.11
  5.4 0.0 copy-done.6
  5.4 0.0 collective-permute-done
  5.4 0.1 fusion.28
  5.5 0.0 copy-start.9
  5.5 0.2 convolution_convert_fusion
  5.7 0.1 copy.36
  5.8 14.3 %all_to_all.10 = bf16[8,2,4096]{2,1,0:T(2,128)(2,1)S(1)} all-to-all(bf16[8,2,4096]{2,1,0:T(2,128)(2,1)S(1)} %copy.36), channel_id=1, replica_groups=mesh['groups'=2,'rows'=8,'heads'=2] {'rows'}, dimensions={0} | all-to-all | bytes 262144 | tf_op jit(solution)/shard_map/all_to_all | solution.py:127
  20.1 0.1 reshape.60
  20.1 0.1 collective-permute-start.2
  20.2 0.0 copy-start.10
  20.2 0.5 %collective-permute-start.1 = (bf16[8,4096]{1,0:T(8,128)(2,1)S(1)}, bf16[8,4096]{1,0:T(8,128)(2,1)S(1)}, u32[]{:S(2)}, u32[]{:S(2)}) collective-permute-start(bf16[8,4096]{1,0:T(8,128)(2,1)S(1)} %fusion.28), channel_id=1, source_target_pairs={{0,1},{1,0},{2,3},{3,2},{4,5},{5,4},{6,7},{7,6},{8,9},{9,8},{10,11... | collective-permute-start | bytes 196616 | tf_op jit(solution)/shard_map/ppermute | solution.py:18
  20.7 0.8 %collective-permute-done.2 = bf16[16,4096]{1,0:T(8,128)(2,1)S(1)} collective-permute-done((bf16[16,4096]{1,0:T(8,128)(2,1)S(1)}, bf16[16,4096]{1,0:T(8,128)(2,1)S(1)}, u32[]{:S(2)}, u32[]{:S(2)}) %collective-permute-start.2) | collective-permute-done | bytes 131104 | tf_op jit(solution)/shard_map/ppermute | solution.py:18
  21.6 0.0 copy-done.9
  21.6 0.2 fusion.34
  21.8 0.0 copy-done.10
  21.8 0.0 copy-start.3
  21.8 0.3 multiply_convert_fusion
  22.1 0.0 copy-start.1
  22.1 0.8 %copy-done.3 = bf16[32,8192]{1,0:T(8,128)(2,1)S(1)} copy-done((bf16[32,8192]{1,0:T(8,128)(2,1)S(1)}, bf16[32,8192]{1,0:T(8,128)(2,1)}, u32[]{:S(2)}) %copy-start.3) | copy-done | bytes 524312
  22.9 0.2 fusion.14
  23.0 0.2 collective-permute-start.3
  23.3 0.0 collective-permute-done.1
  23.3 0.0 copy-start.2
  23.3 1.3 %collective-permute-done.3 = f32[8,2,4096]{2,0,1:T(8,128)S(1)} collective-permute-done((f32[8,2,4096]{2,0,1:T(8,128)S(1)}, f32[8,2,4096]{2,0,1:T(8,128)S(1)}, u32[]{:S(2)}, u32[]{:S(2)}) %collective-permute-start.3) | collective-permute-done | bytes 262176 | tf_op jit(solution)/shard_map/ppermute | solution.py:18
  24.6 0.2 fusion.1
  24.8 0.8 %copy.39 = bf16[8,2,4096]{2,1,0:T(2,128)(2,1)} copy(bf16[8,2,4096]{2,0,1:T(8,128)(2,1)S(1)} %fusion.1) | data formatting | bytes 262144 | tf_op jit(solution)/shard_map/optimization_barrier | solution.py:133
  25.6 3.4 %all-to-all-start.1 = ((bf16[8,2,4096]{2,1,0:T(2,128)(2,1)}), bf16[8,2,4096]{2,1,0:T(2,128)(2,1)S(1)}, u32[]{:S(2)}, u32[]{:S(2)}) async-start(bf16[8,2,4096]{2,1,0:T(2,128)(2,1)} %copy.39), calls=%async_computation.1 | async-start | bytes 262144 | tf_op jit(solution)/shard_map/all_to_all | solution.py:134
  29.0 0.0 copy-done.1
  29.0 0.4 fusion.83
  29.4 0.0 copy-done.2
  29.4 0.4 %fusion.10 = bf16[8,64]{1,0:T(8,128)(2,1)S(1)} fusion(bf16[8,8192]{1,0:T(8,128)(2,1)S(1)} %maximum_select_fusion.1, bf16[64,8192]{1,0:T(8,128)(2,1)S(1)} %copy-done.2, f32[8,64]{1,0:T(8,128)S(1)} %fusion.83), kind=kOutput, calls=%fused_computation.15 | convolution fusion | flops 8391680 | bytes 1182720 | tf_op jit(solution)/shard_map/rd,nd->rn/dot_general | solution.py:62
  29.8 0.0 copy-done
  29.8 0.2 fusion.11
  30.0 0.2 collective-permute-start.4
  30.2 6.3 %all-to-all-done.1 = bf16[8,2,4096]{2,1,0:T(2,128)(2,1)S(1)} async-done(((bf16[8,2,4096]{2,1,0:T(2,128)(2,1)}), bf16[8,2,4096]{2,1,0:T(2,128)(2,1)S(1)}, u32[]{:S(2)}, u32[]{:S(2)}) %all-to-all-start.1) | async-done | bytes 131104 | tf_op jit(solution)/shard_map/all_to_all | solution.py:134
  36.5 0.1 reshape.62
  36.6 0.3 fusion.84
  36.8 0.0 collective-permute-done.4
  36.8 0.8 %fusion.4 = bf16[8,4096]{1,0:T(8,128)(2,1)} fusion(f32[8,4096]{1,0:T(8,128)S(1)} %fusion.84, f32[8,4096]{1,0:T(8,128)S(1)} %collective-permute-done.4, bf16[8,64]{1,0:T(8,128)(2,1)S(1)} %fusion.10, bf16[64,8192]{1,0:T(8,128)(2,1)S(1)} %copy-done, s32[]{:T(128)S(6)} %select_n.39, bf16[8,4096]{1,0:T(8,128)(2,1)S(1)} %get-tuple-element.10), kind=kOutput, calls=%fused_computation.7 | convolution fusion | flops 4358144 | bytes 919556 | tf_op jit(solution)/shard_map/...n,nd->...d/dot_general | solution.py:69
  (10 shorter events, 0.1 us)
Async XLA Ops:
  0.0 29.8 %copy-start = (bf16[64,8192]{1,0:T(8,128)(2,1)S(1)}, bf16[64,8192]{1,0:T(8,128)(2,1)}, u32[]{:S(2)}) copy-start(bf16[64,8192]{1,0:T(8,128)(2,1)} %param.25) | copy-start | bytes 3145732
  0.0 0.8 %copy-start.7 = (bf16[8,2,128]{2,1,0:T(2,128)(2,1)S(1)}, bf16[8,2,128]{2,1,0:T(2,128)(2,1)}, u32[]{:S(2)}) copy-start(bf16[8,2,128]{2,1,0:T(2,128)(2,1)} %param.20) | copy-start | bytes 12292
  0.8 0.7 %copy-start.8 = (s32[8]{0:T(128)S(1)}, s32[8]{0:T(128)}, u32[]{:S(2)}) copy-start(s32[8]{0:T(128)} %param.21) | copy-start | bytes 100
  1.5 1.4 %copy-start.11 = (bf16[8,2,32,128]{3,2,1,0:T(8,128)(2,1)S(1)}, bf16[8,2,32,128]{3,2,1,0:T(8,128)(2,1)}, u32[]{:S(2)}) copy-start(bf16[8,2,32,128]{3,2,1,0:T(8,128)(2,1)} %param.18) | copy-start | bytes 393220
  1.5 1.4 %copy-start.12 = (bf16[8,2,32,128]{3,2,1,0:T(8,128)(2,1)S(1)}, bf16[8,2,32,128]{3,2,1,0:T(8,128)(2,1)}, u32[]{:S(2)}) copy-start(bf16[8,2,32,128]{3,2,1,0:T(8,128)(2,1)} %param.17) | copy-start | bytes 393220
  1.5 1.4 %copy-start.13 = (bf16[8,4096]{1,0:T(8,128)(2,1)S(1)}, bf16[8,4096]{1,0:T(8,128)(2,1)}, u32[]{:S(2)}) copy-start(bf16[8,4096]{1,0:T(8,128)(2,1)} %param.16) | copy-start | bytes 196612
  2.9 0.8 %copy-start.4 = (bf16[8,4096]{1,0:T(8,128)(2,1)S(1)}, bf16[8,4096]{1,0:T(8,128)(2,1)}, u32[]{:S(2)}) copy-start(bf16[8,4096]{1,0:T(8,128)(2,1)} %param.15) | copy-start | bytes 196612
  4.0 1.4 %collective-permute-start = (f32[8]{0:T(128)S(1)}, f32[8]{0:T(128)S(1)}, u32[]{:S(2)}, u32[]{:S(2)}) collective-permute-start(f32[8]{0:T(128)S(1)} %get-tuple-element.9), channel_id=1, source_target_pairs={{0,1},{1,0},{2,3},{3,2},{4,5},{5,4},{6,7},{7,6},{8,9},{9,8},{10,11... | collective-permute-start | bytes 104 | tf_op jit(solution)/shard_map/ppermute | solution.py:18
  4.5 0.7 %copy-start.5 = (s32[8,4]{0,1:T(4,128)S(1)}, s32[8,4]{0,1:T(4,128)}, u32[]{:S(2)}) copy-start(s32[8,4]{0,1:T(4,128)} %param.29) | copy-start | bytes 388
  4.5 0.9 %copy-start.6 = (bf16[8192]{0:T(1024)(128)(2,1)S(1)}, bf16[8192]{0:T(1024)(128)(2,1)}, u32[]{:S(2)}) copy-start(bf16[8192]{0:T(1024)(128)(2,1)} %param.22) | copy-start | bytes 49156
  5.5 16.1 %copy-start.9 = (bf16[32,8192]{1,0:T(8,128)(2,1)S(1)}, bf16[32,8192]{1,0:T(8,128)(2,1)}, u32[]{:S(2)}) copy-start(bf16[32,8192]{1,0:T(8,128)(2,1)} %param.26) | copy-start | bytes 1572868
  20.1 1.4 %collective-permute-start.2 = (bf16[16,4096]{1,0:T(8,128)(2,1)S(1)}, bf16[16,4096]{1,0:T(8,128)(2,1)S(1)}, u32[]{:S(2)}, u32[]{:S(2)}) collective-permute-start(bf16[16,4096]{1,0:T(8,128)(2,1)S(1)} %reshape.60), channel_id=1, source_target_pairs={{0,1},{1,0},{2,3},{3,2},{4,5},{5,4},{6,7},{7,6},{8,9},{9,8},{10,11... | collective-permute-start | bytes 393224 | tf_op jit(solution)/shard_map/ppermute | solution.py:18
  20.2 1.6 %copy-start.10 = (bf16[32,8192]{1,0:T(8,128)(2,1)S(1)}, bf16[32,8192]{1,0:T(8,128)(2,1)}, u32[]{:S(2)}) copy-start(bf16[32,8192]{1,0:T(8,128)(2,1)} %param.27) | copy-start | bytes 1572868
  20.2 3.0 %collective-permute-start.1 = (bf16[8,4096]{1,0:T(8,128)(2,1)S(1)}, bf16[8,4096]{1,0:T(8,128)(2,1)S(1)}, u32[]{:S(2)}, u32[]{:S(2)}) collective-permute-start(bf16[8,4096]{1,0:T(8,128)(2,1)S(1)} %fusion.28), channel_id=1, source_target_pairs={{0,1},{1,0},{2,3},{3,2},{4,5},{5,4},{6,7},{7,6},{8,9},{9,8},{10,11... | collective-permute-start | bytes 196616 | tf_op jit(solution)/shard_map/ppermute | solution.py:18
  21.8 1.1 %copy-start.3 = (bf16[32,8192]{1,0:T(8,128)(2,1)S(1)}, bf16[32,8192]{1,0:T(8,128)(2,1)}, u32[]{:S(2)}) copy-start(bf16[32,8192]{1,0:T(8,128)(2,1)} %param.28) | copy-start | bytes 1572868
  22.1 6.9 %copy-start.1 = (bf16[64,8192]{1,0:T(8,128)(2,1)S(1)}, bf16[64,8192]{1,0:T(8,128)(2,1)}, u32[]{:S(2)}) copy-start(bf16[64,8192]{1,0:T(8,128)(2,1)} %param.23) | copy-start | bytes 3145732
  23.0 1.6 %collective-permute-start.3 = (f32[8,2,4096]{2,0,1:T(8,128)S(1)}, f32[8,2,4096]{2,0,1:T(8,128)S(1)}, u32[]{:S(2)}, u32[]{:S(2)}) collective-permute-start(f32[8,2,4096]{2,0,1:T(8,128)S(1)} %fusion.14), channel_id=1, source_target_pairs={{0,1},{1,0},{2,3},{3,2},{4,5},{5,4},{6,7},{7,6},{8,9},{9,8},{10,11... | collective-permute-start | bytes 786440 | tf_op jit(solution)/shard_map/ppermute | solution.py:18
  23.3 6.1 %copy-start.2 = (bf16[64,8192]{1,0:T(8,128)(2,1)S(1)}, bf16[64,8192]{1,0:T(8,128)(2,1)}, u32[]{:S(2)}) copy-start(bf16[64,8192]{1,0:T(8,128)(2,1)} %param.24) | copy-start | bytes 3145732
  25.6 10.9 %all-to-all-start.1 = ((bf16[8,2,4096]{2,1,0:T(2,128)(2,1)}), bf16[8,2,4096]{2,1,0:T(2,128)(2,1)S(1)}, u32[]{:S(2)}, u32[]{:S(2)}) async-start(bf16[8,2,4096]{2,1,0:T(2,128)(2,1)} %copy.39), calls=%async_computation.1 | async-start | bytes 262144 | tf_op jit(solution)/shard_map/all_to_all | solution.py:134
  30.0 6.9 %collective-permute-start.4 = (f32[8,4096]{1,0:T(8,128)S(1)}, f32[8,4096]{1,0:T(8,128)S(1)}, u32[]{:S(2)}, u32[]{:S(2)}) collective-permute-start(f32[8,4096]{1,0:T(8,128)S(1)} %fusion.11), channel_id=1, source_target_pairs={{0,1},{1,0},{2,3},{3,2},{4,5},{5,4},{6,7},{7,6},{8,9},{9,8},{10,11... | collective-permute-start | bytes 393224 | tf_op jit(solution)/shard_map/ppermute | solution.py:18

commit v5 on v4

--- a/solution.py
+++ b/solution.py
@@ -108,7 +108,6 @@
     scaled = (
         local_wide * lax.rsqrt(square_total / D + 1e-05)[:, None] * gain_half.astype(jnp.float32)
     )
-    normed = join_halves(scaled.astype(jnp.bfloat16), myself)
     owner_count = lax.axis_size("rows")
     block_count = active.shape[1]
     request_count = active.shape[0]
@@ -130,7 +129,8 @@
         incoming, cold_gate, cold_up, cold_down, myself, (owner_count, CAP)
     )
     owner_sum = (kept + partner(given, "heads", 0)).astype(jnp.bfloat16)
-    normed_late, owner_sum = lax.optimization_barrier((normed, owner_sum))
+    scaled_late, owner_sum = lax.optimization_barrier((scaled.astype(jnp.bfloat16), owner_sum))
+    normed_late = join_halves(scaled_late, myself)
     returned = lax.all_to_all(owner_sum, "rows", split_axis=0, concat_axis=0, tiled=True)
     hot_kept, hot_given = swiglu_halves(
         normed_late, hot_gate, hot_up, hot_down, myself, (request_count,)

time: 38.1 us -> 38.5 us (1.010)
  waiting for transfers between devices: 8.52 us -> 9.04 us
    ppermute x5, waiting for transfers between devices: 2.18 us -> 2.71 us  [partner(): return lax.ppermute(block, axis, route)]
where the time goes in v5:
time: 38.5 us; the launch traced here: 38.1 us
  blocking collectives  14.3 us (37%)
  waiting for transfers between devices  9.04 us (23%)
  matrix products  4.87 us (13%)
  starting transfers between devices  4.79 us (12%)
  local copies, waits for them, and re-layouts  4.33 us (11%)
  other arithmetic  0.57 us (1%)
    all_to_all x1, blocking collectives, local(): lax.all_to_all(outgoing, 'rows', split_axis=0, concat_axis=0, tiled=True)  14.3 us
    all_to_all x1, waiting for transfers between devices, local(): lax.all_to_all(owner_sum, 'rows', split_axis=0, concat_axis=0, tiled=True)  6.33 us
    all_to_all x1, starting transfers between devices, local(): lax.all_to_all(owner_sum, 'rows', split_axis=0, concat_axis=0, tiled=True)  3.37 us
    ppermute x5, waiting for transfers between devices, partner(): return lax.ppermute(block, axis, route)  2.71 us
    unnamed x28, local copies, waits for them, and re-layouts  2.48 us
    ppermute x5, starting transfers between devices, partner(): return lax.ppermute(block, axis, route)  1.42 us
    sub x1, matrix products, attention_rows(): expons = jnp.where(visible, jnp.exp(scores - highest[..., None]), 0.0)  1.33 us
    dot_general x2, matrix products, swiglu_halves(): jnp.einsum('...n,nd->...d', hidden, down_kept, preferred_element_type=jnp...  0.99 us
  transfers between devices with their start and end apart: 6, of which 3 were waited for; matrix products, arithmetic and copies ran while one was open for 6% of the time, Pallas kernels for 0%

profile of v5, /device:TPU:0, one launch (start us, length us, event | category | flops | bytes accessed | tf_op | source)
XLA Modules:
  0.0 38.1 jit_solution(6535888177038621339)
XLA Ops:
  0.0 0.0 copy-start
  0.0 0.0 copy-start.7
  0.0 0.8 %copy.31 = bf16[8,2,1,128]{3,2,1,0:T(2,128)(2,1)S(1)} copy(bf16[8,2,1,128]{3,1,0,2:T(2,128)(2,1)} %bitcast.52) | data formatting | bytes 8192 | tf_op jit(solution)/shard_map/broadcast_in_dim | solution.py:34
  0.8 0.0 copy-done.7
  0.8 0.0 copy-start.8
  0.8 0.6 %copy-done.8 = s32[8]{0:T(128)S(1)} copy-done((s32[8]{0:T(128)S(1)}, s32[8]{0:T(128)}, u32[]{:S(2)}) %copy-start.8) | copy-done | bytes 56
  1.5 0.1 fusion.50
  1.5 0.0 copy-start.11
  1.5 0.0 copy-start.12
  1.5 0.0 copy-start.13
  1.6 1.3 %fusion.81 = f32[8,2,16]{2,1,0:T(2,128)S(1)} fusion(bf16[8,2,1,128]{3,2,1,0:T(2,128)(2,1)S(1)} %copy.31, bf16[8,2,32,128]{3,2,1,0:T(8,128)(2,1)} %param.17, bf16[8,2,16,128]{3,0,2,1:T(8,128)(2,1)} %bitcast.54, pred[8,33]{1,0:T(8,128)(4,1)S(1)} %fusion.50), kind=kOutput, calls=%fused_computation.77 | convolution fusion | flops 2475296 | bytes 201992 | tf_op jit(solution)/shard_map/sub | solution.py:44
  2.9 0.0 copy-done.11
  2.9 0.0 copy-done.12
  2.9 0.0 copy-done.13
  2.9 0.0 copy-start.4
  2.9 0.5 %fusion.21 = f32[8,2,16,128]{3,2,1,0:T(8,128)S(1)} fusion(bf16[8,2,1,128]{3,2,1,0:T(2,128)(2,1)S(1)} %copy.34, bf16[8,2,32,128]{3,2,1,0:T(8,128)(2,1)S(1)} %copy-done.11, f32[8,2,16]{2,1,0:T(2,128)S(1)} %fusion.81, pred[8,33]{1,0:T(8,128)(4,1)S(1)} %fusion.50, bf16[8,2,1,128]{3,2,1,0:T(2,128)(2,1)S(1)} %copy.31, bf16[8,2,32,128]{3,2,1,0:T(8,128)(2,1)S(1)} %copy-done.12, ...), kind=kOutput, calls=%fused_computation.28 | convolution fusion | flops 4917024 | bytes 468232 | tf_op jit(solution)/shard_map/rgjp,rgpd->rgjd/dot_general | solution.py:47
  3.4 0.3 copy-done.4
  3.8 0.2 fusion.25
  4.0 0.5 %collective-permute-start = (f32[8]{0:T(128)S(1)}, f32[8]{0:T(128)S(1)}, u32[]{:S(2)}, u32[]{:S(2)}) collective-permute-start(f32[8]{0:T(128)S(1)} %get-tuple-element.9), channel_id=1, source_target_pairs={{0,1},{1,0},{2,3},{3,2},{4,5},{5,4},{6,7},{7,6},{8,9},{9,8},{10,11... | collective-permute-start | bytes 104 | tf_op jit(solution)/shard_map/ppermute | solution.py:18
  4.5 0.0 copy-start.5
  4.5 0.0 copy-start.6
  4.5 0.7 %copy-done.5 = s32[8,4]{0,1:T(4,128)S(1)} copy-done((s32[8,4]{0,1:T(4,128)S(1)}, s32[8,4]{0,1:T(4,128)}, u32[]{:S(2)}) %copy-start.5) | copy-done | bytes 152
  5.2 0.2 reduce_window_sum.11
  5.4 0.0 copy-done.6
  5.4 0.0 collective-permute-done
  5.4 0.1 fusion.27
  5.5 0.0 copy-start.9
  5.5 0.2 convolution_convert_fusion
  5.7 0.1 copy.36
  5.8 14.3 %all_to_all.10 = bf16[8,2,4096]{2,1,0:T(2,128)(2,1)S(1)} all-to-all(bf16[8,2,4096]{2,1,0:T(2,128)(2,1)S(1)} %copy.36), channel_id=1, replica_groups=mesh['groups'=2,'rows'=8,'heads'=2] {'rows'}, dimensions={0} | all-to-all | bytes 262144 | tf_op jit(solution)/shard_map/all_to_all | solution.py:126
  20.1 0.1 reshape.60
  20.1 0.1 collective-permute-start.1
  20.2 0.0 copy-start.10
  20.2 1.3 %collective-permute-done.1 = bf16[16,4096]{1,0:T(8,128)(2,1)S(1)} collective-permute-done((bf16[16,4096]{1,0:T(8,128)(2,1)S(1)}, bf16[16,4096]{1,0:T(8,128)(2,1)S(1)}, u32[]{:S(2)}, u32[]{:S(2)}) %collective-permute-start.1) | collective-permute-done | bytes 131104 | tf_op jit(solution)/shard_map/ppermute | solution.py:18
  21.6 0.0 copy-done.9
  21.6 0.2 fusion.33
  21.8 0.0 copy-done.10
  21.8 0.0 copy-start.3
  21.8 0.3 multiply_convert_fusion
  22.1 0.0 copy-start.1
  22.1 0.8 %copy-done.3 = bf16[32,8192]{1,0:T(8,128)(2,1)S(1)} copy-done((bf16[32,8192]{1,0:T(8,128)(2,1)S(1)}, bf16[32,8192]{1,0:T(8,128)(2,1)}, u32[]{:S(2)}) %copy-start.3) | copy-done | bytes 524312
  22.9 0.2 fusion.13
  23.0 0.0 copy-start.2
  23.1 0.2 collective-permute-start.2
  23.3 1.4 %collective-permute-done.2 = f32[8,2,4096]{2,0,1:T(8,128)S(1)} collective-permute-done((f32[8,2,4096]{2,0,1:T(8,128)S(1)}, f32[8,2,4096]{2,0,1:T(8,128)S(1)}, u32[]{:S(2)}, u32[]{:S(2)}) %collective-permute-start.2) | collective-permute-done | bytes 262176 | tf_op jit(solution)/shard_map/ppermute | solution.py:18
  24.7 0.2 fusion.1
  24.8 0.2 collective-permute-start.3
  25.0 0.8 %copy.39 = bf16[8,2,4096]{2,1,0:T(2,128)(2,1)} copy(bf16[8,2,4096]{2,0,1:T(8,128)(2,1)S(1)} %fusion.1) | data formatting | bytes 262144 | tf_op jit(solution)/shard_map/optimization_barrier | solution.py:132
  25.8 3.4 %all-to-all-start.1 = ((bf16[8,2,4096]{2,1,0:T(2,128)(2,1)}), bf16[8,2,4096]{2,1,0:T(2,128)(2,1)S(1)}, u32[]{:S(2)}, u32[]{:S(2)}) async-start(bf16[8,2,4096]{2,1,0:T(2,128)(2,1)} %copy.39), calls=%async_computation.1 | async-start | bytes 262144 | tf_op jit(solution)/shard_map/all_to_all | solution.py:134
  29.2 0.0 collective-permute-done.3
  29.2 0.0 copy-done.1
  29.2 0.4 fusion.35
  29.6 0.0 copy-done.2
  29.6 0.4 %multiply_convert_fusion.1 = bf16[8,64]{1,0:T(8,128)(2,1)S(1)} fusion(f32[8,64]{1,0:T(8,128)S(1)} %fusion.35, bf16[64,8192]{1,0:T(8,128)(2,1)S(1)} %copy-done.2, bf16[8,4096]{1,0:T(8,128)(2,1)S(1)} %collective-permute-done.3, bf16[8,4096]{1,0:T(8,128)(2,1)S(1)} %fusion.27, pred[]{:T(512)S(6)} %eq.30), kind=kOutput, calls=%fused_computation.49 | convolution fusion | flops 8981504 | bytes 1182721 | tf_op jit(solution)/shard_map/rd,nd->rn/dot_general | solution.py:62
  30.0 0.0 copy-done
  30.0 0.2 fusion.10
  30.2 0.4 %collective-permute-start.4 = (f32[8,4096]{1,0:T(8,128)S(1)}, f32[8,4096]{1,0:T(8,128)S(1)}, u32[]{:S(2)}, u32[]{:S(2)}) collective-permute-start(f32[8,4096]{1,0:T(8,128)S(1)} %fusion.10), channel_id=1, source_target_pairs={{0,1},{1,0},{2,3},{3,2},{4,5},{5,4},{6,7},{7,6},{8,9},{9,8},{10,11... | collective-permute-start | bytes 393224 | tf_op jit(solution)/shard_map/ppermute | solution.py:18
  30.6 6.3 %all-to-all-done.1 = bf16[8,2,4096]{2,1,0:T(2,128)(2,1)S(1)} async-done(((bf16[8,2,4096]{2,1,0:T(2,128)(2,1)}), bf16[8,2,4096]{2,1,0:T(2,128)(2,1)S(1)}, u32[]{:S(2)}, u32[]{:S(2)}) %all-to-all-start.1) | async-done | bytes 131104 | tf_op jit(solution)/shard_map/all_to_all | solution.py:134
  36.9 0.1 reshape.62
  37.0 0.3 fusion.86
  37.3 0.0 collective-permute-done.4
  37.3 0.8 %fusion.4 = bf16[8,4096]{1,0:T(8,128)(2,1)} fusion(f32[8,4096]{1,0:T(8,128)S(1)} %fusion.86, f32[8,4096]{1,0:T(8,128)S(1)} %collective-permute-done.4, bf16[8,64]{1,0:T(8,128)(2,1)S(1)} %multiply_convert_fusion.1, bf16[64,8192]{1,0:T(8,128)(2,1)S(1)} %copy-done, s32[]{:T(128)S(6)} %select_n.39, bf16[8,4096]{1,0:T(8,128)(2,1)S(1)} %get-tuple-element.10), kind=kOutput, calls=%fused_computation.7 | convolution fusion | flops 4358144 | bytes 919556 | tf_op jit(solution)/shard_map/...n,nd->...d/dot_general | solution.py:69
  (9 shorter events, 0.1 us)
Async XLA Ops:
  0.0 30.0 %copy-start = (bf16[64,8192]{1,0:T(8,128)(2,1)S(1)}, bf16[64,8192]{1,0:T(8,128)(2,1)}, u32[]{:S(2)}) copy-start(bf16[64,8192]{1,0:T(8,128)(2,1)} %param.25) | copy-start | bytes 3145732
  0.0 0.8 %copy-start.7 = (bf16[8,2,128]{2,1,0:T(2,128)(2,1)S(1)}, bf16[8,2,128]{2,1,0:T(2,128)(2,1)}, u32[]{:S(2)}) copy-start(bf16[8,2,128]{2,1,0:T(2,128)(2,1)} %param.20) | copy-start | bytes 12292
  0.8 0.7 %copy-start.8 = (s32[8]{0:T(128)S(1)}, s32[8]{0:T(128)}, u32[]{:S(2)}) copy-start(s32[8]{0:T(128)} %param.21) | copy-start | bytes 100
  1.5 1.4 %copy-start.11 = (bf16[8,2,32,128]{3,2,1,0:T(8,128)(2,1)S(1)}, bf16[8,2,32,128]{3,2,1,0:T(8,128)(2,1)}, u32[]{:S(2)}) copy-start(bf16[8,2,32,128]{3,2,1,0:T(8,128)(2,1)} %param.18) | copy-start | bytes 393220
  1.5 1.4 %copy-start.12 = (bf16[8,2,32,128]{3,2,1,0:T(8,128)(2,1)S(1)}, bf16[8,2,32,128]{3,2,1,0:T(8,128)(2,1)}, u32[]{:S(2)}) copy-start(bf16[8,2,32,128]{3,2,1,0:T(8,128)(2,1)} %param.17) | copy-start | bytes 393220
  1.5 1.4 %copy-start.13 = (bf16[8,4096]{1,0:T(8,128)(2,1)S(1)}, bf16[8,4096]{1,0:T(8,128)(2,1)}, u32[]{:S(2)}) copy-start(bf16[8,4096]{1,0:T(8,128)(2,1)} %param.16) | copy-start | bytes 196612
  2.9 0.8 %copy-start.4 = (bf16[8,4096]{1,0:T(8,128)(2,1)S(1)}, bf16[8,4096]{1,0:T(8,128)(2,1)}, u32[]{:S(2)}) copy-start(bf16[8,4096]{1,0:T(8,128)(2,1)} %param.15) | copy-start | bytes 196612
  4.0 1.4 %collective-permute-start = (f32[8]{0:T(128)S(1)}, f32[8]{0:T(128)S(1)}, u32[]{:S(2)}, u32[]{:S(2)}) collective-permute-start(f32[8]{0:T(128)S(1)} %get-tuple-element.9), channel_id=1, source_target_pairs={{0,1},{1,0},{2,3},{3,2},{4,5},{5,4},{6,7},{7,6},{8,9},{9,8},{10,11... | collective-permute-start | bytes 104 | tf_op jit(solution)/shard_map/ppermute | solution.py:18
  4.5 0.7 %copy-start.5 = (s32[8,4]{0,1:T(4,128)S(1)}, s32[8,4]{0,1:T(4,128)}, u32[]{:S(2)}) copy-start(s32[8,4]{0,1:T(4,128)} %param.29) | copy-start | bytes 388
  4.5 0.9 %copy-start.6 = (bf16[8192]{0:T(1024)(128)(2,1)S(1)}, bf16[8192]{0:T(1024)(128)(2,1)}, u32[]{:S(2)}) copy-start(bf16[8192]{0:T(1024)(128)(2,1)} %param.22) | copy-start | bytes 49156
  5.5 16.1 %copy-start.9 = (bf16[32,8192]{1,0:T(8,128)(2,1)S(1)}, bf16[32,8192]{1,0:T(8,128)(2,1)}, u32[]{:S(2)}) copy-start(bf16[32,8192]{1,0:T(8,128)(2,1)} %param.26) | copy-start | bytes 1572868
  20.1 1.4 %collective-permute-start.1 = (bf16[16,4096]{1,0:T(8,128)(2,1)S(1)}, bf16[16,4096]{1,0:T(8,128)(2,1)S(1)}, u32[]{:S(2)}, u32[]{:S(2)}) collective-permute-start(bf16[16,4096]{1,0:T(8,128)(2,1)S(1)} %reshape.60), channel_id=1, source_target_pairs={{0,1},{1,0},{2,3},{3,2},{4,5},{5,4},{6,7},{7,6},{8,9},{9,8},{10,11... | collective-permute-start | bytes 393224 | tf_op jit(solution)/shard_map/ppermute | solution.py:18
  20.2 1.6 %copy-start.10 = (bf16[32,8192]{1,0:T(8,128)(2,1)S(1)}, bf16[32,8192]{1,0:T(8,128)(2,1)}, u32[]{:S(2)}) copy-start(bf16[32,8192]{1,0:T(8,128)(2,1)} %param.27) | copy-start | bytes 1572868
  21.8 1.1 %copy-start.3 = (bf16[32,8192]{1,0:T(8,128)(2,1)S(1)}, bf16[32,8192]{1,0:T(8,128)(2,1)}, u32[]{:S(2)}) copy-start(bf16[32,8192]{1,0:T(8,128)(2,1)} %param.28) | copy-start | bytes 1572868
  22.1 7.1 %copy-start.1 = (bf16[64,8192]{1,0:T(8,128)(2,1)S(1)}, bf16[64,8192]{1,0:T(8,128)(2,1)}, u32[]{:S(2)}) copy-start(bf16[64,8192]{1,0:T(8,128)(2,1)} %param.23) | copy-start | bytes 3145732
  23.0 6.6 %copy-start.2 = (bf16[64,8192]{1,0:T(8,128)(2,1)S(1)}, bf16[64,8192]{1,0:T(8,128)(2,1)}, u32[]{:S(2)}) copy-start(bf16[64,8192]{1,0:T(8,128)(2,1)} %param.24) | copy-start | bytes 3145732
  23.1 1.6 %collective-permute-start.2 = (f32[8,2,4096]{2,0,1:T(8,128)S(1)}, f32[8,2,4096]{2,0,1:T(8,128)S(1)}, u32[]{:S(2)}, u32[]{:S(2)}) collective-permute-start(f32[8,2,4096]{2,0,1:T(8,128)S(1)} %fusion.13), channel_id=1, source_target_pairs={{0,1},{1,0},{2,3},{3,2},{4,5},{5,4},{6,7},{7,6},{8,9},{9,8},{10,11... | collective-permute-start | bytes 786440 | tf_op jit(solution)/shard_map/ppermute | solution.py:18
  24.8 4.4 %collective-permute-start.3 = (bf16[8,4096]{1,0:T(8,128)(2,1)S(1)}, bf16[8,4096]{1,0:T(8,128)(2,1)S(1)}, u32[]{:S(2)}, u32[]{:S(2)}) collective-permute-start(bf16[8,4096]{1,0:T(8,128)(2,1)S(1)} %fusion.27), channel_id=1, source_target_pairs={{0,1},{1,0},{2,3},{3,2},{4,5},{5,4},{6,7},{7,6},{8,9},{9,8},{10,11... | collective-permute-start | bytes 196616 | tf_op jit(solution)/shard_map/ppermute | solution.py:18
  25.8 11.1 %all-to-all-start.1 = ((bf16[8,2,4096]{2,1,0:T(2,128)(2,1)}), bf16[8,2,4096]{2,1,0:T(2,128)(2,1)S(1)}, u32[]{:S(2)}, u32[]{:S(2)}) async-start(bf16[8,2,4096]{2,1,0:T(2,128)(2,1)} %copy.39), calls=%async_computation.1 | async-start | bytes 262144 | tf_op jit(solution)/shard_map/all_to_all | solution.py:134
  30.2 7.1 %collective-permute-start.4 = (f32[8,4096]{1,0:T(8,128)S(1)}, f32[8,4096]{1,0:T(8,128)S(1)}, u32[]{:S(2)}, u32[]{:S(2)}) collective-permute-start(f32[8,4096]{1,0:T(8,128)S(1)} %fusion.10), channel_id=1, source_target_pairs={{0,1},{1,0},{2,3},{3,2},{4,5},{5,4},{6,7},{7,6},{8,9},{9,8},{10,11... | collective-permute-start | bytes 393224 | tf_op jit(solution)/shard_map/ppermute | solution.py:18

commit v6 on v5

--- a/solution.py
+++ b/solution.py
@@ -70,6 +70,23 @@
     return kept, given
 
 
+def cold_split(features, gate_rows, up_rows, myself):
+    width = features.shape[1]
+    gate_cols = lax.dynamic_slice_in_dim(gate_rows, myself * width, width, 1)
+    up_cols = lax.dynamic_slice_in_dim(up_rows, myself * width, width, 1)
+    gate = jnp.einsum("rd,nd->rn", features, gate_cols, preferred_element_type=jnp.float32)
+    upper = jnp.einsum("rd,nd->rn", features, up_cols, preferred_element_type=jnp.float32)
+    return [gate, upper]
+
+
+def cold_down_half(gate, upper, down_rows, myself, rows_shape):
+    hidden = (jax.nn.silu(gate) * upper).astype(jnp.bfloat16)
+    hidden = hidden.reshape(rows_shape + hidden.shape[-1:])
+    width = down_rows.shape[1] // 2
+    down_cols = lax.dynamic_slice_in_dim(down_rows, myself * width, width, 1)
+    return jnp.einsum("...n,nd->...d", hidden, down_cols, preferred_element_type=jnp.float32)
+
+
 def collect_rows(selector, returned):
     return lax.dot_general(
         selector,
@@ -97,6 +114,9 @@
     cold_down,
     active,
 ):
+    gate_other = partner(cold_gate, "heads", 0)
+    up_other = partner(cold_up, "heads", 0)
+    down_other = partner(cold_down, "heads", 0)
     attended = attention_rows(query, key_cache, value_cache, key_new, value_new, lengths)
     stream = (residual_in.astype(jnp.float32) + attended).astype(jnp.bfloat16)
     half_width = stream.shape[1]
@@ -124,11 +144,18 @@
         preferred_element_type=jnp.float32,
     ).astype(jnp.bfloat16)
     incoming_half = lax.all_to_all(outgoing, "rows", split_axis=0, concat_axis=0, tiled=True)
-    incoming = join_halves(incoming_half.reshape(owner_count * CAP, -1), myself)
-    kept, given = swiglu_halves(
-        incoming, cold_gate, cold_up, cold_down, myself, (owner_count, CAP)
-    )
-    owner_sum = (kept + partner(given, "heads", 0)).astype(jnp.bfloat16)
+    features = incoming_half.reshape(owner_count * CAP, -1)
+    mine = cold_split(features, cold_gate, cold_up, myself)
+    theirs = cold_split(features, gate_other, up_other, myself)
+    partials = jnp.stack(mine + theirs)
+    echoed = partner(partials, "heads", 0)
+    gate_mine = partials[0] + echoed[2]
+    upper_mine = partials[1] + echoed[3]
+    gate_theirs = partials[2] + echoed[0]
+    upper_theirs = partials[3] + echoed[1]
+    kept = cold_down_half(gate_mine, upper_mine, cold_down, myself, (owner_count, CAP))
+    given = cold_down_half(gate_theirs, upper_theirs, down_other, myself, (owner_count, CAP))
+    owner_sum = (kept + given).astype(jnp.bfloat16)
     scaled_late, owner_sum = lax.optimization_barrier((scaled.astype(jnp.bfloat16), owner_sum))
     normed_late = join_halves(scaled_late, myself)
     returned = lax.all_to_all(owner_sum, "rows", split_axis=0, concat_axis=0, tiled=True)

time: 38.5 us -> 40.1 us (1.042)
  blocking collectives: 14.3 us -> 0 us
  starting transfers between devices: 4.79 us -> 12.3 us
  waiting for transfers between devices: 9.04 us -> 14.8 us
  matrix products: 4.87 us -> 8.15 us
  local copies, waits for them, and re-layouts: 4.33 us -> 3.48 us
    all_to_all x1 -> x0, blocking collectives: 14.3 us -> none  [local(): lax.all_to_all(outgoing, 'rows', split_axis=0, concat_axis=0, tiled=True)]
    all_to_all x0 -> x1, starting transfers between devices: none -> 7.1 us  [local(): lax.all_to_all(outgoing, 'rows', split_axis=0, concat_axis=0, tiled=True)]
    all_to_all x0 -> x1, waiting for transfers between devices: none -> 6.68 us  [local(): lax.all_to_all(outgoing, 'rows', split_axis=0, concat_axis=0, tiled=True)]
    dot_general x0 -> x6, matrix products: none -> 4.12 us  [the longest x2 1.42 us: cold_split(): jnp.einsum('rd,nd->rn', features, up_cols, preferred_element_type=jnp.flo...]
    unnamed x28, local copies, waits for them, and re-layouts: 2.48 us -> 0.99 us
    ppermute x5 -> x7, waiting for transfers between devices: 2.71 us -> 1.79 us  [partner(): return lax.ppermute(block, axis, route)]
    convert_element_type x1, local copies, waits for them, and re-layouts: 0.14 us -> 0.78 us  [local(): outgoing = jnp.einsum('ocr,rd->ocd', selector3.astype(jnp.bfloat16), scal...]
    ppermute x5 -> x7, starting transfers between devices: 1.42 us -> 1.86 us  [partner(): return lax.ppermute(block, axis, route)]
  transfers between devices with their start and end apart: 6 -> 9, of which waited for: 3 -> 4; matrix products, arithmetic and copies ran while one was open for 6% -> 13% of each run, Pallas kernels for 0% -> 0%
where the time goes in v6:
time: 40.1 us; the launch traced here: 39.7 us
  waiting for transfers between devices  14.8 us (37%)
  starting transfers between devices  12.3 us (31%)
  matrix products  8.15 us (20%)
  local copies, waits for them, and re-layouts  3.48 us (9%)
  other arithmetic  0.61 us (2%)
    all_to_all x1, starting transfers between devices, local(): lax.all_to_all(outgoing, 'rows', split_axis=0, concat_axis=0, tiled=True)  7.1 us
    all_to_all x1, waiting for transfers between devices, local(): lax.all_to_all(outgoing, 'rows', split_axis=0, concat_axis=0, tiled=True)  6.68 us
    all_to_all x1, waiting for transfers between devices, local(): lax.all_to_all(owner_sum, 'rows', split_axis=0, concat_axis=0, tiled=True)  6.33 us
    all_to_all x1, starting transfers between devices, local(): lax.all_to_all(owner_sum, 'rows', split_axis=0, concat_axis=0, tiled=True)  3.37 us
    ppermute x7, starting transfers between devices, partner(): return lax.ppermute(block, axis, route)  1.86 us
    ppermute x7, waiting for transfers between devices, partner(): return lax.ppermute(block, axis, route)  1.79 us
    dot_general x2, matrix products, cold_split(): jnp.einsum('rd,nd->rn', features, up_cols, preferred_element_type=jnp.flo...  1.42 us
    dot_general x2, matrix products, cold_down_half(): jnp.einsum('...n,nd->...d', hidden, down_cols, preferred_element_type=jnp...  1.37 us
  transfers between devices with their start and end apart: 9, of which 4 were waited for; matrix products, arithmetic and copies ran while one was open for 13% of the time, Pallas kernels for 0%

profile of v6, /device:TPU:0, one launch (start us, length us, event | category | flops | bytes accessed | tf_op | source)
XLA Modules:
  0.0 39.7 jit_solution(16585897839239451558)
XLA Ops:
  0.0 0.0 copy-start
  0.0 0.0 copy-start.9
  0.0 0.8 %copy.31 = bf16[8,2,1,128]{3,2,1,0:T(2,128)(2,1)S(1)} copy(bf16[8,2,1,128]{3,1,0,2:T(2,128)(2,1)} %bitcast.91) | data formatting | bytes 8192 | tf_op jit(solution)/shard_map/broadcast_in_dim | solution.py:34
  0.8 0.0 copy-done.9
  0.8 0.0 copy-start.10
  0.8 0.6 %copy-done.10 = s32[8]{0:T(128)S(1)} copy-done((s32[8]{0:T(128)S(1)}, s32[8]{0:T(128)}, u32[]{:S(2)}) %copy-start.10) | copy-done | bytes 56
  1.5 0.1 fusion.66
  1.5 0.0 copy-start.11
  1.6 1.3 %fusion.97 = f32[8,2,16]{2,1,0:T(2,128)S(1)} fusion(bf16[8,2,1,128]{3,2,1,0:T(2,128)(2,1)S(1)} %copy.31, bf16[8,2,32,128]{3,2,1,0:T(8,128)(2,1)} %param.17, bf16[8,2,16,128]{3,0,2,1:T(8,128)(2,1)} %bitcast.93, pred[8,33]{1,0:T(8,128)(4,1)S(1)} %fusion.66), kind=kOutput, calls=%fused_computation.96 | convolution fusion | flops 2475296 | bytes 201992 | tf_op jit(solution)/shard_map/sub | solution.py:44
  2.9 0.0 copy-done.11
  2.9 0.0 copy-done.12
  2.9 0.0 copy-done.13
  2.9 0.0 copy-start.6
  2.9 0.0 copy-start.7
  2.9 0.0 copy-start.8
  3.0 0.0 copy-start.5
  3.0 0.5 %fusion.29 = f32[8,2,16,128]{3,2,1,0:T(8,128)S(1)} fusion(bf16[8,2,1,128]{3,2,1,0:T(2,128)(2,1)S(1)} %copy.34, bf16[8,2,32,128]{3,2,1,0:T(8,128)(2,1)S(1)} %copy-done.11, f32[8,2,16]{2,1,0:T(2,128)S(1)} %fusion.97, pred[8,33]{1,0:T(8,128)(4,1)S(1)} %fusion.66, bf16[8,2,1,128]{3,2,1,0:T(2,128)(2,1)S(1)} %copy.31, bf16[8,2,32,128]{3,2,1,0:T(8,128)(2,1)S(1)} %copy-done.12, ...), kind=kOutput, calls=%fused_computation.35 | convolution fusion | flops 4917024 | bytes 468232 | tf_op jit(solution)/shard_map/rgjp,rgpd->rgjd/dot_general | solution.py:47
  3.5 0.3 copy-done.6
  3.8 0.2 fusion.33
  4.0 0.5 %collective-permute-start = (f32[8]{0:T(128)S(1)}, f32[8]{0:T(128)S(1)}, u32[]{:S(2)}, u32[]{:S(2)}) collective-permute-start(f32[8]{0:T(128)S(1)} %get-tuple-element.9), channel_id=1, source_target_pairs={{0,1},{1,0},{2,3},{3,2},{4,5},{5,4},{6,7},{7,6},{8,9},{9,8},{10,11... | collective-permute-start | bytes 104 | tf_op jit(solution)/shard_map/ppermute | solution.py:18
  4.5 0.0 copy-done.7
  4.5 0.2 reduce_window_sum.11
  4.7 0.0 copy-done.8
  4.7 0.6 %collective-permute-done = f32[8]{0:T(128)S(1)} collective-permute-done((f32[8]{0:T(128)S(1)}, f32[8]{0:T(128)S(1)}, u32[]{:S(2)}, u32[]{:S(2)}) %collective-permute-start) | collective-permute-done | bytes 64 | tf_op jit(solution)/shard_map/ppermute | solution.py:18
  5.3 0.1 fusion.35
  5.4 0.2 convolution_convert_fusion
  5.6 0.8 %copy.36 = bf16[8,2,4096]{2,1,0:T(2,128)(2,1)} copy(bf16[8,2,4096]{2,0,1:T(8,128)(2,1)S(1)} %convolution_convert_fusion) | data formatting | bytes 262144 | tf_op jit(solution)/shard_map/convert_element_type | solution.py:145
  6.4 7.1 %all-to-all-start = ((bf16[8,2,4096]{2,1,0:T(2,128)(2,1)}), bf16[8,2,4096]{2,1,0:T(2,128)(2,1)S(1)}, u32[]{:S(2)}, u32[]{:S(2)}) async-start(bf16[8,2,4096]{2,1,0:T(2,128)(2,1)} %copy.36), calls=%async_computation | async-start | bytes 262144 | tf_op jit(solution)/shard_map/all_to_all | solution.py:146
  13.5 0.0 copy-done.3
  13.5 0.1 collective-permute-start.1
  13.6 0.0 copy-done.4
  13.6 0.5 %collective-permute-start.2 = (bf16[32,8192]{1,0:T(8,128)(2,1)S(1)}, bf16[32,8192]{1,0:T(8,128)(2,1)}, u32[]{:S(2)}, u32[]{:S(2)}) collective-permute-start(bf16[32,8192]{1,0:T(8,128)(2,1)S(1)} %copy-done.4), channel_id=1, source_target_pairs={{0,1},{1,0},{2,3},{3,2},{4,5},{5,4},{6,7},{7,6},{8,9},{9,8},{10,11... | collective-permute-start | bytes 1572872 | tf_op jit(solution)/shard_map/ppermute | solution.py:18
  14.1 0.0 copy-done.5
  14.1 0.1 collective-permute-start.4
  14.1 6.7 %all-to-all-done = bf16[8,2,4096]{2,1,0:T(2,128)(2,1)S(1)} async-done(((bf16[8,2,4096]{2,1,0:T(2,128)(2,1)}), bf16[8,2,4096]{2,1,0:T(2,128)(2,1)S(1)}, u32[]{:S(2)}, u32[]{:S(2)}) %all-to-all-start) | async-done | bytes 131104 | tf_op jit(solution)/shard_map/all_to_all | solution.py:146
  20.8 0.1 reshape.63
  20.9 0.2 fusion.24
  21.1 0.2 fusion.22
  21.3 0.0 collective-permute-done.1
  21.3 1.1 %fusion.20 = f32[16,32]{1,0:T(8,128)S(1)} fusion(bf16[16,4096]{1,0:T(8,128)(2,1)S(1)} %reshape.63, bf16[32,8192]{1,0:T(8,128)(2,1)} %collective-permute-done.1, s32[]{:T(128)S(6)} %select_n.35), kind=kOutput, calls=%fused_computation.24 | convolution fusion | flops 4194304 | bytes 395268 | tf_op jit(solution)/shard_map/rd,nd->rn/dot_general | solution.py:77
  22.4 0.0 collective-permute-done.2
  22.4 1.2 %fusion.18 = f32[16,32]{1,0:T(8,128)S(1)} fusion(bf16[16,4096]{1,0:T(8,128)(2,1)S(1)} %reshape.63, bf16[32,8192]{1,0:T(8,128)(2,1)} %collective-permute-done.2, s32[]{:T(128)S(6)} %select_n.35), kind=kOutput, calls=%fused_computation.22 | convolution fusion | flops 4194304 | bytes 395268 | tf_op jit(solution)/shard_map/rd,nd->rn/dot_general | solution.py:78
  23.7 0.1 collective-permute-start.3
  23.8 1.2 %collective-permute-done.3 = f32[4,16,32]{2,1,0:T(8,128)S(1)} collective-permute-done((f32[4,16,32]{2,1,0:T(8,128)S(1)}, f32[4,16,32]{2,1,0:T(8,128)S(1)}, u32[]{:S(2)}, u32[]{:S(2)}) %collective-permute-start.3) | collective-permute-done | bytes 8224 | tf_op jit(solution)/shard_map/ppermute | solution.py:18
  25.0 0.2 fusion.14
  25.1 0.0 collective-permute-done.4
  25.2 0.0 copy-start.2
  25.2 1.2 %fusion.1 = bf16[8,2,4096]{2,0,1:T(8,128)(2,1)S(1)} fusion(f32[8,2,4096]{2,0,1:T(8,128)S(1)} %fusion.14, bf16[32,8192]{1,0:T(8,128)(2,1)} %collective-permute-done.4, s32[]{:T(128)S(6)} %select_n.35, bf16[8,2,32]{2,1,0:T(2,128)(2,1)S(1)} %bitcast.88), kind=kOutput, calls=%fused_computation.2 | convolution fusion | flops 4325376 | bytes 656388 | tf_op jit(solution)/shard_map/...n,nd->...d/dot_general | solution.py:87
  26.4 0.2 collective-permute-start.5
  26.6 0.8 %copy.39 = bf16[8,2,4096]{2,1,0:T(2,128)(2,1)} copy(bf16[8,2,4096]{2,0,1:T(8,128)(2,1)S(1)} %fusion.1) | data formatting | bytes 262144 | tf_op jit(solution)/shard_map/optimization_barrier | solution.py:159
  27.4 3.4 %all-to-all-start.1 = ((bf16[8,2,4096]{2,1,0:T(2,128)(2,1)}), bf16[8,2,4096]{2,1,0:T(2,128)(2,1)S(1)}, u32[]{:S(2)}, u32[]{:S(2)}) async-start(bf16[8,2,4096]{2,1,0:T(2,128)(2,1)} %copy.39), calls=%async_computation.1 | async-start | bytes 262144 | tf_op jit(solution)/shard_map/all_to_all | solution.py:161
  30.8 0.0 collective-permute-done.5
  30.8 0.0 copy-done.1
  30.8 0.4 fusion.41
  31.2 0.0 copy-done.2
  31.2 0.4 multiply_convert_fusion
  31.6 0.0 copy-done
  31.6 0.2 fusion.10
  31.8 0.4 %collective-permute-start.6 = (f32[8,4096]{1,0:T(8,128)S(1)}, f32[8,4096]{1,0:T(8,128)S(1)}, u32[]{:S(2)}, u32[]{:S(2)}) collective-permute-start(f32[8,4096]{1,0:T(8,128)S(1)} %fusion.10), channel_id=1, source_target_pairs={{0,1},{1,0},{2,3},{3,2},{4,5},{5,4},{6,7},{7,6},{8,9},{9,8},{10,11... | collective-permute-start | bytes 393224 | tf_op jit(solution)/shard_map/ppermute | solution.py:18
  32.2 6.3 %all-to-all-done.1 = bf16[8,2,4096]{2,1,0:T(2,128)(2,1)S(1)} async-done(((bf16[8,2,4096]{2,1,0:T(2,128)(2,1)}), bf16[8,2,4096]{2,1,0:T(2,128)(2,1)S(1)}, u32[]{:S(2)}, u32[]{:S(2)}) %all-to-all-start.1) | async-done | bytes 131104 | tf_op jit(solution)/shard_map/all_to_all | solution.py:161
  38.5 0.1 reshape.66
  38.6 0.3 fusion.102
  38.8 0.0 collective-permute-done.6
  38.8 0.8 %fusion.4 = bf16[8,4096]{1,0:T(8,128)(2,1)} fusion(f32[8,4096]{1,0:T(8,128)S(1)} %fusion.102, f32[8,4096]{1,0:T(8,128)S(1)} %collective-permute-done.6, bf16[8,64]{1,0:T(8,128)(2,1)S(1)} %multiply_convert_fusion, bf16[64,8192]{1,0:T(8,128)(2,1)S(1)} %copy-done, s32[]{:T(128)S(6)} %select_n.35, bf16[8,4096]{1,0:T(8,128)(2,1)S(1)} %get-tuple-element.10), kind=kOutput, calls=%fused_computation.7 | convolution fusion | flops 4358144 | bytes 919556 | tf_op jit(solution)/shard_map/...n,nd->...d/dot_general | solution.py:69
  (16 shorter events, 0.1 us)
Async XLA Ops:
  0.0 31.6 %copy-start = (bf16[64,8192]{1,0:T(8,128)(2,1)S(1)}, bf16[64,8192]{1,0:T(8,128)(2,1)}, u32[]{:S(2)}) copy-start(bf16[64,8192]{1,0:T(8,128)(2,1)} %param.25) | copy-start | bytes 3145732
  0.0 0.8 %copy-start.9 = (bf16[8,2,128]{2,1,0:T(2,128)(2,1)S(1)}, bf16[8,2,128]{2,1,0:T(2,128)(2,1)}, u32[]{:S(2)}) copy-start(bf16[8,2,128]{2,1,0:T(2,128)(2,1)} %param.20) | copy-start | bytes 12292
  0.8 0.7 %copy-start.10 = (s32[8]{0:T(128)S(1)}, s32[8]{0:T(128)}, u32[]{:S(2)}) copy-start(s32[8]{0:T(128)} %param.21) | copy-start | bytes 100
  1.5 1.4 %copy-start.11 = (bf16[8,2,32,128]{3,2,1,0:T(8,128)(2,1)S(1)}, bf16[8,2,32,128]{3,2,1,0:T(8,128)(2,1)}, u32[]{:S(2)}) copy-start(bf16[8,2,32,128]{3,2,1,0:T(8,128)(2,1)} %param.18) | copy-start | bytes 393220
  1.5 1.4 %copy-start.12 = (bf16[8,2,32,128]{3,2,1,0:T(8,128)(2,1)S(1)}, bf16[8,2,32,128]{3,2,1,0:T(8,128)(2,1)}, u32[]{:S(2)}) copy-start(bf16[8,2,32,128]{3,2,1,0:T(8,128)(2,1)} %param.17) | copy-start | bytes 393220
  1.5 1.4 %copy-start.13 = (bf16[8,4096]{1,0:T(8,128)(2,1)S(1)}, bf16[8,4096]{1,0:T(8,128)(2,1)}, u32[]{:S(2)}) copy-start(bf16[8,4096]{1,0:T(8,128)(2,1)} %param.16) | copy-start | bytes 196612
  2.9 0.8 %copy-start.6 = (bf16[8,4096]{1,0:T(8,128)(2,1)S(1)}, bf16[8,4096]{1,0:T(8,128)(2,1)}, u32[]{:S(2)}) copy-start(bf16[8,4096]{1,0:T(8,128)(2,1)} %param.15) | copy-start | bytes 196612
  2.9 1.6 %copy-start.7 = (s32[8,4]{0,1:T(4,128)S(1)}, s32[8,4]{0,1:T(4,128)}, u32[]{:S(2)}) copy-start(s32[8,4]{0,1:T(4,128)} %param.29) | copy-start | bytes 388
  2.9 1.7 %copy-start.8 = (bf16[8192]{0:T(1024)(128)(2,1)S(1)}, bf16[8192]{0:T(1024)(128)(2,1)}, u32[]{:S(2)}) copy-start(bf16[8192]{0:T(1024)(128)(2,1)} %param.22) | copy-start | bytes 49156
  3.0 11.1 %copy-start.5 = (bf16[32,8192]{1,0:T(8,128)(2,1)S(1)}, bf16[32,8192]{1,0:T(8,128)(2,1)}, u32[]{:S(2)}) copy-start(bf16[32,8192]{1,0:T(8,128)(2,1)} %param.28) | copy-start | bytes 1572868
  3.8 9.8 %copy-start.4 = (bf16[32,8192]{1,0:T(8,128)(2,1)S(1)}, bf16[32,8192]{1,0:T(8,128)(2,1)}, u32[]{:S(2)}) copy-start(bf16[32,8192]{1,0:T(8,128)(2,1)} %param.27) | copy-start | bytes 1572868
  4.0 9.5 %copy-start.3 = (bf16[32,8192]{1,0:T(8,128)(2,1)S(1)}, bf16[32,8192]{1,0:T(8,128)(2,1)}, u32[]{:S(2)}) copy-start(bf16[32,8192]{1,0:T(8,128)(2,1)} %param.26) | copy-start | bytes 1572868
  4.0 1.3 %collective-permute-start = (f32[8]{0:T(128)S(1)}, f32[8]{0:T(128)S(1)}, u32[]{:S(2)}, u32[]{:S(2)}) collective-permute-start(f32[8]{0:T(128)S(1)} %get-tuple-element.9), channel_id=1, source_target_pairs={{0,1},{1,0},{2,3},{3,2},{4,5},{5,4},{6,7},{7,6},{8,9},{9,8},{10,11... | collective-permute-start | bytes 104 | tf_op jit(solution)/shard_map/ppermute | solution.py:18
  6.4 14.5 %all-to-all-start = ((bf16[8,2,4096]{2,1,0:T(2,128)(2,1)}), bf16[8,2,4096]{2,1,0:T(2,128)(2,1)S(1)}, u32[]{:S(2)}, u32[]{:S(2)}) async-start(bf16[8,2,4096]{2,1,0:T(2,128)(2,1)} %copy.36), calls=%async_computation | async-start | bytes 262144 | tf_op jit(solution)/shard_map/all_to_all | solution.py:146
  13.5 7.8 %collective-permute-start.1 = (bf16[32,8192]{1,0:T(8,128)(2,1)S(1)}, bf16[32,8192]{1,0:T(8,128)(2,1)}, u32[]{:S(2)}, u32[]{:S(2)}) collective-permute-start(bf16[32,8192]{1,0:T(8,128)(2,1)S(1)} %copy-done.3), channel_id=1, source_target_pairs={{0,1},{1,0},{2,3},{3,2},{4,5},{5,4},{6,7},{7,6},{8,9},{9,8},{10,11... | collective-permute-start | bytes 1572872 | tf_op jit(solution)/shard_map/ppermute | solution.py:18
  13.6 8.9 %collective-permute-start.2 = (bf16[32,8192]{1,0:T(8,128)(2,1)S(1)}, bf16[32,8192]{1,0:T(8,128)(2,1)}, u32[]{:S(2)}, u32[]{:S(2)}) collective-permute-start(bf16[32,8192]{1,0:T(8,128)(2,1)S(1)} %copy-done.4), channel_id=1, source_target_pairs={{0,1},{1,0},{2,3},{3,2},{4,5},{5,4},{6,7},{7,6},{8,9},{9,8},{10,11... | collective-permute-start | bytes 1572872 | tf_op jit(solution)/shard_map/ppermute | solution.py:18
  14.1 11.1 %collective-permute-start.4 = (bf16[32,8192]{1,0:T(8,128)(2,1)S(1)}, bf16[32,8192]{1,0:T(8,128)(2,1)}, u32[]{:S(2)}, u32[]{:S(2)}) collective-permute-start(bf16[32,8192]{1,0:T(8,128)(2,1)S(1)} %copy-done.5), channel_id=1, source_target_pairs={{0,1},{1,0},{2,3},{3,2},{4,5},{5,4},{6,7},{7,6},{8,9},{9,8},{10,11... | collective-permute-start | bytes 1572872 | tf_op jit(solution)/shard_map/ppermute | solution.py:18
  22.4 8.4 %copy-start.1 = (bf16[64,8192]{1,0:T(8,128)(2,1)S(1)}, bf16[64,8192]{1,0:T(8,128)(2,1)}, u32[]{:S(2)}) copy-start(bf16[64,8192]{1,0:T(8,128)(2,1)} %param.23) | copy-start | bytes 3145732
  23.7 1.3 %collective-permute-start.3 = (f32[4,16,32]{2,1,0:T(8,128)S(1)}, f32[4,16,32]{2,1,0:T(8,128)S(1)}, u32[]{:S(2)}, u32[]{:S(2)}) collective-permute-start(f32[4,16,32]{2,1,0:T(8,128)S(1)} %pad_maximum_fusion), channel_id=1, source_target_pairs={{0,1},{1,0},{2,3},{3,2},{4,5},{5,4},{6,7},{7,6},{8,9},{9,8},{10,11... | collective-permute-start | bytes 24584 | tf_op jit(solution)/shard_map/ppermute | solution.py:18
  25.2 6.0 %copy-start.2 = (bf16[64,8192]{1,0:T(8,128)(2,1)S(1)}, bf16[64,8192]{1,0:T(8,128)(2,1)}, u32[]{:S(2)}) copy-start(bf16[64,8192]{1,0:T(8,128)(2,1)} %param.24) | copy-start | bytes 3145732
  26.4 4.4 %collective-permute-start.5 = (bf16[8,4096]{1,0:T(8,128)(2,1)S(1)}, bf16[8,4096]{1,0:T(8,128)(2,1)S(1)}, u32[]{:S(2)}, u32[]{:S(2)}) collective-permute-start(bf16[8,4096]{1,0:T(8,128)(2,1)S(1)} %fusion.35), channel_id=1, source_target_pairs={{0,1},{1,0},{2,3},{3,2},{4,5},{5,4},{6,7},{7,6},{8,9},{9,8},{10,11... | collective-permute-start | bytes 196616 | tf_op jit(solution)/shard_map/ppermute | solution.py:18
  27.4 11.1 %all-to-all-start.1 = ((bf16[8,2,4096]{2,1,0:T(2,128)(2,1)}), bf16[8,2,4096]{2,1,0:T(2,128)(2,1)S(1)}, u32[]{:S(2)}, u32[]{:S(2)}) async-start(bf16[8,2,4096]{2,1,0:T(2,128)(2,1)} %copy.39), calls=%async_computation.1 | async-start | bytes 262144 | tf_op jit(solution)/shard_map/all_to_all | solution.py:161
  31.8 7.1 %collective-permute-start.6 = (f32[8,4096]{1,0:T(8,128)S(1)}, f32[8,4096]{1,0:T(8,128)S(1)}, u32[]{:S(2)}, u32[]{:S(2)}) collective-permute-start(f32[8,4096]{1,0:T(8,128)S(1)} %fusion.10), channel_id=1, source_target_pairs={{0,1},{1,0},{2,3},{3,2},{4,5},{5,4},{6,7},{7,6},{8,9},{9,8},{10,11... | collective-permute-start | bytes 393224 | tf_op jit(solution)/shard_map/ppermute | solution.py:18

commit v7 on v6

--- a/solution.py
+++ b/solution.py
@@ -70,20 +70,25 @@
     return kept, given
 
 
-def cold_split(features, gate_rows, up_rows, myself):
-    width = features.shape[1]
-    gate_cols = lax.dynamic_slice_in_dim(gate_rows, myself * width, width, 1)
-    up_cols = lax.dynamic_slice_in_dim(up_rows, myself * width, width, 1)
+def my_half(rows, myself):
+    width = rows.shape[1] // 2
+    return lax.dynamic_slice_in_dim(rows, myself * width, width, 1)
+
+
+def their_half(rows, myself):
+    width = rows.shape[1] // 2
+    return lax.dynamic_slice_in_dim(rows, (1 - myself) * width, width, 1)
+
+
+def cold_split(features, gate_cols, up_cols):
     gate = jnp.einsum("rd,nd->rn", features, gate_cols, preferred_element_type=jnp.float32)
     upper = jnp.einsum("rd,nd->rn", features, up_cols, preferred_element_type=jnp.float32)
     return [gate, upper]
 
 
-def cold_down_half(gate, upper, down_rows, myself, rows_shape):
+def cold_down_half(gate, upper, down_cols, rows_shape):
     hidden = (jax.nn.silu(gate) * upper).astype(jnp.bfloat16)
     hidden = hidden.reshape(rows_shape + hidden.shape[-1:])
-    width = down_rows.shape[1] // 2
-    down_cols = lax.dynamic_slice_in_dim(down_rows, myself * width, width, 1)
     return jnp.einsum("...n,nd->...d", hidden, down_cols, preferred_element_type=jnp.float32)
 
 
@@ -114,9 +119,10 @@
     cold_down,
     active,
 ):
-    gate_other = partner(cold_gate, "heads", 0)
-    up_other = partner(cold_up, "heads", 0)
-    down_other = partner(cold_down, "heads", 0)
+    myself = lax.axis_index("heads")
+    gate_other = partner(their_half(cold_gate, myself), "heads", 0)
+    up_other = partner(their_half(cold_up, myself), "heads", 0)
+    down_other = partner(their_half(cold_down, myself), "heads", 0)
     attended = attention_rows(query, key_cache, value_cache, key_new, value_new, lengths)
     stream = (residual_in.astype(jnp.float32) + attended).astype(jnp.bfloat16)
     half_width = stream.shape[1]
@@ -144,17 +150,19 @@
         preferred_element_type=jnp.float32,
     ).astype(jnp.bfloat16)
     incoming_half = lax.all_to_all(outgoing, "rows", split_axis=0, concat_axis=0, tiled=True)
-    features = incoming_half.reshape(owner_count * CAP, -1)
-    mine = cold_split(features, cold_gate, cold_up, myself)
-    theirs = cold_split(features, gate_other, up_other, myself)
+    features, gate_other, up_other, down_other = lax.optimization_barrier(
+        (incoming_half.reshape(owner_count * CAP, -1), gate_other, up_other, down_other)
+    )
+    mine = cold_split(features, my_half(cold_gate, myself), my_half(cold_up, myself))
+    theirs = cold_split(features, gate_other, up_other)
     partials = jnp.stack(mine + theirs)
     echoed = partner(partials, "heads", 0)
     gate_mine = partials[0] + echoed[2]
     upper_mine = partials[1] + echoed[3]
     gate_theirs = partials[2] + echoed[0]
     upper_theirs = partials[3] + echoed[1]
-    kept = cold_down_half(gate_mine, upper_mine, cold_down, myself, (owner_count, CAP))
-    given = cold_down_half(gate_theirs, upper_theirs, down_other, myself, (owner_count, CAP))
+    kept = cold_down_half(gate_mine, upper_mine, my_half(cold_down, myself), (owner_count, CAP))
+    given = cold_down_half(gate_theirs, upper_theirs, down_other, (owner_count, CAP))
     owner_sum = (kept + given).astype(jnp.bfloat16)
     scaled_late, owner_sum = lax.optimization_barrier((scaled.astype(jnp.bfloat16), owner_sum))
     normed_late = join_halves(scaled_late, myself)

time: 40.1 us -> 41.6 us (1.037)
  blocking collectives: 0 us -> 14.4 us
  waiting for transfers between devices: 14.8 us -> 7.54 us
  starting transfers between devices: 12.3 us -> 5.21 us
  local copies, waits for them, and re-layouts: 3.48 us -> 4.97 us
    all_to_all x0 -> x1, blocking collectives: none -> 14.4 us  [local(): lax.all_to_all(outgoing, 'rows', split_axis=0, concat_axis=0, tiled=True)]
    all_to_all x1 -> x0, starting transfers between devices: 7.1 us -> none  [local(): lax.all_to_all(outgoing, 'rows', split_axis=0, concat_axis=0, tiled=True)]
    all_to_all x1 -> x0, waiting for transfers between devices: 6.68 us -> none  [local(): lax.all_to_all(outgoing, 'rows', split_axis=0, concat_axis=0, tiled=True)]
    dynamic_slice x0 -> x3, local copies, waits for them, and re-layouts: none -> 1.46 us  [their_half(): return lax.dynamic_slice_in_dim(rows, (1 - myself) * width, width, 1)]
    unnamed x28, local copies, waits for them, and re-layouts: 0.99 us -> 1.68 us
    convert_element_type x1, local copies, waits for them, and re-layouts: 0.78 us -> 0.14 us  [local(): outgoing = jnp.einsum('ocr,rd->ocd', selector3.astype(jnp.bfloat16), scal...]
    ppermute x7, waiting for transfers between devices: 1.79 us -> 1.21 us  [partner(): return lax.ppermute(block, axis, route)]
  transfers between devices with their start and end apart: 9 -> 8, of which waited for: 4 -> 2; matrix products, arithmetic and copies ran while one was open for 13% -> 10% of each run, Pallas kernels for 0% -> 0%
where the time goes in v7:
time: 41.6 us; the launch traced here: 41.1 us
  blocking collectives  14.4 us (35%)
  matrix products  8.15 us (20%)
  waiting for transfers between devices  7.54 us (18%)
  starting transfers between devices  5.21 us (13%)
  local copies, waits for them, and re-layouts  4.97 us (12%)
  other arithmetic  0.61 us (1%)
    all_to_all x1, blocking collectives, local(): lax.all_to_all(outgoing, 'rows', split_axis=0, concat_axis=0, tiled=True)  14.4 us
    all_to_all x1, waiting for transfers between devices, local(): lax.all_to_all(owner_sum, 'rows', split_axis=0, concat_axis=0, tiled=True)  6.33 us
    all_to_all x1, starting transfers between devices, local(): lax.all_to_all(owner_sum, 'rows', split_axis=0, concat_axis=0, tiled=True)  3.37 us
    ppermute x7, starting transfers between devices, partner(): return lax.ppermute(block, axis, route)  1.84 us
    unnamed x28, local copies, waits for them, and re-layouts  1.68 us
    dynamic_slice x3, local copies, waits for them, and re-layouts, their_half(): return lax.dynamic_slice_in_dim(rows, (1 - myself) * width, width, 1)  1.46 us
    dot_general x2, matrix products, cold_split(): jnp.einsum('rd,nd->rn', features, up_cols, preferred_element_type=jnp.flo...  1.43 us
    dot_general x2, matrix products, cold_down_half(): jnp.einsum('...n,nd->...d', hidden, down_cols, preferred_element_type=jnp...  1.37 us
  transfers between devices with their start and end apart: 8, of which 2 were waited for; matrix products, arithmetic and copies ran while one was open for 10% of the time, Pallas kernels for 0%

profile of v7, /device:TPU:0, one launch (start us, length us, event | category | flops | bytes accessed | tf_op | source)
XLA Modules:
  0.0 41.1 jit_solution(3103208806468936872)
XLA Ops:
  0.0 0.0 copy-start
  0.0 0.0 copy-start.9
  0.0 0.8 %copy.31 = bf16[8,2,1,128]{3,2,1,0:T(2,128)(2,1)S(1)} copy(bf16[8,2,1,128]{3,1,0,2:T(2,128)(2,1)} %bitcast.93) | data formatting | bytes 8192 | tf_op jit(solution)/shard_map/broadcast_in_dim | solution.py:34
  0.8 0.0 copy-done.9
  0.8 0.0 copy-start.10
  0.8 0.6 %copy-done.10 = s32[8]{0:T(128)S(1)} copy-done((s32[8]{0:T(128)S(1)}, s32[8]{0:T(128)}, u32[]{:S(2)}) %copy-start.10) | copy-done | bytes 56
  1.5 0.1 fusion.61
  1.5 0.0 copy-start.12
  1.5 0.0 copy-start.13
  1.6 1.3 %fusion.89 = f32[8,2,16]{2,1,0:T(2,128)S(1)} fusion(bf16[8,2,1,128]{3,2,1,0:T(2,128)(2,1)S(1)} %copy.31, bf16[8,2,32,128]{3,2,1,0:T(8,128)(2,1)} %param.17, bf16[8,2,16,128]{3,0,2,1:T(8,128)(2,1)} %bitcast.95, pred[8,33]{1,0:T(8,128)(4,1)S(1)} %fusion.61), kind=kOutput, calls=%fused_computation.91 | convolution fusion | flops 2475296 | bytes 201992 | tf_op jit(solution)/shard_map/sub | solution.py:44
  2.9 0.0 copy-done.11
  2.9 0.0 copy-done.12
  2.9 0.0 copy-done.13
  2.9 0.0 copy-start.6
  2.9 0.0 copy-start.3
  2.9 0.5 %fusion.24 = f32[8,2,16,128]{3,2,1,0:T(8,128)S(1)} fusion(bf16[8,2,1,128]{3,2,1,0:T(2,128)(2,1)S(1)} %copy.34, bf16[8,2,32,128]{3,2,1,0:T(8,128)(2,1)S(1)} %copy-done.11, f32[8,2,16]{2,1,0:T(2,128)S(1)} %fusion.89, pred[8,33]{1,0:T(8,128)(4,1)S(1)} %fusion.61, bf16[8,2,1,128]{3,2,1,0:T(2,128)(2,1)S(1)} %copy.31, bf16[8,2,32,128]{3,2,1,0:T(8,128)(2,1)S(1)} %copy-done.12, ...), kind=kOutput, calls=%fused_computation.30 | convolution fusion | flops 4917024 | bytes 468232 | tf_op jit(solution)/shard_map/rgjp,rgpd->rgjd/dot_general | solution.py:47
  3.5 0.3 copy-done.6
  3.8 0.2 fusion.28
  4.0 0.5 %collective-permute-start = (f32[8]{0:T(128)S(1)}, f32[8]{0:T(128)S(1)}, u32[]{:S(2)}, u32[]{:S(2)}) collective-permute-start(f32[8]{0:T(128)S(1)} %get-tuple-element.17), channel_id=1, source_target_pairs={{0,1},{1,0},{2,3},{3,2},{4,5},{5,4},{6,7},{7,6},{8,9},{9,8},{10,11... | collective-permute-start | bytes 104 | tf_op jit(solution)/shard_map/ppermute | solution.py:18
  4.5 0.0 copy-done.3
  4.5 0.1 collective-permute-start.1
  4.6 0.0 copy-done.4
  4.6 0.7 %constant_dynamic-slice_fusion.1 = bf16[32,4096]{1,0:T(8,128)(2,1)} fusion(bf16[32,8192]{1,0:T(8,128)(2,1)S(1)} %copy-done.4, s32[]{:T(128)S(6)} %select_n.36), kind=kLoop, calls=%fused_computation.74 | loop fusion | bytes 524292 | tf_op jit(solution)/shard_map/dynamic_slice | solution.py:80
  5.3 0.5 %collective-permute-start.2 = (bf16[32,4096]{1,0:T(8,128)(2,1)}, bf16[32,4096]{1,0:T(8,128)(2,1)}, u32[]{:S(2)}, u32[]{:S(2)}) collective-permute-start(bf16[32,4096]{1,0:T(8,128)(2,1)} %constant_dynamic-slice_fusion.1), channel_id=1, source_target_pairs={{0,1},{1,0},{2,3},{3,2},{4,5},{5,4},{6,7},{7,6},{8,9},{9,8},{10,11... | collective-permute-start | bytes 786440 | tf_op jit(solution)/shard_map/ppermute | solution.py:18
  5.8 0.0 copy-done.5
  5.8 0.7 %constant_dynamic-slice_fusion = bf16[32,4096]{1,0:T(8,128)(2,1)} fusion(bf16[32,8192]{1,0:T(8,128)(2,1)S(1)} %copy-done.5, s32[]{:T(128)S(6)} %select_n.36), kind=kLoop, calls=%fused_computation.73 | loop fusion | bytes 524292 | tf_op jit(solution)/shard_map/dynamic_slice | solution.py:80
  6.5 0.1 collective-permute-start.3
  6.6 0.7 %copy-done.7 = s32[8,4]{0,1:T(4,128)S(1)} copy-done((s32[8,4]{0,1:T(4,128)S(1)}, s32[8,4]{0,1:T(4,128)}, u32[]{:S(2)}) %copy-start.7) | copy-done | bytes 152
  7.3 0.2 reduce_window_sum.11
  7.5 0.0 copy-done.8
  7.5 0.0 collective-permute-done
  7.5 0.1 fusion.30
  7.6 0.2 convolution_convert_fusion
  7.8 0.1 copy.36
  7.9 14.4 %all_to_all.10 = bf16[8,2,4096]{2,1,0:T(2,128)(2,1)S(1)} all-to-all(bf16[8,2,4096]{2,1,0:T(2,128)(2,1)S(1)} %copy.36), channel_id=1, replica_groups=mesh['groups'=2,'rows'=8,'heads'=2] {'rows'}, dimensions={0} | all-to-all | bytes 262144 | tf_op jit(solution)/shard_map/all_to_all | solution.py:152
  22.3 0.1 reshape.63
  22.4 0.0 collective-permute-done.1
  22.4 0.0 collective-permute-done.2
  22.4 0.0 collective-permute-done.3
  22.4 0.2 fusion.19
  22.6 0.2 fusion.17
  22.8 1.1 %fusion.94 = f32[16,32]{1,0:T(8,128)S(1)} fusion(bf16[16,4096]{1,0:T(8,128)(2,1)S(1)} %reshape.63, bf16[32,4096]{1,0:T(8,128)(2,1)} %collective-permute-done.1), kind=kOutput, calls=%fused_computation.92 | convolution fusion | flops 4194304 | bytes 395264 | tf_op jit(solution)/shard_map/rd,nd->rn/dot_general | solution.py:84
  23.9 1.2 %fusion.95 = f32[16,32]{1,0:T(8,128)S(1)} fusion(bf16[16,4096]{1,0:T(8,128)(2,1)S(1)} %reshape.63, bf16[32,4096]{1,0:T(8,128)(2,1)} %collective-permute-done.2), kind=kOutput, calls=%fused_computation.93 | convolution fusion | flops 4194304 | bytes 395264 | tf_op jit(solution)/shard_map/rd,nd->rn/dot_general | solution.py:85
  25.2 0.1 collective-permute-start.4
  25.3 1.2 %collective-permute-done.4 = f32[4,16,32]{2,1,0:T(8,128)S(1)} collective-permute-done((f32[4,16,32]{2,1,0:T(8,128)S(1)}, f32[4,16,32]{2,1,0:T(8,128)S(1)}, u32[]{:S(2)}, u32[]{:S(2)}) %collective-permute-start.4) | collective-permute-done | bytes 8224 | tf_op jit(solution)/shard_map/ppermute | solution.py:18
  26.5 0.2 fusion.14
  26.7 0.0 copy-start.2
  26.7 1.2 %fusion.1 = bf16[8,2,4096]{2,0,1:T(8,128)(2,1)S(1)} fusion(f32[8,2,4096]{2,0,1:T(8,128)S(1)} %fusion.14, bf16[32,4096]{1,0:T(8,128)(2,1)} %collective-permute-done.3, bf16[8,2,32]{2,1,0:T(2,128)(2,1)S(1)} %bitcast.90), kind=kOutput, calls=%fused_computation.2 | convolution fusion | flops 4325376 | bytes 656384 | tf_op jit(solution)/shard_map/...n,nd->...d/dot_general | solution.py:92
  27.9 0.2 collective-permute-start.5
  28.1 0.8 %copy.39 = bf16[8,2,4096]{2,1,0:T(2,128)(2,1)} copy(bf16[8,2,4096]{2,0,1:T(8,128)(2,1)S(1)} %fusion.1) | data formatting | bytes 262144 | tf_op jit(solution)/shard_map/optimization_barrier | solution.py:167
  28.9 3.4 %all-to-all-start.1 = ((bf16[8,2,4096]{2,1,0:T(2,128)(2,1)}), bf16[8,2,4096]{2,1,0:T(2,128)(2,1)S(1)}, u32[]{:S(2)}, u32[]{:S(2)}) async-start(bf16[8,2,4096]{2,1,0:T(2,128)(2,1)} %copy.39), calls=%async_computation.1 | async-start | bytes 262144 | tf_op jit(solution)/shard_map/all_to_all | solution.py:169
  32.3 0.0 collective-permute-done.5
  32.3 0.0 copy-done.1
  32.3 0.4 fusion.36
  32.7 0.0 copy-done.2
  32.7 0.4 multiply_convert_fusion
  33.1 0.0 copy-done
  33.1 0.2 fusion.10
  33.3 0.4 collective-permute-start.6
  33.7 6.3 %all-to-all-done.1 = bf16[8,2,4096]{2,1,0:T(2,128)(2,1)S(1)} async-done(((bf16[8,2,4096]{2,1,0:T(2,128)(2,1)}), bf16[8,2,4096]{2,1,0:T(2,128)(2,1)S(1)}, u32[]{:S(2)}, u32[]{:S(2)}) %all-to-all-start.1) | async-done | bytes 131104 | tf_op jit(solution)/shard_map/all_to_all | solution.py:169
  40.0 0.1 reshape.66
  40.0 0.3 fusion.96
  40.3 0.0 collective-permute-done.6
  40.3 0.8 %fusion.4 = bf16[8,4096]{1,0:T(8,128)(2,1)} fusion(f32[8,4096]{1,0:T(8,128)S(1)} %fusion.96, f32[8,4096]{1,0:T(8,128)S(1)} %collective-permute-done.6, bf16[8,64]{1,0:T(8,128)(2,1)S(1)} %multiply_convert_fusion, bf16[64,8192]{1,0:T(8,128)(2,1)S(1)} %copy-done, s32[]{:T(128)S(6)} %select_n.35, bf16[8,4096]{1,0:T(8,128)(2,1)S(1)} %get-tuple-element.18), kind=kOutput, calls=%fused_computation.7 | convolution fusion | flops 4358144 | bytes 919556 | tf_op jit(solution)/shard_map/...n,nd->...d/dot_general | solution.py:69
  (18 shorter events, 0.1 us)
Async XLA Ops:
  0.0 33.1 %copy-start = (bf16[64,8192]{1,0:T(8,128)(2,1)S(1)}, bf16[64,8192]{1,0:T(8,128)(2,1)}, u32[]{:S(2)}) copy-start(bf16[64,8192]{1,0:T(8,128)(2,1)} %param.25) | copy-start | bytes 3145732
  0.0 0.8 %copy-start.9 = (bf16[8,2,128]{2,1,0:T(2,128)(2,1)S(1)}, bf16[8,2,128]{2,1,0:T(2,128)(2,1)}, u32[]{:S(2)}) copy-start(bf16[8,2,128]{2,1,0:T(2,128)(2,1)} %param.20) | copy-start | bytes 12292
  0.8 0.7 %copy-start.10 = (s32[8]{0:T(128)S(1)}, s32[8]{0:T(128)}, u32[]{:S(2)}) copy-start(s32[8]{0:T(128)} %param.21) | copy-start | bytes 100
  1.5 1.4 %copy-start.11 = (bf16[8,2,32,128]{3,2,1,0:T(8,128)(2,1)S(1)}, bf16[8,2,32,128]{3,2,1,0:T(8,128)(2,1)}, u32[]{:S(2)}) copy-start(bf16[8,2,32,128]{3,2,1,0:T(8,128)(2,1)} %param.18) | copy-start | bytes 393220
  1.5 1.4 %copy-start.12 = (bf16[8,2,32,128]{3,2,1,0:T(8,128)(2,1)S(1)}, bf16[8,2,32,128]{3,2,1,0:T(8,128)(2,1)}, u32[]{:S(2)}) copy-start(bf16[8,2,32,128]{3,2,1,0:T(8,128)(2,1)} %param.17) | copy-start | bytes 393220
  1.5 1.4 %copy-start.13 = (bf16[8,4096]{1,0:T(8,128)(2,1)S(1)}, bf16[8,4096]{1,0:T(8,128)(2,1)}, u32[]{:S(2)}) copy-start(bf16[8,4096]{1,0:T(8,128)(2,1)} %param.16) | copy-start | bytes 196612
  2.9 0.8 %copy-start.6 = (bf16[8,4096]{1,0:T(8,128)(2,1)S(1)}, bf16[8,4096]{1,0:T(8,128)(2,1)}, u32[]{:S(2)}) copy-start(bf16[8,4096]{1,0:T(8,128)(2,1)} %param.15) | copy-start | bytes 196612
  2.9 1.5 %copy-start.3 = (bf16[32,8192]{1,0:T(8,128)(2,1)S(1)}, bf16[32,8192]{1,0:T(8,128)(2,1)}, u32[]{:S(2)}) copy-start(bf16[32,8192]{1,0:T(8,128)(2,1)} %param.26) | copy-start | bytes 1572868
  3.4 1.2 %copy-start.4 = (bf16[32,8192]{1,0:T(8,128)(2,1)S(1)}, bf16[32,8192]{1,0:T(8,128)(2,1)}, u32[]{:S(2)}) copy-start(bf16[32,8192]{1,0:T(8,128)(2,1)} %param.27) | copy-start | bytes 1572868
  4.0 3.5 %collective-permute-start = (f32[8]{0:T(128)S(1)}, f32[8]{0:T(128)S(1)}, u32[]{:S(2)}, u32[]{:S(2)}) collective-permute-start(f32[8]{0:T(128)S(1)} %get-tuple-element.17), channel_id=1, source_target_pairs={{0,1},{1,0},{2,3},{3,2},{4,5},{5,4},{6,7},{7,6},{8,9},{9,8},{10,11... | collective-permute-start | bytes 104 | tf_op jit(solution)/shard_map/ppermute | solution.py:18
  4.5 1.3 %copy-start.5 = (bf16[32,8192]{1,0:T(8,128)(2,1)S(1)}, bf16[32,8192]{1,0:T(8,128)(2,1)}, u32[]{:S(2)}) copy-start(bf16[32,8192]{1,0:T(8,128)(2,1)} %param.28) | copy-start | bytes 1572868
  4.5 17.9 %collective-permute-start.1 = (bf16[32,4096]{1,0:T(8,128)(2,1)S(1)}, bf16[32,4096]{1,0:T(8,128)(2,1)}, u32[]{:S(2)}, u32[]{:S(2)}) collective-permute-start(bf16[32,4096]{1,0:T(8,128)(2,1)S(1)} %constant_dynamic-slice_fusion.2), channel_id=1, source_target_pairs={{0,1},{1,0},{2,3},{3,2},{4,5},{5,4},{6,7},{7,6},{8,9},{9,8},{10,11... | collective-permute-start | bytes 786440 | tf_op jit(solution)/shard_map/ppermute | solution.py:18
  5.3 17.1 %collective-permute-start.2 = (bf16[32,4096]{1,0:T(8,128)(2,1)}, bf16[32,4096]{1,0:T(8,128)(2,1)}, u32[]{:S(2)}, u32[]{:S(2)}) collective-permute-start(bf16[32,4096]{1,0:T(8,128)(2,1)} %constant_dynamic-slice_fusion.1), channel_id=1, source_target_pairs={{0,1},{1,0},{2,3},{3,2},{4,5},{5,4},{6,7},{7,6},{8,9},{9,8},{10,11... | collective-permute-start | bytes 786440 | tf_op jit(solution)/shard_map/ppermute | solution.py:18
  6.5 15.9 %collective-permute-start.3 = (bf16[32,4096]{1,0:T(8,128)(2,1)}, bf16[32,4096]{1,0:T(8,128)(2,1)}, u32[]{:S(2)}, u32[]{:S(2)}) collective-permute-start(bf16[32,4096]{1,0:T(8,128)(2,1)} %constant_dynamic-slice_fusion), channel_id=1, source_target_pairs={{0,1},{1,0},{2,3},{3,2},{4,5},{5,4},{6,7},{7,6},{8,9},{9,8},{10,11... | collective-permute-start | bytes 786440 | tf_op jit(solution)/shard_map/ppermute | solution.py:18
  6.6 0.7 %copy-start.7 = (s32[8,4]{0,1:T(4,128)S(1)}, s32[8,4]{0,1:T(4,128)}, u32[]{:S(2)}) copy-start(s32[8,4]{0,1:T(4,128)} %param.29) | copy-start | bytes 388
  6.6 0.9 %copy-start.8 = (bf16[8192]{0:T(1024)(128)(2,1)S(1)}, bf16[8192]{0:T(1024)(128)(2,1)}, u32[]{:S(2)}) copy-start(bf16[8192]{0:T(1024)(128)(2,1)} %param.22) | copy-start | bytes 49156
  23.9 8.3 %copy-start.1 = (bf16[64,8192]{1,0:T(8,128)(2,1)S(1)}, bf16[64,8192]{1,0:T(8,128)(2,1)}, u32[]{:S(2)}) copy-start(bf16[64,8192]{1,0:T(8,128)(2,1)} %param.23) | copy-start | bytes 3145732
  25.2 1.3 %collective-permute-start.4 = (f32[4,16,32]{2,1,0:T(8,128)S(1)}, f32[4,16,32]{2,1,0:T(8,128)S(1)}, u32[]{:S(2)}, u32[]{:S(2)}) collective-permute-start(f32[4,16,32]{2,1,0:T(8,128)S(1)} %pad_maximum_fusion), channel_id=1, source_target_pairs={{0,1},{1,0},{2,3},{3,2},{4,5},{5,4},{6,7},{7,6},{8,9},{9,8},{10,11... | collective-permute-start | bytes 24584 | tf_op jit(solution)/shard_map/ppermute | solution.py:18
  26.7 6.0 %copy-start.2 = (bf16[64,8192]{1,0:T(8,128)(2,1)S(1)}, bf16[64,8192]{1,0:T(8,128)(2,1)}, u32[]{:S(2)}) copy-start(bf16[64,8192]{1,0:T(8,128)(2,1)} %param.24) | copy-start | bytes 3145732
  27.9 4.4 %collective-permute-start.5 = (bf16[8,4096]{1,0:T(8,128)(2,1)S(1)}, bf16[8,4096]{1,0:T(8,128)(2,1)S(1)}, u32[]{:S(2)}, u32[]{:S(2)}) collective-permute-start(bf16[8,4096]{1,0:T(8,128)(2,1)S(1)} %fusion.30), channel_id=1, source_target_pairs={{0,1},{1,0},{2,3},{3,2},{4,5},{5,4},{6,7},{7,6},{8,9},{9,8},{10,11... | collective-permute-start | bytes 196616 | tf_op jit(solution)/shard_map/ppermute | solution.py:18
  28.9 11.1 %all-to-all-start.1 = ((bf16[8,2,4096]{2,1,0:T(2,128)(2,1)}), bf16[8,2,4096]{2,1,0:T(2,128)(2,1)S(1)}, u32[]{:S(2)}, u32[]{:S(2)}) async-start(bf16[8,2,4096]{2,1,0:T(2,128)(2,1)} %copy.39), calls=%async_computation.1 | async-start | bytes 262144 | tf_op jit(solution)/shard_map/all_to_all | solution.py:169
  33.3 7.1 %collective-permute-start.6 = (f32[8,4096]{1,0:T(8,128)S(1)}, f32[8,4096]{1,0:T(8,128)S(1)}, u32[]{:S(2)}, u32[]{:S(2)}) collective-permute-start(f32[8,4096]{1,0:T(8,128)S(1)} %fusion.10), channel_id=1, source_target_pairs={{0,1},{1,0},{2,3},{3,2},{4,5},{5,4},{6,7},{7,6},{8,9},{9,8},{10,11... | collective-permute-start | bytes 393224 | tf_op jit(solution)/shard_map/ppermute | solution.py:18

commit v8 on v4

--- a/solution.py
+++ b/solution.py
@@ -129,7 +129,8 @@
     kept, given = swiglu_halves(
         incoming, cold_gate, cold_up, cold_down, myself, (owner_count, CAP)
     )
-    owner_sum = (kept + partner(given, "heads", 0)).astype(jnp.bfloat16)
+    given_narrow = partner(given.astype(jnp.bfloat16), "heads", 0)
+    owner_sum = (kept + given_narrow.astype(jnp.float32)).astype(jnp.bfloat16)
     normed_late, owner_sum = lax.optimization_barrier((normed, owner_sum))
     returned = lax.all_to_all(owner_sum, "rows", split_axis=0, concat_axis=0, tiled=True)
     hot_kept, hot_given = swiglu_halves(

time: 38.1 us -> 37.9 us (level)
  no operation moved by 1% of the time
where the time goes in v8:
time: 37.9 us; the launch traced here: 37.5 us
  blocking collectives  14.3 us (38%)
  waiting for transfers between devices  8.33 us (22%)
  matrix products  4.87 us (13%)
  starting transfers between devices  4.84 us (13%)
  local copies, waits for them, and re-layouts  4.33 us (11%)
  other arithmetic  0.6 us (2%)
    all_to_all x1, blocking collectives, local(): lax.all_to_all(outgoing, 'rows', split_axis=0, concat_axis=0, tiled=True)  14.3 us
    all_to_all x1, waiting for transfers between devices, local(): lax.all_to_all(owner_sum, 'rows', split_axis=0, concat_axis=0, tiled=True)  6.34 us
    all_to_all x1, starting transfers between devices, local(): lax.all_to_all(owner_sum, 'rows', split_axis=0, concat_axis=0, tiled=True)  3.37 us
    unnamed x28, local copies, waits for them, and re-layouts  2.48 us
    ppermute x5, waiting for transfers between devices, partner(): return lax.ppermute(block, axis, route)  1.99 us
    ppermute x5, starting transfers between devices, partner(): return lax.ppermute(block, axis, route)  1.47 us
    sub x1, matrix products, attention_rows(): expons = jnp.where(visible, jnp.exp(scores - highest[..., None]), 0.0)  1.33 us
    dot_general x2, matrix products, swiglu_halves(): jnp.einsum('...n,nd->...d', hidden, down_kept, preferred_element_type=jnp...  0.99 us
  transfers between devices with their start and end apart: 6, of which 3 were waited for; matrix products, arithmetic and copies ran while one was open for 6% of the time, Pallas kernels for 0%

profile of v8, /device:TPU:0, one launch (start us, length us, event | category | flops | bytes accessed | tf_op | source)
XLA Modules:
  0.0 37.5 jit_solution(7062327843712801951)
XLA Ops:
  0.0 0.0 copy-start
  0.0 0.0 copy-start.7
  0.0 0.8 %copy.31 = bf16[8,2,1,128]{3,2,1,0:T(2,128)(2,1)S(1)} copy(bf16[8,2,1,128]{3,1,0,2:T(2,128)(2,1)} %bitcast.56) | data formatting | bytes 8192 | tf_op jit(solution)/shard_map/broadcast_in_dim | solution.py:34
  0.8 0.0 copy-done.7
  0.8 0.0 copy-start.8
  0.8 0.6 %copy-done.8 = s32[8]{0:T(128)S(1)} copy-done((s32[8]{0:T(128)S(1)}, s32[8]{0:T(128)}, u32[]{:S(2)}) %copy-start.8) | copy-done | bytes 56
  1.5 0.1 fusion.50
  1.5 0.0 copy-start.11
  1.5 0.0 copy-start.12
  1.5 0.0 copy-start.13
  1.6 1.3 %fusion.79 = f32[8,2,16]{2,1,0:T(2,128)S(1)} fusion(bf16[8,2,1,128]{3,2,1,0:T(2,128)(2,1)S(1)} %copy.31, bf16[8,2,32,128]{3,2,1,0:T(8,128)(2,1)} %param.17, bf16[8,2,16,128]{3,0,2,1:T(8,128)(2,1)} %bitcast.58, pred[8,33]{1,0:T(8,128)(4,1)S(1)} %fusion.50), kind=kOutput, calls=%fused_computation.74 | convolution fusion | flops 2475296 | bytes 201992 | tf_op jit(solution)/shard_map/sub | solution.py:44
  2.9 0.0 copy-done.11
  2.9 0.0 copy-done.12
  2.9 0.0 copy-done.13
  2.9 0.0 copy-start.4
  2.9 0.5 %fusion.23 = f32[8,2,16,128]{3,2,1,0:T(8,128)S(1)} fusion(bf16[8,2,1,128]{3,2,1,0:T(2,128)(2,1)S(1)} %copy.34, bf16[8,2,32,128]{3,2,1,0:T(8,128)(2,1)S(1)} %copy-done.11, f32[8,2,16]{2,1,0:T(2,128)S(1)} %fusion.79, pred[8,33]{1,0:T(8,128)(4,1)S(1)} %fusion.50, bf16[8,2,1,128]{3,2,1,0:T(2,128)(2,1)S(1)} %copy.31, bf16[8,2,32,128]{3,2,1,0:T(8,128)(2,1)S(1)} %copy-done.12, ...), kind=kOutput, calls=%fused_computation.30 | convolution fusion | flops 4917024 | bytes 468232 | tf_op jit(solution)/shard_map/rgjp,rgpd->rgjd/dot_general | solution.py:47
  3.4 0.3 copy-done.4
  3.8 0.2 fusion.27
  4.0 0.5 %collective-permute-start = (f32[8]{0:T(128)S(1)}, f32[8]{0:T(128)S(1)}, u32[]{:S(2)}, u32[]{:S(2)}) collective-permute-start(f32[8]{0:T(128)S(1)} %get-tuple-element.9), channel_id=1, source_target_pairs={{0,1},{1,0},{2,3},{3,2},{4,5},{5,4},{6,7},{7,6},{8,9},{9,8},{10,11... | collective-permute-start | bytes 104 | tf_op jit(solution)/shard_map/ppermute | solution.py:18
  4.5 0.0 copy-start.5
  4.5 0.0 copy-start.6
  4.5 0.7 %copy-done.5 = s32[8,4]{0,1:T(4,128)S(1)} copy-done((s32[8,4]{0,1:T(4,128)S(1)}, s32[8,4]{0,1:T(4,128)}, u32[]{:S(2)}) %copy-start.5) | copy-done | bytes 152
  5.2 0.2 reduce_window_sum.11
  5.4 0.0 copy-done.6
  5.4 0.0 collective-permute-done
  5.4 0.1 fusion.29
  5.5 0.0 copy-start.9
  5.5 0.2 convolution_convert_fusion.1
  5.7 0.1 copy.36
  5.8 14.3 %all_to_all.10 = bf16[8,2,4096]{2,1,0:T(2,128)(2,1)S(1)} all-to-all(bf16[8,2,4096]{2,1,0:T(2,128)(2,1)S(1)} %copy.36), channel_id=1, replica_groups=mesh['groups'=2,'rows'=8,'heads'=2] {'rows'}, dimensions={0} | all-to-all | bytes 262144 | tf_op jit(solution)/shard_map/all_to_all | solution.py:127
  20.1 0.1 reshape.60
  20.1 0.1 collective-permute-start.2
  20.2 0.0 copy-start.10
  20.2 0.5 %collective-permute-start.1 = (bf16[8,4096]{1,0:T(8,128)(2,1)S(1)}, bf16[8,4096]{1,0:T(8,128)(2,1)S(1)}, u32[]{:S(2)}, u32[]{:S(2)}) collective-permute-start(bf16[8,4096]{1,0:T(8,128)(2,1)S(1)} %fusion.29), channel_id=1, source_target_pairs={{0,1},{1,0},{2,3},{3,2},{4,5},{5,4},{6,7},{7,6},{8,9},{9,8},{10,11... | collective-permute-start | bytes 196616 | tf_op jit(solution)/shard_map/ppermute | solution.py:18
  20.7 0.8 %collective-permute-done.2 = bf16[16,4096]{1,0:T(8,128)(2,1)S(1)} collective-permute-done((bf16[16,4096]{1,0:T(8,128)(2,1)S(1)}, bf16[16,4096]{1,0:T(8,128)(2,1)S(1)}, u32[]{:S(2)}, u32[]{:S(2)}) %collective-permute-start.2) | collective-permute-done | bytes 131104 | tf_op jit(solution)/shard_map/ppermute | solution.py:18
  21.6 0.0 copy-done.9
  21.6 0.2 fusion.35
  21.8 0.0 copy-done.10
  21.8 0.0 copy-start.3
  21.8 0.3 multiply_convert_fusion
  22.1 0.0 copy-start.1
  22.1 0.8 %copy-done.3 = bf16[32,8192]{1,0:T(8,128)(2,1)S(1)} copy-done((bf16[32,8192]{1,0:T(8,128)(2,1)S(1)}, bf16[32,8192]{1,0:T(8,128)(2,1)}, u32[]{:S(2)}) %copy-start.3) | copy-done | bytes 524312
  22.9 0.2 convolution_convert_fusion
  23.0 0.2 collective-permute-start.3
  23.3 0.0 collective-permute-done.1
  23.3 0.0 copy-start.2
  23.3 1.2 %collective-permute-done.3 = bf16[8,2,4096]{2,0,1:T(8,128)(2,1)S(1)} collective-permute-done((bf16[8,2,4096]{2,0,1:T(8,128)(2,1)S(1)}, bf16[8,2,4096]{2,0,1:T(8,128)(2,1)S(1)}, u32[]{:S(2)}, u32[]{:S(2)}) %collective-permute-start.3) | collective-permute-done | bytes 131104 | tf_op jit(solution)/shard_map/ppermute | solution.py:18
  24.5 0.2 add_convert_fusion
  24.6 0.8 %copy.39 = bf16[8,2,4096]{2,1,0:T(2,128)(2,1)} copy(bf16[8,2,4096]{2,0,1:T(8,128)(2,1)S(1)} %add_convert_fusion) | data formatting | bytes 262144 | tf_op jit(solution)/shard_map/optimization_barrier | solution.py:134
  25.4 3.4 %all-to-all-start.1 = ((bf16[8,2,4096]{2,1,0:T(2,128)(2,1)}), bf16[8,2,4096]{2,1,0:T(2,128)(2,1)S(1)}, u32[]{:S(2)}, u32[]{:S(2)}) async-start(bf16[8,2,4096]{2,1,0:T(2,128)(2,1)} %copy.39), calls=%async_computation.1 | async-start | bytes 262144 | tf_op jit(solution)/shard_map/all_to_all | solution.py:135
  28.8 0.0 copy-done.1
  28.8 0.4 fusion.84
  29.2 0.0 copy-done.2
  29.2 0.4 %fusion.9 = bf16[8,64]{1,0:T(8,128)(2,1)S(1)} fusion(bf16[8,8192]{1,0:T(8,128)(2,1)S(1)} %maximum_select_fusion.1, bf16[64,8192]{1,0:T(8,128)(2,1)S(1)} %copy-done.2, f32[8,64]{1,0:T(8,128)S(1)} %fusion.84), kind=kOutput, calls=%fused_computation.14 | convolution fusion | flops 8391680 | bytes 1182720 | tf_op jit(solution)/shard_map/rd,nd->rn/dot_general | solution.py:62
  29.6 0.0 copy-done
  29.6 0.2 fusion.10
  29.8 0.2 collective-permute-start.4
  30.0 6.3 %all-to-all-done.1 = bf16[8,2,4096]{2,1,0:T(2,128)(2,1)S(1)} async-done(((bf16[8,2,4096]{2,1,0:T(2,128)(2,1)}), bf16[8,2,4096]{2,1,0:T(2,128)(2,1)S(1)}, u32[]{:S(2)}, u32[]{:S(2)}) %all-to-all-start.1) | async-done | bytes 131104 | tf_op jit(solution)/shard_map/all_to_all | solution.py:135
  36.3 0.1 reshape.62
  36.4 0.3 fusion.85
  36.6 0.0 collective-permute-done.4
  36.6 0.8 %fusion.3 = bf16[8,4096]{1,0:T(8,128)(2,1)} fusion(f32[8,4096]{1,0:T(8,128)S(1)} %fusion.85, f32[8,4096]{1,0:T(8,128)S(1)} %collective-permute-done.4, bf16[8,64]{1,0:T(8,128)(2,1)S(1)} %fusion.9, bf16[64,8192]{1,0:T(8,128)(2,1)S(1)} %copy-done, s32[]{:T(128)S(6)} %select_n.39, bf16[8,4096]{1,0:T(8,128)(2,1)S(1)} %get-tuple-element.10), kind=kOutput, calls=%fused_computation.6 | convolution fusion | flops 4358144 | bytes 919556 | tf_op jit(solution)/shard_map/...n,nd->...d/dot_general | solution.py:69
  (10 shorter events, 0.1 us)
Async XLA Ops:
  0.0 29.6 %copy-start = (bf16[64,8192]{1,0:T(8,128)(2,1)S(1)}, bf16[64,8192]{1,0:T(8,128)(2,1)}, u32[]{:S(2)}) copy-start(bf16[64,8192]{1,0:T(8,128)(2,1)} %param.25) | copy-start | bytes 3145732
  0.0 0.8 %copy-start.7 = (bf16[8,2,128]{2,1,0:T(2,128)(2,1)S(1)}, bf16[8,2,128]{2,1,0:T(2,128)(2,1)}, u32[]{:S(2)}) copy-start(bf16[8,2,128]{2,1,0:T(2,128)(2,1)} %param.20) | copy-start | bytes 12292
  0.8 0.7 %copy-start.8 = (s32[8]{0:T(128)S(1)}, s32[8]{0:T(128)}, u32[]{:S(2)}) copy-start(s32[8]{0:T(128)} %param.21) | copy-start | bytes 100
  1.5 1.4 %copy-start.11 = (bf16[8,2,32,128]{3,2,1,0:T(8,128)(2,1)S(1)}, bf16[8,2,32,128]{3,2,1,0:T(8,128)(2,1)}, u32[]{:S(2)}) copy-start(bf16[8,2,32,128]{3,2,1,0:T(8,128)(2,1)} %param.18) | copy-start | bytes 393220
  1.5 1.4 %copy-start.12 = (bf16[8,2,32,128]{3,2,1,0:T(8,128)(2,1)S(1)}, bf16[8,2,32,128]{3,2,1,0:T(8,128)(2,1)}, u32[]{:S(2)}) copy-start(bf16[8,2,32,128]{3,2,1,0:T(8,128)(2,1)} %param.17) | copy-start | bytes 393220
  1.5 1.4 %copy-start.13 = (bf16[8,4096]{1,0:T(8,128)(2,1)S(1)}, bf16[8,4096]{1,0:T(8,128)(2,1)}, u32[]{:S(2)}) copy-start(bf16[8,4096]{1,0:T(8,128)(2,1)} %param.16) | copy-start | bytes 196612
  2.9 0.8 %copy-start.4 = (bf16[8,4096]{1,0:T(8,128)(2,1)S(1)}, bf16[8,4096]{1,0:T(8,128)(2,1)}, u32[]{:S(2)}) copy-start(bf16[8,4096]{1,0:T(8,128)(2,1)} %param.15) | copy-start | bytes 196612
  4.0 1.4 %collective-permute-start = (f32[8]{0:T(128)S(1)}, f32[8]{0:T(128)S(1)}, u32[]{:S(2)}, u32[]{:S(2)}) collective-permute-start(f32[8]{0:T(128)S(1)} %get-tuple-element.9), channel_id=1, source_target_pairs={{0,1},{1,0},{2,3},{3,2},{4,5},{5,4},{6,7},{7,6},{8,9},{9,8},{10,11... | collective-permute-start | bytes 104 | tf_op jit(solution)/shard_map/ppermute | solution.py:18
  4.5 0.7 %copy-start.5 = (s32[8,4]{0,1:T(4,128)S(1)}, s32[8,4]{0,1:T(4,128)}, u32[]{:S(2)}) copy-start(s32[8,4]{0,1:T(4,128)} %param.29) | copy-start | bytes 388
  4.5 0.9 %copy-start.6 = (bf16[8192]{0:T(1024)(128)(2,1)S(1)}, bf16[8192]{0:T(1024)(128)(2,1)}, u32[]{:S(2)}) copy-start(bf16[8192]{0:T(1024)(128)(2,1)} %param.22) | copy-start | bytes 49156
  5.5 16.1 %copy-start.9 = (bf16[32,8192]{1,0:T(8,128)(2,1)S(1)}, bf16[32,8192]{1,0:T(8,128)(2,1)}, u32[]{:S(2)}) copy-start(bf16[32,8192]{1,0:T(8,128)(2,1)} %param.26) | copy-start | bytes 1572868
  20.1 1.4 %collective-permute-start.2 = (bf16[16,4096]{1,0:T(8,128)(2,1)S(1)}, bf16[16,4096]{1,0:T(8,128)(2,1)S(1)}, u32[]{:S(2)}, u32[]{:S(2)}) collective-permute-start(bf16[16,4096]{1,0:T(8,128)(2,1)S(1)} %reshape.60), channel_id=1, source_target_pairs={{0,1},{1,0},{2,3},{3,2},{4,5},{5,4},{6,7},{7,6},{8,9},{9,8},{10,11... | collective-permute-start | bytes 393224 | tf_op jit(solution)/shard_map/ppermute | solution.py:18
  20.2 1.6 %copy-start.10 = (bf16[32,8192]{1,0:T(8,128)(2,1)S(1)}, bf16[32,8192]{1,0:T(8,128)(2,1)}, u32[]{:S(2)}) copy-start(bf16[32,8192]{1,0:T(8,128)(2,1)} %param.27) | copy-start | bytes 1572868
  20.2 3.0 %collective-permute-start.1 = (bf16[8,4096]{1,0:T(8,128)(2,1)S(1)}, bf16[8,4096]{1,0:T(8,128)(2,1)S(1)}, u32[]{:S(2)}, u32[]{:S(2)}) collective-permute-start(bf16[8,4096]{1,0:T(8,128)(2,1)S(1)} %fusion.29), channel_id=1, source_target_pairs={{0,1},{1,0},{2,3},{3,2},{4,5},{5,4},{6,7},{7,6},{8,9},{9,8},{10,11... | collective-permute-start | bytes 196616 | tf_op jit(solution)/shard_map/ppermute | solution.py:18
  21.8 1.1 %copy-start.3 = (bf16[32,8192]{1,0:T(8,128)(2,1)S(1)}, bf16[32,8192]{1,0:T(8,128)(2,1)}, u32[]{:S(2)}) copy-start(bf16[32,8192]{1,0:T(8,128)(2,1)} %param.28) | copy-start | bytes 1572868
  22.1 6.7 %copy-start.1 = (bf16[64,8192]{1,0:T(8,128)(2,1)S(1)}, bf16[64,8192]{1,0:T(8,128)(2,1)}, u32[]{:S(2)}) copy-start(bf16[64,8192]{1,0:T(8,128)(2,1)} %param.23) | copy-start | bytes 3145732
  23.0 1.4 %collective-permute-start.3 = (bf16[8,2,4096]{2,0,1:T(8,128)(2,1)S(1)}, bf16[8,2,4096]{2,0,1:T(8,128)(2,1)S(1)}, u32[]{:S(2)}, u32[]{:S(2)}) collective-permute-start(bf16[8,2,4096]{2,0,1:T(8,128)(2,1)S(1)} %convolution_convert_fusion), channel_id=1, source_target_pairs={{0,1},{1,0},{2,3},{3,2},{4,5},{5,4},{6,7},{7,6},{8,9},{9,8},{10,11... | collective-permute-start | bytes 393224 | tf_op jit(solution)/shard_map/ppermute | solution.py:18
  23.3 5.9 %copy-start.2 = (bf16[64,8192]{1,0:T(8,128)(2,1)S(1)}, bf16[64,8192]{1,0:T(8,128)(2,1)}, u32[]{:S(2)}) copy-start(bf16[64,8192]{1,0:T(8,128)(2,1)} %param.24) | copy-start | bytes 3145732
  25.4 10.9 %all-to-all-start.1 = ((bf16[8,2,4096]{2,1,0:T(2,128)(2,1)}), bf16[8,2,4096]{2,1,0:T(2,128)(2,1)S(1)}, u32[]{:S(2)}, u32[]{:S(2)}) async-start(bf16[8,2,4096]{2,1,0:T(2,128)(2,1)} %copy.39), calls=%async_computation.1 | async-start | bytes 262144 | tf_op jit(solution)/shard_map/all_to_all | solution.py:135
  29.8 6.9 %collective-permute-start.4 = (f32[8,4096]{1,0:T(8,128)S(1)}, f32[8,4096]{1,0:T(8,128)S(1)}, u32[]{:S(2)}, u32[]{:S(2)}) collective-permute-start(f32[8,4096]{1,0:T(8,128)S(1)} %fusion.10), channel_id=1, source_target_pairs={{0,1},{1,0},{2,3},{3,2},{4,5},{5,4},{6,7},{7,6},{8,9},{9,8},{10,11... | collective-permute-start | bytes 393224 | tf_op jit(solution)/shard_map/ppermute | solution.py:18

commit v9 on v8

--- a/solution.py
+++ b/solution.py
@@ -2,6 +2,7 @@
 import jax.numpy as jnp
 from jax import lax
 from jax.sharding import PartitionSpec as P
+from jax.experimental.layout import Layout, with_layout_constraint
 
 HD = 128
 D = 8192
@@ -131,6 +132,7 @@
     )
     given_narrow = partner(given.astype(jnp.bfloat16), "heads", 0)
     owner_sum = (kept + given_narrow.astype(jnp.float32)).astype(jnp.bfloat16)
+    owner_sum = with_layout_constraint(owner_sum, Layout((0, 1, 2)))
     normed_late, owner_sum = lax.optimization_barrier((normed, owner_sum))
     returned = lax.all_to_all(owner_sum, "rows", split_axis=0, concat_axis=0, tiled=True)
     hot_kept, hot_given = swiglu_halves(

time: 37.9 us -> 38.9 us (1.026)
  blocking collectives: 14.3 us -> 0 us
  waiting for transfers between devices: 8.33 us -> 16.1 us
  starting transfers between devices: 4.84 us -> 11.4 us
  other arithmetic: 0.6 us -> 1.6 us
    all_to_all x1 -> x0, blocking collectives: 14.3 us -> none  [local(): lax.all_to_all(outgoing, 'rows', split_axis=0, concat_axis=0, tiled=True)]
    all_to_all x0 -> x1, waiting for transfers between devices: none -> 7.43 us  [local(): lax.all_to_all(outgoing, 'rows', split_axis=0, concat_axis=0, tiled=True)]
    all_to_all x0 -> x1, starting transfers between devices: none -> 6.99 us  [local(): lax.all_to_all(outgoing, 'rows', split_axis=0, concat_axis=0, tiled=True)]
    convert_element_type x0 -> x2, other arithmetic: none -> 1 us  [local(): owner_sum = (kept + given_narrow.astype(jnp.float32)).astype(jnp.bfloat16)]
    optimization_barrier x1 -> x0, local copies, waits for them, and re-layouts: 0.79 us -> none  [local(): normed_late, owner_sum = lax.optimization_barrier((normed, owner_sum))]
    convert_element_type x1, local copies, waits for them, and re-layouts: 0.14 us -> 0.78 us  [local(): outgoing = jnp.einsum('ocr,rd->ocd', selector3.astype(jnp.bfloat16), scal...]
    ppermute x5, starting transfers between devices: 1.47 us -> 1.03 us  [partner(): return lax.ppermute(block, axis, route)]
  transfers between devices with their start and end apart: 6 -> 7, of which waited for: 3 -> 4; matrix products, arithmetic and copies ran while one was open for 6% -> 5% of each run, Pallas kernels for 0% -> 0%
where the time goes in v9:
time: 38.9 us; the launch traced here: 38.4 us
  waiting for transfers between devices  16.1 us (41%)
  starting transfers between devices  11.4 us (29%)
  matrix products  4.87 us (13%)
  local copies, waits for them, and re-layouts  4.18 us (11%)
  other arithmetic  1.6 us (4%)
    all_to_all x1, waiting for transfers between devices, local(): lax.all_to_all(outgoing, 'rows', split_axis=0, concat_axis=0, tiled=True)  7.43 us
    all_to_all x1, starting transfers between devices, local(): lax.all_to_all(outgoing, 'rows', split_axis=0, concat_axis=0, tiled=True)  6.99 us
    all_to_all x1, waiting for transfers between devices, local(): lax.all_to_all(owner_sum, 'rows', split_axis=0, concat_axis=0, tiled=True)  6.34 us
    all_to_all x1, starting transfers between devices, local(): lax.all_to_all(owner_sum, 'rows', split_axis=0, concat_axis=0, tiled=True)  3.37 us
    unnamed x28, local copies, waits for them, and re-layouts  2.48 us
    ppermute x5, waiting for transfers between devices, partner(): return lax.ppermute(block, axis, route)  2.31 us
    sub x1, matrix products, attention_rows(): expons = jnp.where(visible, jnp.exp(scores - highest[..., None]), 0.0)  1.33 us
    ppermute x5, starting transfers between devices, partner(): return lax.ppermute(block, axis, route)  1.03 us
  transfers between devices with their start and end apart: 7, of which 4 were waited for; matrix products, arithmetic and copies ran while one was open for 5% of the time, Pallas kernels for 0%

profile of v9, /device:TPU:0, one launch (start us, length us, event | category | flops | bytes accessed | tf_op | source)
XLA Modules:
  0.0 38.4 jit_solution(8266573557820486026)
XLA Ops:
  0.0 0.0 copy-start
  0.0 0.0 copy-start.7
  0.0 0.8 %copy.45 = bf16[8,2,1,128]{3,2,1,0:T(2,128)(2,1)S(1)} copy(bf16[8,2,1,128]{3,1,0,2:T(2,128)(2,1)} %bitcast.54) | data formatting | bytes 8192 | tf_op jit(solution)/shard_map/broadcast_in_dim | solution.py:35
  0.8 0.0 copy-done.7
  0.8 0.0 copy-start.8
  0.8 0.6 %copy-done.8 = s32[8]{0:T(128)S(1)} copy-done((s32[8]{0:T(128)S(1)}, s32[8]{0:T(128)}, u32[]{:S(2)}) %copy-start.8) | copy-done | bytes 56
  1.5 0.1 fusion.49
  1.5 0.0 copy-start.11
  1.5 0.0 copy-start.12
  1.5 0.0 copy-start.13
  1.6 1.3 %fusion.78 = f32[8,2,16]{2,1,0:T(2,128)S(1)} fusion(bf16[8,2,1,128]{3,2,1,0:T(2,128)(2,1)S(1)} %copy.45, bf16[8,2,32,128]{3,2,1,0:T(8,128)(2,1)} %param.17, bf16[8,2,16,128]{3,0,2,1:T(8,128)(2,1)} %bitcast.56, pred[8,33]{1,0:T(8,128)(4,1)S(1)} %fusion.49), kind=kOutput, calls=%fused_computation.75 | convolution fusion | flops 2475296 | bytes 201992 | tf_op jit(solution)/shard_map/sub | solution.py:45
  2.9 0.0 copy-done.11
  2.9 0.0 copy-done.12
  2.9 0.0 copy-done.13
  2.9 0.0 copy-start.4
  2.9 0.5 %fusion.22 = f32[8,2,16,128]{3,2,1,0:T(8,128)S(1)} fusion(bf16[8,2,1,128]{3,2,1,0:T(2,128)(2,1)S(1)} %copy.48, bf16[8,2,32,128]{3,2,1,0:T(8,128)(2,1)S(1)} %copy-done.11, f32[8,2,16]{2,1,0:T(2,128)S(1)} %fusion.78, pred[8,33]{1,0:T(8,128)(4,1)S(1)} %fusion.49, bf16[8,2,1,128]{3,2,1,0:T(2,128)(2,1)S(1)} %copy.45, bf16[8,2,32,128]{3,2,1,0:T(8,128)(2,1)S(1)} %copy-done.12, ...), kind=kOutput, calls=%fused_computation.31 | convolution fusion | flops 4917024 | bytes 468232 | tf_op jit(solution)/shard_map/rgjp,rgpd->rgjd/dot_general | solution.py:48
  3.4 0.3 copy-done.4
  3.8 0.2 fusion.26
  4.0 0.5 %collective-permute-start = (f32[8]{0:T(128)S(1)}, f32[8]{0:T(128)S(1)}, u32[]{:S(2)}, u32[]{:S(2)}) collective-permute-start(f32[8]{0:T(128)S(1)} %get-tuple-element.9), channel_id=1, source_target_pairs={{0,1},{1,0},{2,3},{3,2},{4,5},{5,4},{6,7},{7,6},{8,9},{9,8},{10,11... | collective-permute-start | bytes 104 | tf_op jit(solution)/shard_map/ppermute | solution.py:19
  4.5 0.0 copy-start.5
  4.5 0.0 copy-start.6
  4.5 0.7 %copy-done.5 = s32[8,4]{0,1:T(4,128)S(1)} copy-done((s32[8,4]{0,1:T(4,128)S(1)}, s32[8,4]{0,1:T(4,128)}, u32[]{:S(2)}) %copy-start.5) | copy-done | bytes 152
  5.2 0.2 reduce_window_sum.11
  5.4 0.0 copy-done.6
  5.4 0.0 collective-permute-done
  5.4 0.1 fusion.28
  5.5 0.2 convolution_convert_fusion.1
  5.7 0.0 copy-start.9
  5.7 0.8 %copy.50 = bf16[8,2,4096]{2,1,0:T(2,128)(2,1)} copy(bf16[8,2,4096]{2,0,1:T(8,128)(2,1)S(1)} %convolution_convert_fusion.1) | data formatting | bytes 262144 | tf_op jit(solution)/shard_map/convert_element_type | solution.py:127
  6.5 7.0 %all-to-all-start = ((bf16[8,2,4096]{2,1,0:T(2,128)(2,1)}), bf16[8,2,4096]{2,1,0:T(2,128)(2,1)S(1)}, u32[]{:S(2)}, u32[]{:S(2)}) async-start(bf16[8,2,4096]{2,1,0:T(2,128)(2,1)} %copy.50), calls=%async_computation | async-start | bytes 262144 | tf_op jit(solution)/shard_map/all_to_all | solution.py:128
  13.5 0.0 collective-permute-start.1
  13.5 7.4 %all-to-all-done = bf16[8,2,4096]{2,1,0:T(2,128)(2,1)S(1)} async-done(((bf16[8,2,4096]{2,1,0:T(2,128)(2,1)}), bf16[8,2,4096]{2,1,0:T(2,128)(2,1)S(1)}, u32[]{:S(2)}, u32[]{:S(2)}) %all-to-all-start) | async-done | bytes 131104 | tf_op jit(solution)/shard_map/all_to_all | solution.py:128
  20.9 0.1 reshape.60
  21.0 0.1 collective-permute-start.2
  21.1 0.0 collective-permute-done.1
  21.1 0.0 copy-start.10
  21.1 1.3 %collective-permute-done.2 = bf16[16,4096]{1,0:T(8,128)(2,1)S(1)} collective-permute-done((bf16[16,4096]{1,0:T(8,128)(2,1)S(1)}, bf16[16,4096]{1,0:T(8,128)(2,1)S(1)}, u32[]{:S(2)}, u32[]{:S(2)}) %collective-permute-start.2) | collective-permute-done | bytes 131104 | tf_op jit(solution)/shard_map/ppermute | solution.py:19
  22.4 0.0 copy-done.9
  22.4 0.2 fusion.34
  22.6 0.0 copy-done.10
  22.7 0.0 copy-start.3
  22.7 0.3 multiply_convert_fusion
  22.9 0.8 %copy-done.3 = bf16[32,8192]{1,0:T(8,128)(2,1)S(1)} copy-done((bf16[32,8192]{1,0:T(8,128)(2,1)S(1)}, bf16[32,8192]{1,0:T(8,128)(2,1)}, u32[]{:S(2)}) %copy-start.3) | copy-done | bytes 524312
  23.7 0.0 copy-start.1
  23.7 0.2 convolution_convert_fusion
  23.9 0.2 collective-permute-start.3
  24.1 0.2 fusion.14
  24.3 1.0 %collective-permute-done.3 = bf16[8,2,4096]{2,0,1:T(8,128)(2,1)S(1)} collective-permute-done((bf16[8,2,4096]{2,0,1:T(8,128)(2,1)S(1)}, bf16[8,2,4096]{2,0,1:T(8,128)(2,1)S(1)}, u32[]{:S(2)}, u32[]{:S(2)}) %collective-permute-start.3) | collective-permute-done | bytes 131104 | tf_op jit(solution)/shard_map/ppermute | solution.py:19
  25.3 0.0 copy-start.2
  25.3 1.0 %fusion.16 = bf16[8,2,4096]{2,1,0:T(2,128)(2,1)} fusion(f32[8,2,4096]{2,0,1:T(8,128)S(1)} %convert_element_type.68, f32[8,2,4096]{2,0,1:T(8,128)S(1)} %fusion.14), kind=kLoop, calls=%fused_computation.23 | loop fusion | flops 131072 | bytes 655360 | tf_op jit(solution)/shard_map/convert_element_type | solution.py:134
  26.3 3.4 %all-to-all-start.1 = ((bf16[8,2,4096]{2,1,0:T(2,128)(2,1)}), bf16[8,2,4096]{2,1,0:T(2,128)(2,1)S(1)}, u32[]{:S(2)}, u32[]{:S(2)}) async-start(bf16[8,2,4096]{2,1,0:T(2,128)(2,1)} %fusion.16), calls=%async_computation.1 | async-start | bytes 262144 | tf_op jit(solution)/shard_map/all_to_all | solution.py:137
  29.7 0.0 copy-done.1
  29.7 0.4 fusion.83
  30.1 0.0 copy-done.2
  30.1 0.4 %fusion.9 = bf16[8,64]{1,0:T(8,128)(2,1)S(1)} fusion(bf16[8,8192]{1,0:T(8,128)(2,1)S(1)} %maximum_select_fusion.1, bf16[64,8192]{1,0:T(8,128)(2,1)S(1)} %copy-done.2, f32[8,64]{1,0:T(8,128)S(1)} %fusion.83), kind=kOutput, calls=%fused_computation.14 | convolution fusion | flops 8391680 | bytes 1182720 | tf_op jit(solution)/shard_map/rd,nd->rn/dot_general | solution.py:63
  30.5 0.0 copy-done
  30.5 0.2 fusion.10
  30.7 0.2 collective-permute-start.4
  30.9 6.3 %all-to-all-done.1 = bf16[8,2,4096]{2,1,0:T(2,128)(2,1)S(1)} async-done(((bf16[8,2,4096]{2,1,0:T(2,128)(2,1)}), bf16[8,2,4096]{2,1,0:T(2,128)(2,1)S(1)}, u32[]{:S(2)}, u32[]{:S(2)}) %all-to-all-start.1) | async-done | bytes 131104 | tf_op jit(solution)/shard_map/all_to_all | solution.py:137
  37.2 0.1 reshape.62
  37.3 0.3 fusion.84
  37.5 0.0 collective-permute-done.4
  37.5 0.8 %fusion.3 = bf16[8,4096]{1,0:T(8,128)(2,1)} fusion(f32[8,4096]{1,0:T(8,128)S(1)} %fusion.84, f32[8,4096]{1,0:T(8,128)S(1)} %collective-permute-done.4, bf16[8,64]{1,0:T(8,128)(2,1)S(1)} %fusion.9, bf16[64,8192]{1,0:T(8,128)(2,1)S(1)} %copy-done, s32[]{:T(128)S(6)} %select_n.39, bf16[8,4096]{1,0:T(8,128)(2,1)S(1)} %get-tuple-element.10), kind=kOutput, calls=%fused_computation.6 | convolution fusion | flops 4358144 | bytes 919556 | tf_op jit(solution)/shard_map/...n,nd->...d/dot_general | solution.py:70
  (11 shorter events, 0.1 us)
Async XLA Ops:
  0.0 30.5 %copy-start = (bf16[64,8192]{1,0:T(8,128)(2,1)S(1)}, bf16[64,8192]{1,0:T(8,128)(2,1)}, u32[]{:S(2)}) copy-start(bf16[64,8192]{1,0:T(8,128)(2,1)} %param.25) | copy-start | bytes 3145732
  0.0 0.8 %copy-start.7 = (bf16[8,2,128]{2,1,0:T(2,128)(2,1)S(1)}, bf16[8,2,128]{2,1,0:T(2,128)(2,1)}, u32[]{:S(2)}) copy-start(bf16[8,2,128]{2,1,0:T(2,128)(2,1)} %param.20) | copy-start | bytes 12292
  0.8 0.7 %copy-start.8 = (s32[8]{0:T(128)S(1)}, s32[8]{0:T(128)}, u32[]{:S(2)}) copy-start(s32[8]{0:T(128)} %param.21) | copy-start | bytes 100
  1.5 1.4 %copy-start.11 = (bf16[8,2,32,128]{3,2,1,0:T(8,128)(2,1)S(1)}, bf16[8,2,32,128]{3,2,1,0:T(8,128)(2,1)}, u32[]{:S(2)}) copy-start(bf16[8,2,32,128]{3,2,1,0:T(8,128)(2,1)} %param.18) | copy-start | bytes 393220
  1.5 1.4 %copy-start.12 = (bf16[8,2,32,128]{3,2,1,0:T(8,128)(2,1)S(1)}, bf16[8,2,32,128]{3,2,1,0:T(8,128)(2,1)}, u32[]{:S(2)}) copy-start(bf16[8,2,32,128]{3,2,1,0:T(8,128)(2,1)} %param.17) | copy-start | bytes 393220
  1.5 1.4 %copy-start.13 = (bf16[8,4096]{1,0:T(8,128)(2,1)S(1)}, bf16[8,4096]{1,0:T(8,128)(2,1)}, u32[]{:S(2)}) copy-start(bf16[8,4096]{1,0:T(8,128)(2,1)} %param.16) | copy-start | bytes 196612
  2.9 0.8 %copy-start.4 = (bf16[8,4096]{1,0:T(8,128)(2,1)S(1)}, bf16[8,4096]{1,0:T(8,128)(2,1)}, u32[]{:S(2)}) copy-start(bf16[8,4096]{1,0:T(8,128)(2,1)} %param.15) | copy-start | bytes 196612
  4.0 1.4 %collective-permute-start = (f32[8]{0:T(128)S(1)}, f32[8]{0:T(128)S(1)}, u32[]{:S(2)}, u32[]{:S(2)}) collective-permute-start(f32[8]{0:T(128)S(1)} %get-tuple-element.9), channel_id=1, source_target_pairs={{0,1},{1,0},{2,3},{3,2},{4,5},{5,4},{6,7},{7,6},{8,9},{9,8},{10,11... | collective-permute-start | bytes 104 | tf_op jit(solution)/shard_map/ppermute | solution.py:19
  4.5 0.7 %copy-start.5 = (s32[8,4]{0,1:T(4,128)S(1)}, s32[8,4]{0,1:T(4,128)}, u32[]{:S(2)}) copy-start(s32[8,4]{0,1:T(4,128)} %param.29) | copy-start | bytes 388
  4.5 0.9 %copy-start.6 = (bf16[8192]{0:T(1024)(128)(2,1)S(1)}, bf16[8192]{0:T(1024)(128)(2,1)}, u32[]{:S(2)}) copy-start(bf16[8192]{0:T(1024)(128)(2,1)} %param.22) | copy-start | bytes 49156
  5.7 16.7 %copy-start.9 = (bf16[32,8192]{1,0:T(8,128)(2,1)S(1)}, bf16[32,8192]{1,0:T(8,128)(2,1)}, u32[]{:S(2)}) copy-start(bf16[32,8192]{1,0:T(8,128)(2,1)} %param.26) | copy-start | bytes 1572868
  6.5 14.5 %all-to-all-start = ((bf16[8,2,4096]{2,1,0:T(2,128)(2,1)}), bf16[8,2,4096]{2,1,0:T(2,128)(2,1)S(1)}, u32[]{:S(2)}, u32[]{:S(2)}) async-start(bf16[8,2,4096]{2,1,0:T(2,128)(2,1)} %copy.50), calls=%async_computation | async-start | bytes 262144 | tf_op jit(solution)/shard_map/all_to_all | solution.py:128
  13.5 7.6 %collective-permute-start.1 = (bf16[8,4096]{1,0:T(8,128)(2,1)S(1)}, bf16[8,4096]{1,0:T(8,128)(2,1)S(1)}, u32[]{:S(2)}, u32[]{:S(2)}) collective-permute-start(bf16[8,4096]{1,0:T(8,128)(2,1)S(1)} %fusion.28), channel_id=1, source_target_pairs={{0,1},{1,0},{2,3},{3,2},{4,5},{5,4},{6,7},{7,6},{8,9},{9,8},{10,11... | collective-permute-start | bytes 196616 | tf_op jit(solution)/shard_map/ppermute | solution.py:19
  21.0 1.4 %collective-permute-start.2 = (bf16[16,4096]{1,0:T(8,128)(2,1)S(1)}, bf16[16,4096]{1,0:T(8,128)(2,1)S(1)}, u32[]{:S(2)}, u32[]{:S(2)}) collective-permute-start(bf16[16,4096]{1,0:T(8,128)(2,1)S(1)} %reshape.60), channel_id=1, source_target_pairs={{0,1},{1,0},{2,3},{3,2},{4,5},{5,4},{6,7},{7,6},{8,9},{9,8},{10,11... | collective-permute-start | bytes 393224 | tf_op jit(solution)/shard_map/ppermute | solution.py:19
  21.1 1.5 %copy-start.10 = (bf16[32,8192]{1,0:T(8,128)(2,1)S(1)}, bf16[32,8192]{1,0:T(8,128)(2,1)}, u32[]{:S(2)}) copy-start(bf16[32,8192]{1,0:T(8,128)(2,1)} %param.27) | copy-start | bytes 1572868
  22.7 1.1 %copy-start.3 = (bf16[32,8192]{1,0:T(8,128)(2,1)S(1)}, bf16[32,8192]{1,0:T(8,128)(2,1)}, u32[]{:S(2)}) copy-start(bf16[32,8192]{1,0:T(8,128)(2,1)} %param.28) | copy-start | bytes 1572868
  23.7 6.0 %copy-start.1 = (bf16[64,8192]{1,0:T(8,128)(2,1)S(1)}, bf16[64,8192]{1,0:T(8,128)(2,1)}, u32[]{:S(2)}) copy-start(bf16[64,8192]{1,0:T(8,128)(2,1)} %param.23) | copy-start | bytes 3145732
  23.9 1.4 %collective-permute-start.3 = (bf16[8,2,4096]{2,0,1:T(8,128)(2,1)S(1)}, bf16[8,2,4096]{2,0,1:T(8,128)(2,1)S(1)}, u32[]{:S(2)}, u32[]{:S(2)}) collective-permute-start(bf16[8,2,4096]{2,0,1:T(8,128)(2,1)S(1)} %convolution_convert_fusion), channel_id=1, source_target_pairs={{0,1},{1,0},{2,3},{3,2},{4,5},{5,4},{6,7},{7,6},{8,9},{9,8},{10,11... | collective-permute-start | bytes 393224 | tf_op jit(solution)/shard_map/ppermute | solution.py:19
  25.3 4.8 %copy-start.2 = (bf16[64,8192]{1,0:T(8,128)(2,1)S(1)}, bf16[64,8192]{1,0:T(8,128)(2,1)}, u32[]{:S(2)}) copy-start(bf16[64,8192]{1,0:T(8,128)(2,1)} %param.24) | copy-start | bytes 3145732
  26.3 10.9 %all-to-all-start.1 = ((bf16[8,2,4096]{2,1,0:T(2,128)(2,1)}), bf16[8,2,4096]{2,1,0:T(2,128)(2,1)S(1)}, u32[]{:S(2)}, u32[]{:S(2)}) async-start(bf16[8,2,4096]{2,1,0:T(2,128)(2,1)} %fusion.16), calls=%async_computation.1 | async-start | bytes 262144 | tf_op jit(solution)/shard_map/all_to_all | solution.py:137
  30.7 6.9 %collective-permute-start.4 = (f32[8,4096]{1,0:T(8,128)S(1)}, f32[8,4096]{1,0:T(8,128)S(1)}, u32[]{:S(2)}, u32[]{:S(2)}) collective-permute-start(f32[8,4096]{1,0:T(8,128)S(1)} %fusion.10), channel_id=1, source_target_pairs={{0,1},{1,0},{2,3},{3,2},{4,5},{5,4},{6,7},{7,6},{8,9},{9,8},{10,11... | collective-permute-start | bytes 393224 | tf_op jit(solution)/shard_map/ppermute | solution.py:19

commit v10 on v8

--- a/solution.py
+++ b/solution.py
@@ -2,6 +2,8 @@
 import jax.numpy as jnp
 from jax import lax
 from jax.sharding import PartitionSpec as P
+from jax.experimental import pallas as pl
+from jax.experimental.pallas import tpu as pltpu
 
 HD = 128
 D = 8192
@@ -25,28 +27,48 @@
     return jnp.where(myself == 0, low_first, high_first)
 
 
+def attention_kernel(len_ref, q_ref, k_ref, v_ref, kn_ref, vn_ref, out_ref):
+    count, groups, heads, _ = q_ref.shape
+    slots = k_ref.shape[2]
+    scale_factor = 1.0 / HD**0.5
+    for r in range(count):
+        length = len_ref[r]
+        for g in range(groups):
+            q = q_ref[r, g]
+            k = k_ref[r, g]
+            scores = (
+                lax.dot_general(q, k, (((1,), (1,)), ((), ())), preferred_element_type=jnp.float32)
+                * scale_factor
+            )
+            key_new = kn_ref[r, pl.ds(g, 1), :].astype(jnp.float32)
+            own = jnp.sum(q.astype(jnp.float32) * key_new, axis=1, keepdims=True) * scale_factor
+            visible = lax.broadcasted_iota(jnp.int32, (heads, slots), 1) < length
+            scores = jnp.where(visible, scores, -1e30)
+            highest = jnp.maximum(jnp.max(scores, axis=1, keepdims=True), own)
+            expons = jnp.where(visible, jnp.exp(scores - highest), 0.0)
+            own_expon = jnp.exp(own - highest)
+            totals = jnp.sum(expons, axis=1, keepdims=True) + own_expon
+            weights = (expons / totals).astype(jnp.bfloat16)
+            own_weight = (own_expon / totals).astype(jnp.bfloat16).astype(jnp.float32)
+            blended = jnp.dot(weights, v_ref[r, g], preferred_element_type=jnp.float32)
+            value_new = vn_ref[r, pl.ds(g, 1), :].astype(jnp.float32)
+            out_ref[r, g] = blended + own_weight * value_new
+
+
 def attention_rows(query, key_cache, value_cache, key_new, value_new, lengths):
-    count = key_cache.shape[0]
-    kv_local = key_cache.shape[1]
-    slots = key_cache.shape[2]
-    scale_factor = 1.0 / HD**0.5
+    count, kv_local, slots, _ = key_cache.shape
     queries = query.reshape(count, kv_local, -1, HD)
-    keys_all = jnp.concatenate([key_cache, key_new[:, :, None, :]], axis=2)
-    values_all = jnp.concatenate([value_cache, value_new[:, :, None, :]], axis=2)
-    scores = (
-        jnp.einsum("rgjd,rgpd->rgjp", queries, keys_all, preferred_element_type=jnp.float32)
-        * scale_factor
-    )
-    positions = jnp.arange(slots + 1, dtype=jnp.int32)[None, :]
-    visible = ((positions < lengths[:, None]) | (positions == slots))[:, None, None, :]
-    scores = jnp.where(visible, scores, -1e30)
-    highest = jnp.max(scores, axis=-1)
-    expons = jnp.where(visible, jnp.exp(scores - highest[..., None]), 0.0)
-    totals = jnp.sum(expons, axis=-1)
-    weights = (expons / totals[..., None]).astype(jnp.bfloat16)
-    blended = jnp.einsum(
-        "rgjp,rgpd->rgjd", weights, values_all, preferred_element_type=jnp.float32
-    )
+    vmem = pl.BlockSpec(memory_space=pltpu.VMEM)
+    blended = pl.pallas_call(
+        attention_kernel,
+        out_shape=jax.ShapeDtypeStruct(queries.shape, jnp.float32),
+        in_specs=[pl.BlockSpec(memory_space=pltpu.SMEM)] + [vmem] * 5,
+        out_specs=vmem,
+        cost_estimate=pl.CostEstimate(
+            flops=4 * queries.size * slots, transcendentals=queries.size // HD * slots,
+            bytes_accessed=2 * (queries.size + 2 * key_cache.size) + 4 * queries.size,
+        ),
+    )(lengths, queries, key_cache, value_cache, key_new, value_new)
     return blended.reshape(count, -1)
 
 

time: 37.9 us -> 43.1 us (1.14)
  Pallas kernels: 0 us -> 6.51 us
  matrix products: 4.87 us -> 3.04 us
  other arithmetic: 0.6 us -> 1.42 us
    pallas_call x0 -> x1, Pallas kernels: none -> 6.51 us  [attention_rows(): pl.pallas_call(attention_kernel, out_shape=jax.ShapeDtypeStruct(queries.s...]
    sub x1 -> x0, matrix products: 1.33 us -> none  [attention_rows(): expons = jnp.where(visible, jnp.exp(scores - highest[..., None]), 0.0)]
    reduce_sum x1, other arithmetic: 0.19 us -> 1.1 us  [local(): square_part = jnp.sum(local_wide * local_wide, axis=-1)]
    broadcast_in_dim x2 -> x0, local copies, waits for them, and re-layouts: 0.8 us -> none  [the longest x1 0.79 us: attention_rows(): keys_all = jnp.concatenate([key_cache, key_new[:, :, None, :]], axis=2)]
    unnamed x28 -> x19, local copies, waits for them, and re-layouts: 2.48 us -> 3.07 us
    dot_general x1 -> x0, matrix products: 0.5 us -> none  [attention_rows(): jnp.einsum('rgjp,rgpd->rgjd', weights, values_all, preferred_element_type...]
  transfers between devices with their start and end apart: 6 -> 6, of which waited for: 3 -> 3; matrix products, arithmetic and copies ran while one was open for 6% -> 5% of each run, Pallas kernels for 0% -> 0%
where the time goes in v10:
time: 43.1 us; the launch traced here: 42.7 us
  blocking collectives  14.3 us (33%)
  waiting for transfers between devices  8.33 us (19%)
  Pallas kernels  6.51 us (15%)
  starting transfers between devices  4.84 us (11%)
  local copies, waits for them, and re-layouts  4.11 us (10%)
  matrix products  3.04 us (7%)
  other arithmetic  1.42 us (3%)
    all_to_all x1, blocking collectives, local(): lax.all_to_all(outgoing, 'rows', split_axis=0, concat_axis=0, tiled=True)  14.3 us
    pallas_call x1, Pallas kernels, attention_rows(): pl.pallas_call(attention_kernel, out_shape=jax.ShapeDtypeStruct(queries.s...  6.51 us
    all_to_all x1, waiting for transfers between devices, local(): lax.all_to_all(owner_sum, 'rows', split_axis=0, concat_axis=0, tiled=True)  6.34 us
    all_to_all x1, starting transfers between devices, local(): lax.all_to_all(owner_sum, 'rows', split_axis=0, concat_axis=0, tiled=True)  3.37 us
    unnamed x19, local copies, waits for them, and re-layouts  3.07 us
    ppermute x5, waiting for transfers between devices, partner(): return lax.ppermute(block, axis, route)  1.99 us
    ppermute x5, starting transfers between devices, partner(): return lax.ppermute(block, axis, route)  1.47 us
    reduce_sum x1, other arithmetic, local(): square_part = jnp.sum(local_wide * local_wide, axis=-1)  1.1 us
  transfers between devices with their start and end apart: 6, of which 3 were waited for; matrix products, arithmetic and copies ran while one was open for 5% of the time, Pallas kernels for 0%

profile of v10, /device:TPU:0, one launch (start us, length us, event | category | flops | bytes accessed | tf_op | source)
XLA Modules:
  0.0 42.7 jit_solution(1156133450441275856)
XLA Ops:
  0.0 0.0 copy-start
  0.0 1.6 %copy.29 = bf16[1,8,32,128]{3,2,1,0:T(8,128)(2,1)} copy(bf16[1,8,32,128]{3,1,2,0:T(8,128)(2,1)} %bitcast.39) | data formatting | bytes 131072
  1.6 0.0 copy-start.4
  1.6 6.5 %shard_map.145 = f32[8,2,16,128]{3,2,1,0:T(8,128)} custom-call(s32[8]{0:T(128)} %len_ref.1, bf16[8,2,16,128]{3,2,1,0:T(8,128)(2,1)} %bitcast.38, bf16[8,2,32,128]{3,2,1,0:T(8,128)(2,1)} %k_ref.1, bf16[8,2,32,128]{3,2,1,0:T(8,128)(2,1)} %v_ref.1, bf16[8,2,128]{2,1,0:T(2,128)(2,1)} %kn_ref.1, bf16[8,2,128]{2,1,0:T(2,128)(2,1)} %vn_ref.1), custom_call_target="tpu_custom_call" | custom-call | flops 4194304 | bytes 458752 | tf_op jit(solution)/shard_map/pallas_call | solution.py:62
  8.1 0.0 copy-done.4
  8.1 1.1 %fusion.14 = (f32[8]{0:T(128)S(1)}, bf16[8,4096]{1,0:T(8,128)(2,1)S(1)}) fusion(f32[1,8,32,128]{3,2,1,0:T(8,128)} %bitcast.37, bf16[8,4096]{1,0:T(8,128)(2,1)S(1)} %copy-done.4), kind=kLoop, calls=%fused_computation.20 | loop fusion | flops 196600 | bytes 262176 | tf_op jit(solution)/shard_map/reduce_sum | solution.py:127
  9.2 0.5 %collective-permute-start = (f32[8]{0:T(128)S(1)}, f32[8]{0:T(128)S(1)}, u32[]{:S(2)}, u32[]{:S(2)}) collective-permute-start(f32[8]{0:T(128)S(1)} %get-tuple-element.9), channel_id=1, source_target_pairs={{0,1},{1,0},{2,3},{3,2},{4,5},{5,4},{6,7},{7,6},{8,9},{9,8},{10,11... | collective-permute-start | bytes 104 | tf_op jit(solution)/shard_map/ppermute | solution.py:20
  9.7 0.0 copy-start.5
  9.7 0.0 copy-start.6
  9.7 0.7 %copy-done.5 = s32[8,4]{0,1:T(4,128)S(1)} copy-done((s32[8,4]{0,1:T(4,128)S(1)}, s32[8,4]{0,1:T(4,128)}, u32[]{:S(2)}) %copy-start.5) | copy-done | bytes 152
  10.4 0.2 reduce_window_sum.11
  10.6 0.0 copy-done.6
  10.6 0.0 collective-permute-done
  10.6 0.1 fusion.16
  10.7 0.0 copy-start.7
  10.8 0.2 convolution_convert_fusion.1
  10.9 0.1 copy.25
  11.1 14.3 %all_to_all.10 = bf16[8,2,4096]{2,1,0:T(2,128)(2,1)S(1)} all-to-all(bf16[8,2,4096]{2,1,0:T(2,128)(2,1)S(1)} %copy.25), channel_id=1, replica_groups=mesh['groups'=2,'rows'=8,'heads'=2] {'rows'}, dimensions={0} | all-to-all | bytes 262144 | tf_op jit(solution)/shard_map/all_to_all | solution.py:149
  25.3 0.1 reshape.24
  25.4 0.1 collective-permute-start.2
  25.5 0.0 copy-start.8
  25.5 0.5 %collective-permute-start.1 = (bf16[8,4096]{1,0:T(8,128)(2,1)S(1)}, bf16[8,4096]{1,0:T(8,128)(2,1)S(1)}, u32[]{:S(2)}, u32[]{:S(2)}) collective-permute-start(bf16[8,4096]{1,0:T(8,128)(2,1)S(1)} %fusion.16), channel_id=1, source_target_pairs={{0,1},{1,0},{2,3},{3,2},{4,5},{5,4},{6,7},{7,6},{8,9},{9,8},{10,11... | collective-permute-start | bytes 196616 | tf_op jit(solution)/shard_map/ppermute | solution.py:20
  25.9 0.8 %collective-permute-done.2 = bf16[16,4096]{1,0:T(8,128)(2,1)S(1)} collective-permute-done((bf16[16,4096]{1,0:T(8,128)(2,1)S(1)}, bf16[16,4096]{1,0:T(8,128)(2,1)S(1)}, u32[]{:S(2)}, u32[]{:S(2)}) %collective-permute-start.2) | collective-permute-done | bytes 131104 | tf_op jit(solution)/shard_map/ppermute | solution.py:20
  26.8 0.0 copy-done.7
  26.8 0.2 fusion.20
  27.0 0.0 copy-done.8
  27.0 0.0 copy-start.3
  27.0 0.3 multiply_convert_fusion
  27.3 0.0 copy-start.1
  27.3 0.8 %copy-done.3 = bf16[32,8192]{1,0:T(8,128)(2,1)S(1)} copy-done((bf16[32,8192]{1,0:T(8,128)(2,1)S(1)}, bf16[32,8192]{1,0:T(8,128)(2,1)}, u32[]{:S(2)}) %copy-start.3) | copy-done | bytes 524312
  28.1 0.2 convolution_convert_fusion
  28.3 0.2 collective-permute-start.3
  28.5 0.0 collective-permute-done.1
  28.5 0.0 copy-start.2
  28.5 1.2 %collective-permute-done.3 = bf16[8,2,4096]{2,0,1:T(8,128)(2,1)S(1)} collective-permute-done((bf16[8,2,4096]{2,0,1:T(8,128)(2,1)S(1)}, bf16[8,2,4096]{2,0,1:T(8,128)(2,1)S(1)}, u32[]{:S(2)}, u32[]{:S(2)}) %collective-permute-start.3) | collective-permute-done | bytes 131104 | tf_op jit(solution)/shard_map/ppermute | solution.py:20
  29.7 0.2 add_convert_fusion
  29.9 0.8 %copy.28 = bf16[8,2,4096]{2,1,0:T(2,128)(2,1)} copy(bf16[8,2,4096]{2,0,1:T(8,128)(2,1)S(1)} %add_convert_fusion) | data formatting | bytes 262144 | tf_op jit(solution)/shard_map/optimization_barrier | solution.py:156
  30.6 3.4 %all-to-all-start.1 = ((bf16[8,2,4096]{2,1,0:T(2,128)(2,1)}), bf16[8,2,4096]{2,1,0:T(2,128)(2,1)S(1)}, u32[]{:S(2)}, u32[]{:S(2)}) async-start(bf16[8,2,4096]{2,1,0:T(2,128)(2,1)} %copy.28), calls=%async_computation.1 | async-start | bytes 262144 | tf_op jit(solution)/shard_map/all_to_all | solution.py:157
  34.0 0.0 copy-done.1
  34.0 0.4 fusion.32
  34.4 0.0 copy-done.2
  34.4 0.4 fusion.3
  34.8 0.0 copy-done
  34.8 0.2 fusion.4
  35.0 0.2 collective-permute-start.4
  35.2 6.3 %all-to-all-done.1 = bf16[8,2,4096]{2,1,0:T(2,128)(2,1)S(1)} async-done(((bf16[8,2,4096]{2,1,0:T(2,128)(2,1)}), bf16[8,2,4096]{2,1,0:T(2,128)(2,1)S(1)}, u32[]{:S(2)}, u32[]{:S(2)}) %all-to-all-start.1) | async-done | bytes 131104 | tf_op jit(solution)/shard_map/all_to_all | solution.py:157
  41.5 0.1 reshape.26
  41.6 0.3 fusion.33
  41.9 0.0 collective-permute-done.4
  41.9 0.8 %fusion.2 = bf16[8,4096]{1,0:T(8,128)(2,1)} fusion(f32[8,4096]{1,0:T(8,128)S(1)} %fusion.33, f32[8,4096]{1,0:T(8,128)S(1)} %collective-permute-done.4, bf16[8,64]{1,0:T(8,128)(2,1)S(1)} %fusion.3, bf16[64,8192]{1,0:T(8,128)(2,1)S(1)} %copy-done, s32[]{:T(128)S(6)} %select_n.26, bf16[8,4096]{1,0:T(8,128)(2,1)S(1)} %get-tuple-element.10), kind=kOutput, calls=%fused_computation.5 | convolution fusion | flops 4358144 | bytes 919556 | tf_op jit(solution)/shard_map/...n,nd->...d/dot_general | solution.py:91
  (8 shorter events, 0.1 us)
Async XLA Ops:
  0.0 34.8 %copy-start = (bf16[64,8192]{1,0:T(8,128)(2,1)S(1)}, bf16[64,8192]{1,0:T(8,128)(2,1)}, u32[]{:S(2)}) copy-start(bf16[64,8192]{1,0:T(8,128)(2,1)} %param.25) | copy-start | bytes 3145732
  1.6 6.5 %copy-start.4 = (bf16[8,4096]{1,0:T(8,128)(2,1)S(1)}, bf16[8,4096]{1,0:T(8,128)(2,1)}, u32[]{:S(2)}) copy-start(bf16[8,4096]{1,0:T(8,128)(2,1)} %param.15) | copy-start | bytes 196612
  9.2 1.4 %collective-permute-start = (f32[8]{0:T(128)S(1)}, f32[8]{0:T(128)S(1)}, u32[]{:S(2)}, u32[]{:S(2)}) collective-permute-start(f32[8]{0:T(128)S(1)} %get-tuple-element.9), channel_id=1, source_target_pairs={{0,1},{1,0},{2,3},{3,2},{4,5},{5,4},{6,7},{7,6},{8,9},{9,8},{10,11... | collective-permute-start | bytes 104 | tf_op jit(solution)/shard_map/ppermute | solution.py:20
  9.7 0.7 %copy-start.5 = (s32[8,4]{0,1:T(4,128)S(1)}, s32[8,4]{0,1:T(4,128)}, u32[]{:S(2)}) copy-start(s32[8,4]{0,1:T(4,128)} %param.29) | copy-start | bytes 388
  9.7 0.9 %copy-start.6 = (bf16[8192]{0:T(1024)(128)(2,1)S(1)}, bf16[8192]{0:T(1024)(128)(2,1)}, u32[]{:S(2)}) copy-start(bf16[8192]{0:T(1024)(128)(2,1)} %param.22) | copy-start | bytes 49156
  10.7 16.1 %copy-start.7 = (bf16[32,8192]{1,0:T(8,128)(2,1)S(1)}, bf16[32,8192]{1,0:T(8,128)(2,1)}, u32[]{:S(2)}) copy-start(bf16[32,8192]{1,0:T(8,128)(2,1)} %param.26) | copy-start | bytes 1572868
  25.4 1.4 %collective-permute-start.2 = (bf16[16,4096]{1,0:T(8,128)(2,1)S(1)}, bf16[16,4096]{1,0:T(8,128)(2,1)S(1)}, u32[]{:S(2)}, u32[]{:S(2)}) collective-permute-start(bf16[16,4096]{1,0:T(8,128)(2,1)S(1)} %reshape.24), channel_id=1, source_target_pairs={{0,1},{1,0},{2,3},{3,2},{4,5},{5,4},{6,7},{7,6},{8,9},{9,8},{10,11... | collective-permute-start | bytes 393224 | tf_op jit(solution)/shard_map/ppermute | solution.py:20
  25.5 1.6 %copy-start.8 = (bf16[32,8192]{1,0:T(8,128)(2,1)S(1)}, bf16[32,8192]{1,0:T(8,128)(2,1)}, u32[]{:S(2)}) copy-start(bf16[32,8192]{1,0:T(8,128)(2,1)} %param.27) | copy-start | bytes 1572868
  25.5 3.0 %collective-permute-start.1 = (bf16[8,4096]{1,0:T(8,128)(2,1)S(1)}, bf16[8,4096]{1,0:T(8,128)(2,1)S(1)}, u32[]{:S(2)}, u32[]{:S(2)}) collective-permute-start(bf16[8,4096]{1,0:T(8,128)(2,1)S(1)} %fusion.16), channel_id=1, source_target_pairs={{0,1},{1,0},{2,3},{3,2},{4,5},{5,4},{6,7},{7,6},{8,9},{9,8},{10,11... | collective-permute-start | bytes 196616 | tf_op jit(solution)/shard_map/ppermute | solution.py:20
  27.0 1.1 %copy-start.3 = (bf16[32,8192]{1,0:T(8,128)(2,1)S(1)}, bf16[32,8192]{1,0:T(8,128)(2,1)}, u32[]{:S(2)}) copy-start(bf16[32,8192]{1,0:T(8,128)(2,1)} %param.28) | copy-start | bytes 1572868
  27.3 6.7 %copy-start.1 = (bf16[64,8192]{1,0:T(8,128)(2,1)S(1)}, bf16[64,8192]{1,0:T(8,128)(2,1)}, u32[]{:S(2)}) copy-start(bf16[64,8192]{1,0:T(8,128)(2,1)} %param.23) | copy-start | bytes 3145732
  28.3 1.4 %collective-permute-start.3 = (bf16[8,2,4096]{2,0,1:T(8,128)(2,1)S(1)}, bf16[8,2,4096]{2,0,1:T(8,128)(2,1)S(1)}, u32[]{:S(2)}, u32[]{:S(2)}) collective-permute-start(bf16[8,2,4096]{2,0,1:T(8,128)(2,1)S(1)} %convolution_convert_fusion), channel_id=1, source_target_pairs={{0,1},{1,0},{2,3},{3,2},{4,5},{5,4},{6,7},{7,6},{8,9},{9,8},{10,11... | collective-permute-start | bytes 393224 | tf_op jit(solution)/shard_map/ppermute | solution.py:20
  28.5 5.9 %copy-start.2 = (bf16[64,8192]{1,0:T(8,128)(2,1)S(1)}, bf16[64,8192]{1,0:T(8,128)(2,1)}, u32[]{:S(2)}) copy-start(bf16[64,8192]{1,0:T(8,128)(2,1)} %param.24) | copy-start | bytes 3145732
  30.6 10.9 %all-to-all-start.1 = ((bf16[8,2,4096]{2,1,0:T(2,128)(2,1)}), bf16[8,2,4096]{2,1,0:T(2,128)(2,1)S(1)}, u32[]{:S(2)}, u32[]{:S(2)}) async-start(bf16[8,2,4096]{2,1,0:T(2,128)(2,1)} %copy.28), calls=%async_computation.1 | async-start | bytes 262144 | tf_op jit(solution)/shard_map/all_to_all | solution.py:157
  35.0 6.9 %collective-permute-start.4 = (f32[8,4096]{1,0:T(8,128)S(1)}, f32[8,4096]{1,0:T(8,128)S(1)}, u32[]{:S(2)}, u32[]{:S(2)}) collective-permute-start(f32[8,4096]{1,0:T(8,128)S(1)} %fusion.4), channel_id=1, source_target_pairs={{0,1},{1,0},{2,3},{3,2},{4,5},{5,4},{6,7},{7,6},{8,9},{9,8},{10,11... | collective-permute-start | bytes 393224 | tf_op jit(solution)/shard_map/ppermute | solution.py:20

commit v11 on v8

--- a/solution.py
+++ b/solution.py
@@ -48,6 +48,13 @@
         "rgjp,rgpd->rgjd", weights, values_all, preferred_element_type=jnp.float32
     )
     return blended.reshape(count, -1)
+
+
+def normalize_rows(rows, norm_gain):
+    wide = rows.astype(jnp.float32)
+    mean_square = jnp.sum(wide * wide, axis=-1, keepdims=True) / D
+    scaled = wide * lax.rsqrt(mean_square + 1e-05) * norm_gain.astype(jnp.float32)
+    return scaled.astype(jnp.bfloat16)
 
 
 def swiglu_rows(normed, gate_rows, up_rows, down_rows):
@@ -101,14 +108,6 @@
     stream = (residual_in.astype(jnp.float32) + attended).astype(jnp.bfloat16)
     half_width = stream.shape[1]
     myself = lax.axis_index("heads")
-    local_wide = stream.astype(jnp.float32)
-    square_part = jnp.sum(local_wide * local_wide, axis=-1)
-    square_total = square_part + partner(square_part, "heads", 0)
-    gain_half = lax.dynamic_slice_in_dim(norm_gain, myself * half_width, half_width)
-    scaled = (
-        local_wide * lax.rsqrt(square_total / D + 1e-05)[:, None] * gain_half.astype(jnp.float32)
-    )
-    normed = join_halves(scaled.astype(jnp.bfloat16), myself)
     owner_count = lax.axis_size("rows")
     block_count = active.shape[1]
     request_count = active.shape[0]
@@ -121,20 +120,21 @@
     outgoing = jnp.einsum(
         "ocr,rd->ocd",
         selector3.astype(jnp.bfloat16),
-        scaled.astype(jnp.bfloat16),
+        stream,
         preferred_element_type=jnp.float32,
     ).astype(jnp.bfloat16)
     incoming_half = lax.all_to_all(outgoing, "rows", split_axis=0, concat_axis=0, tiled=True)
-    incoming = join_halves(incoming_half.reshape(owner_count * CAP, -1), myself)
+    incoming = normalize_rows(join_halves(incoming_half.reshape(owner_count * CAP, -1), myself), norm_gain)
     kept, given = swiglu_halves(
         incoming, cold_gate, cold_up, cold_down, myself, (owner_count, CAP)
     )
     given_narrow = partner(given.astype(jnp.bfloat16), "heads", 0)
     owner_sum = (kept + given_narrow.astype(jnp.float32)).astype(jnp.bfloat16)
-    normed_late, owner_sum = lax.optimization_barrier((normed, owner_sum))
+    stream_late, owner_sum = lax.optimization_barrier((stream, owner_sum))
     returned = lax.all_to_all(owner_sum, "rows", split_axis=0, concat_axis=0, tiled=True)
+    normed = normalize_rows(join_halves(stream_late, myself), norm_gain)
     hot_kept, hot_given = swiglu_halves(
-        normed_late, hot_gate, hot_up, hot_down, myself, (request_count,)
+        normed, hot_gate, hot_up, hot_down, myself, (request_count,)
     )
     hot_total = hot_kept + partner(hot_given, "heads", 0)
     cold_sum = collect_rows(

time: 37.9 us -> 39.5 us (1.042)
  local copies, waits for them, and re-layouts: 4.33 us -> 6.19 us
  starting transfers between devices: 4.84 us -> 4.28 us
    unnamed x28 -> x30, local copies, waits for them, and re-layouts: 2.48 us -> 5.14 us
    broadcast_in_dim x1, local copies, waits for them, and re-layouts: 0.79 us -> 0.01 us  [attention_rows(): keys_all = jnp.concatenate([key_cache, key_new[:, :, None, :]], axis=2)]
    ppermute x5 -> x4, starting transfers between devices: 1.47 us -> 0.91 us  [partner(): return lax.ppermute(block, axis, route)]
    ppermute x5 -> x4, waiting for transfers between devices: 1.99 us -> 1.95 us  [partner(): return lax.ppermute(block, axis, route)]
  transfers between devices with their start and end apart: 6 -> 5, of which waited for: 3 -> 3; matrix products, arithmetic and copies ran while one was open for 6% -> 6% of each run, Pallas kernels for 0% -> 0%
where the time goes in v11:
time: 39.5 us; the launch traced here: 38.9 us
  blocking collectives  14.4 us (36%)
  waiting for transfers between devices  7.98 us (20%)
  local copies, waits for them, and re-layouts  6.19 us (16%)
  matrix products  5.1 us (13%)
  starting transfers between devices  4.28 us (11%)
  other arithmetic  0.78 us (2%)
    all_to_all x1, blocking collectives, local(): lax.all_to_all(outgoing, 'rows', split_axis=0, concat_axis=0, tiled=True)  14.4 us
    all_to_all x1, waiting for transfers between devices, local(): lax.all_to_all(owner_sum, 'rows', split_axis=0, concat_axis=0, tiled=True)  6.03 us
    unnamed x30, local copies, waits for them, and re-layouts  5.14 us
    all_to_all x1, starting transfers between devices, local(): lax.all_to_all(owner_sum, 'rows', split_axis=0, concat_axis=0, tiled=True)  3.37 us
    ppermute x4, waiting for transfers between devices, partner(): return lax.ppermute(block, axis, route)  1.95 us
    sub x1, matrix products, attention_rows(): expons = jnp.where(visible, jnp.exp(scores - highest[..., None]), 0.0)  1.33 us
    dot_general x2, matrix products, swiglu_halves(): jnp.einsum('...n,nd->...d', hidden, down_kept, preferred_element_type=jnp...  0.99 us
    ppermute x4, starting transfers between devices, partner(): return lax.ppermute(block, axis, route)  0.91 us
  transfers between devices with their start and end apart: 5, of which 3 were waited for; matrix products, arithmetic and copies ran while one was open for 6% of the time, Pallas kernels for 0%

profile of v11, /device:TPU:0, one launch (start us, length us, event | category | flops | bytes accessed | tf_op | source)
XLA Modules:
  0.0 38.9 jit_solution(8961775656715866337)
XLA Ops:
  0.0 0.0 copy-start
  0.0 0.0 copy-start.5
  0.0 0.8 %copy-done.5 = s32[8,4]{0,1:T(4,128)S(1)} copy-done((s32[8,4]{0,1:T(4,128)S(1)}, s32[8,4]{0,1:T(4,128)}, u32[]{:S(2)}) %copy-start.5) | copy-done | bytes 152
  0.8 0.2 reduce_window_sum.11
  1.0 0.0 copy-start.7
  1.0 0.7 %copy-done.7 = bf16[8,2,128]{2,1,0:T(2,128)(2,1)S(1)} copy-done((bf16[8,2,128]{2,1,0:T(2,128)(2,1)S(1)}, bf16[8,2,128]{2,1,0:T(2,128)(2,1)}, u32[]{:S(2)}) %copy-start.7) | copy-done | bytes 4120
  1.7 0.0 copy-start.8
  1.7 0.7 %copy-done.8 = bf16[8,2,128]{2,1,0:T(2,128)(2,1)S(1)} copy-done((bf16[8,2,128]{2,1,0:T(2,128)(2,1)S(1)}, bf16[8,2,128]{2,1,0:T(2,128)(2,1)}, u32[]{:S(2)}) %copy-start.8) | copy-done | bytes 4120
  2.3 0.0 copy-start.9
  2.4 0.6 %copy-done.9 = s32[8]{0:T(128)S(1)} copy-done((s32[8]{0:T(128)S(1)}, s32[8]{0:T(128)}, u32[]{:S(2)}) %copy-start.9) | copy-done | bytes 56
  3.0 0.1 fusion.55
  3.1 0.0 copy-start.12
  3.1 0.0 copy-start.13
  3.1 0.0 copy-start.14
  3.1 1.3 %fusion.84 = f32[8,2,16]{2,1,0:T(2,128)S(1)} fusion(bf16[8,2,1,128]{3,2,1,0:T(2,128)(2,1)S(1)} %copy.31, bf16[8,2,32,128]{3,2,1,0:T(8,128)(2,1)} %param.17, bf16[8,2,16,128]{3,0,2,1:T(8,128)(2,1)} %bitcast.55, pred[8,33]{1,0:T(8,128)(4,1)S(1)} %fusion.55), kind=kOutput, calls=%fused_computation.78 | convolution fusion | flops 2475296 | bytes 201992 | tf_op jit(solution)/shard_map/sub | solution.py:44
  4.4 0.0 copy-done.12
  4.4 0.0 copy-done.13
  4.4 0.0 copy-done.14
  4.5 0.0 copy-start.4
  4.5 0.5 %fusion.30 = f32[8,2,16,128]{3,2,1,0:T(8,128)S(1)} fusion(bf16[8,2,1,128]{3,2,1,0:T(2,128)(2,1)S(1)} %copy.34, bf16[8,2,32,128]{3,2,1,0:T(8,128)(2,1)S(1)} %copy-done.12, f32[8,2,16]{2,1,0:T(2,128)S(1)} %fusion.84, pred[8,33]{1,0:T(8,128)(4,1)S(1)} %fusion.55, bf16[8,2,1,128]{3,2,1,0:T(2,128)(2,1)S(1)} %copy.31, bf16[8,2,32,128]{3,2,1,0:T(8,128)(2,1)S(1)} %copy-done.13, ...), kind=kOutput, calls=%fused_computation.40 | convolution fusion | flops 4917024 | bytes 468232 | tf_op jit(solution)/shard_map/rgjp,rgpd->rgjd/dot_general | solution.py:47
  5.0 0.3 copy-done.4
  5.3 0.1 fusion.34
  5.4 0.2 convolution_convert_fusion.1
  5.6 0.0 copy-start.10
  5.6 0.1 copy.36
  5.7 14.4 %all_to_all.10 = bf16[8,2,4096]{2,1,0:T(2,128)(2,1)S(1)} all-to-all(bf16[8,2,4096]{2,1,0:T(2,128)(2,1)S(1)} %copy.36), channel_id=1, replica_groups=mesh['groups'=2,'rows'=8,'heads'=2] {'rows'}, dimensions={0} | all-to-all | bytes 262144 | tf_op jit(solution)/shard_map/all_to_all | solution.py:126
  20.1 0.0 copy-start.6
  20.1 0.1 reshape.75
  20.2 0.1 collective-permute-start
  20.3 0.6 %copy-done.6 = bf16[8192]{0:T(1024)(128)(2,1)S(1)} copy-done((bf16[8192]{0:T(1024)(128)(2,1)S(1)}, bf16[8192]{0:T(1024)(128)(2,1)}, u32[]{:S(2)}) %copy-start.6) | copy-done | bytes 16408
  20.8 0.7 %collective-permute-done = bf16[16,4096]{1,0:T(8,128)(2,1)S(1)} collective-permute-done((bf16[16,4096]{1,0:T(8,128)(2,1)S(1)}, bf16[16,4096]{1,0:T(8,128)(2,1)S(1)}, u32[]{:S(2)}, u32[]{:S(2)}) %collective-permute-start) | collective-permute-done | bytes 131104 | tf_op jit(solution)/shard_map/ppermute | solution.py:18
  21.6 0.2 fusion.11
  21.8 0.0 copy-done.10
  21.8 0.0 copy-start.11
  21.8 0.3 fusion.39
  22.1 0.7 %copy-done.11 = bf16[32,8192]{1,0:T(8,128)(2,1)S(1)} copy-done((bf16[32,8192]{1,0:T(8,128)(2,1)S(1)}, bf16[32,8192]{1,0:T(8,128)(2,1)}, u32[]{:S(2)}) %copy-start.11) | copy-done | bytes 524312
  22.9 0.0 copy-start.3
  22.9 0.3 fusion.9
  23.2 0.0 copy-start.1
  23.2 0.7 %copy-done.3 = bf16[32,8192]{1,0:T(8,128)(2,1)S(1)} copy-done((bf16[32,8192]{1,0:T(8,128)(2,1)S(1)}, bf16[32,8192]{1,0:T(8,128)(2,1)}, u32[]{:S(2)}) %copy-start.3) | copy-done | bytes 524312
  23.9 0.2 convolution_convert_fusion
  24.1 0.2 collective-permute-start.1
  24.3 1.2 %collective-permute-done.1 = bf16[8,2,4096]{2,0,1:T(8,128)(2,1)S(1)} collective-permute-done((bf16[8,2,4096]{2,0,1:T(8,128)(2,1)S(1)}, bf16[8,2,4096]{2,0,1:T(8,128)(2,1)S(1)}, u32[]{:S(2)}, u32[]{:S(2)}) %collective-permute-start.1) | collective-permute-done | bytes 131104 | tf_op jit(solution)/shard_map/ppermute | solution.py:18
  25.5 0.2 add_convert_fusion
  25.7 0.0 copy-start.2
  25.7 0.2 collective-permute-start.2
  25.9 0.8 %copy.39 = bf16[8,2,4096]{2,1,0:T(2,128)(2,1)} copy(bf16[8,2,4096]{2,0,1:T(8,128)(2,1)S(1)} %add_convert_fusion) | data formatting | bytes 262144 | tf_op jit(solution)/shard_map/optimization_barrier | solution.py:133
  26.7 3.4 %all-to-all-start.1 = ((bf16[8,2,4096]{2,1,0:T(2,128)(2,1)}), bf16[8,2,4096]{2,1,0:T(2,128)(2,1)S(1)}, u32[]{:S(2)}, u32[]{:S(2)}) async-start(bf16[8,2,4096]{2,1,0:T(2,128)(2,1)} %copy.39), calls=%async_computation.1 | async-start | bytes 262144 | tf_op jit(solution)/shard_map/all_to_all | solution.py:134
  30.0 0.0 collective-permute-done.2
  30.1 0.2 fusion.17
  30.3 0.0 copy-done.1
  30.3 0.4 %fusion.82 = f32[8,64]{1,0:T(8,128)S(1)} fusion(bf16[64,8192]{1,0:T(8,128)(2,1)S(1)} %copy-done.1, f32[8192]{0:T(1024)S(1)} %convert_element_type.73, f32[8]{0:T(128)S(1)} %add_rsqrt_fusion, bf16[8,4096]{1,0:T(8,128)(2,1)S(1)} %fusion.34, bf16[8,4096]{1,0:T(8,128)(2,1)S(1)} %collective-permute-done.2, pred[]{:T(512)S(6)} %eq.30), kind=kOutput, calls=%fused_computation.77 | convolution fusion | flops 9240576 | bytes 1214497 | tf_op jit(solution)/shard_map/rd,nd->rn/dot_general | solution.py:68
  30.7 0.0 copy-done.2
  30.7 0.4 %fusion.10 = bf16[8,64]{1,0:T(8,128)(2,1)S(1)} fusion(bf16[64,8192]{1,0:T(8,128)(2,1)S(1)} %copy-done.2, f32[8,64]{1,0:T(8,128)S(1)} %fusion.82, f32[8192]{0:T(1024)S(1)} %convert_element_type.73, f32[8]{0:T(128)S(1)} %add_rsqrt_fusion, bf16[8,4096]{1,0:T(8,128)(2,1)S(1)} %fusion.34, bf16[8,4096]{1,0:T(8,128)(2,1)S(1)} %collective-permute-done.2, pred[]{:T(512)S(6)} %eq.30), kind=kOutput, calls=%fused_computation.16 | convolution fusion | flops 9243648 | bytes 1215521 | tf_op jit(solution)/shard_map/rd,nd->rn/dot_general | solution.py:69
  31.1 0.0 copy-done
  31.1 0.2 fusion.14
  31.3 0.4 %collective-permute-start.3 = (f32[8,4096]{1,0:T(8,128)S(1)}, f32[8,4096]{1,0:T(8,128)S(1)}, u32[]{:S(2)}, u32[]{:S(2)}) collective-permute-start(f32[8,4096]{1,0:T(8,128)S(1)} %fusion.14), channel_id=1, source_target_pairs={{0,1},{1,0},{2,3},{3,2},{4,5},{5,4},{6,7},{7,6},{8,9},{9,8},{10,11... | collective-permute-start | bytes 393224 | tf_op jit(solution)/shard_map/ppermute | solution.py:18
  31.7 6.0 %all-to-all-done.1 = bf16[8,2,4096]{2,1,0:T(2,128)(2,1)S(1)} async-done(((bf16[8,2,4096]{2,1,0:T(2,128)(2,1)}), bf16[8,2,4096]{2,1,0:T(2,128)(2,1)S(1)}, u32[]{:S(2)}, u32[]{:S(2)}) %all-to-all-start.1) | async-done | bytes 131104 | tf_op jit(solution)/shard_map/all_to_all | solution.py:134
  37.8 0.1 reshape.77
  37.8 0.3 fusion.89
  38.1 0.0 collective-permute-done.3
  38.1 0.8 %fusion.3 = bf16[8,4096]{1,0:T(8,128)(2,1)} fusion(f32[8,4096]{1,0:T(8,128)S(1)} %fusion.89, f32[8,4096]{1,0:T(8,128)S(1)} %collective-permute-done.3, bf16[8,64]{1,0:T(8,128)(2,1)S(1)} %fusion.10, bf16[64,8192]{1,0:T(8,128)(2,1)S(1)} %copy-done, s32[]{:T(128)S(6)} %select_n.40, bf16[8,4096]{1,0:T(8,128)(2,1)S(1)} %fusion.34), kind=kOutput, calls=%fused_computation.6 | convolution fusion | flops 4358144 | bytes 919556 | tf_op jit(solution)/shard_map/...n,nd->...d/dot_general | solution.py:76
  (11 shorter events, 0.1 us)
Async XLA Ops:
  0.0 31.1 %copy-start = (bf16[64,8192]{1,0:T(8,128)(2,1)S(1)}, bf16[64,8192]{1,0:T(8,128)(2,1)}, u32[]{:S(2)}) copy-start(bf16[64,8192]{1,0:T(8,128)(2,1)} %param.25) | copy-start | bytes 3145732
  0.0 0.8 %copy-start.5 = (s32[8,4]{0,1:T(4,128)S(1)}, s32[8,4]{0,1:T(4,128)}, u32[]{:S(2)}) copy-start(s32[8,4]{0,1:T(4,128)} %param.29) | copy-start | bytes 388
  1.0 0.7 %copy-start.7 = (bf16[8,2,128]{2,1,0:T(2,128)(2,1)S(1)}, bf16[8,2,128]{2,1,0:T(2,128)(2,1)}, u32[]{:S(2)}) copy-start(bf16[8,2,128]{2,1,0:T(2,128)(2,1)} %param.19) | copy-start | bytes 12292
  1.7 0.7 %copy-start.8 = (bf16[8,2,128]{2,1,0:T(2,128)(2,1)S(1)}, bf16[8,2,128]{2,1,0:T(2,128)(2,1)}, u32[]{:S(2)}) copy-start(bf16[8,2,128]{2,1,0:T(2,128)(2,1)} %param.20) | copy-start | bytes 12292
  2.3 0.7 %copy-start.9 = (s32[8]{0:T(128)S(1)}, s32[8]{0:T(128)}, u32[]{:S(2)}) copy-start(s32[8]{0:T(128)} %param.21) | copy-start | bytes 100
  3.1 1.4 %copy-start.12 = (bf16[8,2,32,128]{3,2,1,0:T(8,128)(2,1)S(1)}, bf16[8,2,32,128]{3,2,1,0:T(8,128)(2,1)}, u32[]{:S(2)}) copy-start(bf16[8,2,32,128]{3,2,1,0:T(8,128)(2,1)} %param.18) | copy-start | bytes 393220
  3.1 1.4 %copy-start.13 = (bf16[8,2,32,128]{3,2,1,0:T(8,128)(2,1)S(1)}, bf16[8,2,32,128]{3,2,1,0:T(8,128)(2,1)}, u32[]{:S(2)}) copy-start(bf16[8,2,32,128]{3,2,1,0:T(8,128)(2,1)} %param.17) | copy-start | bytes 393220
  3.1 1.4 %copy-start.14 = (bf16[8,4096]{1,0:T(8,128)(2,1)S(1)}, bf16[8,4096]{1,0:T(8,128)(2,1)}, u32[]{:S(2)}) copy-start(bf16[8,4096]{1,0:T(8,128)(2,1)} %param.16) | copy-start | bytes 196612
  4.5 0.8 %copy-start.4 = (bf16[8,4096]{1,0:T(8,128)(2,1)S(1)}, bf16[8,4096]{1,0:T(8,128)(2,1)}, u32[]{:S(2)}) copy-start(bf16[8,4096]{1,0:T(8,128)(2,1)} %param.15) | copy-start | bytes 196612
  5.6 16.2 %copy-start.10 = (bf16[32,8192]{1,0:T(8,128)(2,1)S(1)}, bf16[32,8192]{1,0:T(8,128)(2,1)}, u32[]{:S(2)}) copy-start(bf16[32,8192]{1,0:T(8,128)(2,1)} %param.26) | copy-start | bytes 1572868
  20.1 0.7 %copy-start.6 = (bf16[8192]{0:T(1024)(128)(2,1)S(1)}, bf16[8192]{0:T(1024)(128)(2,1)}, u32[]{:S(2)}) copy-start(bf16[8192]{0:T(1024)(128)(2,1)} %param.22) | copy-start | bytes 49156
  20.2 1.4 %collective-permute-start = (bf16[16,4096]{1,0:T(8,128)(2,1)S(1)}, bf16[16,4096]{1,0:T(8,128)(2,1)S(1)}, u32[]{:S(2)}, u32[]{:S(2)}) collective-permute-start(bf16[16,4096]{1,0:T(8,128)(2,1)S(1)} %reshape.75), channel_id=1, source_target_pairs={{0,1},{1,0},{2,3},{3,2},{4,5},{5,4},{6,7},{7,6},{8,9},{9,8},{10,11... | collective-permute-start | bytes 393224 | tf_op jit(solution)/shard_map/ppermute | solution.py:18
  21.8 1.0 %copy-start.11 = (bf16[32,8192]{1,0:T(8,128)(2,1)S(1)}, bf16[32,8192]{1,0:T(8,128)(2,1)}, u32[]{:S(2)}) copy-start(bf16[32,8192]{1,0:T(8,128)(2,1)} %param.27) | copy-start | bytes 1572868
  22.9 1.0 %copy-start.3 = (bf16[32,8192]{1,0:T(8,128)(2,1)S(1)}, bf16[32,8192]{1,0:T(8,128)(2,1)}, u32[]{:S(2)}) copy-start(bf16[32,8192]{1,0:T(8,128)(2,1)} %param.28) | copy-start | bytes 1572868
  23.2 7.1 %copy-start.1 = (bf16[64,8192]{1,0:T(8,128)(2,1)S(1)}, bf16[64,8192]{1,0:T(8,128)(2,1)}, u32[]{:S(2)}) copy-start(bf16[64,8192]{1,0:T(8,128)(2,1)} %param.23) | copy-start | bytes 3145732
  24.1 1.4 %collective-permute-start.1 = (bf16[8,2,4096]{2,0,1:T(8,128)(2,1)S(1)}, bf16[8,2,4096]{2,0,1:T(8,128)(2,1)S(1)}, u32[]{:S(2)}, u32[]{:S(2)}) collective-permute-start(bf16[8,2,4096]{2,0,1:T(8,128)(2,1)S(1)} %convolution_convert_fusion), channel_id=1, source_target_pairs={{0,1},{1,0},{2,3},{3,2},{4,5},{5,4},{6,7},{7,6},{8,9},{9,8},{10,11... | collective-permute-start | bytes 393224 | tf_op jit(solution)/shard_map/ppermute | solution.py:18
  25.7 5.0 %copy-start.2 = (bf16[64,8192]{1,0:T(8,128)(2,1)S(1)}, bf16[64,8192]{1,0:T(8,128)(2,1)}, u32[]{:S(2)}) copy-start(bf16[64,8192]{1,0:T(8,128)(2,1)} %param.24) | copy-start | bytes 3145732
  25.7 4.4 %collective-permute-start.2 = (bf16[8,4096]{1,0:T(8,128)(2,1)S(1)}, bf16[8,4096]{1,0:T(8,128)(2,1)S(1)}, u32[]{:S(2)}, u32[]{:S(2)}) collective-permute-start(bf16[8,4096]{1,0:T(8,128)(2,1)S(1)} %fusion.34), channel_id=1, source_target_pairs={{0,1},{1,0},{2,3},{3,2},{4,5},{5,4},{6,7},{7,6},{8,9},{9,8},{10,11... | collective-permute-start | bytes 196616 | tf_op jit(solution)/shard_map/ppermute | solution.py:18
  26.7 11.1 %all-to-all-start.1 = ((bf16[8,2,4096]{2,1,0:T(2,128)(2,1)}), bf16[8,2,4096]{2,1,0:T(2,128)(2,1)S(1)}, u32[]{:S(2)}, u32[]{:S(2)}) async-start(bf16[8,2,4096]{2,1,0:T(2,128)(2,1)} %copy.39), calls=%async_computation.1 | async-start | bytes 262144 | tf_op jit(solution)/shard_map/all_to_all | solution.py:134
  31.3 6.8 %collective-permute-start.3 = (f32[8,4096]{1,0:T(8,128)S(1)}, f32[8,4096]{1,0:T(8,128)S(1)}, u32[]{:S(2)}, u32[]{:S(2)}) collective-permute-start(f32[8,4096]{1,0:T(8,128)S(1)} %fusion.14), channel_id=1, source_target_pairs={{0,1},{1,0},{2,3},{3,2},{4,5},{5,4},{6,7},{7,6},{8,9},{9,8},{10,11... | collective-permute-start | bytes 393224 | tf_op jit(solution)/shard_map/ppermute | solution.py:18

commit v12 on v8

--- a/solution.py
+++ b/solution.py
@@ -39,7 +39,7 @@
     )
     positions = jnp.arange(slots + 1, dtype=jnp.int32)[None, :]
     visible = ((positions < lengths[:, None]) | (positions == slots))[:, None, None, :]
-    scores = jnp.where(visible, scores, -1e30)
+    scores = lax.optimization_barrier(jnp.where(visible, scores, -1e30))
     highest = jnp.max(scores, axis=-1)
     expons = jnp.where(visible, jnp.exp(scores - highest[..., None]), 0.0)
     totals = jnp.sum(expons, axis=-1)

time: 37.9 us -> 37.9 us (level)
    sub x1 -> x0, matrix products: 1.33 us -> none  [attention_rows(): expons = jnp.where(visible, jnp.exp(scores - highest[..., None]), 0.0)]
    dot_general x0 -> x1, matrix products: none -> 1.1 us  [attention_rows(): jnp.einsum('rgjd,rgpd->rgjp', queries, keys_all, preferred_element_type=j...]
    unnamed x28 -> x24, local copies, waits for them, and re-layouts: 2.48 us -> 2.55 us
where the time goes in v12:
time: 37.9 us; the launch traced here: 37.5 us
  blocking collectives  14.3 us (38%)
  waiting for transfers between devices  8.33 us (22%)
  starting transfers between devices  4.84 us (13%)
  matrix products  4.62 us (12%)
  local copies, waits for them, and re-layouts  4.39 us (12%)
  other arithmetic  0.81 us (2%)
    all_to_all x1, blocking collectives, local(): lax.all_to_all(outgoing, 'rows', split_axis=0, concat_axis=0, tiled=True)  14.3 us
    all_to_all x1, waiting for transfers between devices, local(): lax.all_to_all(owner_sum, 'rows', split_axis=0, concat_axis=0, tiled=True)  6.34 us
    all_to_all x1, starting transfers between devices, local(): lax.all_to_all(owner_sum, 'rows', split_axis=0, concat_axis=0, tiled=True)  3.37 us
    unnamed x24, local copies, waits for them, and re-layouts  2.55 us
    ppermute x5, waiting for transfers between devices, partner(): return lax.ppermute(block, axis, route)  1.99 us
    ppermute x5, starting transfers between devices, partner(): return lax.ppermute(block, axis, route)  1.47 us
    dot_general x1, matrix products, attention_rows(): jnp.einsum('rgjd,rgpd->rgjp', queries, keys_all, preferred_element_type=j...  1.1 us
    dot_general x2, matrix products, swiglu_halves(): jnp.einsum('...n,nd->...d', hidden, down_kept, preferred_element_type=jnp...  0.99 us
  transfers between devices with their start and end apart: 6, of which 3 were waited for; matrix products, arithmetic and copies ran while one was open for 6% of the time, Pallas kernels for 0%

profile of v12, /device:TPU:0, one launch (start us, length us, event | category | flops | bytes accessed | tf_op | source)
XLA Modules:
  0.0 37.5 jit_solution(14502424617561323011)
XLA Ops:
  0.0 0.0 copy-start
  0.0 0.0 copy-start.8
  0.0 0.8 %copy.31 = bf16[8,2,1,128]{3,2,1,0:T(2,128)(2,1)S(1)} copy(bf16[8,2,1,128]{3,1,0,2:T(2,128)(2,1)} %bitcast.48) | data formatting | bytes 8192 | tf_op jit(solution)/shard_map/broadcast_in_dim | solution.py:34
  0.8 0.0 copy-done.8
  0.8 0.1 fusion.38
  0.9 1.1 %fusion.8 = f32[8,2,16,33]{3,2,1,0:T(8,128)S(1)} fusion(bf16[8,2,1,128]{3,2,1,0:T(2,128)(2,1)S(1)} %copy.31, bf16[8,2,32,128]{3,2,1,0:T(8,128)(2,1)} %param.17, bf16[8,2,16,128]{3,0,2,1:T(8,128)(2,1)} %bitcast.50, pred[8,33]{1,0:T(8,128)(4,1)S(1)} %fusion.38), kind=kOutput, calls=%fused_computation.12 | convolution fusion | flops 2449920 | bytes 234760 | tf_op jit(solution)/shard_map/rgjd,rgpd->rgjp/dot_general | solution.py:37
  2.0 0.0 copy-start.7
  2.0 0.0 copy-start.11
  2.0 0.2 fusion.52
  2.2 0.5 %copy-done.7 = bf16[8,2,128]{2,1,0:T(2,128)(2,1)S(1)} copy-done((bf16[8,2,128]{2,1,0:T(2,128)(2,1)S(1)}, bf16[8,2,128]{2,1,0:T(2,128)(2,1)}, u32[]{:S(2)}) %copy-start.7) | copy-done | bytes 4120
  2.7 0.2 copy-done.11
  2.9 0.0 copy-start.4
  2.9 0.5 %fusion.23 = f32[8,2,16,128]{3,2,1,0:T(8,128)S(1)} fusion(bf16[8,2,1,128]{3,2,1,0:T(2,128)(2,1)S(1)} %copy.34, bf16[8,2,32,128]{3,2,1,0:T(8,128)(2,1)S(1)} %copy-done.11, f32[8,2,16]{2,1,0:T(2,128)S(1)} %fusion.52, f32[8,2,16,33]{3,2,1,0:T(8,128)S(1)} %fusion.8, pred[8,33]{1,0:T(8,128)(4,1)S(1)} %fusion.38), kind=kOutput, calls=%fused_computation.30 | convolution fusion | flops 2467104 | bytes 301320 | tf_op jit(solution)/shard_map/rgjp,rgpd->rgjd/dot_general | solution.py:47
  3.4 0.3 copy-done.4
  3.8 0.2 fusion.27
  4.0 0.5 %collective-permute-start = (f32[8]{0:T(128)S(1)}, f32[8]{0:T(128)S(1)}, u32[]{:S(2)}, u32[]{:S(2)}) collective-permute-start(f32[8]{0:T(128)S(1)} %get-tuple-element.9), channel_id=1, source_target_pairs={{0,1},{1,0},{2,3},{3,2},{4,5},{5,4},{6,7},{7,6},{8,9},{9,8},{10,11... | collective-permute-start | bytes 104 | tf_op jit(solution)/shard_map/ppermute | solution.py:18
  4.5 0.0 copy-start.5
  4.5 0.0 copy-start.6
  4.5 0.7 %copy-done.5 = s32[8,4]{0,1:T(4,128)S(1)} copy-done((s32[8,4]{0,1:T(4,128)S(1)}, s32[8,4]{0,1:T(4,128)}, u32[]{:S(2)}) %copy-start.5) | copy-done | bytes 152
  5.1 0.2 reduce_window_sum.11
  5.4 0.0 copy-done.6
  5.4 0.0 collective-permute-done
  5.4 0.1 fusion.29
  5.5 0.0 copy-start.9
  5.5 0.2 convolution_convert_fusion.1
  5.7 0.1 copy.36
  5.8 14.3 %all_to_all.10 = bf16[8,2,4096]{2,1,0:T(2,128)(2,1)S(1)} all-to-all(bf16[8,2,4096]{2,1,0:T(2,128)(2,1)S(1)} %copy.36), channel_id=1, replica_groups=mesh['groups'=2,'rows'=8,'heads'=2] {'rows'}, dimensions={0} | all-to-all | bytes 262144 | tf_op jit(solution)/shard_map/all_to_all | solution.py:127
  20.1 0.1 reshape.60
  20.1 0.1 collective-permute-start.2
  20.2 0.0 copy-start.10
  20.2 0.5 %collective-permute-start.1 = (bf16[8,4096]{1,0:T(8,128)(2,1)S(1)}, bf16[8,4096]{1,0:T(8,128)(2,1)S(1)}, u32[]{:S(2)}, u32[]{:S(2)}) collective-permute-start(bf16[8,4096]{1,0:T(8,128)(2,1)S(1)} %fusion.29), channel_id=1, source_target_pairs={{0,1},{1,0},{2,3},{3,2},{4,5},{5,4},{6,7},{7,6},{8,9},{9,8},{10,11... | collective-permute-start | bytes 196616 | tf_op jit(solution)/shard_map/ppermute | solution.py:18
  20.7 0.8 %collective-permute-done.2 = bf16[16,4096]{1,0:T(8,128)(2,1)S(1)} collective-permute-done((bf16[16,4096]{1,0:T(8,128)(2,1)S(1)}, bf16[16,4096]{1,0:T(8,128)(2,1)S(1)}, u32[]{:S(2)}, u32[]{:S(2)}) %collective-permute-start.2) | collective-permute-done | bytes 131104 | tf_op jit(solution)/shard_map/ppermute | solution.py:18
  21.6 0.0 copy-done.9
  21.6 0.2 fusion.35
  21.8 0.0 copy-done.10
  21.8 0.0 copy-start.3
  21.8 0.3 multiply_convert_fusion
  22.1 0.0 copy-start.1
  22.1 0.8 %copy-done.3 = bf16[32,8192]{1,0:T(8,128)(2,1)S(1)} copy-done((bf16[32,8192]{1,0:T(8,128)(2,1)S(1)}, bf16[32,8192]{1,0:T(8,128)(2,1)}, u32[]{:S(2)}) %copy-start.3) | copy-done | bytes 524312
  22.9 0.2 convolution_convert_fusion
  23.0 0.2 collective-permute-start.3
  23.2 0.0 collective-permute-done.1
  23.3 0.0 copy-start.2
  23.3 1.2 %collective-permute-done.3 = bf16[8,2,4096]{2,0,1:T(8,128)(2,1)S(1)} collective-permute-done((bf16[8,2,4096]{2,0,1:T(8,128)(2,1)S(1)}, bf16[8,2,4096]{2,0,1:T(8,128)(2,1)S(1)}, u32[]{:S(2)}, u32[]{:S(2)}) %collective-permute-start.3) | collective-permute-done | bytes 131104 | tf_op jit(solution)/shard_map/ppermute | solution.py:18
  24.4 0.2 add_convert_fusion
  24.6 0.8 %copy.39 = bf16[8,2,4096]{2,1,0:T(2,128)(2,1)} copy(bf16[8,2,4096]{2,0,1:T(8,128)(2,1)S(1)} %add_convert_fusion) | data formatting | bytes 262144 | tf_op jit(solution)/shard_map/optimization_barrier | solution.py:134
  25.4 3.4 %all-to-all-start.1 = ((bf16[8,2,4096]{2,1,0:T(2,128)(2,1)}), bf16[8,2,4096]{2,1,0:T(2,128)(2,1)S(1)}, u32[]{:S(2)}, u32[]{:S(2)}) async-start(bf16[8,2,4096]{2,1,0:T(2,128)(2,1)} %copy.39), calls=%async_computation.1 | async-start | bytes 262144 | tf_op jit(solution)/shard_map/all_to_all | solution.py:135
  28.8 0.0 copy-done.1
  28.8 0.4 fusion.53
  29.2 0.0 copy-done.2
  29.2 0.4 %fusion.9 = bf16[8,64]{1,0:T(8,128)(2,1)S(1)} fusion(bf16[8,8192]{1,0:T(8,128)(2,1)S(1)} %maximum_select_fusion.1, bf16[64,8192]{1,0:T(8,128)(2,1)S(1)} %copy-done.2, f32[8,64]{1,0:T(8,128)S(1)} %fusion.53), kind=kOutput, calls=%fused_computation.14 | convolution fusion | flops 8391680 | bytes 1182720 | tf_op jit(solution)/shard_map/rd,nd->rn/dot_general | solution.py:62
  29.6 0.0 copy-done
  29.6 0.2 fusion.10
  29.8 0.2 collective-permute-start.4
  30.0 6.3 %all-to-all-done.1 = bf16[8,2,4096]{2,1,0:T(2,128)(2,1)S(1)} async-done(((bf16[8,2,4096]{2,1,0:T(2,128)(2,1)}), bf16[8,2,4096]{2,1,0:T(2,128)(2,1)S(1)}, u32[]{:S(2)}, u32[]{:S(2)}) %all-to-all-start.1) | async-done | bytes 131104 | tf_op jit(solution)/shard_map/all_to_all | solution.py:135
  36.3 0.1 reshape.62
  36.4 0.3 fusion.54
  36.6 0.0 collective-permute-done.4
  36.6 0.8 %fusion.3 = bf16[8,4096]{1,0:T(8,128)(2,1)} fusion(f32[8,4096]{1,0:T(8,128)S(1)} %fusion.54, f32[8,4096]{1,0:T(8,128)S(1)} %collective-permute-done.4, bf16[8,64]{1,0:T(8,128)(2,1)S(1)} %fusion.9, bf16[64,8192]{1,0:T(8,128)(2,1)S(1)} %copy-done, s32[]{:T(128)S(6)} %select_n.39, bf16[8,4096]{1,0:T(8,128)(2,1)S(1)} %get-tuple-element.10), kind=kOutput, calls=%fused_computation.6 | convolution fusion | flops 4358144 | bytes 919556 | tf_op jit(solution)/shard_map/...n,nd->...d/dot_general | solution.py:69
  (10 shorter events, 0.1 us)
Async XLA Ops:
  0.0 29.6 %copy-start = (bf16[64,8192]{1,0:T(8,128)(2,1)S(1)}, bf16[64,8192]{1,0:T(8,128)(2,1)}, u32[]{:S(2)}) copy-start(bf16[64,8192]{1,0:T(8,128)(2,1)} %param.25) | copy-start | bytes 3145732
  0.0 0.8 %copy-start.8 = (s32[8]{0:T(128)S(1)}, s32[8]{0:T(128)}, u32[]{:S(2)}) copy-start(s32[8]{0:T(128)} %param.21) | copy-start | bytes 100
  2.0 0.7 %copy-start.7 = (bf16[8,2,128]{2,1,0:T(2,128)(2,1)S(1)}, bf16[8,2,128]{2,1,0:T(2,128)(2,1)}, u32[]{:S(2)}) copy-start(bf16[8,2,128]{2,1,0:T(2,128)(2,1)} %param.20) | copy-start | bytes 12292
  2.0 0.9 %copy-start.11 = (bf16[8,2,32,128]{3,2,1,0:T(8,128)(2,1)S(1)}, bf16[8,2,32,128]{3,2,1,0:T(8,128)(2,1)}, u32[]{:S(2)}) copy-start(bf16[8,2,32,128]{3,2,1,0:T(8,128)(2,1)} %param.18) | copy-start | bytes 393220
  2.9 0.8 %copy-start.4 = (bf16[8,4096]{1,0:T(8,128)(2,1)S(1)}, bf16[8,4096]{1,0:T(8,128)(2,1)}, u32[]{:S(2)}) copy-start(bf16[8,4096]{1,0:T(8,128)(2,1)} %param.15) | copy-start | bytes 196612
  4.0 1.4 %collective-permute-start = (f32[8]{0:T(128)S(1)}, f32[8]{0:T(128)S(1)}, u32[]{:S(2)}, u32[]{:S(2)}) collective-permute-start(f32[8]{0:T(128)S(1)} %get-tuple-element.9), channel_id=1, source_target_pairs={{0,1},{1,0},{2,3},{3,2},{4,5},{5,4},{6,7},{7,6},{8,9},{9,8},{10,11... | collective-permute-start | bytes 104 | tf_op jit(solution)/shard_map/ppermute | solution.py:18
  4.5 0.7 %copy-start.5 = (s32[8,4]{0,1:T(4,128)S(1)}, s32[8,4]{0,1:T(4,128)}, u32[]{:S(2)}) copy-start(s32[8,4]{0,1:T(4,128)} %param.29) | copy-start | bytes 388
  4.5 0.9 %copy-start.6 = (bf16[8192]{0:T(1024)(128)(2,1)S(1)}, bf16[8192]{0:T(1024)(128)(2,1)}, u32[]{:S(2)}) copy-start(bf16[8192]{0:T(1024)(128)(2,1)} %param.22) | copy-start | bytes 49156
  5.5 16.1 %copy-start.9 = (bf16[32,8192]{1,0:T(8,128)(2,1)S(1)}, bf16[32,8192]{1,0:T(8,128)(2,1)}, u32[]{:S(2)}) copy-start(bf16[32,8192]{1,0:T(8,128)(2,1)} %param.26) | copy-start | bytes 1572868
  20.1 1.4 %collective-permute-start.2 = (bf16[16,4096]{1,0:T(8,128)(2,1)S(1)}, bf16[16,4096]{1,0:T(8,128)(2,1)S(1)}, u32[]{:S(2)}, u32[]{:S(2)}) collective-permute-start(bf16[16,4096]{1,0:T(8,128)(2,1)S(1)} %reshape.60), channel_id=1, source_target_pairs={{0,1},{1,0},{2,3},{3,2},{4,5},{5,4},{6,7},{7,6},{8,9},{9,8},{10,11... | collective-permute-start | bytes 393224 | tf_op jit(solution)/shard_map/ppermute | solution.py:18
  20.2 1.6 %copy-start.10 = (bf16[32,8192]{1,0:T(8,128)(2,1)S(1)}, bf16[32,8192]{1,0:T(8,128)(2,1)}, u32[]{:S(2)}) copy-start(bf16[32,8192]{1,0:T(8,128)(2,1)} %param.27) | copy-start | bytes 1572868
  20.2 3.0 %collective-permute-start.1 = (bf16[8,4096]{1,0:T(8,128)(2,1)S(1)}, bf16[8,4096]{1,0:T(8,128)(2,1)S(1)}, u32[]{:S(2)}, u32[]{:S(2)}) collective-permute-start(bf16[8,4096]{1,0:T(8,128)(2,1)S(1)} %fusion.29), channel_id=1, source_target_pairs={{0,1},{1,0},{2,3},{3,2},{4,5},{5,4},{6,7},{7,6},{8,9},{9,8},{10,11... | collective-permute-start | bytes 196616 | tf_op jit(solution)/shard_map/ppermute | solution.py:18
  21.8 1.1 %copy-start.3 = (bf16[32,8192]{1,0:T(8,128)(2,1)S(1)}, bf16[32,8192]{1,0:T(8,128)(2,1)}, u32[]{:S(2)}) copy-start(bf16[32,8192]{1,0:T(8,128)(2,1)} %param.28) | copy-start | bytes 1572868
  22.1 6.7 %copy-start.1 = (bf16[64,8192]{1,0:T(8,128)(2,1)S(1)}, bf16[64,8192]{1,0:T(8,128)(2,1)}, u32[]{:S(2)}) copy-start(bf16[64,8192]{1,0:T(8,128)(2,1)} %param.23) | copy-start | bytes 3145732
  23.0 1.4 %collective-permute-start.3 = (bf16[8,2,4096]{2,0,1:T(8,128)(2,1)S(1)}, bf16[8,2,4096]{2,0,1:T(8,128)(2,1)S(1)}, u32[]{:S(2)}, u32[]{:S(2)}) collective-permute-start(bf16[8,2,4096]{2,0,1:T(8,128)(2,1)S(1)} %convolution_convert_fusion), channel_id=1, source_target_pairs={{0,1},{1,0},{2,3},{3,2},{4,5},{5,4},{6,7},{7,6},{8,9},{9,8},{10,11... | collective-permute-start | bytes 393224 | tf_op jit(solution)/shard_map/ppermute | solution.py:18
  23.3 5.9 %copy-start.2 = (bf16[64,8192]{1,0:T(8,128)(2,1)S(1)}, bf16[64,8192]{1,0:T(8,128)(2,1)}, u32[]{:S(2)}) copy-start(bf16[64,8192]{1,0:T(8,128)(2,1)} %param.24) | copy-start | bytes 3145732
  25.4 10.9 %all-to-all-start.1 = ((bf16[8,2,4096]{2,1,0:T(2,128)(2,1)}), bf16[8,2,4096]{2,1,0:T(2,128)(2,1)S(1)}, u32[]{:S(2)}, u32[]{:S(2)}) async-start(bf16[8,2,4096]{2,1,0:T(2,128)(2,1)} %copy.39), calls=%async_computation.1 | async-start | bytes 262144 | tf_op jit(solution)/shard_map/all_to_all | solution.py:135
  29.8 6.9 %collective-permute-start.4 = (f32[8,4096]{1,0:T(8,128)S(1)}, f32[8,4096]{1,0:T(8,128)S(1)}, u32[]{:S(2)}, u32[]{:S(2)}) collective-permute-start(f32[8,4096]{1,0:T(8,128)S(1)} %fusion.10), channel_id=1, source_target_pairs={{0,1},{1,0},{2,3},{3,2},{4,5},{5,4},{6,7},{7,6},{8,9},{9,8},{10,11... | collective-permute-start | bytes 393224 | tf_op jit(solution)/shard_map/ppermute | solution.py:18

commit v13 on v8

--- a/solution.py
+++ b/solution.py
@@ -31,13 +31,18 @@
     slots = key_cache.shape[2]
     scale_factor = 1.0 / HD**0.5
     queries = query.reshape(count, kv_local, -1, HD)
-    keys_all = jnp.concatenate([key_cache, key_new[:, :, None, :]], axis=2)
-    values_all = jnp.concatenate([value_cache, value_new[:, :, None, :]], axis=2)
+    copies = (count, kv_local, 8, HD)
+    keys_all = jnp.concatenate(
+        [key_cache, jnp.broadcast_to(key_new[:, :, None, :], copies)], axis=2
+    )
+    values_all = jnp.concatenate(
+        [value_cache, jnp.broadcast_to(value_new[:, :, None, :], copies)], axis=2
+    )
     scores = (
         jnp.einsum("rgjd,rgpd->rgjp", queries, keys_all, preferred_element_type=jnp.float32)
         * scale_factor
     )
-    positions = jnp.arange(slots + 1, dtype=jnp.int32)[None, :]
+    positions = jnp.arange(slots + 8, dtype=jnp.int32)[None, :]
     visible = ((positions < lengths[:, None]) | (positions == slots))[:, None, None, :]
     scores = jnp.where(visible, scores, -1e30)
     highest = jnp.max(scores, axis=-1)

time: 37.9 us -> 37.9 us (level)
  no operation moved by 1% of the time
where the time goes in v13:
time: 37.9 us; the launch traced here: 37.5 us
  blocking collectives  14.3 us (38%)
  waiting for transfers between devices  8.33 us (22%)
  matrix products  4.88 us (13%)
  starting transfers between devices  4.84 us (13%)
  local copies, waits for them, and re-layouts  4.33 us (11%)
  other arithmetic  0.6 us (2%)
    all_to_all x1, blocking collectives, local(): lax.all_to_all(outgoing, 'rows', split_axis=0, concat_axis=0, tiled=True)  14.3 us
    all_to_all x1, waiting for transfers between devices, local(): lax.all_to_all(owner_sum, 'rows', split_axis=0, concat_axis=0, tiled=True)  6.34 us
    all_to_all x1, starting transfers between devices, local(): lax.all_to_all(owner_sum, 'rows', split_axis=0, concat_axis=0, tiled=True)  3.37 us
    unnamed x28, local copies, waits for them, and re-layouts  2.59 us
    ppermute x5, waiting for transfers between devices, partner(): return lax.ppermute(block, axis, route)  1.99 us
    ppermute x5, starting transfers between devices, partner(): return lax.ppermute(block, axis, route)  1.47 us
    sub x1, matrix products, attention_rows(): expons = jnp.where(visible, jnp.exp(scores - highest[..., None]), 0.0)  1.34 us
    dot_general x2, matrix products, swiglu_halves(): jnp.einsum('...n,nd->...d', hidden, down_kept, preferred_element_type=jnp...  0.99 us
  transfers between devices with their start and end apart: 6, of which 3 were waited for; matrix products, arithmetic and copies ran while one was open for 6% of the time, Pallas kernels for 0%

profile of v13, /device:TPU:0, one launch (start us, length us, event | category | flops | bytes accessed | tf_op | source)
XLA Modules:
  0.0 37.5 jit_solution(15426144467263866488)
XLA Ops:
  0.0 0.0 copy-start
  0.0 0.0 copy-start.8
  0.0 0.7 %copy-done.8 = s32[8]{0:T(128)S(1)} copy-done((s32[8]{0:T(128)S(1)}, s32[8]{0:T(128)}, u32[]{:S(2)}) %copy-start.8) | copy-done | bytes 56
  0.7 0.1 fusion.50
  0.8 0.7 %broadcast_in_dim.49 = bf16[8,2,8,128]{3,2,1,0:T(8,128)(2,1)S(1)} broadcast(bf16[8,2,128]{2,1,0:T(2,128)(2,1)} %param.19), dimensions={0,1,3} | broadcast | bytes 36864 | tf_op jit(solution)/shard_map/broadcast_in_dim | solution.py:36
  1.5 0.0 copy-start.7
  1.5 0.0 copy-start.11
  1.5 0.0 copy-start.12
  1.5 0.0 copy-start.13
  1.5 1.3 %fusion.79 = f32[8,2,16]{2,1,0:T(2,128)S(1)} fusion(bf16[8,2,8,128]{3,2,1,0:T(8,128)(2,1)S(1)} %broadcast_in_dim.49, bf16[8,2,32,128]{3,2,1,0:T(8,128)(2,1)} %param.17, bf16[8,2,16,128]{3,0,2,1:T(8,128)(2,1)} %bitcast.54, pred[8,40]{1,0:T(8,128)(4,1)S(1)} %fusion.50), kind=kOutput, calls=%fused_computation.74 | convolution fusion | flops 3000359 | bytes 230720 | tf_op jit(solution)/shard_map/sub | solution.py:49
  2.9 0.0 copy-done.7
  2.9 0.0 copy-done.11
  2.9 0.0 copy-done.12
  2.9 0.0 copy-done.13
  3.0 0.0 copy-start.4
  3.0 0.5 %fusion.23 = f32[8,2,16,128]{3,2,1,0:T(8,128)S(1)} fusion(bf16[8,2,8,128]{3,2,1,0:T(8,128)(2,1)S(1)} %broadcast_in_dim.52, bf16[8,2,32,128]{3,2,1,0:T(8,128)(2,1)S(1)} %copy-done.11, f32[8,2,16]{2,1,0:T(2,128)S(1)} %fusion.79, pred[8,40]{1,0:T(8,128)(4,1)S(1)} %fusion.50, bf16[8,2,8,128]{3,2,1,0:T(8,128)(2,1)S(1)} %broadcast_in_dim.49, ...), kind=kOutput, calls=%fused_computation.30 | convolution fusion | flops 5959975 | bytes 525632 | tf_op jit(solution)/shard_map/rgjp,rgpd->rgjd/dot_general | solution.py:52
  3.5 0.3 copy-done.4
  3.8 0.2 fusion.27
  4.0 0.5 %collective-permute-start = (f32[8]{0:T(128)S(1)}, f32[8]{0:T(128)S(1)}, u32[]{:S(2)}, u32[]{:S(2)}) collective-permute-start(f32[8]{0:T(128)S(1)} %get-tuple-element.9), channel_id=1, source_target_pairs={{0,1},{1,0},{2,3},{3,2},{4,5},{5,4},{6,7},{7,6},{8,9},{9,8},{10,11... | collective-permute-start | bytes 104 | tf_op jit(solution)/shard_map/ppermute | solution.py:18
  4.5 0.0 copy-start.5
  4.5 0.0 copy-start.6
  4.5 0.7 %copy-done.5 = s32[8,4]{0,1:T(4,128)S(1)} copy-done((s32[8,4]{0,1:T(4,128)S(1)}, s32[8,4]{0,1:T(4,128)}, u32[]{:S(2)}) %copy-start.5) | copy-done | bytes 152
  5.2 0.2 reduce_window_sum.11
  5.4 0.0 copy-done.6
  5.4 0.0 collective-permute-done
  5.4 0.1 fusion.29
  5.5 0.0 copy-start.9
  5.6 0.2 convolution_convert_fusion.1
  5.7 0.1 copy.28
  5.9 14.3 %all_to_all.10 = bf16[8,2,4096]{2,1,0:T(2,128)(2,1)S(1)} all-to-all(bf16[8,2,4096]{2,1,0:T(2,128)(2,1)S(1)} %copy.28), channel_id=1, replica_groups=mesh['groups'=2,'rows'=8,'heads'=2] {'rows'}, dimensions={0} | all-to-all | bytes 262144 | tf_op jit(solution)/shard_map/all_to_all | solution.py:132
  20.1 0.1 reshape.62
  20.2 0.1 collective-permute-start.2
  20.3 0.0 copy-start.10
  20.3 0.5 %collective-permute-start.1 = (bf16[8,4096]{1,0:T(8,128)(2,1)S(1)}, bf16[8,4096]{1,0:T(8,128)(2,1)S(1)}, u32[]{:S(2)}, u32[]{:S(2)}) collective-permute-start(bf16[8,4096]{1,0:T(8,128)(2,1)S(1)} %fusion.29), channel_id=1, source_target_pairs={{0,1},{1,0},{2,3},{3,2},{4,5},{5,4},{6,7},{7,6},{8,9},{9,8},{10,11... | collective-permute-start | bytes 196616 | tf_op jit(solution)/shard_map/ppermute | solution.py:18
  20.8 0.8 %collective-permute-done.2 = bf16[16,4096]{1,0:T(8,128)(2,1)S(1)} collective-permute-done((bf16[16,4096]{1,0:T(8,128)(2,1)S(1)}, bf16[16,4096]{1,0:T(8,128)(2,1)S(1)}, u32[]{:S(2)}, u32[]{:S(2)}) %collective-permute-start.2) | collective-permute-done | bytes 131104 | tf_op jit(solution)/shard_map/ppermute | solution.py:18
  21.6 0.0 copy-done.9
  21.6 0.2 fusion.35
  21.8 0.0 copy-done.10
  21.8 0.0 copy-start.3
  21.8 0.3 multiply_convert_fusion
  22.1 0.0 copy-start.1
  22.1 0.8 %copy-done.3 = bf16[32,8192]{1,0:T(8,128)(2,1)S(1)} copy-done((bf16[32,8192]{1,0:T(8,128)(2,1)S(1)}, bf16[32,8192]{1,0:T(8,128)(2,1)}, u32[]{:S(2)}) %copy-start.3) | copy-done | bytes 524312
  22.9 0.2 convolution_convert_fusion
  23.1 0.2 collective-permute-start.3
  23.3 0.0 collective-permute-done.1
  23.3 0.0 copy-start.2
  23.3 1.2 %collective-permute-done.3 = bf16[8,2,4096]{2,0,1:T(8,128)(2,1)S(1)} collective-permute-done((bf16[8,2,4096]{2,0,1:T(8,128)(2,1)S(1)}, bf16[8,2,4096]{2,0,1:T(8,128)(2,1)S(1)}, u32[]{:S(2)}, u32[]{:S(2)}) %collective-permute-start.3) | collective-permute-done | bytes 131104 | tf_op jit(solution)/shard_map/ppermute | solution.py:18
  24.5 0.2 add_convert_fusion
  24.7 0.8 %copy.31 = bf16[8,2,4096]{2,1,0:T(2,128)(2,1)} copy(bf16[8,2,4096]{2,0,1:T(8,128)(2,1)S(1)} %add_convert_fusion) | data formatting | bytes 262144 | tf_op jit(solution)/shard_map/optimization_barrier | solution.py:139
  25.4 3.4 %all-to-all-start.1 = ((bf16[8,2,4096]{2,1,0:T(2,128)(2,1)}), bf16[8,2,4096]{2,1,0:T(2,128)(2,1)S(1)}, u32[]{:S(2)}, u32[]{:S(2)}) async-start(bf16[8,2,4096]{2,1,0:T(2,128)(2,1)} %copy.31), calls=%async_computation.1 | async-start | bytes 262144 | tf_op jit(solution)/shard_map/all_to_all | solution.py:140
  28.8 0.0 copy-done.1
  28.8 0.4 fusion.84
  29.2 0.0 copy-done.2
  29.2 0.4 %fusion.9 = bf16[8,64]{1,0:T(8,128)(2,1)S(1)} fusion(bf16[8,8192]{1,0:T(8,128)(2,1)S(1)} %maximum_select_fusion.1, bf16[64,8192]{1,0:T(8,128)(2,1)S(1)} %copy-done.2, f32[8,64]{1,0:T(8,128)S(1)} %fusion.84), kind=kOutput, calls=%fused_computation.14 | convolution fusion | flops 8391680 | bytes 1182720 | tf_op jit(solution)/shard_map/rd,nd->rn/dot_general | solution.py:67
  29.6 0.0 copy-done
  29.6 0.2 fusion.10
  29.8 0.2 collective-permute-start.4
  30.0 6.3 %all-to-all-done.1 = bf16[8,2,4096]{2,1,0:T(2,128)(2,1)S(1)} async-done(((bf16[8,2,4096]{2,1,0:T(2,128)(2,1)}), bf16[8,2,4096]{2,1,0:T(2,128)(2,1)S(1)}, u32[]{:S(2)}, u32[]{:S(2)}) %all-to-all-start.1) | async-done | bytes 131104 | tf_op jit(solution)/shard_map/all_to_all | solution.py:140
  36.3 0.1 reshape.64
  36.4 0.3 fusion.85
  36.7 0.0 collective-permute-done.4
  36.7 0.8 %fusion.3 = bf16[8,4096]{1,0:T(8,128)(2,1)} fusion(f32[8,4096]{1,0:T(8,128)S(1)} %fusion.85, f32[8,4096]{1,0:T(8,128)S(1)} %collective-permute-done.4, bf16[8,64]{1,0:T(8,128)(2,1)S(1)} %fusion.9, bf16[64,8192]{1,0:T(8,128)(2,1)S(1)} %copy-done, s32[]{:T(128)S(6)} %select_n.39, bf16[8,4096]{1,0:T(8,128)(2,1)S(1)} %get-tuple-element.10), kind=kOutput, calls=%fused_computation.6 | convolution fusion | flops 4358144 | bytes 919556 | tf_op jit(solution)/shard_map/...n,nd->...d/dot_general | solution.py:74
  (10 shorter events, 0.1 us)
Async XLA Ops:
  0.0 29.6 %copy-start = (bf16[64,8192]{1,0:T(8,128)(2,1)S(1)}, bf16[64,8192]{1,0:T(8,128)(2,1)}, u32[]{:S(2)}) copy-start(bf16[64,8192]{1,0:T(8,128)(2,1)} %param.25) | copy-start | bytes 3145732
  0.0 0.7 %copy-start.8 = (s32[8]{0:T(128)S(1)}, s32[8]{0:T(128)}, u32[]{:S(2)}) copy-start(s32[8]{0:T(128)} %param.21) | copy-start | bytes 100
  1.5 1.4 %copy-start.7 = (bf16[8,2,128]{2,1,0:T(2,128)(2,1)S(1)}, bf16[8,2,128]{2,1,0:T(2,128)(2,1)}, u32[]{:S(2)}) copy-start(bf16[8,2,128]{2,1,0:T(2,128)(2,1)} %param.20) | copy-start | bytes 12292
  1.5 1.4 %copy-start.11 = (bf16[8,2,32,128]{3,2,1,0:T(8,128)(2,1)S(1)}, bf16[8,2,32,128]{3,2,1,0:T(8,128)(2,1)}, u32[]{:S(2)}) copy-start(bf16[8,2,32,128]{3,2,1,0:T(8,128)(2,1)} %param.18) | copy-start | bytes 393220
  1.5 1.4 %copy-start.12 = (bf16[8,2,32,128]{3,2,1,0:T(8,128)(2,1)S(1)}, bf16[8,2,32,128]{3,2,1,0:T(8,128)(2,1)}, u32[]{:S(2)}) copy-start(bf16[8,2,32,128]{3,2,1,0:T(8,128)(2,1)} %param.17) | copy-start | bytes 393220
  1.5 1.4 %copy-start.13 = (bf16[8,4096]{1,0:T(8,128)(2,1)S(1)}, bf16[8,4096]{1,0:T(8,128)(2,1)}, u32[]{:S(2)}) copy-start(bf16[8,4096]{1,0:T(8,128)(2,1)} %param.16) | copy-start | bytes 196612
  3.0 0.8 %copy-start.4 = (bf16[8,4096]{1,0:T(8,128)(2,1)S(1)}, bf16[8,4096]{1,0:T(8,128)(2,1)}, u32[]{:S(2)}) copy-start(bf16[8,4096]{1,0:T(8,128)(2,1)} %param.15) | copy-start | bytes 196612
  4.0 1.4 %collective-permute-start = (f32[8]{0:T(128)S(1)}, f32[8]{0:T(128)S(1)}, u32[]{:S(2)}, u32[]{:S(2)}) collective-permute-start(f32[8]{0:T(128)S(1)} %get-tuple-element.9), channel_id=1, source_target_pairs={{0,1},{1,0},{2,3},{3,2},{4,5},{5,4},{6,7},{7,6},{8,9},{9,8},{10,11... | collective-permute-start | bytes 104 | tf_op jit(solution)/shard_map/ppermute | solution.py:18
  4.5 0.7 %copy-start.5 = (s32[8,4]{0,1:T(4,128)S(1)}, s32[8,4]{0,1:T(4,128)}, u32[]{:S(2)}) copy-start(s32[8,4]{0,1:T(4,128)} %param.29) | copy-start | bytes 388
  4.5 0.9 %copy-start.6 = (bf16[8192]{0:T(1024)(128)(2,1)S(1)}, bf16[8192]{0:T(1024)(128)(2,1)}, u32[]{:S(2)}) copy-start(bf16[8192]{0:T(1024)(128)(2,1)} %param.22) | copy-start | bytes 49156
  5.5 16.1 %copy-start.9 = (bf16[32,8192]{1,0:T(8,128)(2,1)S(1)}, bf16[32,8192]{1,0:T(8,128)(2,1)}, u32[]{:S(2)}) copy-start(bf16[32,8192]{1,0:T(8,128)(2,1)} %param.26) | copy-start | bytes 1572868
  20.2 1.4 %collective-permute-start.2 = (bf16[16,4096]{1,0:T(8,128)(2,1)S(1)}, bf16[16,4096]{1,0:T(8,128)(2,1)S(1)}, u32[]{:S(2)}, u32[]{:S(2)}) collective-permute-start(bf16[16,4096]{1,0:T(8,128)(2,1)S(1)} %reshape.62), channel_id=1, source_target_pairs={{0,1},{1,0},{2,3},{3,2},{4,5},{5,4},{6,7},{7,6},{8,9},{9,8},{10,11... | collective-permute-start | bytes 393224 | tf_op jit(solution)/shard_map/ppermute | solution.py:18
  20.3 1.6 %copy-start.10 = (bf16[32,8192]{1,0:T(8,128)(2,1)S(1)}, bf16[32,8192]{1,0:T(8,128)(2,1)}, u32[]{:S(2)}) copy-start(bf16[32,8192]{1,0:T(8,128)(2,1)} %param.27) | copy-start | bytes 1572868
  20.3 3.0 %collective-permute-start.1 = (bf16[8,4096]{1,0:T(8,128)(2,1)S(1)}, bf16[8,4096]{1,0:T(8,128)(2,1)S(1)}, u32[]{:S(2)}, u32[]{:S(2)}) collective-permute-start(bf16[8,4096]{1,0:T(8,128)(2,1)S(1)} %fusion.29), channel_id=1, source_target_pairs={{0,1},{1,0},{2,3},{3,2},{4,5},{5,4},{6,7},{7,6},{8,9},{9,8},{10,11... | collective-permute-start | bytes 196616 | tf_op jit(solution)/shard_map/ppermute | solution.py:18
  21.8 1.1 %copy-start.3 = (bf16[32,8192]{1,0:T(8,128)(2,1)S(1)}, bf16[32,8192]{1,0:T(8,128)(2,1)}, u32[]{:S(2)}) copy-start(bf16[32,8192]{1,0:T(8,128)(2,1)} %param.28) | copy-start | bytes 1572868
  22.1 6.7 %copy-start.1 = (bf16[64,8192]{1,0:T(8,128)(2,1)S(1)}, bf16[64,8192]{1,0:T(8,128)(2,1)}, u32[]{:S(2)}) copy-start(bf16[64,8192]{1,0:T(8,128)(2,1)} %param.23) | copy-start | bytes 3145732
  23.1 1.4 %collective-permute-start.3 = (bf16[8,2,4096]{2,0,1:T(8,128)(2,1)S(1)}, bf16[8,2,4096]{2,0,1:T(8,128)(2,1)S(1)}, u32[]{:S(2)}, u32[]{:S(2)}) collective-permute-start(bf16[8,2,4096]{2,0,1:T(8,128)(2,1)S(1)} %convolution_convert_fusion), channel_id=1, source_target_pairs={{0,1},{1,0},{2,3},{3,2},{4,5},{5,4},{6,7},{7,6},{8,9},{9,8},{10,11... | collective-permute-start | bytes 393224 | tf_op jit(solution)/shard_map/ppermute | solution.py:18
  23.3 5.9 %copy-start.2 = (bf16[64,8192]{1,0:T(8,128)(2,1)S(1)}, bf16[64,8192]{1,0:T(8,128)(2,1)}, u32[]{:S(2)}) copy-start(bf16[64,8192]{1,0:T(8,128)(2,1)} %param.24) | copy-start | bytes 3145732
  25.4 10.9 %all-to-all-start.1 = ((bf16[8,2,4096]{2,1,0:T(2,128)(2,1)}), bf16[8,2,4096]{2,1,0:T(2,128)(2,1)S(1)}, u32[]{:S(2)}, u32[]{:S(2)}) async-start(bf16[8,2,4096]{2,1,0:T(2,128)(2,1)} %copy.31), calls=%async_computation.1 | async-start | bytes 262144 | tf_op jit(solution)/shard_map/all_to_all | solution.py:140
  29.8 6.9 %collective-permute-start.4 = (f32[8,4096]{1,0:T(8,128)S(1)}, f32[8,4096]{1,0:T(8,128)S(1)}, u32[]{:S(2)}, u32[]{:S(2)}) collective-permute-start(f32[8,4096]{1,0:T(8,128)S(1)} %fusion.10), channel_id=1, source_target_pairs={{0,1},{1,0},{2,3},{3,2},{4,5},{5,4},{6,7},{7,6},{8,9},{9,8},{10,11... | collective-permute-start | bytes 393224 | tf_op jit(solution)/shard_map/ppermute | solution.py:18

commit v14 on v13

--- a/solution.py
+++ b/solution.py
@@ -38,7 +38,7 @@
     values_all = jnp.concatenate(
         [value_cache, jnp.broadcast_to(value_new[:, :, None, :], copies)], axis=2
     )
-    scores = (
+    scores = lax.optimization_barrier(
         jnp.einsum("rgjd,rgpd->rgjp", queries, keys_all, preferred_element_type=jnp.float32)
         * scale_factor
     )

time: 37.9 us -> 37.8 us (level)
    sub x1 -> x0, matrix products: 1.34 us -> none  [attention_rows(): expons = jnp.where(visible, jnp.exp(scores - highest[..., None]), 0.0)]
    dot_general x0 -> x1, matrix products: none -> 1.11 us  [attention_rows(): jnp.einsum('rgjd,rgpd->rgjp', queries, keys_all, preferred_element_type=j...]
    unnamed x28 -> x24, local copies, waits for them, and re-layouts: 2.59 us -> 2.44 us
where the time goes in v14:
time: 37.8 us; the launch traced here: 37.4 us
  blocking collectives  14.3 us (38%)
  waiting for transfers between devices  8.33 us (22%)
  starting transfers between devices  4.84 us (13%)
  matrix products  4.64 us (12%)
  local copies, waits for them, and re-layouts  4.27 us (11%)
  other arithmetic  0.82 us (2%)
    all_to_all x1, blocking collectives, local(): lax.all_to_all(outgoing, 'rows', split_axis=0, concat_axis=0, tiled=True)  14.3 us
    all_to_all x1, waiting for transfers between devices, local(): lax.all_to_all(owner_sum, 'rows', split_axis=0, concat_axis=0, tiled=True)  6.34 us
    all_to_all x1, starting transfers between devices, local(): lax.all_to_all(owner_sum, 'rows', split_axis=0, concat_axis=0, tiled=True)  3.37 us
    unnamed x24, local copies, waits for them, and re-layouts  2.44 us
    ppermute x5, waiting for transfers between devices, partner(): return lax.ppermute(block, axis, route)  1.99 us
    ppermute x5, starting transfers between devices, partner(): return lax.ppermute(block, axis, route)  1.47 us
    dot_general x1, matrix products, attention_rows(): jnp.einsum('rgjd,rgpd->rgjp', queries, keys_all, preferred_element_type=j...  1.11 us
    dot_general x2, matrix products, swiglu_halves(): jnp.einsum('...n,nd->...d', hidden, down_kept, preferred_element_type=jnp...  0.99 us
  transfers between devices with their start and end apart: 6, of which 3 were waited for; matrix products, arithmetic and copies ran while one was open for 6% of the time, Pallas kernels for 0%

profile of v14, /device:TPU:0, one launch (start us, length us, event | category | flops | bytes accessed | tf_op | source)
XLA Modules:
  0.0 37.4 jit_solution(8488803706264957918)
XLA Ops:
  0.0 0.0 copy-start
  0.0 0.8 %broadcast_in_dim.46 = bf16[8,2,8,128]{3,2,1,0:T(8,128)(2,1)S(1)} broadcast(bf16[8,2,128]{2,1,0:T(2,128)(2,1)} %param.19), dimensions={0,1,3} | broadcast | bytes 36864 | tf_op jit(solution)/shard_map/broadcast_in_dim | solution.py:36
  0.8 0.0 copy-start.8
  0.8 1.1 %fusion.7 = f32[8,2,16,40]{3,2,1,0:T(8,128)S(1)} fusion(bf16[8,2,8,128]{3,2,1,0:T(8,128)(2,1)S(1)} %broadcast_in_dim.46, bf16[8,2,32,128]{3,2,1,0:T(8,128)(2,1)} %param.17, bf16[8,2,16,128]{3,0,2,1:T(8,128)(2,1)} %bitcast.44), kind=kOutput, calls=%fused_computation.11 | convolution fusion | flops 2959360 | bytes 270336 | tf_op jit(solution)/shard_map/rgjd,rgpd->rgjp/dot_general | solution.py:42
  1.9 0.0 copy-done.8
  1.9 0.0 copy-start.11
  1.9 0.1 fusion.44
  2.0 0.0 copy-start.7
  2.0 0.2 fusion.61
  2.2 0.5 %copy-done.7 = bf16[8,2,128]{2,1,0:T(2,128)(2,1)S(1)} copy-done((bf16[8,2,128]{2,1,0:T(2,128)(2,1)S(1)}, bf16[8,2,128]{2,1,0:T(2,128)(2,1)}, u32[]{:S(2)}) %copy-start.7) | copy-done | bytes 4120
  2.7 0.1 copy-done.11
  2.8 0.0 copy-start.4
  2.8 0.5 %fusion.22 = f32[8,2,16,128]{3,2,1,0:T(8,128)S(1)} fusion(bf16[8,2,8,128]{3,2,1,0:T(8,128)(2,1)S(1)} %broadcast_in_dim.49, bf16[8,2,32,128]{3,2,1,0:T(8,128)(2,1)S(1)} %copy-done.11, f32[8,2,16]{2,1,0:T(2,128)S(1)} %fusion.61, f32[8,2,16,40]{3,2,1,0:T(8,128)S(1)} %fusion.7, pred[8,40]{1,0:T(8,128)(4,1)S(1)} %fusion.44), kind=kOutput, calls=%fused_computation.29 | convolution fusion | flops 3000615 | bytes 337216 | tf_op jit(solution)/shard_map/rgjp,rgpd->rgjd/dot_general | solution.py:52
  3.3 0.3 copy-done.4
  3.7 0.2 fusion.26
  3.9 0.5 %collective-permute-start = (f32[8]{0:T(128)S(1)}, f32[8]{0:T(128)S(1)}, u32[]{:S(2)}, u32[]{:S(2)}) collective-permute-start(f32[8]{0:T(128)S(1)} %get-tuple-element.9), channel_id=1, source_target_pairs={{0,1},{1,0},{2,3},{3,2},{4,5},{5,4},{6,7},{7,6},{8,9},{9,8},{10,11... | collective-permute-start | bytes 104 | tf_op jit(solution)/shard_map/ppermute | solution.py:18
  4.4 0.0 copy-start.5
  4.4 0.0 copy-start.6
  4.4 0.7 %copy-done.5 = s32[8,4]{0,1:T(4,128)S(1)} copy-done((s32[8,4]{0,1:T(4,128)S(1)}, s32[8,4]{0,1:T(4,128)}, u32[]{:S(2)}) %copy-start.5) | copy-done | bytes 152
  5.1 0.2 reduce_window_sum.11
  5.3 0.0 copy-done.6
  5.3 0.0 collective-permute-done
  5.3 0.1 fusion.28
  5.4 0.0 copy-start.9
  5.4 0.2 convolution_convert_fusion.1
  5.6 0.1 copy.28
  5.7 14.3 %all_to_all.10 = bf16[8,2,4096]{2,1,0:T(2,128)(2,1)S(1)} all-to-all(bf16[8,2,4096]{2,1,0:T(2,128)(2,1)S(1)} %copy.28), channel_id=1, replica_groups=mesh['groups'=2,'rows'=8,'heads'=2] {'rows'}, dimensions={0} | all-to-all | bytes 262144 | tf_op jit(solution)/shard_map/all_to_all | solution.py:132
  20.0 0.1 reshape.62
  20.0 0.1 collective-permute-start.2
  20.1 0.0 copy-start.10
  20.1 0.5 %collective-permute-start.1 = (bf16[8,4096]{1,0:T(8,128)(2,1)S(1)}, bf16[8,4096]{1,0:T(8,128)(2,1)S(1)}, u32[]{:S(2)}, u32[]{:S(2)}) collective-permute-start(bf16[8,4096]{1,0:T(8,128)(2,1)S(1)} %fusion.28), channel_id=1, source_target_pairs={{0,1},{1,0},{2,3},{3,2},{4,5},{5,4},{6,7},{7,6},{8,9},{9,8},{10,11... | collective-permute-start | bytes 196616 | tf_op jit(solution)/shard_map/ppermute | solution.py:18
  20.6 0.8 %collective-permute-done.2 = bf16[16,4096]{1,0:T(8,128)(2,1)S(1)} collective-permute-done((bf16[16,4096]{1,0:T(8,128)(2,1)S(1)}, bf16[16,4096]{1,0:T(8,128)(2,1)S(1)}, u32[]{:S(2)}, u32[]{:S(2)}) %collective-permute-start.2) | collective-permute-done | bytes 131104 | tf_op jit(solution)/shard_map/ppermute | solution.py:18
  21.5 0.0 copy-done.9
  21.5 0.2 fusion.37
  21.7 0.0 copy-done.10
  21.7 0.0 copy-start.3
  21.7 0.3 multiply_convert_fusion
  22.0 0.0 copy-start.1
  22.0 0.8 %copy-done.3 = bf16[32,8192]{1,0:T(8,128)(2,1)S(1)} copy-done((bf16[32,8192]{1,0:T(8,128)(2,1)S(1)}, bf16[32,8192]{1,0:T(8,128)(2,1)}, u32[]{:S(2)}) %copy-start.3) | copy-done | bytes 524312
  22.8 0.2 convolution_convert_fusion
  22.9 0.2 collective-permute-start.3
  23.2 0.0 collective-permute-done.1
  23.2 0.0 copy-start.2
  23.2 1.2 %collective-permute-done.3 = bf16[8,2,4096]{2,0,1:T(8,128)(2,1)S(1)} collective-permute-done((bf16[8,2,4096]{2,0,1:T(8,128)(2,1)S(1)}, bf16[8,2,4096]{2,0,1:T(8,128)(2,1)S(1)}, u32[]{:S(2)}, u32[]{:S(2)}) %collective-permute-start.3) | collective-permute-done | bytes 131104 | tf_op jit(solution)/shard_map/ppermute | solution.py:18
  24.4 0.2 add_convert_fusion
  24.5 0.8 %copy.31 = bf16[8,2,4096]{2,1,0:T(2,128)(2,1)} copy(bf16[8,2,4096]{2,0,1:T(8,128)(2,1)S(1)} %add_convert_fusion) | data formatting | bytes 262144 | tf_op jit(solution)/shard_map/optimization_barrier | solution.py:139
  25.3 3.4 %all-to-all-start.1 = ((bf16[8,2,4096]{2,1,0:T(2,128)(2,1)}), bf16[8,2,4096]{2,1,0:T(2,128)(2,1)S(1)}, u32[]{:S(2)}, u32[]{:S(2)}) async-start(bf16[8,2,4096]{2,1,0:T(2,128)(2,1)} %copy.31), calls=%async_computation.1 | async-start | bytes 262144 | tf_op jit(solution)/shard_map/all_to_all | solution.py:140
  28.7 0.0 copy-done.1
  28.7 0.4 fusion.62
  29.1 0.0 copy-done.2
  29.1 0.4 %fusion.8 = bf16[8,64]{1,0:T(8,128)(2,1)S(1)} fusion(bf16[8,8192]{1,0:T(8,128)(2,1)S(1)} %maximum_select_fusion.1, bf16[64,8192]{1,0:T(8,128)(2,1)S(1)} %copy-done.2, f32[8,64]{1,0:T(8,128)S(1)} %fusion.62), kind=kOutput, calls=%fused_computation.13 | convolution fusion | flops 8391680 | bytes 1182720 | tf_op jit(solution)/shard_map/rd,nd->rn/dot_general | solution.py:67
  29.5 0.0 copy-done
  29.5 0.2 fusion.9
  29.7 0.2 collective-permute-start.4
  29.9 6.3 %all-to-all-done.1 = bf16[8,2,4096]{2,1,0:T(2,128)(2,1)S(1)} async-done(((bf16[8,2,4096]{2,1,0:T(2,128)(2,1)}), bf16[8,2,4096]{2,1,0:T(2,128)(2,1)S(1)}, u32[]{:S(2)}, u32[]{:S(2)}) %all-to-all-start.1) | async-done | bytes 131104 | tf_op jit(solution)/shard_map/all_to_all | solution.py:140
  36.2 0.1 reshape.64
  36.3 0.3 fusion.63
  36.5 0.0 collective-permute-done.4
  36.5 0.8 %fusion.3 = bf16[8,4096]{1,0:T(8,128)(2,1)} fusion(f32[8,4096]{1,0:T(8,128)S(1)} %fusion.63, f32[8,4096]{1,0:T(8,128)S(1)} %collective-permute-done.4, bf16[8,64]{1,0:T(8,128)(2,1)S(1)} %fusion.8, bf16[64,8192]{1,0:T(8,128)(2,1)S(1)} %copy-done, s32[]{:T(128)S(6)} %select_n.35, bf16[8,4096]{1,0:T(8,128)(2,1)S(1)} %get-tuple-element.10), kind=kOutput, calls=%fused_computation.6 | convolution fusion | flops 4358144 | bytes 919556 | tf_op jit(solution)/shard_map/...n,nd->...d/dot_general | solution.py:74
  (10 shorter events, 0.1 us)
Async XLA Ops:
  0.0 29.5 %copy-start = (bf16[64,8192]{1,0:T(8,128)(2,1)S(1)}, bf16[64,8192]{1,0:T(8,128)(2,1)}, u32[]{:S(2)}) copy-start(bf16[64,8192]{1,0:T(8,128)(2,1)} %param.25) | copy-start | bytes 3145732
  0.8 1.1 %copy-start.8 = (s32[8]{0:T(128)S(1)}, s32[8]{0:T(128)}, u32[]{:S(2)}) copy-start(s32[8]{0:T(128)} %param.21) | copy-start | bytes 100
  1.9 0.9 %copy-start.11 = (bf16[8,2,32,128]{3,2,1,0:T(8,128)(2,1)S(1)}, bf16[8,2,32,128]{3,2,1,0:T(8,128)(2,1)}, u32[]{:S(2)}) copy-start(bf16[8,2,32,128]{3,2,1,0:T(8,128)(2,1)} %param.18) | copy-start | bytes 393220
  2.0 0.7 %copy-start.7 = (bf16[8,2,128]{2,1,0:T(2,128)(2,1)S(1)}, bf16[8,2,128]{2,1,0:T(2,128)(2,1)}, u32[]{:S(2)}) copy-start(bf16[8,2,128]{2,1,0:T(2,128)(2,1)} %param.20) | copy-start | bytes 12292
  2.8 0.8 %copy-start.4 = (bf16[8,4096]{1,0:T(8,128)(2,1)S(1)}, bf16[8,4096]{1,0:T(8,128)(2,1)}, u32[]{:S(2)}) copy-start(bf16[8,4096]{1,0:T(8,128)(2,1)} %param.15) | copy-start | bytes 196612
  3.9 1.4 %collective-permute-start = (f32[8]{0:T(128)S(1)}, f32[8]{0:T(128)S(1)}, u32[]{:S(2)}, u32[]{:S(2)}) collective-permute-start(f32[8]{0:T(128)S(1)} %get-tuple-element.9), channel_id=1, source_target_pairs={{0,1},{1,0},{2,3},{3,2},{4,5},{5,4},{6,7},{7,6},{8,9},{9,8},{10,11... | collective-permute-start | bytes 104 | tf_op jit(solution)/shard_map/ppermute | solution.py:18
  4.4 0.7 %copy-start.5 = (s32[8,4]{0,1:T(4,128)S(1)}, s32[8,4]{0,1:T(4,128)}, u32[]{:S(2)}) copy-start(s32[8,4]{0,1:T(4,128)} %param.29) | copy-start | bytes 388
  4.4 0.9 %copy-start.6 = (bf16[8192]{0:T(1024)(128)(2,1)S(1)}, bf16[8192]{0:T(1024)(128)(2,1)}, u32[]{:S(2)}) copy-start(bf16[8192]{0:T(1024)(128)(2,1)} %param.22) | copy-start | bytes 49156
  5.4 16.1 %copy-start.9 = (bf16[32,8192]{1,0:T(8,128)(2,1)S(1)}, bf16[32,8192]{1,0:T(8,128)(2,1)}, u32[]{:S(2)}) copy-start(bf16[32,8192]{1,0:T(8,128)(2,1)} %param.26) | copy-start | bytes 1572868
  20.0 1.4 %collective-permute-start.2 = (bf16[16,4096]{1,0:T(8,128)(2,1)S(1)}, bf16[16,4096]{1,0:T(8,128)(2,1)S(1)}, u32[]{:S(2)}, u32[]{:S(2)}) collective-permute-start(bf16[16,4096]{1,0:T(8,128)(2,1)S(1)} %reshape.62), channel_id=1, source_target_pairs={{0,1},{1,0},{2,3},{3,2},{4,5},{5,4},{6,7},{7,6},{8,9},{9,8},{10,11... | collective-permute-start | bytes 393224 | tf_op jit(solution)/shard_map/ppermute | solution.py:18
  20.1 1.6 %copy-start.10 = (bf16[32,8192]{1,0:T(8,128)(2,1)S(1)}, bf16[32,8192]{1,0:T(8,128)(2,1)}, u32[]{:S(2)}) copy-start(bf16[32,8192]{1,0:T(8,128)(2,1)} %param.27) | copy-start | bytes 1572868
  20.1 3.0 %collective-permute-start.1 = (bf16[8,4096]{1,0:T(8,128)(2,1)S(1)}, bf16[8,4096]{1,0:T(8,128)(2,1)S(1)}, u32[]{:S(2)}, u32[]{:S(2)}) collective-permute-start(bf16[8,4096]{1,0:T(8,128)(2,1)S(1)} %fusion.28), channel_id=1, source_target_pairs={{0,1},{1,0},{2,3},{3,2},{4,5},{5,4},{6,7},{7,6},{8,9},{9,8},{10,11... | collective-permute-start | bytes 196616 | tf_op jit(solution)/shard_map/ppermute | solution.py:18
  21.7 1.1 %copy-start.3 = (bf16[32,8192]{1,0:T(8,128)(2,1)S(1)}, bf16[32,8192]{1,0:T(8,128)(2,1)}, u32[]{:S(2)}) copy-start(bf16[32,8192]{1,0:T(8,128)(2,1)} %param.28) | copy-start | bytes 1572868
  22.0 6.7 %copy-start.1 = (bf16[64,8192]{1,0:T(8,128)(2,1)S(1)}, bf16[64,8192]{1,0:T(8,128)(2,1)}, u32[]{:S(2)}) copy-start(bf16[64,8192]{1,0:T(8,128)(2,1)} %param.23) | copy-start | bytes 3145732
  22.9 1.4 %collective-permute-start.3 = (bf16[8,2,4096]{2,0,1:T(8,128)(2,1)S(1)}, bf16[8,2,4096]{2,0,1:T(8,128)(2,1)S(1)}, u32[]{:S(2)}, u32[]{:S(2)}) collective-permute-start(bf16[8,2,4096]{2,0,1:T(8,128)(2,1)S(1)} %convolution_convert_fusion), channel_id=1, source_target_pairs={{0,1},{1,0},{2,3},{3,2},{4,5},{5,4},{6,7},{7,6},{8,9},{9,8},{10,11... | collective-permute-start | bytes 393224 | tf_op jit(solution)/shard_map/ppermute | solution.py:18
  23.2 5.9 %copy-start.2 = (bf16[64,8192]{1,0:T(8,128)(2,1)S(1)}, bf16[64,8192]{1,0:T(8,128)(2,1)}, u32[]{:S(2)}) copy-start(bf16[64,8192]{1,0:T(8,128)(2,1)} %param.24) | copy-start | bytes 3145732
  25.3 10.9 %all-to-all-start.1 = ((bf16[8,2,4096]{2,1,0:T(2,128)(2,1)}), bf16[8,2,4096]{2,1,0:T(2,128)(2,1)S(1)}, u32[]{:S(2)}, u32[]{:S(2)}) async-start(bf16[8,2,4096]{2,1,0:T(2,128)(2,1)} %copy.31), calls=%async_computation.1 | async-start | bytes 262144 | tf_op jit(solution)/shard_map/all_to_all | solution.py:140
  29.7 6.9 %collective-permute-start.4 = (f32[8,4096]{1,0:T(8,128)S(1)}, f32[8,4096]{1,0:T(8,128)S(1)}, u32[]{:S(2)}, u32[]{:S(2)}) collective-permute-start(f32[8,4096]{1,0:T(8,128)S(1)} %fusion.9), channel_id=1, source_target_pairs={{0,1},{1,0},{2,3},{3,2},{4,5},{5,4},{6,7},{7,6},{8,9},{9,8},{10,11... | collective-permute-start | bytes 393224 | tf_op jit(solution)/shard_map/ppermute | solution.py:18

commit v15 on v14

--- a/solution.py
+++ b/solution.py
@@ -31,13 +31,12 @@
     slots = key_cache.shape[2]
     scale_factor = 1.0 / HD**0.5
     queries = query.reshape(count, kv_local, -1, HD)
-    copies = (count, kv_local, 8, HD)
-    keys_all = jnp.concatenate(
-        [key_cache, jnp.broadcast_to(key_new[:, :, None, :], copies)], axis=2
+    news = jnp.stack([key_new, value_new])
+    news = lax.optimization_barrier(
+        jnp.broadcast_to(news[:, :, :, None, :], (2, count, kv_local, 8, HD))
     )
-    values_all = jnp.concatenate(
-        [value_cache, jnp.broadcast_to(value_new[:, :, None, :], copies)], axis=2
-    )
+    keys_all = jnp.concatenate([key_cache, news[0]], axis=2)
+    values_all = jnp.concatenate([value_cache, news[1]], axis=2)
     scores = lax.optimization_barrier(
         jnp.einsum("rgjd,rgpd->rgjp", queries, keys_all, preferred_element_type=jnp.float32)
         * scale_factor

time: 37.8 us -> 38.9 us (1.029)
  local copies, waits for them, and re-layouts: 4.27 us -> 5.54 us
  matrix products: 4.64 us -> 3.72 us
  other arithmetic: 0.82 us -> 1.52 us
    unnamed x24 -> x28, local copies, waits for them, and re-layouts: 2.44 us -> 4.49 us
    dot_general x1, matrix products: 1.11 us -> 0.19 us  [attention_rows(): jnp.einsum('rgjd,rgpd->rgjp', queries, keys_all, preferred_element_type=j...]
    broadcast_in_dim x2 -> x1, local copies, waits for them, and re-layouts: 0.79 us -> 0.01 us  [attention_rows(): jnp.broadcast_to(news[:, :, :, None, :], (2, count, kv_local, 8, HD))]
    another operation x0 -> x1, other arithmetic: none -> 0.7 us  [attention_rows(): news = jnp.stack([key_new, value_new])]
where the time goes in v15:
time: 38.9 us; the launch traced here: 38.4 us
  blocking collectives  14.3 us (37%)
  waiting for transfers between devices  8.33 us (21%)
  local copies, waits for them, and re-layouts  5.54 us (14%)
  starting transfers between devices  4.84 us (12%)
  matrix products  3.72 us (10%)
  other arithmetic  1.52 us (4%)
    all_to_all x1, blocking collectives, local(): lax.all_to_all(outgoing, 'rows', split_axis=0, concat_axis=0, tiled=True)  14.3 us
    all_to_all x1, waiting for transfers between devices, local(): lax.all_to_all(owner_sum, 'rows', split_axis=0, concat_axis=0, tiled=True)  6.34 us
    unnamed x28, local copies, waits for them, and re-layouts  4.49 us
    all_to_all x1, starting transfers between devices, local(): lax.all_to_all(owner_sum, 'rows', split_axis=0, concat_axis=0, tiled=True)  3.37 us
    ppermute x5, waiting for transfers between devices, partner(): return lax.ppermute(block, axis, route)  1.99 us
    ppermute x5, starting transfers between devices, partner(): return lax.ppermute(block, axis, route)  1.47 us
    dot_general x2, matrix products, swiglu_halves(): jnp.einsum('...n,nd->...d', hidden, down_kept, preferred_element_type=jnp...  0.99 us
    optimization_barrier x1, local copies, waits for them, and re-layouts, local(): normed_late, owner_sum = lax.optimization_barrier((normed, owner_sum))  0.78 us
  transfers between devices with their start and end apart: 6, of which 3 were waited for; matrix products, arithmetic and copies ran while one was open for 6% of the time, Pallas kernels for 0%

profile of v15, /device:TPU:0, one launch (start us, length us, event | category | flops | bytes accessed | tf_op | source)
XLA Modules:
  0.0 38.4 jit_solution(9739153855795032885)
XLA Ops:
  0.0 0.0 copy-start
  0.0 0.0 copy-start.7
  0.0 0.0 copy-start.11
  0.0 0.8 %copy-done.7 = bf16[8,2,128]{2,1,0:T(2,128)(2,1)S(1)} copy-done((bf16[8,2,128]{2,1,0:T(2,128)(2,1)S(1)}, bf16[8,2,128]{2,1,0:T(2,128)(2,1)}, u32[]{:S(2)}) %copy-start.7) | copy-done | bytes 4120
  0.8 0.7 %pad_maximum_fusion = bf16[2,8,2,128]{3,2,1,0:T(2,128)(2,1)S(1)} fusion(bf16[1,8,2,128]{3,2,1,0:T(2,128)(2,1)S(1)} %bitcast.50, bf16[1,8,2,128]{3,2,1,0:T(2,128)(2,1)} %bitcast.51), kind=kLoop, calls=%fused_computation.51 | loop fusion | flops 4096 | bytes 16384 | tf_op jit(solution)/shard_map/stack | solution.py:34
  1.5 0.0 copy-start.13
  1.5 0.0 copy-done.11
  1.5 0.8 %copy-done.13 = bf16[8,4096]{1,0:T(8,128)(2,1)S(1)} copy-done((bf16[8,4096]{1,0:T(8,128)(2,1)S(1)}, bf16[8,4096]{1,0:T(8,128)(2,1)}, u32[]{:S(2)}) %copy-start.13) | copy-done | bytes 65560
  2.3 0.0 copy-start.8
  2.3 0.2 fusion.7
  2.5 0.5 %copy-done.8 = s32[8]{0:T(128)S(1)} copy-done((s32[8]{0:T(128)S(1)}, s32[8]{0:T(128)}, u32[]{:S(2)}) %copy-start.8) | copy-done | bytes 56
  3.0 0.0 copy-start.12
  3.0 0.1 fusion.44
  3.1 0.2 fusion.61
  3.3 0.6 %copy-done.12 = bf16[8,2,32,128]{3,2,1,0:T(8,128)(2,1)S(1)} copy-done((bf16[8,2,32,128]{3,2,1,0:T(8,128)(2,1)S(1)}, bf16[8,2,32,128]{3,2,1,0:T(8,128)(2,1)}, u32[]{:S(2)}) %copy-start.12) | copy-done | bytes 131096
  3.9 0.0 copy-start.4
  3.9 0.5 %fusion.22 = f32[8,2,16,128]{3,2,1,0:T(8,128)S(1)} fusion(bf16[8,2,8,128]{3,2,1,0:T(8,128)(2,1)S(1)} %get-tuple-element.12, bf16[8,2,32,128]{3,2,1,0:T(8,128)(2,1)S(1)} %copy-done.12, f32[8,2,16]{2,1,0:T(2,128)S(1)} %fusion.61, f32[8,2,16,40]{3,2,1,0:T(8,128)S(1)} %fusion.7, pred[8,40]{1,0:T(8,128)(4,1)S(1)} %fusion.44), kind=kOutput, calls=%fused_computation.29 | convolution fusion | flops 3000615 | bytes 337216 | tf_op jit(solution)/shard_map/rgjp,rgpd->rgjd/dot_general | solution.py:51
  4.4 0.3 copy-done.4
  4.7 0.2 fusion.26
  4.9 0.5 %collective-permute-start = (f32[8]{0:T(128)S(1)}, f32[8]{0:T(128)S(1)}, u32[]{:S(2)}, u32[]{:S(2)}) collective-permute-start(f32[8]{0:T(128)S(1)} %get-tuple-element.9), channel_id=1, source_target_pairs={{0,1},{1,0},{2,3},{3,2},{4,5},{5,4},{6,7},{7,6},{8,9},{9,8},{10,11... | collective-permute-start | bytes 104 | tf_op jit(solution)/shard_map/ppermute | solution.py:18
  5.5 0.0 copy-start.5
  5.5 0.0 copy-start.6
  5.5 0.7 %copy-done.5 = s32[8,4]{0,1:T(4,128)S(1)} copy-done((s32[8,4]{0,1:T(4,128)S(1)}, s32[8,4]{0,1:T(4,128)}, u32[]{:S(2)}) %copy-start.5) | copy-done | bytes 152
  6.1 0.2 reduce_window_sum.11
  6.3 0.0 copy-done.6
  6.4 0.0 collective-permute-done
  6.4 0.1 fusion.28
  6.5 0.0 copy-start.9
  6.5 0.2 convolution_convert_fusion.1
  6.7 0.1 copy.28
  6.8 14.3 %all_to_all.10 = bf16[8,2,4096]{2,1,0:T(2,128)(2,1)S(1)} all-to-all(bf16[8,2,4096]{2,1,0:T(2,128)(2,1)S(1)} %copy.28), channel_id=1, replica_groups=mesh['groups'=2,'rows'=8,'heads'=2] {'rows'}, dimensions={0} | all-to-all | bytes 262144 | tf_op jit(solution)/shard_map/all_to_all | solution.py:131
  21.1 0.1 reshape.61
  21.1 0.1 collective-permute-start.2
  21.2 0.0 copy-start.10
  21.2 0.5 %collective-permute-start.1 = (bf16[8,4096]{1,0:T(8,128)(2,1)S(1)}, bf16[8,4096]{1,0:T(8,128)(2,1)S(1)}, u32[]{:S(2)}, u32[]{:S(2)}) collective-permute-start(bf16[8,4096]{1,0:T(8,128)(2,1)S(1)} %fusion.28), channel_id=1, source_target_pairs={{0,1},{1,0},{2,3},{3,2},{4,5},{5,4},{6,7},{7,6},{8,9},{9,8},{10,11... | collective-permute-start | bytes 196616 | tf_op jit(solution)/shard_map/ppermute | solution.py:18
  21.7 0.8 %collective-permute-done.2 = bf16[16,4096]{1,0:T(8,128)(2,1)S(1)} collective-permute-done((bf16[16,4096]{1,0:T(8,128)(2,1)S(1)}, bf16[16,4096]{1,0:T(8,128)(2,1)S(1)}, u32[]{:S(2)}, u32[]{:S(2)}) %collective-permute-start.2) | collective-permute-done | bytes 131104 | tf_op jit(solution)/shard_map/ppermute | solution.py:18
  22.5 0.0 copy-done.9
  22.5 0.2 fusion.37
  22.8 0.0 copy-done.10
  22.8 0.0 copy-start.3
  22.8 0.3 multiply_convert_fusion
  23.1 0.0 copy-start.1
  23.1 0.8 %copy-done.3 = bf16[32,8192]{1,0:T(8,128)(2,1)S(1)} copy-done((bf16[32,8192]{1,0:T(8,128)(2,1)S(1)}, bf16[32,8192]{1,0:T(8,128)(2,1)}, u32[]{:S(2)}) %copy-start.3) | copy-done | bytes 524312
  23.8 0.2 convolution_convert_fusion
  24.0 0.2 collective-permute-start.3
  24.2 0.0 collective-permute-done.1
  24.3 0.0 copy-start.2
  24.3 1.2 %collective-permute-done.3 = bf16[8,2,4096]{2,0,1:T(8,128)(2,1)S(1)} collective-permute-done((bf16[8,2,4096]{2,0,1:T(8,128)(2,1)S(1)}, bf16[8,2,4096]{2,0,1:T(8,128)(2,1)S(1)}, u32[]{:S(2)}, u32[]{:S(2)}) %collective-permute-start.3) | collective-permute-done | bytes 131104 | tf_op jit(solution)/shard_map/ppermute | solution.py:18
  25.4 0.2 add_convert_fusion
  25.6 0.8 %copy.31 = bf16[8,2,4096]{2,1,0:T(2,128)(2,1)} copy(bf16[8,2,4096]{2,0,1:T(8,128)(2,1)S(1)} %add_convert_fusion) | data formatting | bytes 262144 | tf_op jit(solution)/shard_map/optimization_barrier | solution.py:138
  26.4 3.4 %all-to-all-start.1 = ((bf16[8,2,4096]{2,1,0:T(2,128)(2,1)}), bf16[8,2,4096]{2,1,0:T(2,128)(2,1)S(1)}, u32[]{:S(2)}, u32[]{:S(2)}) async-start(bf16[8,2,4096]{2,1,0:T(2,128)(2,1)} %copy.31), calls=%async_computation.1 | async-start | bytes 262144 | tf_op jit(solution)/shard_map/all_to_all | solution.py:139
  29.8 0.0 copy-done.1
  29.8 0.4 fusion.62
  30.1 0.0 copy-done.2
  30.1 0.4 %fusion.8 = bf16[8,64]{1,0:T(8,128)(2,1)S(1)} fusion(bf16[8,8192]{1,0:T(8,128)(2,1)S(1)} %maximum_select_fusion.1, bf16[64,8192]{1,0:T(8,128)(2,1)S(1)} %copy-done.2, f32[8,64]{1,0:T(8,128)S(1)} %fusion.62), kind=kOutput, calls=%fused_computation.13 | convolution fusion | flops 8391680 | bytes 1182720 | tf_op jit(solution)/shard_map/rd,nd->rn/dot_general | solution.py:66
  30.5 0.0 copy-done
  30.5 0.2 fusion.9
  30.7 0.2 collective-permute-start.4
  30.9 6.3 %all-to-all-done.1 = bf16[8,2,4096]{2,1,0:T(2,128)(2,1)S(1)} async-done(((bf16[8,2,4096]{2,1,0:T(2,128)(2,1)}), bf16[8,2,4096]{2,1,0:T(2,128)(2,1)S(1)}, u32[]{:S(2)}, u32[]{:S(2)}) %all-to-all-start.1) | async-done | bytes 131104 | tf_op jit(solution)/shard_map/all_to_all | solution.py:139
  37.3 0.1 reshape.63
  37.3 0.3 fusion.63
  37.6 0.0 collective-permute-done.4
  37.6 0.8 %fusion.3 = bf16[8,4096]{1,0:T(8,128)(2,1)} fusion(f32[8,4096]{1,0:T(8,128)S(1)} %fusion.63, f32[8,4096]{1,0:T(8,128)S(1)} %collective-permute-done.4, bf16[8,64]{1,0:T(8,128)(2,1)S(1)} %fusion.8, bf16[64,8192]{1,0:T(8,128)(2,1)S(1)} %copy-done, s32[]{:T(128)S(6)} %select_n.35, bf16[8,4096]{1,0:T(8,128)(2,1)S(1)} %get-tuple-element.10), kind=kOutput, calls=%fused_computation.6 | convolution fusion | flops 4358144 | bytes 919556 | tf_op jit(solution)/shard_map/...n,nd->...d/dot_general | solution.py:73
  (11 shorter events, 0.1 us)
Async XLA Ops:
  0.0 30.5 %copy-start = (bf16[64,8192]{1,0:T(8,128)(2,1)S(1)}, bf16[64,8192]{1,0:T(8,128)(2,1)}, u32[]{:S(2)}) copy-start(bf16[64,8192]{1,0:T(8,128)(2,1)} %param.25) | copy-start | bytes 3145732
  0.0 0.8 %copy-start.7 = (bf16[8,2,128]{2,1,0:T(2,128)(2,1)S(1)}, bf16[8,2,128]{2,1,0:T(2,128)(2,1)}, u32[]{:S(2)}) copy-start(bf16[8,2,128]{2,1,0:T(2,128)(2,1)} %param.20) | copy-start | bytes 12292
  0.0 1.5 %copy-start.11 = (bf16[8,2,32,128]{3,2,1,0:T(8,128)(2,1)S(1)}, bf16[8,2,32,128]{3,2,1,0:T(8,128)(2,1)}, u32[]{:S(2)}) copy-start(bf16[8,2,32,128]{3,2,1,0:T(8,128)(2,1)} %param.17) | copy-start | bytes 393220
  1.5 0.8 %copy-start.13 = (bf16[8,4096]{1,0:T(8,128)(2,1)S(1)}, bf16[8,4096]{1,0:T(8,128)(2,1)}, u32[]{:S(2)}) copy-start(bf16[8,4096]{1,0:T(8,128)(2,1)} %param.16) | copy-start | bytes 196612
  2.3 0.7 %copy-start.8 = (s32[8]{0:T(128)S(1)}, s32[8]{0:T(128)}, u32[]{:S(2)}) copy-start(s32[8]{0:T(128)} %param.21) | copy-start | bytes 100
  3.0 0.9 %copy-start.12 = (bf16[8,2,32,128]{3,2,1,0:T(8,128)(2,1)S(1)}, bf16[8,2,32,128]{3,2,1,0:T(8,128)(2,1)}, u32[]{:S(2)}) copy-start(bf16[8,2,32,128]{3,2,1,0:T(8,128)(2,1)} %param.18) | copy-start | bytes 393220
  3.9 0.8 %copy-start.4 = (bf16[8,4096]{1,0:T(8,128)(2,1)S(1)}, bf16[8,4096]{1,0:T(8,128)(2,1)}, u32[]{:S(2)}) copy-start(bf16[8,4096]{1,0:T(8,128)(2,1)} %param.15) | copy-start | bytes 196612
  4.9 1.4 %collective-permute-start = (f32[8]{0:T(128)S(1)}, f32[8]{0:T(128)S(1)}, u32[]{:S(2)}, u32[]{:S(2)}) collective-permute-start(f32[8]{0:T(128)S(1)} %get-tuple-element.9), channel_id=1, source_target_pairs={{0,1},{1,0},{2,3},{3,2},{4,5},{5,4},{6,7},{7,6},{8,9},{9,8},{10,11... | collective-permute-start | bytes 104 | tf_op jit(solution)/shard_map/ppermute | solution.py:18
  5.5 0.7 %copy-start.5 = (s32[8,4]{0,1:T(4,128)S(1)}, s32[8,4]{0,1:T(4,128)}, u32[]{:S(2)}) copy-start(s32[8,4]{0,1:T(4,128)} %param.29) | copy-start | bytes 388
  5.5 0.9 %copy-start.6 = (bf16[8192]{0:T(1024)(128)(2,1)S(1)}, bf16[8192]{0:T(1024)(128)(2,1)}, u32[]{:S(2)}) copy-start(bf16[8192]{0:T(1024)(128)(2,1)} %param.22) | copy-start | bytes 49156
  6.5 16.1 %copy-start.9 = (bf16[32,8192]{1,0:T(8,128)(2,1)S(1)}, bf16[32,8192]{1,0:T(8,128)(2,1)}, u32[]{:S(2)}) copy-start(bf16[32,8192]{1,0:T(8,128)(2,1)} %param.26) | copy-start | bytes 1572868
  21.1 1.4 %collective-permute-start.2 = (bf16[16,4096]{1,0:T(8,128)(2,1)S(1)}, bf16[16,4096]{1,0:T(8,128)(2,1)S(1)}, u32[]{:S(2)}, u32[]{:S(2)}) collective-permute-start(bf16[16,4096]{1,0:T(8,128)(2,1)S(1)} %reshape.61), channel_id=1, source_target_pairs={{0,1},{1,0},{2,3},{3,2},{4,5},{5,4},{6,7},{7,6},{8,9},{9,8},{10,11... | collective-permute-start | bytes 393224 | tf_op jit(solution)/shard_map/ppermute | solution.py:18
  21.2 1.6 %copy-start.10 = (bf16[32,8192]{1,0:T(8,128)(2,1)S(1)}, bf16[32,8192]{1,0:T(8,128)(2,1)}, u32[]{:S(2)}) copy-start(bf16[32,8192]{1,0:T(8,128)(2,1)} %param.27) | copy-start | bytes 1572868
  21.2 3.0 %collective-permute-start.1 = (bf16[8,4096]{1,0:T(8,128)(2,1)S(1)}, bf16[8,4096]{1,0:T(8,128)(2,1)S(1)}, u32[]{:S(2)}, u32[]{:S(2)}) collective-permute-start(bf16[8,4096]{1,0:T(8,128)(2,1)S(1)} %fusion.28), channel_id=1, source_target_pairs={{0,1},{1,0},{2,3},{3,2},{4,5},{5,4},{6,7},{7,6},{8,9},{9,8},{10,11... | collective-permute-start | bytes 196616 | tf_op jit(solution)/shard_map/ppermute | solution.py:18
  22.8 1.1 %copy-start.3 = (bf16[32,8192]{1,0:T(8,128)(2,1)S(1)}, bf16[32,8192]{1,0:T(8,128)(2,1)}, u32[]{:S(2)}) copy-start(bf16[32,8192]{1,0:T(8,128)(2,1)} %param.28) | copy-start | bytes 1572868
  23.1 6.7 %copy-start.1 = (bf16[64,8192]{1,0:T(8,128)(2,1)S(1)}, bf16[64,8192]{1,0:T(8,128)(2,1)}, u32[]{:S(2)}) copy-start(bf16[64,8192]{1,0:T(8,128)(2,1)} %param.23) | copy-start | bytes 3145732
  24.0 1.4 %collective-permute-start.3 = (bf16[8,2,4096]{2,0,1:T(8,128)(2,1)S(1)}, bf16[8,2,4096]{2,0,1:T(8,128)(2,1)S(1)}, u32[]{:S(2)}, u32[]{:S(2)}) collective-permute-start(bf16[8,2,4096]{2,0,1:T(8,128)(2,1)S(1)} %convolution_convert_fusion), channel_id=1, source_target_pairs={{0,1},{1,0},{2,3},{3,2},{4,5},{5,4},{6,7},{7,6},{8,9},{9,8},{10,11... | collective-permute-start | bytes 393224 | tf_op jit(solution)/shard_map/ppermute | solution.py:18
  24.3 5.9 %copy-start.2 = (bf16[64,8192]{1,0:T(8,128)(2,1)S(1)}, bf16[64,8192]{1,0:T(8,128)(2,1)}, u32[]{:S(2)}) copy-start(bf16[64,8192]{1,0:T(8,128)(2,1)} %param.24) | copy-start | bytes 3145732
  26.4 10.9 %all-to-all-start.1 = ((bf16[8,2,4096]{2,1,0:T(2,128)(2,1)}), bf16[8,2,4096]{2,1,0:T(2,128)(2,1)S(1)}, u32[]{:S(2)}, u32[]{:S(2)}) async-start(bf16[8,2,4096]{2,1,0:T(2,128)(2,1)} %copy.31), calls=%async_computation.1 | async-start | bytes 262144 | tf_op jit(solution)/shard_map/all_to_all | solution.py:139
  30.7 6.9 %collective-permute-start.4 = (f32[8,4096]{1,0:T(8,128)S(1)}, f32[8,4096]{1,0:T(8,128)S(1)}, u32[]{:S(2)}, u32[]{:S(2)}) collective-permute-start(f32[8,4096]{1,0:T(8,128)S(1)} %fusion.9), channel_id=1, source_target_pairs={{0,1},{1,0},{2,3},{3,2},{4,5},{5,4},{6,7},{7,6},{8,9},{9,8},{10,11... | collective-permute-start | bytes 393224 | tf_op jit(solution)/shard_map/ppermute | solution.py:18

commit v16 on v8

--- a/solution.py
+++ b/solution.py
@@ -136,12 +136,13 @@
     hot_kept, hot_given = swiglu_halves(
         normed_late, hot_gate, hot_up, hot_down, myself, (request_count,)
     )
-    hot_total = hot_kept + partner(hot_given, "heads", 0)
+    hot_received = partner(hot_given, "heads", 0)
+    settled = lax.optimization_barrier(stream.astype(jnp.float32) + hot_kept)
     cold_sum = collect_rows(
         selector.astype(jnp.float32),
         returned.reshape(owner_count * CAP, -1).astype(jnp.float32),
     )
-    result = stream.astype(jnp.float32) + hot_total + cold_sum
+    result = settled + hot_received + cold_sum
     return result.astype(jnp.bfloat16)
 
 

time: 37.9 us -> 37.7 us (level)
    dot_general x2, matrix products: 0.99 us -> 0.35 us  [swiglu_halves(): jnp.einsum('...n,nd->...d', hidden, down_kept, preferred_element_type=jnp...]
    dot_general x1, matrix products: 0.25 us -> 0.89 us  [collect_rows(): lax.dot_general(selector, returned, (((0,), (0,)), ((), ())), precision=l...]
where the time goes in v16:
time: 37.7 us; the launch traced here: 37.3 us
  blocking collectives  14.3 us (38%)
  waiting for transfers between devices  8.15 us (22%)
  matrix products  4.86 us (13%)
  starting transfers between devices  4.84 us (13%)
  local copies, waits for them, and re-layouts  4.33 us (11%)
  other arithmetic  0.6 us (2%)
    all_to_all x1, blocking collectives, local(): lax.all_to_all(outgoing, 'rows', split_axis=0, concat_axis=0, tiled=True)  14.3 us
    all_to_all x1, waiting for transfers between devices, local(): lax.all_to_all(owner_sum, 'rows', split_axis=0, concat_axis=0, tiled=True)  6.15 us
    all_to_all x1, starting transfers between devices, local(): lax.all_to_all(owner_sum, 'rows', split_axis=0, concat_axis=0, tiled=True)  3.37 us
    unnamed x28, local copies, waits for them, and re-layouts  2.48 us
    ppermute x5, waiting for transfers between devices, partner(): return lax.ppermute(block, axis, route)  1.99 us
    ppermute x5, starting transfers between devices, partner(): return lax.ppermute(block, axis, route)  1.47 us
    sub x1, matrix products, attention_rows(): expons = jnp.where(visible, jnp.exp(scores - highest[..., None]), 0.0)  1.33 us
    dot_general x1, matrix products, collect_rows(): lax.dot_general(selector, returned, (((0,), (0,)), ((), ())), precision=l...  0.89 us
  transfers between devices with their start and end apart: 6, of which 3 were waited for; matrix products, arithmetic and copies ran while one was open for 6% of the time, Pallas kernels for 0%

profile of v16, /device:TPU:0, one launch (start us, length us, event | category | flops | bytes accessed | tf_op | source)
XLA Modules:
  0.0 37.3 jit_solution(1290985684471123872)
XLA Ops:
  0.0 0.0 copy-start
  0.0 0.0 copy-start.7
  0.0 0.8 %copy.31 = bf16[8,2,1,128]{3,2,1,0:T(2,128)(2,1)S(1)} copy(bf16[8,2,1,128]{3,1,0,2:T(2,128)(2,1)} %bitcast.56) | data formatting | bytes 8192 | tf_op jit(solution)/shard_map/broadcast_in_dim | solution.py:34
  0.8 0.0 copy-done.7
  0.8 0.0 copy-start.8
  0.8 0.6 %copy-done.8 = s32[8]{0:T(128)S(1)} copy-done((s32[8]{0:T(128)S(1)}, s32[8]{0:T(128)}, u32[]{:S(2)}) %copy-start.8) | copy-done | bytes 56
  1.5 0.1 fusion.47
  1.5 0.0 copy-start.11
  1.5 0.0 copy-start.12
  1.5 0.0 copy-start.13
  1.6 1.3 %fusion.76 = f32[8,2,16]{2,1,0:T(2,128)S(1)} fusion(bf16[8,2,1,128]{3,2,1,0:T(2,128)(2,1)S(1)} %copy.31, bf16[8,2,32,128]{3,2,1,0:T(8,128)(2,1)} %param.17, bf16[8,2,16,128]{3,0,2,1:T(8,128)(2,1)} %bitcast.58, pred[8,33]{1,0:T(8,128)(4,1)S(1)} %fusion.47), kind=kOutput, calls=%fused_computation.72 | convolution fusion | flops 2475296 | bytes 201992 | tf_op jit(solution)/shard_map/sub | solution.py:44
  2.9 0.0 copy-done.11
  2.9 0.0 copy-done.12
  2.9 0.0 copy-done.13
  2.9 0.0 copy-start.4
  2.9 0.5 %fusion.20 = f32[8,2,16,128]{3,2,1,0:T(8,128)S(1)} fusion(bf16[8,2,1,128]{3,2,1,0:T(2,128)(2,1)S(1)} %copy.34, bf16[8,2,32,128]{3,2,1,0:T(8,128)(2,1)S(1)} %copy-done.11, f32[8,2,16]{2,1,0:T(2,128)S(1)} %fusion.76, pred[8,33]{1,0:T(8,128)(4,1)S(1)} %fusion.47, bf16[8,2,1,128]{3,2,1,0:T(2,128)(2,1)S(1)} %copy.31, bf16[8,2,32,128]{3,2,1,0:T(8,128)(2,1)S(1)} %copy-done.12, ...), kind=kOutput, calls=%fused_computation.27 | convolution fusion | flops 4917024 | bytes 468232 | tf_op jit(solution)/shard_map/rgjp,rgpd->rgjd/dot_general | solution.py:47
  3.4 0.3 copy-done.4
  3.8 0.2 fusion.24
  4.0 0.5 %collective-permute-start = (f32[8]{0:T(128)S(1)}, f32[8]{0:T(128)S(1)}, u32[]{:S(2)}, u32[]{:S(2)}) collective-permute-start(f32[8]{0:T(128)S(1)} %get-tuple-element.9), channel_id=1, source_target_pairs={{0,1},{1,0},{2,3},{3,2},{4,5},{5,4},{6,7},{7,6},{8,9},{9,8},{10,11... | collective-permute-start | bytes 104 | tf_op jit(solution)/shard_map/ppermute | solution.py:18
  4.5 0.0 copy-start.5
  4.5 0.0 copy-start.6
  4.5 0.7 %copy-done.5 = s32[8,4]{0,1:T(4,128)S(1)} copy-done((s32[8,4]{0,1:T(4,128)S(1)}, s32[8,4]{0,1:T(4,128)}, u32[]{:S(2)}) %copy-start.5) | copy-done | bytes 152
  5.2 0.2 reduce_window_sum.11
  5.4 0.0 copy-done.6
  5.4 0.0 collective-permute-done
  5.4 0.1 fusion.26
  5.5 0.0 copy-start.9
  5.5 0.2 convolution_convert_fusion.1
  5.7 0.1 copy.36
  5.8 14.3 %all_to_all.10 = bf16[8,2,4096]{2,1,0:T(2,128)(2,1)S(1)} all-to-all(bf16[8,2,4096]{2,1,0:T(2,128)(2,1)S(1)} %copy.36), channel_id=1, replica_groups=mesh['groups'=2,'rows'=8,'heads'=2] {'rows'}, dimensions={0} | all-to-all | bytes 262144 | tf_op jit(solution)/shard_map/all_to_all | solution.py:127
  20.1 0.1 reshape.60
  20.1 0.1 collective-permute-start.2
  20.2 0.0 copy-start.10
  20.2 0.5 %collective-permute-start.1 = (bf16[8,4096]{1,0:T(8,128)(2,1)S(1)}, bf16[8,4096]{1,0:T(8,128)(2,1)S(1)}, u32[]{:S(2)}, u32[]{:S(2)}) collective-permute-start(bf16[8,4096]{1,0:T(8,128)(2,1)S(1)} %fusion.26), channel_id=1, source_target_pairs={{0,1},{1,0},{2,3},{3,2},{4,5},{5,4},{6,7},{7,6},{8,9},{9,8},{10,11... | collective-permute-start | bytes 196616 | tf_op jit(solution)/shard_map/ppermute | solution.py:18
  20.7 0.8 %collective-permute-done.2 = bf16[16,4096]{1,0:T(8,128)(2,1)S(1)} collective-permute-done((bf16[16,4096]{1,0:T(8,128)(2,1)S(1)}, bf16[16,4096]{1,0:T(8,128)(2,1)S(1)}, u32[]{:S(2)}, u32[]{:S(2)}) %collective-permute-start.2) | collective-permute-done | bytes 131104 | tf_op jit(solution)/shard_map/ppermute | solution.py:18
  21.6 0.0 copy-done.9
  21.6 0.2 fusion.32
  21.8 0.0 copy-done.10
  21.8 0.0 copy-start.3
  21.8 0.3 multiply_convert_fusion
  22.1 0.0 copy-start.1
  22.1 0.8 %copy-done.3 = bf16[32,8192]{1,0:T(8,128)(2,1)S(1)} copy-done((bf16[32,8192]{1,0:T(8,128)(2,1)S(1)}, bf16[32,8192]{1,0:T(8,128)(2,1)}, u32[]{:S(2)}) %copy-start.3) | copy-done | bytes 524312
  22.9 0.2 convolution_convert_fusion
  23.0 0.2 collective-permute-start.3
  23.3 0.0 collective-permute-done.1
  23.3 0.0 copy-start.2
  23.3 1.2 %collective-permute-done.3 = bf16[8,2,4096]{2,0,1:T(8,128)(2,1)S(1)} collective-permute-done((bf16[8,2,4096]{2,0,1:T(8,128)(2,1)S(1)}, bf16[8,2,4096]{2,0,1:T(8,128)(2,1)S(1)}, u32[]{:S(2)}, u32[]{:S(2)}) %collective-permute-start.3) | collective-permute-done | bytes 131104 | tf_op jit(solution)/shard_map/ppermute | solution.py:18
  24.5 0.2 add_convert_fusion
  24.6 0.8 %copy.39 = bf16[8,2,4096]{2,1,0:T(2,128)(2,1)} copy(bf16[8,2,4096]{2,0,1:T(8,128)(2,1)S(1)} %add_convert_fusion) | data formatting | bytes 262144 | tf_op jit(solution)/shard_map/optimization_barrier | solution.py:134
  25.4 3.4 %all-to-all-start.1 = ((bf16[8,2,4096]{2,1,0:T(2,128)(2,1)}), bf16[8,2,4096]{2,1,0:T(2,128)(2,1)S(1)}, u32[]{:S(2)}, u32[]{:S(2)}) async-start(bf16[8,2,4096]{2,1,0:T(2,128)(2,1)} %copy.39), calls=%async_computation.1 | async-start | bytes 262144 | tf_op jit(solution)/shard_map/all_to_all | solution.py:135
  28.8 0.0 copy-done.1
  28.8 0.4 fusion.81
  29.2 0.0 copy-done.2
  29.2 0.4 %fusion.6 = bf16[8,64]{1,0:T(8,128)(2,1)S(1)} fusion(bf16[8,8192]{1,0:T(8,128)(2,1)S(1)} %maximum_select_fusion.1, bf16[64,8192]{1,0:T(8,128)(2,1)S(1)} %copy-done.2, f32[8,64]{1,0:T(8,128)S(1)} %fusion.81), kind=kOutput, calls=%fused_computation.11 | convolution fusion | flops 8391680 | bytes 1182720 | tf_op jit(solution)/shard_map/rd,nd->rn/dot_general | solution.py:62
  29.6 0.0 copy-done
  29.6 0.2 fusion.7
  29.8 0.2 collective-permute-start.4
  30.0 0.2 convolution_add_fusion
  30.1 6.2 %all-to-all-done.1 = bf16[8,2,4096]{2,1,0:T(2,128)(2,1)S(1)} async-done(((bf16[8,2,4096]{2,1,0:T(2,128)(2,1)}), bf16[8,2,4096]{2,1,0:T(2,128)(2,1)S(1)}, u32[]{:S(2)}, u32[]{:S(2)}) %all-to-all-start.1) | async-done | bytes 131104 | tf_op jit(solution)/shard_map/all_to_all | solution.py:135
  36.3 0.1 reshape.62
  36.4 0.0 collective-permute-done.4
  36.4 0.9 %add_convert_fusion.1 = bf16[8,4096]{1,0:T(8,128)(2,1)} fusion(f32[8,4096]{1,0:T(8,128)S(1)} %convolution_add_fusion, f32[8,4096]{1,0:T(8,128)S(1)} %collective-permute-done.4, f32[16,8]{1,0:T(8,128)S(1)} %bitcast.50, bf16[16,4096]{1,0:T(8,128)(2,1)S(1)} %reshape.62), kind=kOutput, calls=%fused_computation.37 | convolution fusion | flops 6389760 | bytes 459264 | tf_op jit(solution)/shard_map/dot_general | solution.py:74
  (10 shorter events, 0.1 us)
Async XLA Ops:
  0.0 29.6 %copy-start = (bf16[64,8192]{1,0:T(8,128)(2,1)S(1)}, bf16[64,8192]{1,0:T(8,128)(2,1)}, u32[]{:S(2)}) copy-start(bf16[64,8192]{1,0:T(8,128)(2,1)} %param.25) | copy-start | bytes 3145732
  0.0 0.8 %copy-start.7 = (bf16[8,2,128]{2,1,0:T(2,128)(2,1)S(1)}, bf16[8,2,128]{2,1,0:T(2,128)(2,1)}, u32[]{:S(2)}) copy-start(bf16[8,2,128]{2,1,0:T(2,128)(2,1)} %param.20) | copy-start | bytes 12292
  0.8 0.7 %copy-start.8 = (s32[8]{0:T(128)S(1)}, s32[8]{0:T(128)}, u32[]{:S(2)}) copy-start(s32[8]{0:T(128)} %param.21) | copy-start | bytes 100
  1.5 1.4 %copy-start.11 = (bf16[8,2,32,128]{3,2,1,0:T(8,128)(2,1)S(1)}, bf16[8,2,32,128]{3,2,1,0:T(8,128)(2,1)}, u32[]{:S(2)}) copy-start(bf16[8,2,32,128]{3,2,1,0:T(8,128)(2,1)} %param.18) | copy-start | bytes 393220
  1.5 1.4 %copy-start.12 = (bf16[8,2,32,128]{3,2,1,0:T(8,128)(2,1)S(1)}, bf16[8,2,32,128]{3,2,1,0:T(8,128)(2,1)}, u32[]{:S(2)}) copy-start(bf16[8,2,32,128]{3,2,1,0:T(8,128)(2,1)} %param.17) | copy-start | bytes 393220
  1.5 1.4 %copy-start.13 = (bf16[8,4096]{1,0:T(8,128)(2,1)S(1)}, bf16[8,4096]{1,0:T(8,128)(2,1)}, u32[]{:S(2)}) copy-start(bf16[8,4096]{1,0:T(8,128)(2,1)} %param.16) | copy-start | bytes 196612
  2.9 0.8 %copy-start.4 = (bf16[8,4096]{1,0:T(8,128)(2,1)S(1)}, bf16[8,4096]{1,0:T(8,128)(2,1)}, u32[]{:S(2)}) copy-start(bf16[8,4096]{1,0:T(8,128)(2,1)} %param.15) | copy-start | bytes 196612
  4.0 1.4 %collective-permute-start = (f32[8]{0:T(128)S(1)}, f32[8]{0:T(128)S(1)}, u32[]{:S(2)}, u32[]{:S(2)}) collective-permute-start(f32[8]{0:T(128)S(1)} %get-tuple-element.9), channel_id=1, source_target_pairs={{0,1},{1,0},{2,3},{3,2},{4,5},{5,4},{6,7},{7,6},{8,9},{9,8},{10,11... | collective-permute-start | bytes 104 | tf_op jit(solution)/shard_map/ppermute | solution.py:18
  4.5 0.7 %copy-start.5 = (s32[8,4]{0,1:T(4,128)S(1)}, s32[8,4]{0,1:T(4,128)}, u32[]{:S(2)}) copy-start(s32[8,4]{0,1:T(4,128)} %param.29) | copy-start | bytes 388
  4.5 0.9 %copy-start.6 = (bf16[8192]{0:T(1024)(128)(2,1)S(1)}, bf16[8192]{0:T(1024)(128)(2,1)}, u32[]{:S(2)}) copy-start(bf16[8192]{0:T(1024)(128)(2,1)} %param.22) | copy-start | bytes 49156
  5.5 16.1 %copy-start.9 = (bf16[32,8192]{1,0:T(8,128)(2,1)S(1)}, bf16[32,8192]{1,0:T(8,128)(2,1)}, u32[]{:S(2)}) copy-start(bf16[32,8192]{1,0:T(8,128)(2,1)} %param.26) | copy-start | bytes 1572868
  20.1 1.4 %collective-permute-start.2 = (bf16[16,4096]{1,0:T(8,128)(2,1)S(1)}, bf16[16,4096]{1,0:T(8,128)(2,1)S(1)}, u32[]{:S(2)}, u32[]{:S(2)}) collective-permute-start(bf16[16,4096]{1,0:T(8,128)(2,1)S(1)} %reshape.60), channel_id=1, source_target_pairs={{0,1},{1,0},{2,3},{3,2},{4,5},{5,4},{6,7},{7,6},{8,9},{9,8},{10,11... | collective-permute-start | bytes 393224 | tf_op jit(solution)/shard_map/ppermute | solution.py:18
  20.2 1.6 %copy-start.10 = (bf16[32,8192]{1,0:T(8,128)(2,1)S(1)}, bf16[32,8192]{1,0:T(8,128)(2,1)}, u32[]{:S(2)}) copy-start(bf16[32,8192]{1,0:T(8,128)(2,1)} %param.27) | copy-start | bytes 1572868
  20.2 3.0 %collective-permute-start.1 = (bf16[8,4096]{1,0:T(8,128)(2,1)S(1)}, bf16[8,4096]{1,0:T(8,128)(2,1)S(1)}, u32[]{:S(2)}, u32[]{:S(2)}) collective-permute-start(bf16[8,4096]{1,0:T(8,128)(2,1)S(1)} %fusion.26), channel_id=1, source_target_pairs={{0,1},{1,0},{2,3},{3,2},{4,5},{5,4},{6,7},{7,6},{8,9},{9,8},{10,11... | collective-permute-start | bytes 196616 | tf_op jit(solution)/shard_map/ppermute | solution.py:18
  21.8 1.1 %copy-start.3 = (bf16[32,8192]{1,0:T(8,128)(2,1)S(1)}, bf16[32,8192]{1,0:T(8,128)(2,1)}, u32[]{:S(2)}) copy-start(bf16[32,8192]{1,0:T(8,128)(2,1)} %param.28) | copy-start | bytes 1572868
  22.1 6.7 %copy-start.1 = (bf16[64,8192]{1,0:T(8,128)(2,1)S(1)}, bf16[64,8192]{1,0:T(8,128)(2,1)}, u32[]{:S(2)}) copy-start(bf16[64,8192]{1,0:T(8,128)(2,1)} %param.23) | copy-start | bytes 3145732
  23.0 1.4 %collective-permute-start.3 = (bf16[8,2,4096]{2,0,1:T(8,128)(2,1)S(1)}, bf16[8,2,4096]{2,0,1:T(8,128)(2,1)S(1)}, u32[]{:S(2)}, u32[]{:S(2)}) collective-permute-start(bf16[8,2,4096]{2,0,1:T(8,128)(2,1)S(1)} %convolution_convert_fusion), channel_id=1, source_target_pairs={{0,1},{1,0},{2,3},{3,2},{4,5},{5,4},{6,7},{7,6},{8,9},{9,8},{10,11... | collective-permute-start | bytes 393224 | tf_op jit(solution)/shard_map/ppermute | solution.py:18
  23.3 5.9 %copy-start.2 = (bf16[64,8192]{1,0:T(8,128)(2,1)S(1)}, bf16[64,8192]{1,0:T(8,128)(2,1)}, u32[]{:S(2)}) copy-start(bf16[64,8192]{1,0:T(8,128)(2,1)} %param.24) | copy-start | bytes 3145732
  25.4 10.9 %all-to-all-start.1 = ((bf16[8,2,4096]{2,1,0:T(2,128)(2,1)}), bf16[8,2,4096]{2,1,0:T(2,128)(2,1)S(1)}, u32[]{:S(2)}, u32[]{:S(2)}) async-start(bf16[8,2,4096]{2,1,0:T(2,128)(2,1)} %copy.39), calls=%async_computation.1 | async-start | bytes 262144 | tf_op jit(solution)/shard_map/all_to_all | solution.py:135
  29.8 6.6 %collective-permute-start.4 = (f32[8,4096]{1,0:T(8,128)S(1)}, f32[8,4096]{1,0:T(8,128)S(1)}, u32[]{:S(2)}, u32[]{:S(2)}) collective-permute-start(f32[8,4096]{1,0:T(8,128)S(1)} %fusion.7), channel_id=1, source_target_pairs={{0,1},{1,0},{2,3},{3,2},{4,5},{5,4},{6,7},{7,6},{8,9},{9,8},{10,11... | collective-permute-start | bytes 393224 | tf_op jit(solution)/shard_map/ppermute | solution.py:18

commit v17 on v16

--- a/solution.py
+++ b/solution.py
@@ -138,9 +138,11 @@
     )
     hot_received = partner(hot_given, "heads", 0)
     settled = lax.optimization_barrier(stream.astype(jnp.float32) + hot_kept)
-    cold_sum = collect_rows(
-        selector.astype(jnp.float32),
-        returned.reshape(owner_count * CAP, -1).astype(jnp.float32),
+    cold_sum = jnp.einsum(
+        "sr,sd->rd",
+        selector.astype(jnp.bfloat16),
+        returned.reshape(owner_count * CAP, -1),
+        preferred_element_type=jnp.float32,
     )
     result = settled + hot_received + cold_sum
     return result.astype(jnp.bfloat16)

time: 37.7 us -> 37.6 us (level)
    unnamed x28 -> x29, local copies, waits for them, and re-layouts: 2.48 us -> 2.49 us
where the time goes in v17:
time: 37.6 us; the launch traced here: 37.2 us
  blocking collectives  14.3 us (38%)
  waiting for transfers between devices  8.15 us (22%)
  starting transfers between devices  4.84 us (13%)
  matrix products  4.81 us (13%)
  local copies, waits for them, and re-layouts  4.33 us (12%)
  other arithmetic  0.6 us (2%)
    all_to_all x1, blocking collectives, local(): lax.all_to_all(outgoing, 'rows', split_axis=0, concat_axis=0, tiled=True)  14.3 us
    all_to_all x1, waiting for transfers between devices, local(): lax.all_to_all(owner_sum, 'rows', split_axis=0, concat_axis=0, tiled=True)  6.15 us
    all_to_all x1, starting transfers between devices, local(): lax.all_to_all(owner_sum, 'rows', split_axis=0, concat_axis=0, tiled=True)  3.37 us
    unnamed x29, local copies, waits for them, and re-layouts  2.49 us
    ppermute x5, waiting for transfers between devices, partner(): return lax.ppermute(block, axis, route)  1.99 us
    ppermute x5, starting transfers between devices, partner(): return lax.ppermute(block, axis, route)  1.47 us
    sub x1, matrix products, attention_rows(): expons = jnp.where(visible, jnp.exp(scores - highest[..., None]), 0.0)  1.33 us
    dot_general x1, matrix products, local(): jnp.einsum('sr,sd->rd', selector.astype(jnp.bfloat16), returned.reshape(o...  0.84 us
  transfers between devices with their start and end apart: 6, of which 3 were waited for; matrix products, arithmetic and copies ran while one was open for 6% of the time, Pallas kernels for 0%

profile of v17, /device:TPU:0, one launch (start us, length us, event | category | flops | bytes accessed | tf_op | source)
XLA Modules:
  0.0 37.2 jit_solution(4005484428237654497)
XLA Ops:
  0.0 0.0 copy-start
  0.0 0.0 copy-start.7
  0.0 0.8 %copy.31 = bf16[8,2,1,128]{3,2,1,0:T(2,128)(2,1)S(1)} copy(bf16[8,2,1,128]{3,1,0,2:T(2,128)(2,1)} %bitcast.56) | data formatting | bytes 8192 | tf_op jit(solution)/shard_map/broadcast_in_dim | solution.py:34
  0.8 0.0 copy-done.7
  0.8 0.0 copy-start.8
  0.8 0.6 %copy-done.8 = s32[8]{0:T(128)S(1)} copy-done((s32[8]{0:T(128)S(1)}, s32[8]{0:T(128)}, u32[]{:S(2)}) %copy-start.8) | copy-done | bytes 56
  1.5 0.1 fusion.46
  1.5 0.0 copy-start.11
  1.5 0.0 copy-start.12
  1.5 0.0 copy-start.13
  1.6 1.3 %fusion.75 = f32[8,2,16]{2,1,0:T(2,128)S(1)} fusion(bf16[8,2,1,128]{3,2,1,0:T(2,128)(2,1)S(1)} %copy.31, bf16[8,2,32,128]{3,2,1,0:T(8,128)(2,1)} %param.17, bf16[8,2,16,128]{3,0,2,1:T(8,128)(2,1)} %bitcast.58, pred[8,33]{1,0:T(8,128)(4,1)S(1)} %fusion.46), kind=kOutput, calls=%fused_computation.71 | convolution fusion | flops 2475296 | bytes 201992 | tf_op jit(solution)/shard_map/sub | solution.py:44
  2.9 0.0 copy-done.11
  2.9 0.0 copy-done.12
  2.9 0.0 copy-done.13
  2.9 0.0 copy-start.4
  2.9 0.5 %fusion.20 = f32[8,2,16,128]{3,2,1,0:T(8,128)S(1)} fusion(bf16[8,2,1,128]{3,2,1,0:T(2,128)(2,1)S(1)} %copy.34, bf16[8,2,32,128]{3,2,1,0:T(8,128)(2,1)S(1)} %copy-done.11, f32[8,2,16]{2,1,0:T(2,128)S(1)} %fusion.75, pred[8,33]{1,0:T(8,128)(4,1)S(1)} %fusion.46, bf16[8,2,1,128]{3,2,1,0:T(2,128)(2,1)S(1)} %copy.31, bf16[8,2,32,128]{3,2,1,0:T(8,128)(2,1)S(1)} %copy-done.12, ...), kind=kOutput, calls=%fused_computation.27 | convolution fusion | flops 4917024 | bytes 468232 | tf_op jit(solution)/shard_map/rgjp,rgpd->rgjd/dot_general | solution.py:47
  3.4 0.3 copy-done.4
  3.8 0.2 fusion.24
  4.0 0.5 %collective-permute-start = (f32[8]{0:T(128)S(1)}, f32[8]{0:T(128)S(1)}, u32[]{:S(2)}, u32[]{:S(2)}) collective-permute-start(f32[8]{0:T(128)S(1)} %get-tuple-element.9), channel_id=1, source_target_pairs={{0,1},{1,0},{2,3},{3,2},{4,5},{5,4},{6,7},{7,6},{8,9},{9,8},{10,11... | collective-permute-start | bytes 104 | tf_op jit(solution)/shard_map/ppermute | solution.py:18
  4.5 0.0 copy-start.5
  4.5 0.0 copy-start.6
  4.5 0.7 %copy-done.5 = s32[8,4]{0,1:T(4,128)S(1)} copy-done((s32[8,4]{0,1:T(4,128)S(1)}, s32[8,4]{0,1:T(4,128)}, u32[]{:S(2)}) %copy-start.5) | copy-done | bytes 152
  5.2 0.2 reduce_window_sum.11
  5.4 0.0 copy-done.6
  5.4 0.0 collective-permute-done
  5.4 0.1 fusion.26
  5.5 0.0 copy-start.9
  5.5 0.2 convolution_convert_fusion.1
  5.7 0.1 copy.36
  5.8 14.3 %all_to_all.10 = bf16[8,2,4096]{2,1,0:T(2,128)(2,1)S(1)} all-to-all(bf16[8,2,4096]{2,1,0:T(2,128)(2,1)S(1)} %copy.36), channel_id=1, replica_groups=mesh['groups'=2,'rows'=8,'heads'=2] {'rows'}, dimensions={0} | all-to-all | bytes 262144 | tf_op jit(solution)/shard_map/all_to_all | solution.py:127
  20.1 0.1 reshape.60
  20.1 0.1 collective-permute-start.2
  20.2 0.0 copy-start.10
  20.2 0.5 %collective-permute-start.1 = (bf16[8,4096]{1,0:T(8,128)(2,1)S(1)}, bf16[8,4096]{1,0:T(8,128)(2,1)S(1)}, u32[]{:S(2)}, u32[]{:S(2)}) collective-permute-start(bf16[8,4096]{1,0:T(8,128)(2,1)S(1)} %fusion.26), channel_id=1, source_target_pairs={{0,1},{1,0},{2,3},{3,2},{4,5},{5,4},{6,7},{7,6},{8,9},{9,8},{10,11... | collective-permute-start | bytes 196616 | tf_op jit(solution)/shard_map/ppermute | solution.py:18
  20.7 0.8 %collective-permute-done.2 = bf16[16,4096]{1,0:T(8,128)(2,1)S(1)} collective-permute-done((bf16[16,4096]{1,0:T(8,128)(2,1)S(1)}, bf16[16,4096]{1,0:T(8,128)(2,1)S(1)}, u32[]{:S(2)}, u32[]{:S(2)}) %collective-permute-start.2) | collective-permute-done | bytes 131104 | tf_op jit(solution)/shard_map/ppermute | solution.py:18
  21.6 0.0 copy-done.9
  21.6 0.2 fusion.32
  21.8 0.0 copy-done.10
  21.8 0.0 copy-start.3
  21.8 0.3 multiply_convert_fusion
  22.1 0.0 copy-start.1
  22.1 0.8 %copy-done.3 = bf16[32,8192]{1,0:T(8,128)(2,1)S(1)} copy-done((bf16[32,8192]{1,0:T(8,128)(2,1)S(1)}, bf16[32,8192]{1,0:T(8,128)(2,1)}, u32[]{:S(2)}) %copy-start.3) | copy-done | bytes 524312
  22.9 0.2 convolution_convert_fusion
  23.0 0.2 collective-permute-start.3
  23.3 0.0 collective-permute-done.1
  23.3 0.0 copy-start.2
  23.3 1.2 %collective-permute-done.3 = bf16[8,2,4096]{2,0,1:T(8,128)(2,1)S(1)} collective-permute-done((bf16[8,2,4096]{2,0,1:T(8,128)(2,1)S(1)}, bf16[8,2,4096]{2,0,1:T(8,128)(2,1)S(1)}, u32[]{:S(2)}, u32[]{:S(2)}) %collective-permute-start.3) | collective-permute-done | bytes 131104 | tf_op jit(solution)/shard_map/ppermute | solution.py:18
  24.5 0.2 add_convert_fusion
  24.6 0.8 %copy.39 = bf16[8,2,4096]{2,1,0:T(2,128)(2,1)} copy(bf16[8,2,4096]{2,0,1:T(8,128)(2,1)S(1)} %add_convert_fusion) | data formatting | bytes 262144 | tf_op jit(solution)/shard_map/optimization_barrier | solution.py:134
  25.4 3.4 %all-to-all-start.1 = ((bf16[8,2,4096]{2,1,0:T(2,128)(2,1)}), bf16[8,2,4096]{2,1,0:T(2,128)(2,1)S(1)}, u32[]{:S(2)}, u32[]{:S(2)}) async-start(bf16[8,2,4096]{2,1,0:T(2,128)(2,1)} %copy.39), calls=%async_computation.1 | async-start | bytes 262144 | tf_op jit(solution)/shard_map/all_to_all | solution.py:135
  28.8 0.0 copy-done.1
  28.8 0.4 fusion.80
  29.2 0.0 copy-done.2
  29.2 0.4 %fusion.6 = bf16[8,64]{1,0:T(8,128)(2,1)S(1)} fusion(bf16[8,8192]{1,0:T(8,128)(2,1)S(1)} %maximum_select_fusion.1, bf16[64,8192]{1,0:T(8,128)(2,1)S(1)} %copy-done.2, f32[8,64]{1,0:T(8,128)S(1)} %fusion.80), kind=kOutput, calls=%fused_computation.11 | convolution fusion | flops 8391680 | bytes 1182720 | tf_op jit(solution)/shard_map/rd,nd->rn/dot_general | solution.py:62
  29.6 0.0 copy-done
  29.6 0.2 fusion.7
  29.8 0.2 collective-permute-start.4
  30.0 0.2 convolution_add_fusion
  30.2 6.2 %all-to-all-done.1 = bf16[8,2,4096]{2,1,0:T(2,128)(2,1)S(1)} async-done(((bf16[8,2,4096]{2,1,0:T(2,128)(2,1)}), bf16[8,2,4096]{2,1,0:T(2,128)(2,1)S(1)}, u32[]{:S(2)}, u32[]{:S(2)}) %all-to-all-start.1) | async-done | bytes 131104 | tf_op jit(solution)/shard_map/all_to_all | solution.py:135
  36.3 0.1 reshape.62
  36.4 0.0 collective-permute-done.4
  36.4 0.8 %add_convert_fusion.1 = bf16[8,4096]{1,0:T(8,128)(2,1)} fusion(f32[8,4096]{1,0:T(8,128)S(1)} %convolution_add_fusion, f32[8,4096]{1,0:T(8,128)S(1)} %collective-permute-done.4, bf16[16,8]{1,0:T(8,128)(2,1)S(1)} %bitcast.54, bf16[16,4096]{1,0:T(8,128)(2,1)S(1)} %reshape.62), kind=kOutput, calls=%fused_computation.37 | convolution fusion | flops 1146880 | bytes 459008 | tf_op jit(solution)/shard_map/sr,sd->rd/dot_general | solution.py:141
  (10 shorter events, 0.1 us)
Async XLA Ops:
  0.0 29.6 %copy-start = (bf16[64,8192]{1,0:T(8,128)(2,1)S(1)}, bf16[64,8192]{1,0:T(8,128)(2,1)}, u32[]{:S(2)}) copy-start(bf16[64,8192]{1,0:T(8,128)(2,1)} %param.25) | copy-start | bytes 3145732
  0.0 0.8 %copy-start.7 = (bf16[8,2,128]{2,1,0:T(2,128)(2,1)S(1)}, bf16[8,2,128]{2,1,0:T(2,128)(2,1)}, u32[]{:S(2)}) copy-start(bf16[8,2,128]{2,1,0:T(2,128)(2,1)} %param.20) | copy-start | bytes 12292
  0.8 0.7 %copy-start.8 = (s32[8]{0:T(128)S(1)}, s32[8]{0:T(128)}, u32[]{:S(2)}) copy-start(s32[8]{0:T(128)} %param.21) | copy-start | bytes 100
  1.5 1.4 %copy-start.11 = (bf16[8,2,32,128]{3,2,1,0:T(8,128)(2,1)S(1)}, bf16[8,2,32,128]{3,2,1,0:T(8,128)(2,1)}, u32[]{:S(2)}) copy-start(bf16[8,2,32,128]{3,2,1,0:T(8,128)(2,1)} %param.18) | copy-start | bytes 393220
  1.5 1.4 %copy-start.12 = (bf16[8,2,32,128]{3,2,1,0:T(8,128)(2,1)S(1)}, bf16[8,2,32,128]{3,2,1,0:T(8,128)(2,1)}, u32[]{:S(2)}) copy-start(bf16[8,2,32,128]{3,2,1,0:T(8,128)(2,1)} %param.17) | copy-start | bytes 393220
  1.5 1.4 %copy-start.13 = (bf16[8,4096]{1,0:T(8,128)(2,1)S(1)}, bf16[8,4096]{1,0:T(8,128)(2,1)}, u32[]{:S(2)}) copy-start(bf16[8,4096]{1,0:T(8,128)(2,1)} %param.16) | copy-start | bytes 196612
  2.9 0.8 %copy-start.4 = (bf16[8,4096]{1,0:T(8,128)(2,1)S(1)}, bf16[8,4096]{1,0:T(8,128)(2,1)}, u32[]{:S(2)}) copy-start(bf16[8,4096]{1,0:T(8,128)(2,1)} %param.15) | copy-start | bytes 196612
  4.0 1.4 %collective-permute-start = (f32[8]{0:T(128)S(1)}, f32[8]{0:T(128)S(1)}, u32[]{:S(2)}, u32[]{:S(2)}) collective-permute-start(f32[8]{0:T(128)S(1)} %get-tuple-element.9), channel_id=1, source_target_pairs={{0,1},{1,0},{2,3},{3,2},{4,5},{5,4},{6,7},{7,6},{8,9},{9,8},{10,11... | collective-permute-start | bytes 104 | tf_op jit(solution)/shard_map/ppermute | solution.py:18
  4.5 0.7 %copy-start.5 = (s32[8,4]{0,1:T(4,128)S(1)}, s32[8,4]{0,1:T(4,128)}, u32[]{:S(2)}) copy-start(s32[8,4]{0,1:T(4,128)} %param.29) | copy-start | bytes 388
  4.5 0.9 %copy-start.6 = (bf16[8192]{0:T(1024)(128)(2,1)S(1)}, bf16[8192]{0:T(1024)(128)(2,1)}, u32[]{:S(2)}) copy-start(bf16[8192]{0:T(1024)(128)(2,1)} %param.22) | copy-start | bytes 49156
  5.5 16.1 %copy-start.9 = (bf16[32,8192]{1,0:T(8,128)(2,1)S(1)}, bf16[32,8192]{1,0:T(8,128)(2,1)}, u32[]{:S(2)}) copy-start(bf16[32,8192]{1,0:T(8,128)(2,1)} %param.26) | copy-start | bytes 1572868
  20.1 1.4 %collective-permute-start.2 = (bf16[16,4096]{1,0:T(8,128)(2,1)S(1)}, bf16[16,4096]{1,0:T(8,128)(2,1)S(1)}, u32[]{:S(2)}, u32[]{:S(2)}) collective-permute-start(bf16[16,4096]{1,0:T(8,128)(2,1)S(1)} %reshape.60), channel_id=1, source_target_pairs={{0,1},{1,0},{2,3},{3,2},{4,5},{5,4},{6,7},{7,6},{8,9},{9,8},{10,11... | collective-permute-start | bytes 393224 | tf_op jit(solution)/shard_map/ppermute | solution.py:18
  20.2 1.6 %copy-start.10 = (bf16[32,8192]{1,0:T(8,128)(2,1)S(1)}, bf16[32,8192]{1,0:T(8,128)(2,1)}, u32[]{:S(2)}) copy-start(bf16[32,8192]{1,0:T(8,128)(2,1)} %param.27) | copy-start | bytes 1572868
  20.2 3.0 %collective-permute-start.1 = (bf16[8,4096]{1,0:T(8,128)(2,1)S(1)}, bf16[8,4096]{1,0:T(8,128)(2,1)S(1)}, u32[]{:S(2)}, u32[]{:S(2)}) collective-permute-start(bf16[8,4096]{1,0:T(8,128)(2,1)S(1)} %fusion.26), channel_id=1, source_target_pairs={{0,1},{1,0},{2,3},{3,2},{4,5},{5,4},{6,7},{7,6},{8,9},{9,8},{10,11... | collective-permute-start | bytes 196616 | tf_op jit(solution)/shard_map/ppermute | solution.py:18
  21.8 1.1 %copy-start.3 = (bf16[32,8192]{1,0:T(8,128)(2,1)S(1)}, bf16[32,8192]{1,0:T(8,128)(2,1)}, u32[]{:S(2)}) copy-start(bf16[32,8192]{1,0:T(8,128)(2,1)} %param.28) | copy-start | bytes 1572868
  22.1 6.7 %copy-start.1 = (bf16[64,8192]{1,0:T(8,128)(2,1)S(1)}, bf16[64,8192]{1,0:T(8,128)(2,1)}, u32[]{:S(2)}) copy-start(bf16[64,8192]{1,0:T(8,128)(2,1)} %param.23) | copy-start | bytes 3145732
  23.0 1.4 %collective-permute-start.3 = (bf16[8,2,4096]{2,0,1:T(8,128)(2,1)S(1)}, bf16[8,2,4096]{2,0,1:T(8,128)(2,1)S(1)}, u32[]{:S(2)}, u32[]{:S(2)}) collective-permute-start(bf16[8,2,4096]{2,0,1:T(8,128)(2,1)S(1)} %convolution_convert_fusion), channel_id=1, source_target_pairs={{0,1},{1,0},{2,3},{3,2},{4,5},{5,4},{6,7},{7,6},{8,9},{9,8},{10,11... | collective-permute-start | bytes 393224 | tf_op jit(solution)/shard_map/ppermute | solution.py:18
  23.3 5.9 %copy-start.2 = (bf16[64,8192]{1,0:T(8,128)(2,1)S(1)}, bf16[64,8192]{1,0:T(8,128)(2,1)}, u32[]{:S(2)}) copy-start(bf16[64,8192]{1,0:T(8,128)(2,1)} %param.24) | copy-start | bytes 3145732
  25.4 10.9 %all-to-all-start.1 = ((bf16[8,2,4096]{2,1,0:T(2,128)(2,1)}), bf16[8,2,4096]{2,1,0:T(2,128)(2,1)S(1)}, u32[]{:S(2)}, u32[]{:S(2)}) async-start(bf16[8,2,4096]{2,1,0:T(2,128)(2,1)} %copy.39), calls=%async_computation.1 | async-start | bytes 262144 | tf_op jit(solution)/shard_map/all_to_all | solution.py:135
  29.8 6.6 %collective-permute-start.4 = (f32[8,4096]{1,0:T(8,128)S(1)}, f32[8,4096]{1,0:T(8,128)S(1)}, u32[]{:S(2)}, u32[]{:S(2)}) collective-permute-start(f32[8,4096]{1,0:T(8,128)S(1)} %fusion.7), channel_id=1, source_target_pairs={{0,1},{1,0},{2,3},{3,2},{4,5},{5,4},{6,7},{7,6},{8,9},{9,8},{10,11... | collective-permute-start | bytes 393224 | tf_op jit(solution)/shard_map/ppermute | solution.py:18

commit v18 on v8

--- a/solution.py
+++ b/solution.py
@@ -129,9 +129,10 @@
     kept, given = swiglu_halves(
         incoming, cold_gate, cold_up, cold_down, myself, (owner_count, CAP)
     )
-    given_narrow = partner(given.astype(jnp.bfloat16), "heads", 0)
+    given_bf16 = given.astype(jnp.bfloat16)
+    normed_late, given_bf16 = lax.optimization_barrier((normed, given_bf16))
+    given_narrow = partner(given_bf16, "heads", 0)
     owner_sum = (kept + given_narrow.astype(jnp.float32)).astype(jnp.bfloat16)
-    normed_late, owner_sum = lax.optimization_barrier((normed, owner_sum))
     returned = lax.all_to_all(owner_sum, "rows", split_axis=0, concat_axis=0, tiled=True)
     hot_kept, hot_given = swiglu_halves(
         normed_late, hot_gate, hot_up, hot_down, myself, (request_count,)

time: 37.9 us -> 38.5 us (1.016)
  blocking collectives: 14.3 us -> 0 us
  waiting for transfers between devices: 8.33 us -> 16.2 us
  starting transfers between devices: 4.84 us -> 11.4 us
  local copies, waits for them, and re-layouts: 4.33 us -> 4.76 us
    all_to_all x1 -> x0, blocking collectives: 14.3 us -> none  [local(): lax.all_to_all(outgoing, 'rows', split_axis=0, concat_axis=0, tiled=True)]
    all_to_all x0 -> x1, waiting for transfers between devices: none -> 7.43 us  [local(): lax.all_to_all(outgoing, 'rows', split_axis=0, concat_axis=0, tiled=True)]
    all_to_all x0 -> x1, starting transfers between devices: none -> 6.99 us  [local(): lax.all_to_all(outgoing, 'rows', split_axis=0, concat_axis=0, tiled=True)]
    optimization_barrier x1 -> x0, local copies, waits for them, and re-layouts: 0.79 us -> none  [local(): normed_late, owner_sum = lax.optimization_barrier((normed, owner_sum))]
    convert_element_type x0 -> x1, local copies, waits for them, and re-layouts: none -> 0.78 us  [local(): owner_sum = (kept + given_narrow.astype(jnp.float32)).astype(jnp.bfloat16)]
    convert_element_type x1, local copies, waits for them, and re-layouts: 0.14 us -> 0.78 us  [local(): outgoing = jnp.einsum('ocr,rd->ocd', selector3.astype(jnp.bfloat16), scal...]
    ppermute x5, starting transfers between devices: 1.47 us -> 1.08 us  [partner(): return lax.ppermute(block, axis, route)]
    all_to_all x1, waiting for transfers between devices: 6.34 us -> 6.73 us  [local(): lax.all_to_all(owner_sum, 'rows', split_axis=0, concat_axis=0, tiled=True)]
  transfers between devices with their start and end apart: 6 -> 7, of which waited for: 3 -> 4; matrix products, arithmetic and copies ran while one was open for 6% -> 4% of each run, Pallas kernels for 0% -> 0%
where the time goes in v18:
time: 38.5 us; the launch traced here: 38.1 us
  waiting for transfers between devices  16.2 us (42%)
  starting transfers between devices  11.4 us (30%)
  matrix products  4.85 us (13%)
  local copies, waits for them, and re-layouts  4.76 us (12%)
  other arithmetic  0.6 us (2%)
    all_to_all x1, waiting for transfers between devices, local(): lax.all_to_all(outgoing, 'rows', split_axis=0, concat_axis=0, tiled=True)  7.43 us
    all_to_all x1, starting transfers between devices, local(): lax.all_to_all(outgoing, 'rows', split_axis=0, concat_axis=0, tiled=True)  6.99 us
    all_to_all x1, waiting for transfers between devices, local(): lax.all_to_all(owner_sum, 'rows', split_axis=0, concat_axis=0, tiled=True)  6.73 us
    all_to_all x1, starting transfers between devices, local(): lax.all_to_all(owner_sum, 'rows', split_axis=0, concat_axis=0, tiled=True)  3.37 us
    unnamed x28, local copies, waits for them, and re-layouts  2.28 us
    ppermute x5, waiting for transfers between devices, partner(): return lax.ppermute(block, axis, route)  2.02 us
    sub x1, matrix products, attention_rows(): expons = jnp.where(visible, jnp.exp(scores - highest[..., None]), 0.0)  1.33 us
    ppermute x5, starting transfers between devices, partner(): return lax.ppermute(block, axis, route)  1.08 us
  transfers between devices with their start and end apart: 7, of which 4 were waited for; matrix products, arithmetic and copies ran while one was open for 4% of the time, Pallas kernels for 0%

profile of v18, /device:TPU:0, one launch (start us, length us, event | category | flops | bytes accessed | tf_op | source)
XLA Modules:
  0.0 38.1 jit_solution(5630908063104063112)
XLA Ops:
  0.0 0.0 copy-start
  0.0 0.0 copy-start.7
  0.0 0.8 %copy.31 = bf16[8,2,1,128]{3,2,1,0:T(2,128)(2,1)S(1)} copy(bf16[8,2,1,128]{3,1,0,2:T(2,128)(2,1)} %bitcast.56) | data formatting | bytes 8192 | tf_op jit(solution)/shard_map/broadcast_in_dim | solution.py:34
  0.8 0.0 copy-done.7
  0.8 0.0 copy-start.8
  0.8 0.6 %copy-done.8 = s32[8]{0:T(128)S(1)} copy-done((s32[8]{0:T(128)S(1)}, s32[8]{0:T(128)}, u32[]{:S(2)}) %copy-start.8) | copy-done | bytes 56
  1.5 0.1 fusion.50
  1.5 0.0 copy-start.11
  1.5 0.0 copy-start.12
  1.5 0.0 copy-start.13
  1.6 1.3 %fusion.79 = f32[8,2,16]{2,1,0:T(2,128)S(1)} fusion(bf16[8,2,1,128]{3,2,1,0:T(2,128)(2,1)S(1)} %copy.31, bf16[8,2,32,128]{3,2,1,0:T(8,128)(2,1)} %param.17, bf16[8,2,16,128]{3,0,2,1:T(8,128)(2,1)} %bitcast.58, pred[8,33]{1,0:T(8,128)(4,1)S(1)} %fusion.50), kind=kOutput, calls=%fused_computation.74 | convolution fusion | flops 2475296 | bytes 201992 | tf_op jit(solution)/shard_map/sub | solution.py:44
  2.9 0.0 copy-done.11
  2.9 0.0 copy-done.12
  2.9 0.0 copy-done.13
  2.9 0.0 copy-start.4
  2.9 0.5 %fusion.23 = f32[8,2,16,128]{3,2,1,0:T(8,128)S(1)} fusion(bf16[8,2,1,128]{3,2,1,0:T(2,128)(2,1)S(1)} %copy.34, bf16[8,2,32,128]{3,2,1,0:T(8,128)(2,1)S(1)} %copy-done.11, f32[8,2,16]{2,1,0:T(2,128)S(1)} %fusion.79, pred[8,33]{1,0:T(8,128)(4,1)S(1)} %fusion.50, bf16[8,2,1,128]{3,2,1,0:T(2,128)(2,1)S(1)} %copy.31, bf16[8,2,32,128]{3,2,1,0:T(8,128)(2,1)S(1)} %copy-done.12, ...), kind=kOutput, calls=%fused_computation.30 | convolution fusion | flops 4917024 | bytes 468232 | tf_op jit(solution)/shard_map/rgjp,rgpd->rgjd/dot_general | solution.py:47
  3.4 0.3 copy-done.4
  3.8 0.2 fusion.27
  4.0 0.5 %collective-permute-start = (f32[8]{0:T(128)S(1)}, f32[8]{0:T(128)S(1)}, u32[]{:S(2)}, u32[]{:S(2)}) collective-permute-start(f32[8]{0:T(128)S(1)} %get-tuple-element.9), channel_id=1, source_target_pairs={{0,1},{1,0},{2,3},{3,2},{4,5},{5,4},{6,7},{7,6},{8,9},{9,8},{10,11... | collective-permute-start | bytes 104 | tf_op jit(solution)/shard_map/ppermute | solution.py:18
  4.5 0.0 copy-start.5
  4.5 0.0 copy-start.6
  4.5 0.7 %copy-done.5 = s32[8,4]{0,1:T(4,128)S(1)} copy-done((s32[8,4]{0,1:T(4,128)S(1)}, s32[8,4]{0,1:T(4,128)}, u32[]{:S(2)}) %copy-start.5) | copy-done | bytes 152
  5.2 0.2 reduce_window_sum.11
  5.4 0.0 copy-done.6
  5.4 0.0 collective-permute-done
  5.4 0.1 fusion.29
  5.5 0.2 convolution_convert_fusion.1
  5.7 0.0 copy-start.9
  5.7 0.8 %copy.36 = bf16[8,2,4096]{2,1,0:T(2,128)(2,1)} copy(bf16[8,2,4096]{2,0,1:T(8,128)(2,1)S(1)} %convolution_convert_fusion.1) | data formatting | bytes 262144 | tf_op jit(solution)/shard_map/convert_element_type | solution.py:126
  6.5 7.0 %all-to-all-start = ((bf16[8,2,4096]{2,1,0:T(2,128)(2,1)}), bf16[8,2,4096]{2,1,0:T(2,128)(2,1)S(1)}, u32[]{:S(2)}, u32[]{:S(2)}) async-start(bf16[8,2,4096]{2,1,0:T(2,128)(2,1)} %copy.36), calls=%async_computation | async-start | bytes 262144 | tf_op jit(solution)/shard_map/all_to_all | solution.py:127
  13.5 0.0 collective-permute-start.1
  13.5 7.4 %all-to-all-done = bf16[8,2,4096]{2,1,0:T(2,128)(2,1)S(1)} async-done(((bf16[8,2,4096]{2,1,0:T(2,128)(2,1)}), bf16[8,2,4096]{2,1,0:T(2,128)(2,1)S(1)}, u32[]{:S(2)}, u32[]{:S(2)}) %all-to-all-start) | async-done | bytes 131104 | tf_op jit(solution)/shard_map/all_to_all | solution.py:127
  20.9 0.1 reshape.60
  21.0 0.1 collective-permute-start.2
  21.1 0.0 collective-permute-done.1
  21.1 0.0 copy-start.10
  21.1 1.3 %collective-permute-done.2 = bf16[16,4096]{1,0:T(8,128)(2,1)S(1)} collective-permute-done((bf16[16,4096]{1,0:T(8,128)(2,1)S(1)}, bf16[16,4096]{1,0:T(8,128)(2,1)S(1)}, u32[]{:S(2)}, u32[]{:S(2)}) %collective-permute-start.2) | collective-permute-done | bytes 131104 | tf_op jit(solution)/shard_map/ppermute | solution.py:18
  22.4 0.0 copy-done.9
  22.4 0.0 copy-start.3
  22.4 0.2 fusion.35
  22.7 0.0 copy-done.10
  22.7 0.0 copy-start.1
  22.7 0.3 multiply_convert_fusion
  22.9 0.5 %copy-done.3 = bf16[32,8192]{1,0:T(8,128)(2,1)S(1)} copy-done((bf16[32,8192]{1,0:T(8,128)(2,1)S(1)}, bf16[32,8192]{1,0:T(8,128)(2,1)}, u32[]{:S(2)}) %copy-start.3) | copy-done | bytes 524312
  23.4 0.2 convolution_convert_fusion
  23.6 0.0 copy-start.2
  23.6 0.2 collective-permute-start.4
  23.9 0.1 copy-done.1
  23.9 0.4 fusion.84
  24.3 0.7 %collective-permute-done.4 = bf16[8,2,4096]{2,0,1:T(8,128)(2,1)S(1)} collective-permute-done((bf16[8,2,4096]{2,0,1:T(8,128)(2,1)S(1)}, bf16[8,2,4096]{2,0,1:T(8,128)(2,1)S(1)}, u32[]{:S(2)}, u32[]{:S(2)}) %collective-permute-start.4) | collective-permute-done | bytes 131104 | tf_op jit(solution)/shard_map/ppermute | solution.py:18
  25.0 0.2 add_convert_fusion
  25.2 0.8 %copy.39 = bf16[8,2,4096]{2,1,0:T(2,128)(2,1)} copy(bf16[8,2,4096]{2,0,1:T(8,128)(2,1)S(1)} %add_convert_fusion) | data formatting | bytes 262144 | tf_op jit(solution)/shard_map/convert_element_type | solution.py:135
  26.0 3.4 %all-to-all-start.1 = ((bf16[8,2,4096]{2,1,0:T(2,128)(2,1)}), bf16[8,2,4096]{2,1,0:T(2,128)(2,1)S(1)}, u32[]{:S(2)}, u32[]{:S(2)}) async-start(bf16[8,2,4096]{2,1,0:T(2,128)(2,1)} %copy.39), calls=%async_computation.1 | async-start | bytes 262144 | tf_op jit(solution)/shard_map/all_to_all | solution.py:136
  29.4 0.0 copy-done.2
  29.4 0.4 fusion.9
  29.8 0.0 copy-done
  29.8 0.2 fusion.10
  30.0 0.2 collective-permute-start.3
  30.2 6.7 %all-to-all-done.1 = bf16[8,2,4096]{2,1,0:T(2,128)(2,1)S(1)} async-done(((bf16[8,2,4096]{2,1,0:T(2,128)(2,1)}), bf16[8,2,4096]{2,1,0:T(2,128)(2,1)S(1)}, u32[]{:S(2)}, u32[]{:S(2)}) %all-to-all-start.1) | async-done | bytes 131104 | tf_op jit(solution)/shard_map/all_to_all | solution.py:136
  36.9 0.1 reshape.62
  37.0 0.3 fusion.85
  37.2 0.0 collective-permute-done.3
  37.2 0.8 %fusion.3 = bf16[8,4096]{1,0:T(8,128)(2,1)} fusion(f32[8,4096]{1,0:T(8,128)S(1)} %fusion.85, f32[8,4096]{1,0:T(8,128)S(1)} %collective-permute-done.3, bf16[8,64]{1,0:T(8,128)(2,1)S(1)} %fusion.9, bf16[64,8192]{1,0:T(8,128)(2,1)S(1)} %copy-done, s32[]{:T(128)S(6)} %select_n.39, bf16[8,4096]{1,0:T(8,128)(2,1)S(1)} %get-tuple-element.10), kind=kOutput, calls=%fused_computation.6 | convolution fusion | flops 4358144 | bytes 919556 | tf_op jit(solution)/shard_map/...n,nd->...d/dot_general | solution.py:69
  (10 shorter events, 0.1 us)
Async XLA Ops:
  0.0 29.8 %copy-start = (bf16[64,8192]{1,0:T(8,128)(2,1)S(1)}, bf16[64,8192]{1,0:T(8,128)(2,1)}, u32[]{:S(2)}) copy-start(bf16[64,8192]{1,0:T(8,128)(2,1)} %param.25) | copy-start | bytes 3145732
  0.0 0.8 %copy-start.7 = (bf16[8,2,128]{2,1,0:T(2,128)(2,1)S(1)}, bf16[8,2,128]{2,1,0:T(2,128)(2,1)}, u32[]{:S(2)}) copy-start(bf16[8,2,128]{2,1,0:T(2,128)(2,1)} %param.20) | copy-start | bytes 12292
  0.8 0.7 %copy-start.8 = (s32[8]{0:T(128)S(1)}, s32[8]{0:T(128)}, u32[]{:S(2)}) copy-start(s32[8]{0:T(128)} %param.21) | copy-start | bytes 100
  1.5 1.4 %copy-start.11 = (bf16[8,2,32,128]{3,2,1,0:T(8,128)(2,1)S(1)}, bf16[8,2,32,128]{3,2,1,0:T(8,128)(2,1)}, u32[]{:S(2)}) copy-start(bf16[8,2,32,128]{3,2,1,0:T(8,128)(2,1)} %param.18) | copy-start | bytes 393220
  1.5 1.4 %copy-start.12 = (bf16[8,2,32,128]{3,2,1,0:T(8,128)(2,1)S(1)}, bf16[8,2,32,128]{3,2,1,0:T(8,128)(2,1)}, u32[]{:S(2)}) copy-start(bf16[8,2,32,128]{3,2,1,0:T(8,128)(2,1)} %param.17) | copy-start | bytes 393220
  1.5 1.4 %copy-start.13 = (bf16[8,4096]{1,0:T(8,128)(2,1)S(1)}, bf16[8,4096]{1,0:T(8,128)(2,1)}, u32[]{:S(2)}) copy-start(bf16[8,4096]{1,0:T(8,128)(2,1)} %param.16) | copy-start | bytes 196612
  2.9 0.8 %copy-start.4 = (bf16[8,4096]{1,0:T(8,128)(2,1)S(1)}, bf16[8,4096]{1,0:T(8,128)(2,1)}, u32[]{:S(2)}) copy-start(bf16[8,4096]{1,0:T(8,128)(2,1)} %param.15) | copy-start | bytes 196612
  4.0 1.4 %collective-permute-start = (f32[8]{0:T(128)S(1)}, f32[8]{0:T(128)S(1)}, u32[]{:S(2)}, u32[]{:S(2)}) collective-permute-start(f32[8]{0:T(128)S(1)} %get-tuple-element.9), channel_id=1, source_target_pairs={{0,1},{1,0},{2,3},{3,2},{4,5},{5,4},{6,7},{7,6},{8,9},{9,8},{10,11... | collective-permute-start | bytes 104 | tf_op jit(solution)/shard_map/ppermute | solution.py:18
  4.5 0.7 %copy-start.5 = (s32[8,4]{0,1:T(4,128)S(1)}, s32[8,4]{0,1:T(4,128)}, u32[]{:S(2)}) copy-start(s32[8,4]{0,1:T(4,128)} %param.29) | copy-start | bytes 388
  4.5 0.9 %copy-start.6 = (bf16[8192]{0:T(1024)(128)(2,1)S(1)}, bf16[8192]{0:T(1024)(128)(2,1)}, u32[]{:S(2)}) copy-start(bf16[8192]{0:T(1024)(128)(2,1)} %param.22) | copy-start | bytes 49156
  5.7 16.7 %copy-start.9 = (bf16[32,8192]{1,0:T(8,128)(2,1)S(1)}, bf16[32,8192]{1,0:T(8,128)(2,1)}, u32[]{:S(2)}) copy-start(bf16[32,8192]{1,0:T(8,128)(2,1)} %param.26) | copy-start | bytes 1572868
  6.5 14.5 %all-to-all-start = ((bf16[8,2,4096]{2,1,0:T(2,128)(2,1)}), bf16[8,2,4096]{2,1,0:T(2,128)(2,1)S(1)}, u32[]{:S(2)}, u32[]{:S(2)}) async-start(bf16[8,2,4096]{2,1,0:T(2,128)(2,1)} %copy.36), calls=%async_computation | async-start | bytes 262144 | tf_op jit(solution)/shard_map/all_to_all | solution.py:127
  13.5 7.6 %collective-permute-start.1 = (bf16[8,4096]{1,0:T(8,128)(2,1)S(1)}, bf16[8,4096]{1,0:T(8,128)(2,1)S(1)}, u32[]{:S(2)}, u32[]{:S(2)}) collective-permute-start(bf16[8,4096]{1,0:T(8,128)(2,1)S(1)} %fusion.29), channel_id=1, source_target_pairs={{0,1},{1,0},{2,3},{3,2},{4,5},{5,4},{6,7},{7,6},{8,9},{9,8},{10,11... | collective-permute-start | bytes 196616 | tf_op jit(solution)/shard_map/ppermute | solution.py:18
  21.0 1.4 %collective-permute-start.2 = (bf16[16,4096]{1,0:T(8,128)(2,1)S(1)}, bf16[16,4096]{1,0:T(8,128)(2,1)S(1)}, u32[]{:S(2)}, u32[]{:S(2)}) collective-permute-start(bf16[16,4096]{1,0:T(8,128)(2,1)S(1)} %reshape.60), channel_id=1, source_target_pairs={{0,1},{1,0},{2,3},{3,2},{4,5},{5,4},{6,7},{7,6},{8,9},{9,8},{10,11... | collective-permute-start | bytes 393224 | tf_op jit(solution)/shard_map/ppermute | solution.py:18
  21.1 1.5 %copy-start.10 = (bf16[32,8192]{1,0:T(8,128)(2,1)S(1)}, bf16[32,8192]{1,0:T(8,128)(2,1)}, u32[]{:S(2)}) copy-start(bf16[32,8192]{1,0:T(8,128)(2,1)} %param.27) | copy-start | bytes 1572868
  22.4 1.0 %copy-start.3 = (bf16[32,8192]{1,0:T(8,128)(2,1)S(1)}, bf16[32,8192]{1,0:T(8,128)(2,1)}, u32[]{:S(2)}) copy-start(bf16[32,8192]{1,0:T(8,128)(2,1)} %param.28) | copy-start | bytes 1572868
  22.7 1.3 %copy-start.1 = (bf16[64,8192]{1,0:T(8,128)(2,1)S(1)}, bf16[64,8192]{1,0:T(8,128)(2,1)}, u32[]{:S(2)}) copy-start(bf16[64,8192]{1,0:T(8,128)(2,1)} %param.23) | copy-start | bytes 3145732
  23.6 5.8 %copy-start.2 = (bf16[64,8192]{1,0:T(8,128)(2,1)S(1)}, bf16[64,8192]{1,0:T(8,128)(2,1)}, u32[]{:S(2)}) copy-start(bf16[64,8192]{1,0:T(8,128)(2,1)} %param.24) | copy-start | bytes 3145732
  23.6 1.4 %collective-permute-start.4 = (bf16[8,2,4096]{2,0,1:T(8,128)(2,1)S(1)}, bf16[8,2,4096]{2,0,1:T(8,128)(2,1)S(1)}, u32[]{:S(2)}, u32[]{:S(2)}) collective-permute-start(bf16[8,2,4096]{2,0,1:T(8,128)(2,1)S(1)} %convolution_convert_fusion), channel_id=1, source_target_pairs={{0,1},{1,0},{2,3},{3,2},{4,5},{5,4},{6,7},{7,6},{8,9},{9,8},{10,11... | collective-permute-start | bytes 393224 | tf_op jit(solution)/shard_map/ppermute | solution.py:18
  26.0 10.9 %all-to-all-start.1 = ((bf16[8,2,4096]{2,1,0:T(2,128)(2,1)}), bf16[8,2,4096]{2,1,0:T(2,128)(2,1)S(1)}, u32[]{:S(2)}, u32[]{:S(2)}) async-start(bf16[8,2,4096]{2,1,0:T(2,128)(2,1)} %copy.39), calls=%async_computation.1 | async-start | bytes 262144 | tf_op jit(solution)/shard_map/all_to_all | solution.py:136
  30.0 7.3 %collective-permute-start.3 = (f32[8,4096]{1,0:T(8,128)S(1)}, f32[8,4096]{1,0:T(8,128)S(1)}, u32[]{:S(2)}, u32[]{:S(2)}) collective-permute-start(f32[8,4096]{1,0:T(8,128)S(1)} %fusion.10), channel_id=1, source_target_pairs={{0,1},{1,0},{2,3},{3,2},{4,5},{5,4},{6,7},{7,6},{8,9},{9,8},{10,11... | collective-permute-start | bytes 393224 | tf_op jit(solution)/shard_map/ppermute | solution.py:18

commit v19 on v8

--- a/solution.py
+++ b/solution.py
@@ -70,6 +70,28 @@
     return kept, given
 
 
+def split_dot(features_mine, features_other, rows, myself):
+    width = features_mine.shape[1]
+    rows_mine = lax.dynamic_slice_in_dim(rows, myself * width, width, 1)
+    rows_other = lax.dynamic_slice_in_dim(rows, (1 - myself) * width, width, 1)
+    first = jnp.einsum("rd,nd->rn", features_mine, rows_mine, preferred_element_type=jnp.float32)
+    second = jnp.einsum("rd,nd->rn", features_other, rows_other, preferred_element_type=jnp.float32)
+    return first + second
+
+
+def swiglu_split(features_mine, features_other, gate_rows, up_rows, down_rows, myself, rows_shape):
+    gate = split_dot(features_mine, features_other, gate_rows, myself)
+    upper = split_dot(features_mine, features_other, up_rows, myself)
+    hidden = (jax.nn.silu(gate) * upper).astype(jnp.bfloat16)
+    hidden = hidden.reshape(rows_shape + hidden.shape[-1:])
+    half_width = down_rows.shape[1] // 2
+    down_given = lax.dynamic_slice_in_dim(down_rows, (1 - myself) * half_width, half_width, 1)
+    down_kept = lax.dynamic_slice_in_dim(down_rows, myself * half_width, half_width, 1)
+    given = jnp.einsum("...n,nd->...d", hidden, down_given, preferred_element_type=jnp.float32)
+    kept = jnp.einsum("...n,nd->...d", hidden, down_kept, preferred_element_type=jnp.float32)
+    return kept, given
+
+
 def collect_rows(selector, returned):
     return lax.dot_general(
         selector,
@@ -125,9 +147,10 @@
         preferred_element_type=jnp.float32,
     ).astype(jnp.bfloat16)
     incoming_half = lax.all_to_all(outgoing, "rows", split_axis=0, concat_axis=0, tiled=True)
-    incoming = join_halves(incoming_half.reshape(owner_count * CAP, -1), myself)
-    kept, given = swiglu_halves(
-        incoming, cold_gate, cold_up, cold_down, myself, (owner_count, CAP)
+    features_mine = incoming_half.reshape(owner_count * CAP, -1)
+    features_other = partner(features_mine, "heads", 0)
+    kept, given = swiglu_split(
+        features_mine, features_other, cold_gate, cold_up, cold_down, myself, (owner_count, CAP)
     )
     given_narrow = partner(given.astype(jnp.bfloat16), "heads", 0)
     owner_sum = (kept + given_narrow.astype(jnp.float32)).astype(jnp.bfloat16)

time: 37.9 us -> 38 us (level)
  blocking collectives: 14.3 us -> 0 us
  waiting for transfers between devices: 8.33 us -> 15.9 us
  starting transfers between devices: 4.84 us -> 11.5 us
    all_to_all x1 -> x0, blocking collectives: 14.3 us -> none  [local(): lax.all_to_all(outgoing, 'rows', split_axis=0, concat_axis=0, tiled=True)]
    all_to_all x0 -> x1, waiting for transfers between devices: none -> 7.43 us  [local(): lax.all_to_all(outgoing, 'rows', split_axis=0, concat_axis=0, tiled=True)]
    all_to_all x0 -> x1, starting transfers between devices: none -> 7.12 us  [local(): lax.all_to_all(outgoing, 'rows', split_axis=0, concat_axis=0, tiled=True)]
    dot_general x0 -> x6, matrix products: none -> 1.09 us  [the longest x2 0.38 us: split_dot(): jnp.einsum('rd,nd->rn', features_mine, rows_mine, preferred_element_type=...]
    unnamed x28 -> x30, local copies, waits for them, and re-layouts: 2.48 us -> 1.71 us
    convert_element_type x1, local copies, waits for them, and re-layouts: 0.14 us -> 0.77 us  [local(): outgoing = jnp.einsum('ocr,rd->ocd', selector3.astype(jnp.bfloat16), scal...]
    ppermute x5, starting transfers between devices: 1.47 us -> 1.03 us  [partner(): return lax.ppermute(block, axis, route)]
    dot_general x2 -> x1, matrix products: 0.99 us -> 0.83 us  [swiglu_halves(): jnp.einsum('...n,nd->...d', hidden, down_kept, preferred_element_type=jnp...]
  transfers between devices with their start and end apart: 6 -> 7, of which waited for: 3 -> 4; matrix products, arithmetic and copies ran while one was open for 6% -> 7% of each run, Pallas kernels for 0% -> 0%
where the time goes in v19:
time: 38 us; the launch traced here: 37.6 us
  waiting for transfers between devices  15.9 us (42%)
  starting transfers between devices  11.5 us (30%)
  matrix products  5.12 us (13%)
  local copies, waits for them, and re-layouts  4.17 us (11%)
  other arithmetic  0.6 us (2%)
    all_to_all x1, waiting for transfers between devices, local(): lax.all_to_all(outgoing, 'rows', split_axis=0, concat_axis=0, tiled=True)  7.43 us
    all_to_all x1, starting transfers between devices, local(): lax.all_to_all(outgoing, 'rows', split_axis=0, concat_axis=0, tiled=True)  7.12 us
    all_to_all x1, waiting for transfers between devices, local(): lax.all_to_all(owner_sum, 'rows', split_axis=0, concat_axis=0, tiled=True)  6.34 us
    all_to_all x1, starting transfers between devices, local(): lax.all_to_all(owner_sum, 'rows', split_axis=0, concat_axis=0, tiled=True)  3.37 us
    ppermute x5, waiting for transfers between devices, partner(): return lax.ppermute(block, axis, route)  2.09 us
    unnamed x30, local copies, waits for them, and re-layouts  1.71 us
    sub x1, matrix products, attention_rows(): expons = jnp.where(visible, jnp.exp(scores - highest[..., None]), 0.0)  1.33 us
    ppermute x5, starting transfers between devices, partner(): return lax.ppermute(block, axis, route)  1.03 us
  transfers between devices with their start and end apart: 7, of which 4 were waited for; matrix products, arithmetic and copies ran while one was open for 7% of the time, Pallas kernels for 0%

profile of v19, /device:TPU:0, one launch (start us, length us, event | category | flops | bytes accessed | tf_op | source)
XLA Modules:
  0.0 37.6 jit_solution(1983019133707730954)
XLA Ops:
  0.0 0.0 copy-start
  0.0 0.0 copy-start.10
  0.0 0.8 %copy.31 = bf16[8,2,1,128]{3,2,1,0:T(2,128)(2,1)S(1)} copy(bf16[8,2,1,128]{3,1,0,2:T(2,128)(2,1)} %bitcast.58) | data formatting | bytes 8192 | tf_op jit(solution)/shard_map/broadcast_in_dim | solution.py:34
  0.8 0.0 copy-done.10
  0.8 0.0 copy-start.11
  0.8 0.6 %copy-done.11 = s32[8]{0:T(128)S(1)} copy-done((s32[8]{0:T(128)S(1)}, s32[8]{0:T(128)}, u32[]{:S(2)}) %copy-start.11) | copy-done | bytes 56
  1.5 0.1 fusion.56
  1.5 0.0 copy-start.13
  1.5 0.0 copy-start.14
  1.6 1.3 %fusion.87 = f32[8,2,16]{2,1,0:T(2,128)S(1)} fusion(bf16[8,2,1,128]{3,2,1,0:T(2,128)(2,1)S(1)} %copy.31, bf16[8,2,32,128]{3,2,1,0:T(8,128)(2,1)} %param.17, bf16[8,2,16,128]{3,0,2,1:T(8,128)(2,1)} %bitcast.60, pred[8,33]{1,0:T(8,128)(4,1)S(1)} %fusion.56), kind=kOutput, calls=%fused_computation.82 | convolution fusion | flops 2475296 | bytes 201992 | tf_op jit(solution)/shard_map/sub | solution.py:44
  2.9 0.0 copy-done.12
  2.9 0.0 copy-done.13
  2.9 0.0 copy-done.14
  2.9 0.0 copy-start.7
  2.9 0.5 %fusion.31 = f32[8,2,16,128]{3,2,1,0:T(8,128)S(1)} fusion(bf16[8,2,1,128]{3,2,1,0:T(2,128)(2,1)S(1)} %copy.34, bf16[8,2,32,128]{3,2,1,0:T(8,128)(2,1)S(1)} %copy-done.12, f32[8,2,16]{2,1,0:T(2,128)S(1)} %fusion.87, pred[8,33]{1,0:T(8,128)(4,1)S(1)} %fusion.56, bf16[8,2,1,128]{3,2,1,0:T(2,128)(2,1)S(1)} %copy.31, bf16[8,2,32,128]{3,2,1,0:T(8,128)(2,1)S(1)} %copy-done.13, ...), kind=kOutput, calls=%fused_computation.39 | convolution fusion | flops 4917024 | bytes 468232 | tf_op jit(solution)/shard_map/rgjp,rgpd->rgjd/dot_general | solution.py:47
  3.4 0.3 copy-done.7
  3.8 0.2 fusion.35
  4.0 0.5 %collective-permute-start = (f32[8]{0:T(128)S(1)}, f32[8]{0:T(128)S(1)}, u32[]{:S(2)}, u32[]{:S(2)}) collective-permute-start(f32[8]{0:T(128)S(1)} %get-tuple-element.9), channel_id=1, source_target_pairs={{0,1},{1,0},{2,3},{3,2},{4,5},{5,4},{6,7},{7,6},{8,9},{9,8},{10,11... | collective-permute-start | bytes 104 | tf_op jit(solution)/shard_map/ppermute | solution.py:18
  4.5 0.0 copy-start.8
  4.5 0.0 copy-start.9
  4.5 0.7 %copy-done.8 = s32[8,4]{0,1:T(4,128)S(1)} copy-done((s32[8,4]{0,1:T(4,128)S(1)}, s32[8,4]{0,1:T(4,128)}, u32[]{:S(2)}) %copy-start.8) | copy-done | bytes 152
  5.2 0.2 reduce_window_sum.11
  5.4 0.0 copy-done.9
  5.4 0.0 collective-permute-done
  5.4 0.1 fusion.37
  5.5 0.0 copy-start.3
  5.5 0.2 convolution_convert_fusion.1
  5.7 0.8 %copy.36 = bf16[8,2,4096]{2,1,0:T(2,128)(2,1)} copy(bf16[8,2,4096]{2,0,1:T(8,128)(2,1)S(1)} %convolution_convert_fusion.1) | data formatting | bytes 262144 | tf_op jit(solution)/shard_map/convert_element_type | solution.py:148
  6.5 7.1 %all-to-all-start = ((bf16[8,2,4096]{2,1,0:T(2,128)(2,1)}), bf16[8,2,4096]{2,1,0:T(2,128)(2,1)S(1)}, u32[]{:S(2)}, u32[]{:S(2)}) async-start(bf16[8,2,4096]{2,1,0:T(2,128)(2,1)} %copy.36), calls=%async_computation | async-start | bytes 262144 | tf_op jit(solution)/shard_map/all_to_all | solution.py:149
  13.6 0.0 collective-permute-start.1
  13.6 7.4 %all-to-all-done = bf16[8,2,4096]{2,1,0:T(2,128)(2,1)S(1)} async-done(((bf16[8,2,4096]{2,1,0:T(2,128)(2,1)}), bf16[8,2,4096]{2,1,0:T(2,128)(2,1)S(1)}, u32[]{:S(2)}, u32[]{:S(2)}) %all-to-all-start) | async-done | bytes 131104 | tf_op jit(solution)/shard_map/all_to_all | solution.py:149
  21.1 0.1 reshape.60
  21.1 0.0 copy-start.5
  21.1 0.1 collective-permute-start.2
  21.2 0.0 copy-done.3
  21.2 0.2 fusion.26
  21.4 0.0 copy-done.4
  21.4 0.2 fusion.23
  21.6 0.9 %collective-permute-done.2 = bf16[16,4096]{1,0:T(8,128)(2,1)S(1)} collective-permute-done((bf16[16,4096]{1,0:T(8,128)(2,1)S(1)}, bf16[16,4096]{1,0:T(8,128)(2,1)S(1)}, u32[]{:S(2)}, u32[]{:S(2)}) %collective-permute-start.2) | collective-permute-done | bytes 131104 | tf_op jit(solution)/shard_map/ppermute | solution.py:18
  22.5 0.2 convolution_add_fusion.2
  22.7 0.0 copy-done.5
  22.7 0.0 copy-start.1
  22.7 0.2 fusion.10
  22.9 0.0 copy-done.6
  23.0 0.2 convolution_convert_fusion
  23.1 0.2 collective-permute-start.3
  23.3 0.0 collective-permute-done.1
  23.4 0.0 copy-start.2
  23.4 1.2 %collective-permute-done.3 = bf16[8,2,4096]{2,0,1:T(8,128)(2,1)S(1)} collective-permute-done((bf16[8,2,4096]{2,0,1:T(8,128)(2,1)S(1)}, bf16[8,2,4096]{2,0,1:T(8,128)(2,1)S(1)}, u32[]{:S(2)}, u32[]{:S(2)}) %collective-permute-start.3) | collective-permute-done | bytes 131104 | tf_op jit(solution)/shard_map/ppermute | solution.py:18
  24.5 0.2 add_convert_fusion
  24.7 0.8 %copy.39 = bf16[8,2,4096]{2,1,0:T(2,128)(2,1)} copy(bf16[8,2,4096]{2,0,1:T(8,128)(2,1)S(1)} %add_convert_fusion) | data formatting | bytes 262144 | tf_op jit(solution)/shard_map/optimization_barrier | solution.py:157
  25.5 3.4 %all-to-all-start.1 = ((bf16[8,2,4096]{2,1,0:T(2,128)(2,1)}), bf16[8,2,4096]{2,1,0:T(2,128)(2,1)S(1)}, u32[]{:S(2)}, u32[]{:S(2)}) async-start(bf16[8,2,4096]{2,1,0:T(2,128)(2,1)} %copy.39), calls=%async_computation.1 | async-start | bytes 262144 | tf_op jit(solution)/shard_map/all_to_all | solution.py:158
  28.9 0.0 copy-done.1
  28.9 0.4 fusion.92
  29.3 0.0 copy-done.2
  29.3 0.4 %fusion.11 = bf16[8,64]{1,0:T(8,128)(2,1)S(1)} fusion(bf16[8,8192]{1,0:T(8,128)(2,1)S(1)} %maximum_select_fusion, bf16[64,8192]{1,0:T(8,128)(2,1)S(1)} %copy-done.2, f32[8,64]{1,0:T(8,128)S(1)} %fusion.92), kind=kOutput, calls=%fused_computation.18 | convolution fusion | flops 8391680 | bytes 1182720 | tf_op jit(solution)/shard_map/rd,nd->rn/dot_general | solution.py:62
  29.6 0.0 copy-done
  29.7 0.2 fusion.12
  29.8 0.2 collective-permute-start.4
  30.0 6.3 %all-to-all-done.1 = bf16[8,2,4096]{2,1,0:T(2,128)(2,1)S(1)} async-done(((bf16[8,2,4096]{2,1,0:T(2,128)(2,1)}), bf16[8,2,4096]{2,1,0:T(2,128)(2,1)S(1)}, u32[]{:S(2)}, u32[]{:S(2)}) %all-to-all-start.1) | async-done | bytes 131104 | tf_op jit(solution)/shard_map/all_to_all | solution.py:158
  36.4 0.1 reshape.62
  36.5 0.3 fusion.93
  36.7 0.0 collective-permute-done.4
  36.7 0.8 %fusion.3 = bf16[8,4096]{1,0:T(8,128)(2,1)} fusion(f32[8,4096]{1,0:T(8,128)S(1)} %fusion.93, f32[8,4096]{1,0:T(8,128)S(1)} %collective-permute-done.4, bf16[8,64]{1,0:T(8,128)(2,1)S(1)} %fusion.11, bf16[64,8192]{1,0:T(8,128)(2,1)S(1)} %copy-done, s32[]{:T(128)S(6)} %select_n.35, bf16[8,4096]{1,0:T(8,128)(2,1)S(1)} %get-tuple-element.10), kind=kOutput, calls=%fused_computation.6 | convolution fusion | flops 4358144 | bytes 919556 | tf_op jit(solution)/shard_map/...n,nd->...d/dot_general | solution.py:69
  (13 shorter events, 0.1 us)
Async XLA Ops:
  0.0 29.6 %copy-start = (bf16[64,8192]{1,0:T(8,128)(2,1)S(1)}, bf16[64,8192]{1,0:T(8,128)(2,1)}, u32[]{:S(2)}) copy-start(bf16[64,8192]{1,0:T(8,128)(2,1)} %param.25) | copy-start | bytes 3145732
  0.0 0.8 %copy-start.10 = (bf16[8,2,128]{2,1,0:T(2,128)(2,1)S(1)}, bf16[8,2,128]{2,1,0:T(2,128)(2,1)}, u32[]{:S(2)}) copy-start(bf16[8,2,128]{2,1,0:T(2,128)(2,1)} %param.20) | copy-start | bytes 12292
  0.8 0.7 %copy-start.11 = (s32[8]{0:T(128)S(1)}, s32[8]{0:T(128)}, u32[]{:S(2)}) copy-start(s32[8]{0:T(128)} %param.21) | copy-start | bytes 100
  1.5 1.4 %copy-start.12 = (bf16[8,2,32,128]{3,2,1,0:T(8,128)(2,1)S(1)}, bf16[8,2,32,128]{3,2,1,0:T(8,128)(2,1)}, u32[]{:S(2)}) copy-start(bf16[8,2,32,128]{3,2,1,0:T(8,128)(2,1)} %param.18) | copy-start | bytes 393220
  1.5 1.4 %copy-start.13 = (bf16[8,2,32,128]{3,2,1,0:T(8,128)(2,1)S(1)}, bf16[8,2,32,128]{3,2,1,0:T(8,128)(2,1)}, u32[]{:S(2)}) copy-start(bf16[8,2,32,128]{3,2,1,0:T(8,128)(2,1)} %param.17) | copy-start | bytes 393220
  1.5 1.4 %copy-start.14 = (bf16[8,4096]{1,0:T(8,128)(2,1)S(1)}, bf16[8,4096]{1,0:T(8,128)(2,1)}, u32[]{:S(2)}) copy-start(bf16[8,4096]{1,0:T(8,128)(2,1)} %param.16) | copy-start | bytes 196612
  2.9 0.8 %copy-start.7 = (bf16[8,4096]{1,0:T(8,128)(2,1)S(1)}, bf16[8,4096]{1,0:T(8,128)(2,1)}, u32[]{:S(2)}) copy-start(bf16[8,4096]{1,0:T(8,128)(2,1)} %param.15) | copy-start | bytes 196612
  4.0 1.4 %collective-permute-start = (f32[8]{0:T(128)S(1)}, f32[8]{0:T(128)S(1)}, u32[]{:S(2)}, u32[]{:S(2)}) collective-permute-start(f32[8]{0:T(128)S(1)} %get-tuple-element.9), channel_id=1, source_target_pairs={{0,1},{1,0},{2,3},{3,2},{4,5},{5,4},{6,7},{7,6},{8,9},{9,8},{10,11... | collective-permute-start | bytes 104 | tf_op jit(solution)/shard_map/ppermute | solution.py:18
  4.5 0.7 %copy-start.8 = (s32[8,4]{0,1:T(4,128)S(1)}, s32[8,4]{0,1:T(4,128)}, u32[]{:S(2)}) copy-start(s32[8,4]{0,1:T(4,128)} %param.29) | copy-start | bytes 388
  4.5 0.9 %copy-start.9 = (bf16[8192]{0:T(1024)(128)(2,1)S(1)}, bf16[8192]{0:T(1024)(128)(2,1)}, u32[]{:S(2)}) copy-start(bf16[8192]{0:T(1024)(128)(2,1)} %param.22) | copy-start | bytes 49156
  5.5 15.7 %copy-start.3 = (bf16[32,8192]{1,0:T(8,128)(2,1)S(1)}, bf16[32,8192]{1,0:T(8,128)(2,1)}, u32[]{:S(2)}) copy-start(bf16[32,8192]{1,0:T(8,128)(2,1)} %param.26) | copy-start | bytes 1572868
  6.5 14.9 %copy-start.4 = (bf16[32,8192]{1,0:T(8,128)(2,1)S(1)}, bf16[32,8192]{1,0:T(8,128)(2,1)}, u32[]{:S(2)}) copy-start(bf16[32,8192]{1,0:T(8,128)(2,1)} %param.27) | copy-start | bytes 1572868
  6.5 14.6 %all-to-all-start = ((bf16[8,2,4096]{2,1,0:T(2,128)(2,1)}), bf16[8,2,4096]{2,1,0:T(2,128)(2,1)S(1)}, u32[]{:S(2)}, u32[]{:S(2)}) async-start(bf16[8,2,4096]{2,1,0:T(2,128)(2,1)} %copy.36), calls=%async_computation | async-start | bytes 262144 | tf_op jit(solution)/shard_map/all_to_all | solution.py:149
  13.6 9.8 %collective-permute-start.1 = (bf16[8,4096]{1,0:T(8,128)(2,1)S(1)}, bf16[8,4096]{1,0:T(8,128)(2,1)S(1)}, u32[]{:S(2)}, u32[]{:S(2)}) collective-permute-start(bf16[8,4096]{1,0:T(8,128)(2,1)S(1)} %fusion.37), channel_id=1, source_target_pairs={{0,1},{1,0},{2,3},{3,2},{4,5},{5,4},{6,7},{7,6},{8,9},{9,8},{10,11... | collective-permute-start | bytes 196616 | tf_op jit(solution)/shard_map/ppermute | solution.py:18
  21.1 1.6 %copy-start.5 = (bf16[32,8192]{1,0:T(8,128)(2,1)S(1)}, bf16[32,8192]{1,0:T(8,128)(2,1)}, u32[]{:S(2)}) copy-start(bf16[32,8192]{1,0:T(8,128)(2,1)} %param.27) | copy-start | bytes 1572868
  21.1 1.4 %collective-permute-start.2 = (bf16[16,4096]{1,0:T(8,128)(2,1)S(1)}, bf16[16,4096]{1,0:T(8,128)(2,1)S(1)}, u32[]{:S(2)}, u32[]{:S(2)}) collective-permute-start(bf16[16,4096]{1,0:T(8,128)(2,1)S(1)} %reshape.60), channel_id=1, source_target_pairs={{0,1},{1,0},{2,3},{3,2},{4,5},{5,4},{6,7},{7,6},{8,9},{9,8},{10,11... | collective-permute-start | bytes 393224 | tf_op jit(solution)/shard_map/ppermute | solution.py:18
  21.4 1.5 %copy-start.6 = (bf16[32,8192]{1,0:T(8,128)(2,1)S(1)}, bf16[32,8192]{1,0:T(8,128)(2,1)}, u32[]{:S(2)}) copy-start(bf16[32,8192]{1,0:T(8,128)(2,1)} %param.28) | copy-start | bytes 1572868
  22.7 6.1 %copy-start.1 = (bf16[64,8192]{1,0:T(8,128)(2,1)S(1)}, bf16[64,8192]{1,0:T(8,128)(2,1)}, u32[]{:S(2)}) copy-start(bf16[64,8192]{1,0:T(8,128)(2,1)} %param.23) | copy-start | bytes 3145732
  23.1 1.4 %collective-permute-start.3 = (bf16[8,2,4096]{2,0,1:T(8,128)(2,1)S(1)}, bf16[8,2,4096]{2,0,1:T(8,128)(2,1)S(1)}, u32[]{:S(2)}, u32[]{:S(2)}) collective-permute-start(bf16[8,2,4096]{2,0,1:T(8,128)(2,1)S(1)} %convolution_convert_fusion), channel_id=1, source_target_pairs={{0,1},{1,0},{2,3},{3,2},{4,5},{5,4},{6,7},{7,6},{8,9},{9,8},{10,11... | collective-permute-start | bytes 393224 | tf_op jit(solution)/shard_map/ppermute | solution.py:18
  23.4 5.9 %copy-start.2 = (bf16[64,8192]{1,0:T(8,128)(2,1)S(1)}, bf16[64,8192]{1,0:T(8,128)(2,1)}, u32[]{:S(2)}) copy-start(bf16[64,8192]{1,0:T(8,128)(2,1)} %param.24) | copy-start | bytes 3145732
  25.5 10.9 %all-to-all-start.1 = ((bf16[8,2,4096]{2,1,0:T(2,128)(2,1)}), bf16[8,2,4096]{2,1,0:T(2,128)(2,1)S(1)}, u32[]{:S(2)}, u32[]{:S(2)}) async-start(bf16[8,2,4096]{2,1,0:T(2,128)(2,1)} %copy.39), calls=%async_computation.1 | async-start | bytes 262144 | tf_op jit(solution)/shard_map/all_to_all | solution.py:158
  29.8 6.9 %collective-permute-start.4 = (f32[8,4096]{1,0:T(8,128)S(1)}, f32[8,4096]{1,0:T(8,128)S(1)}, u32[]{:S(2)}, u32[]{:S(2)}) collective-permute-start(f32[8,4096]{1,0:T(8,128)S(1)} %fusion.12), channel_id=1, source_target_pairs={{0,1},{1,0},{2,3},{3,2},{4,5},{5,4},{6,7},{7,6},{8,9},{9,8},{10,11... | collective-permute-start | bytes 393224 | tf_op jit(solution)/shard_map/ppermute | solution.py:18

commit v20 on v14

--- a/solution.py
+++ b/solution.py
@@ -141,12 +141,13 @@
     hot_kept, hot_given = swiglu_halves(
         normed_late, hot_gate, hot_up, hot_down, myself, (request_count,)
     )
-    hot_total = hot_kept + partner(hot_given, "heads", 0)
+    hot_received = partner(hot_given, "heads", 0)
+    settled = lax.optimization_barrier(stream.astype(jnp.float32) + hot_kept)
     cold_sum = collect_rows(
         selector.astype(jnp.float32),
         returned.reshape(owner_count * CAP, -1).astype(jnp.float32),
     )
-    result = stream.astype(jnp.float32) + hot_total + cold_sum
+    result = settled + hot_received + cold_sum
     return result.astype(jnp.bfloat16)
 
 

time: 37.8 us -> 37.6 us (level)
    dot_general x2, matrix products: 0.99 us -> 0.35 us  [swiglu_halves(): jnp.einsum('...n,nd->...d', hidden, down_kept, preferred_element_type=jnp...]
    dot_general x1, matrix products: 0.26 us -> 0.89 us  [collect_rows(): lax.dot_general(selector, returned, (((0,), (0,)), ((), ())), precision=l...]
where the time goes in v20:
time: 37.6 us; the launch traced here: 37.2 us
  blocking collectives  14.3 us (38%)
  waiting for transfers between devices  8.15 us (22%)
  starting transfers between devices  4.84 us (13%)
  matrix products  4.63 us (12%)
  local copies, waits for them, and re-layouts  4.27 us (11%)
  other arithmetic  0.82 us (2%)
    all_to_all x1, blocking collectives, local(): lax.all_to_all(outgoing, 'rows', split_axis=0, concat_axis=0, tiled=True)  14.3 us
    all_to_all x1, waiting for transfers between devices, local(): lax.all_to_all(owner_sum, 'rows', split_axis=0, concat_axis=0, tiled=True)  6.15 us
    all_to_all x1, starting transfers between devices, local(): lax.all_to_all(owner_sum, 'rows', split_axis=0, concat_axis=0, tiled=True)  3.37 us
    unnamed x24, local copies, waits for them, and re-layouts  2.44 us
    ppermute x5, waiting for transfers between devices, partner(): return lax.ppermute(block, axis, route)  1.99 us
    ppermute x5, starting transfers between devices, partner(): return lax.ppermute(block, axis, route)  1.47 us
    dot_general x1, matrix products, attention_rows(): jnp.einsum('rgjd,rgpd->rgjp', queries, keys_all, preferred_element_type=j...  1.11 us
    dot_general x1, matrix products, collect_rows(): lax.dot_general(selector, returned, (((0,), (0,)), ((), ())), precision=l...  0.89 us
  transfers between devices with their start and end apart: 6, of which 3 were waited for; matrix products, arithmetic and copies ran while one was open for 6% of the time, Pallas kernels for 0%

profile of v20, /device:TPU:0, one launch (start us, length us, event | category | flops | bytes accessed | tf_op | source)
XLA Modules:
  0.0 37.2 jit_solution(13418200579976847765)
XLA Ops:
  0.0 0.0 copy-start
  0.0 0.8 %broadcast_in_dim.46 = bf16[8,2,8,128]{3,2,1,0:T(8,128)(2,1)S(1)} broadcast(bf16[8,2,128]{2,1,0:T(2,128)(2,1)} %param.19), dimensions={0,1,3} | broadcast | bytes 36864 | tf_op jit(solution)/shard_map/broadcast_in_dim | solution.py:36
  0.8 0.0 copy-start.8
  0.8 1.1 %fusion.4 = f32[8,2,16,40]{3,2,1,0:T(8,128)S(1)} fusion(bf16[8,2,8,128]{3,2,1,0:T(8,128)(2,1)S(1)} %broadcast_in_dim.46, bf16[8,2,32,128]{3,2,1,0:T(8,128)(2,1)} %param.17, bf16[8,2,16,128]{3,0,2,1:T(8,128)(2,1)} %bitcast.44), kind=kOutput, calls=%fused_computation.8 | convolution fusion | flops 2959360 | bytes 270336 | tf_op jit(solution)/shard_map/rgjd,rgpd->rgjp/dot_general | solution.py:42
  1.9 0.0 copy-done.8
  1.9 0.0 copy-start.11
  1.9 0.1 fusion.41
  2.0 0.0 copy-start.7
  2.0 0.2 fusion.58
  2.2 0.5 %copy-done.7 = bf16[8,2,128]{2,1,0:T(2,128)(2,1)S(1)} copy-done((bf16[8,2,128]{2,1,0:T(2,128)(2,1)S(1)}, bf16[8,2,128]{2,1,0:T(2,128)(2,1)}, u32[]{:S(2)}) %copy-start.7) | copy-done | bytes 4120
  2.7 0.1 copy-done.11
  2.8 0.0 copy-start.4
  2.8 0.5 %fusion.19 = f32[8,2,16,128]{3,2,1,0:T(8,128)S(1)} fusion(bf16[8,2,8,128]{3,2,1,0:T(8,128)(2,1)S(1)} %broadcast_in_dim.49, bf16[8,2,32,128]{3,2,1,0:T(8,128)(2,1)S(1)} %copy-done.11, f32[8,2,16]{2,1,0:T(2,128)S(1)} %fusion.58, f32[8,2,16,40]{3,2,1,0:T(8,128)S(1)} %fusion.4, pred[8,40]{1,0:T(8,128)(4,1)S(1)} %fusion.41), kind=kOutput, calls=%fused_computation.26 | convolution fusion | flops 3000615 | bytes 337216 | tf_op jit(solution)/shard_map/rgjp,rgpd->rgjd/dot_general | solution.py:52
  3.3 0.3 copy-done.4
  3.7 0.2 fusion.23
  3.9 0.5 %collective-permute-start = (f32[8]{0:T(128)S(1)}, f32[8]{0:T(128)S(1)}, u32[]{:S(2)}, u32[]{:S(2)}) collective-permute-start(f32[8]{0:T(128)S(1)} %get-tuple-element.9), channel_id=1, source_target_pairs={{0,1},{1,0},{2,3},{3,2},{4,5},{5,4},{6,7},{7,6},{8,9},{9,8},{10,11... | collective-permute-start | bytes 104 | tf_op jit(solution)/shard_map/ppermute | solution.py:18
  4.4 0.0 copy-start.5
  4.4 0.0 copy-start.6
  4.4 0.7 %copy-done.5 = s32[8,4]{0,1:T(4,128)S(1)} copy-done((s32[8,4]{0,1:T(4,128)S(1)}, s32[8,4]{0,1:T(4,128)}, u32[]{:S(2)}) %copy-start.5) | copy-done | bytes 152
  5.1 0.2 reduce_window_sum.11
  5.3 0.0 copy-done.6
  5.3 0.0 collective-permute-done
  5.3 0.1 fusion.25
  5.4 0.0 copy-start.9
  5.4 0.2 convolution_convert_fusion.1
  5.6 0.1 copy.28
  5.7 14.3 %all_to_all.10 = bf16[8,2,4096]{2,1,0:T(2,128)(2,1)S(1)} all-to-all(bf16[8,2,4096]{2,1,0:T(2,128)(2,1)S(1)} %copy.28), channel_id=1, replica_groups=mesh['groups'=2,'rows'=8,'heads'=2] {'rows'}, dimensions={0} | all-to-all | bytes 262144 | tf_op jit(solution)/shard_map/all_to_all | solution.py:132
  20.0 0.1 reshape.62
  20.0 0.1 collective-permute-start.2
  20.1 0.0 copy-start.10
  20.1 0.5 %collective-permute-start.1 = (bf16[8,4096]{1,0:T(8,128)(2,1)S(1)}, bf16[8,4096]{1,0:T(8,128)(2,1)S(1)}, u32[]{:S(2)}, u32[]{:S(2)}) collective-permute-start(bf16[8,4096]{1,0:T(8,128)(2,1)S(1)} %fusion.25), channel_id=1, source_target_pairs={{0,1},{1,0},{2,3},{3,2},{4,5},{5,4},{6,7},{7,6},{8,9},{9,8},{10,11... | collective-permute-start | bytes 196616 | tf_op jit(solution)/shard_map/ppermute | solution.py:18
  20.6 0.8 %collective-permute-done.2 = bf16[16,4096]{1,0:T(8,128)(2,1)S(1)} collective-permute-done((bf16[16,4096]{1,0:T(8,128)(2,1)S(1)}, bf16[16,4096]{1,0:T(8,128)(2,1)S(1)}, u32[]{:S(2)}, u32[]{:S(2)}) %collective-permute-start.2) | collective-permute-done | bytes 131104 | tf_op jit(solution)/shard_map/ppermute | solution.py:18
  21.5 0.0 copy-done.9
  21.5 0.2 fusion.34
  21.7 0.0 copy-done.10
  21.7 0.0 copy-start.3
  21.7 0.3 multiply_convert_fusion
  22.0 0.0 copy-start.1
  22.0 0.8 %copy-done.3 = bf16[32,8192]{1,0:T(8,128)(2,1)S(1)} copy-done((bf16[32,8192]{1,0:T(8,128)(2,1)S(1)}, bf16[32,8192]{1,0:T(8,128)(2,1)}, u32[]{:S(2)}) %copy-start.3) | copy-done | bytes 524312
  22.8 0.2 convolution_convert_fusion
  22.9 0.2 collective-permute-start.3
  23.2 0.0 collective-permute-done.1
  23.2 0.0 copy-start.2
  23.2 1.2 %collective-permute-done.3 = bf16[8,2,4096]{2,0,1:T(8,128)(2,1)S(1)} collective-permute-done((bf16[8,2,4096]{2,0,1:T(8,128)(2,1)S(1)}, bf16[8,2,4096]{2,0,1:T(8,128)(2,1)S(1)}, u32[]{:S(2)}, u32[]{:S(2)}) %collective-permute-start.3) | collective-permute-done | bytes 131104 | tf_op jit(solution)/shard_map/ppermute | solution.py:18
  24.4 0.2 add_convert_fusion
  24.5 0.8 %copy.31 = bf16[8,2,4096]{2,1,0:T(2,128)(2,1)} copy(bf16[8,2,4096]{2,0,1:T(8,128)(2,1)S(1)} %add_convert_fusion) | data formatting | bytes 262144 | tf_op jit(solution)/shard_map/optimization_barrier | solution.py:139
  25.3 3.4 %all-to-all-start.1 = ((bf16[8,2,4096]{2,1,0:T(2,128)(2,1)}), bf16[8,2,4096]{2,1,0:T(2,128)(2,1)S(1)}, u32[]{:S(2)}, u32[]{:S(2)}) async-start(bf16[8,2,4096]{2,1,0:T(2,128)(2,1)} %copy.31), calls=%async_computation.1 | async-start | bytes 262144 | tf_op jit(solution)/shard_map/all_to_all | solution.py:140
  28.7 0.0 copy-done.1
  28.7 0.4 fusion.59
  29.1 0.0 copy-done.2
  29.1 0.4 %fusion.5 = bf16[8,64]{1,0:T(8,128)(2,1)S(1)} fusion(bf16[8,8192]{1,0:T(8,128)(2,1)S(1)} %maximum_select_fusion.1, bf16[64,8192]{1,0:T(8,128)(2,1)S(1)} %copy-done.2, f32[8,64]{1,0:T(8,128)S(1)} %fusion.59), kind=kOutput, calls=%fused_computation.10 | convolution fusion | flops 8391680 | bytes 1182720 | tf_op jit(solution)/shard_map/rd,nd->rn/dot_general | solution.py:67
  29.5 0.0 copy-done
  29.5 0.2 fusion.6
  29.7 0.2 collective-permute-start.4
  29.9 0.2 convolution_add_fusion
  30.0 6.2 %all-to-all-done.1 = bf16[8,2,4096]{2,1,0:T(2,128)(2,1)S(1)} async-done(((bf16[8,2,4096]{2,1,0:T(2,128)(2,1)}), bf16[8,2,4096]{2,1,0:T(2,128)(2,1)S(1)}, u32[]{:S(2)}, u32[]{:S(2)}) %all-to-all-start.1) | async-done | bytes 131104 | tf_op jit(solution)/shard_map/all_to_all | solution.py:140
  36.2 0.1 reshape.64
  36.3 0.0 collective-permute-done.4
  36.3 0.9 %add_convert_fusion.1 = bf16[8,4096]{1,0:T(8,128)(2,1)} fusion(f32[8,4096]{1,0:T(8,128)S(1)} %convolution_add_fusion, f32[8,4096]{1,0:T(8,128)S(1)} %collective-permute-done.4, f32[16,8]{1,0:T(8,128)S(1)} %bitcast.38, bf16[16,4096]{1,0:T(8,128)(2,1)S(1)} %reshape.64), kind=kOutput, calls=%fused_computation.36 | convolution fusion | flops 6389760 | bytes 459264 | tf_op jit(solution)/shard_map/dot_general | solution.py:79
  (10 shorter events, 0.1 us)
Async XLA Ops:
  0.0 29.5 %copy-start = (bf16[64,8192]{1,0:T(8,128)(2,1)S(1)}, bf16[64,8192]{1,0:T(8,128)(2,1)}, u32[]{:S(2)}) copy-start(bf16[64,8192]{1,0:T(8,128)(2,1)} %param.25) | copy-start | bytes 3145732
  0.8 1.1 %copy-start.8 = (s32[8]{0:T(128)S(1)}, s32[8]{0:T(128)}, u32[]{:S(2)}) copy-start(s32[8]{0:T(128)} %param.21) | copy-start | bytes 100
  1.9 0.9 %copy-start.11 = (bf16[8,2,32,128]{3,2,1,0:T(8,128)(2,1)S(1)}, bf16[8,2,32,128]{3,2,1,0:T(8,128)(2,1)}, u32[]{:S(2)}) copy-start(bf16[8,2,32,128]{3,2,1,0:T(8,128)(2,1)} %param.18) | copy-start | bytes 393220
  2.0 0.7 %copy-start.7 = (bf16[8,2,128]{2,1,0:T(2,128)(2,1)S(1)}, bf16[8,2,128]{2,1,0:T(2,128)(2,1)}, u32[]{:S(2)}) copy-start(bf16[8,2,128]{2,1,0:T(2,128)(2,1)} %param.20) | copy-start | bytes 12292
  2.8 0.8 %copy-start.4 = (bf16[8,4096]{1,0:T(8,128)(2,1)S(1)}, bf16[8,4096]{1,0:T(8,128)(2,1)}, u32[]{:S(2)}) copy-start(bf16[8,4096]{1,0:T(8,128)(2,1)} %param.15) | copy-start | bytes 196612
  3.9 1.4 %collective-permute-start = (f32[8]{0:T(128)S(1)}, f32[8]{0:T(128)S(1)}, u32[]{:S(2)}, u32[]{:S(2)}) collective-permute-start(f32[8]{0:T(128)S(1)} %get-tuple-element.9), channel_id=1, source_target_pairs={{0,1},{1,0},{2,3},{3,2},{4,5},{5,4},{6,7},{7,6},{8,9},{9,8},{10,11... | collective-permute-start | bytes 104 | tf_op jit(solution)/shard_map/ppermute | solution.py:18
  4.4 0.7 %copy-start.5 = (s32[8,4]{0,1:T(4,128)S(1)}, s32[8,4]{0,1:T(4,128)}, u32[]{:S(2)}) copy-start(s32[8,4]{0,1:T(4,128)} %param.29) | copy-start | bytes 388
  4.4 0.9 %copy-start.6 = (bf16[8192]{0:T(1024)(128)(2,1)S(1)}, bf16[8192]{0:T(1024)(128)(2,1)}, u32[]{:S(2)}) copy-start(bf16[8192]{0:T(1024)(128)(2,1)} %param.22) | copy-start | bytes 49156
  5.4 16.1 %copy-start.9 = (bf16[32,8192]{1,0:T(8,128)(2,1)S(1)}, bf16[32,8192]{1,0:T(8,128)(2,1)}, u32[]{:S(2)}) copy-start(bf16[32,8192]{1,0:T(8,128)(2,1)} %param.26) | copy-start | bytes 1572868
  20.0 1.4 %collective-permute-start.2 = (bf16[16,4096]{1,0:T(8,128)(2,1)S(1)}, bf16[16,4096]{1,0:T(8,128)(2,1)S(1)}, u32[]{:S(2)}, u32[]{:S(2)}) collective-permute-start(bf16[16,4096]{1,0:T(8,128)(2,1)S(1)} %reshape.62), channel_id=1, source_target_pairs={{0,1},{1,0},{2,3},{3,2},{4,5},{5,4},{6,7},{7,6},{8,9},{9,8},{10,11... | collective-permute-start | bytes 393224 | tf_op jit(solution)/shard_map/ppermute | solution.py:18
  20.1 1.6 %copy-start.10 = (bf16[32,8192]{1,0:T(8,128)(2,1)S(1)}, bf16[32,8192]{1,0:T(8,128)(2,1)}, u32[]{:S(2)}) copy-start(bf16[32,8192]{1,0:T(8,128)(2,1)} %param.27) | copy-start | bytes 1572868
  20.1 3.0 %collective-permute-start.1 = (bf16[8,4096]{1,0:T(8,128)(2,1)S(1)}, bf16[8,4096]{1,0:T(8,128)(2,1)S(1)}, u32[]{:S(2)}, u32[]{:S(2)}) collective-permute-start(bf16[8,4096]{1,0:T(8,128)(2,1)S(1)} %fusion.25), channel_id=1, source_target_pairs={{0,1},{1,0},{2,3},{3,2},{4,5},{5,4},{6,7},{7,6},{8,9},{9,8},{10,11... | collective-permute-start | bytes 196616 | tf_op jit(solution)/shard_map/ppermute | solution.py:18
  21.7 1.1 %copy-start.3 = (bf16[32,8192]{1,0:T(8,128)(2,1)S(1)}, bf16[32,8192]{1,0:T(8,128)(2,1)}, u32[]{:S(2)}) copy-start(bf16[32,8192]{1,0:T(8,128)(2,1)} %param.28) | copy-start | bytes 1572868
  22.0 6.7 %copy-start.1 = (bf16[64,8192]{1,0:T(8,128)(2,1)S(1)}, bf16[64,8192]{1,0:T(8,128)(2,1)}, u32[]{:S(2)}) copy-start(bf16[64,8192]{1,0:T(8,128)(2,1)} %param.23) | copy-start | bytes 3145732
  22.9 1.4 %collective-permute-start.3 = (bf16[8,2,4096]{2,0,1:T(8,128)(2,1)S(1)}, bf16[8,2,4096]{2,0,1:T(8,128)(2,1)S(1)}, u32[]{:S(2)}, u32[]{:S(2)}) collective-permute-start(bf16[8,2,4096]{2,0,1:T(8,128)(2,1)S(1)} %convolution_convert_fusion), channel_id=1, source_target_pairs={{0,1},{1,0},{2,3},{3,2},{4,5},{5,4},{6,7},{7,6},{8,9},{9,8},{10,11... | collective-permute-start | bytes 393224 | tf_op jit(solution)/shard_map/ppermute | solution.py:18
  23.2 5.9 %copy-start.2 = (bf16[64,8192]{1,0:T(8,128)(2,1)S(1)}, bf16[64,8192]{1,0:T(8,128)(2,1)}, u32[]{:S(2)}) copy-start(bf16[64,8192]{1,0:T(8,128)(2,1)} %param.24) | copy-start | bytes 3145732
  25.3 10.9 %all-to-all-start.1 = ((bf16[8,2,4096]{2,1,0:T(2,128)(2,1)}), bf16[8,2,4096]{2,1,0:T(2,128)(2,1)S(1)}, u32[]{:S(2)}, u32[]{:S(2)}) async-start(bf16[8,2,4096]{2,1,0:T(2,128)(2,1)} %copy.31), calls=%async_computation.1 | async-start | bytes 262144 | tf_op jit(solution)/shard_map/all_to_all | solution.py:140
  29.7 6.6 %collective-permute-start.4 = (f32[8,4096]{1,0:T(8,128)S(1)}, f32[8,4096]{1,0:T(8,128)S(1)}, u32[]{:S(2)}, u32[]{:S(2)}) collective-permute-start(f32[8,4096]{1,0:T(8,128)S(1)} %fusion.6), channel_id=1, source_target_pairs={{0,1},{1,0},{2,3},{3,2},{4,5},{5,4},{6,7},{7,6},{8,9},{9,8},{10,11... | collective-permute-start | bytes 393224 | tf_op jit(solution)/shard_map/ppermute | solution.py:18

commit v21 on v20

--- a/solution.py
+++ b/solution.py
@@ -38,9 +38,12 @@
     values_all = jnp.concatenate(
         [value_cache, jnp.broadcast_to(value_new[:, :, None, :], copies)], axis=2
     )
-    scores = lax.optimization_barrier(
-        jnp.einsum("rgjd,rgpd->rgjp", queries, keys_all, preferred_element_type=jnp.float32)
-        * scale_factor
+    scores, values_all = lax.optimization_barrier(
+        (
+            jnp.einsum("rgjd,rgpd->rgjp", queries, keys_all, preferred_element_type=jnp.float32)
+            * scale_factor,
+            values_all,
+        )
     )
     positions = jnp.arange(slots + 8, dtype=jnp.int32)[None, :]
     visible = ((positions < lengths[:, None]) | (positions == slots))[:, None, None, :]

time: 37.6 us -> 37.5 us (level)
  other arithmetic: 0.82 us -> 1.79 us
  matrix products: 4.63 us -> 3.72 us
    concatenate x0 -> x1, other arithmetic: none -> 0.97 us  [attention_rows(): jnp.concatenate([value_cache, jnp.broadcast_to(value_new[:, :, None, :],...]
    dot_general x1, matrix products: 1.11 us -> 0.19 us  [attention_rows(): jnp.einsum('rgjd,rgpd->rgjp', queries, keys_all, preferred_element_type=j...]
    broadcast_in_dim x1, local copies, waits for them, and re-layouts: 0.01 us -> 0.78 us  [attention_rows(): jnp.broadcast_to(value_new[:, :, None, :], copies)]
    broadcast_in_dim x1, local copies, waits for them, and re-layouts: 0.78 us -> 0.01 us  [attention_rows(): jnp.broadcast_to(key_new[:, :, None, :], copies)]
    unnamed x24 -> x26, local copies, waits for them, and re-layouts: 2.44 us -> 2.3 us
where the time goes in v21:
time: 37.5 us; the launch traced here: 37.1 us
  blocking collectives  14.3 us (38%)
  waiting for transfers between devices  8.15 us (22%)
  starting transfers between devices  4.84 us (13%)
  local copies, waits for them, and re-layouts  4.14 us (11%)
  matrix products  3.72 us (10%)
  other arithmetic  1.79 us (5%)
    all_to_all x1, blocking collectives, local(): lax.all_to_all(outgoing, 'rows', split_axis=0, concat_axis=0, tiled=True)  14.3 us
    all_to_all x1, waiting for transfers between devices, local(): lax.all_to_all(owner_sum, 'rows', split_axis=0, concat_axis=0, tiled=True)  6.15 us
    all_to_all x1, starting transfers between devices, local(): lax.all_to_all(owner_sum, 'rows', split_axis=0, concat_axis=0, tiled=True)  3.37 us
    unnamed x26, local copies, waits for them, and re-layouts  2.3 us
    ppermute x5, waiting for transfers between devices, partner(): return lax.ppermute(block, axis, route)  1.99 us
    ppermute x5, starting transfers between devices, partner(): return lax.ppermute(block, axis, route)  1.47 us
    concatenate x1, other arithmetic, attention_rows(): jnp.concatenate([value_cache, jnp.broadcast_to(value_new[:, :, None, :],...  0.97 us
    dot_general x1, matrix products, collect_rows(): lax.dot_general(selector, returned, (((0,), (0,)), ((), ())), precision=l...  0.89 us
  transfers between devices with their start and end apart: 6, of which 3 were waited for; matrix products, arithmetic and copies ran while one was open for 6% of the time, Pallas kernels for 0%

profile of v21, /device:TPU:0, one launch (start us, length us, event | category | flops | bytes accessed | tf_op | source)
XLA Modules:
  0.0 37.1 jit_solution(13995371544480932540)
XLA Ops:
  0.0 0.0 copy-start
  0.0 0.8 %broadcast_in_dim.47 = bf16[8,2,8,128]{3,2,1,0:T(8,128)(2,1)S(1)} broadcast(bf16[8,2,128]{2,1,0:T(2,128)(2,1)} %param.20), dimensions={0,1,3} | broadcast | bytes 36864 | tf_op jit(solution)/shard_map/broadcast_in_dim | solution.py:39
  0.8 0.0 copy-start.7
  0.8 0.0 copy-start.11
  0.8 0.0 copy-start.12
  0.8 1.0 %pad_maximum_fusion = bf16[8,2,40,128]{3,2,1,0:T(8,128)(2,1)S(1)} fusion(bf16[8,2,8,128]{3,2,1,0:T(8,128)(2,1)S(1)} %broadcast_in_dim.47, bf16[8,2,32,128]{3,2,1,0:T(8,128)(2,1)} %param.18), kind=kLoop, calls=%fused_computation.26 | loop fusion | flops 327680 | bytes 327680 | tf_op jit(solution)/shard_map/concatenate | solution.py:38
  1.8 0.0 copy-done.7
  1.8 0.0 copy-done.11
  1.8 0.0 copy-done.12
  1.8 0.0 copy-start.8
  1.8 0.2 fusion.4
  2.0 0.4 %copy-done.8 = s32[8]{0:T(128)S(1)} copy-done((s32[8]{0:T(128)S(1)}, s32[8]{0:T(128)}, u32[]{:S(2)}) %copy-start.8) | copy-done | bytes 56
  2.5 0.1 fusion.38
  2.6 0.2 fusion.54
  2.8 0.0 copy-start.4
  2.8 0.5 %fusion.24 = f32[8,2,16,128]{3,2,1,0:T(8,128)S(1)} fusion(bf16[8,2,40,128]{3,2,1,0:T(8,128)(2,1)S(1)} %pad_maximum_fusion, f32[8,2,16]{2,1,0:T(2,128)S(1)} %fusion.54, f32[8,2,16,40]{3,2,1,0:T(8,128)S(1)} %fusion.4, pred[8,40]{1,0:T(8,128)(4,1)S(1)} %fusion.38), kind=kOutput, calls=%fused_computation.37 | convolution fusion | flops 2672935 | bytes 337216 | tf_op jit(solution)/shard_map/rgjp,rgpd->rgjd/dot_general | solution.py:55
  3.3 0.3 copy-done.4
  3.6 0.2 fusion.19
  3.8 0.5 %collective-permute-start = (f32[8]{0:T(128)S(1)}, f32[8]{0:T(128)S(1)}, u32[]{:S(2)}, u32[]{:S(2)}) collective-permute-start(f32[8]{0:T(128)S(1)} %get-tuple-element.13), channel_id=1, source_target_pairs={{0,1},{1,0},{2,3},{3,2},{4,5},{5,4},{6,7},{7,6},{8,9},{9,8},{10,11... | collective-permute-start | bytes 104 | tf_op jit(solution)/shard_map/ppermute | solution.py:18
  4.3 0.0 copy-start.5
  4.3 0.0 copy-start.6
  4.3 0.7 %copy-done.5 = s32[8,4]{0,1:T(4,128)S(1)} copy-done((s32[8,4]{0,1:T(4,128)S(1)}, s32[8,4]{0,1:T(4,128)}, u32[]{:S(2)}) %copy-start.5) | copy-done | bytes 152
  5.0 0.2 reduce_window_sum.11
  5.2 0.0 copy-done.6
  5.3 0.0 collective-permute-done
  5.3 0.1 fusion.21
  5.4 0.0 copy-start.9
  5.4 0.2 convolution_convert_fusion.1
  5.6 0.1 copy.28
  5.7 14.3 %all_to_all.10 = bf16[8,2,4096]{2,1,0:T(2,128)(2,1)S(1)} all-to-all(bf16[8,2,4096]{2,1,0:T(2,128)(2,1)S(1)} %copy.28), channel_id=1, replica_groups=mesh['groups'=2,'rows'=8,'heads'=2] {'rows'}, dimensions={0} | all-to-all | bytes 262144 | tf_op jit(solution)/shard_map/all_to_all | solution.py:135
  20.0 0.1 reshape.62
  20.0 0.1 collective-permute-start.2
  20.1 0.0 copy-start.10
  20.1 0.5 %collective-permute-start.1 = (bf16[8,4096]{1,0:T(8,128)(2,1)S(1)}, bf16[8,4096]{1,0:T(8,128)(2,1)S(1)}, u32[]{:S(2)}, u32[]{:S(2)}) collective-permute-start(bf16[8,4096]{1,0:T(8,128)(2,1)S(1)} %fusion.21), channel_id=1, source_target_pairs={{0,1},{1,0},{2,3},{3,2},{4,5},{5,4},{6,7},{7,6},{8,9},{9,8},{10,11... | collective-permute-start | bytes 196616 | tf_op jit(solution)/shard_map/ppermute | solution.py:18
  20.6 0.8 %collective-permute-done.2 = bf16[16,4096]{1,0:T(8,128)(2,1)S(1)} collective-permute-done((bf16[16,4096]{1,0:T(8,128)(2,1)S(1)}, bf16[16,4096]{1,0:T(8,128)(2,1)S(1)}, u32[]{:S(2)}, u32[]{:S(2)}) %collective-permute-start.2) | collective-permute-done | bytes 131104 | tf_op jit(solution)/shard_map/ppermute | solution.py:18
  21.4 0.0 copy-done.9
  21.4 0.2 fusion.31
  21.7 0.0 copy-done.10
  21.7 0.0 copy-start.3
  21.7 0.3 multiply_convert_fusion
  21.9 0.0 copy-start.1
  21.9 0.8 %copy-done.3 = bf16[32,8192]{1,0:T(8,128)(2,1)S(1)} copy-done((bf16[32,8192]{1,0:T(8,128)(2,1)S(1)}, bf16[32,8192]{1,0:T(8,128)(2,1)}, u32[]{:S(2)}) %copy-start.3) | copy-done | bytes 524312
  22.7 0.2 convolution_convert_fusion
  22.9 0.2 collective-permute-start.3
  23.1 0.0 collective-permute-done.1
  23.2 0.0 copy-start.2
  23.2 1.2 %collective-permute-done.3 = bf16[8,2,4096]{2,0,1:T(8,128)(2,1)S(1)} collective-permute-done((bf16[8,2,4096]{2,0,1:T(8,128)(2,1)S(1)}, bf16[8,2,4096]{2,0,1:T(8,128)(2,1)S(1)}, u32[]{:S(2)}, u32[]{:S(2)}) %collective-permute-start.3) | collective-permute-done | bytes 131104 | tf_op jit(solution)/shard_map/ppermute | solution.py:18
  24.3 0.2 add_convert_fusion
  24.5 0.8 %copy.31 = bf16[8,2,4096]{2,1,0:T(2,128)(2,1)} copy(bf16[8,2,4096]{2,0,1:T(8,128)(2,1)S(1)} %add_convert_fusion) | data formatting | bytes 262144 | tf_op jit(solution)/shard_map/optimization_barrier | solution.py:142
  25.3 3.4 %all-to-all-start.1 = ((bf16[8,2,4096]{2,1,0:T(2,128)(2,1)}), bf16[8,2,4096]{2,1,0:T(2,128)(2,1)S(1)}, u32[]{:S(2)}, u32[]{:S(2)}) async-start(bf16[8,2,4096]{2,1,0:T(2,128)(2,1)} %copy.31), calls=%async_computation.1 | async-start | bytes 262144 | tf_op jit(solution)/shard_map/all_to_all | solution.py:143
  28.7 0.0 copy-done.1
  28.7 0.4 %fusion.55 = f32[8,64]{1,0:T(8,128)S(1)} fusion(bf16[8,8192]{1,0:T(8,128)(2,1)S(1)} %maximum_select_fusion.1, bf16[64,8192]{1,0:T(8,128)(2,1)S(1)} %copy-done.1), kind=kOutput, calls=%fused_computation.69 | convolution fusion | flops 8388608 | bytes 1181696 | tf_op jit(solution)/shard_map/rd,nd->rn/dot_general | solution.py:69
  29.0 0.0 copy-done.2
  29.0 0.4 %fusion.5 = bf16[8,64]{1,0:T(8,128)(2,1)S(1)} fusion(bf16[8,8192]{1,0:T(8,128)(2,1)S(1)} %maximum_select_fusion.1, bf16[64,8192]{1,0:T(8,128)(2,1)S(1)} %copy-done.2, f32[8,64]{1,0:T(8,128)S(1)} %fusion.55), kind=kOutput, calls=%fused_computation.10 | convolution fusion | flops 8391680 | bytes 1182720 | tf_op jit(solution)/shard_map/rd,nd->rn/dot_general | solution.py:70
  29.4 0.0 copy-done
  29.4 0.2 fusion.6
  29.6 0.2 collective-permute-start.4
  29.8 0.2 convolution_add_fusion
  30.0 6.2 %all-to-all-done.1 = bf16[8,2,4096]{2,1,0:T(2,128)(2,1)S(1)} async-done(((bf16[8,2,4096]{2,1,0:T(2,128)(2,1)}), bf16[8,2,4096]{2,1,0:T(2,128)(2,1)S(1)}, u32[]{:S(2)}, u32[]{:S(2)}) %all-to-all-start.1) | async-done | bytes 131104 | tf_op jit(solution)/shard_map/all_to_all | solution.py:143
  36.2 0.1 reshape.64
  36.2 0.0 collective-permute-done.4
  36.2 0.9 %add_convert_fusion.1 = bf16[8,4096]{1,0:T(8,128)(2,1)} fusion(f32[8,4096]{1,0:T(8,128)S(1)} %convolution_add_fusion, f32[8,4096]{1,0:T(8,128)S(1)} %collective-permute-done.4, f32[16,8]{1,0:T(8,128)S(1)} %bitcast.39, bf16[16,4096]{1,0:T(8,128)(2,1)S(1)} %reshape.64), kind=kOutput, calls=%fused_computation.33 | convolution fusion | flops 6389760 | bytes 459264 | tf_op jit(solution)/shard_map/dot_general | solution.py:82
  (10 shorter events, 0.1 us)
Async XLA Ops:
  0.0 29.4 %copy-start = (bf16[64,8192]{1,0:T(8,128)(2,1)S(1)}, bf16[64,8192]{1,0:T(8,128)(2,1)}, u32[]{:S(2)}) copy-start(bf16[64,8192]{1,0:T(8,128)(2,1)} %param.25) | copy-start | bytes 3145732
  0.8 1.0 %copy-start.7 = (bf16[8,2,128]{2,1,0:T(2,128)(2,1)S(1)}, bf16[8,2,128]{2,1,0:T(2,128)(2,1)}, u32[]{:S(2)}) copy-start(bf16[8,2,128]{2,1,0:T(2,128)(2,1)} %param.19) | copy-start | bytes 12292
  0.8 1.0 %copy-start.11 = (bf16[8,2,32,128]{3,2,1,0:T(8,128)(2,1)S(1)}, bf16[8,2,32,128]{3,2,1,0:T(8,128)(2,1)}, u32[]{:S(2)}) copy-start(bf16[8,2,32,128]{3,2,1,0:T(8,128)(2,1)} %param.17) | copy-start | bytes 393220
  0.8 1.0 %copy-start.12 = (bf16[8,4096]{1,0:T(8,128)(2,1)S(1)}, bf16[8,4096]{1,0:T(8,128)(2,1)}, u32[]{:S(2)}) copy-start(bf16[8,4096]{1,0:T(8,128)(2,1)} %param.16) | copy-start | bytes 196612
  1.8 0.7 %copy-start.8 = (s32[8]{0:T(128)S(1)}, s32[8]{0:T(128)}, u32[]{:S(2)}) copy-start(s32[8]{0:T(128)} %param.21) | copy-start | bytes 100
  2.8 0.8 %copy-start.4 = (bf16[8,4096]{1,0:T(8,128)(2,1)S(1)}, bf16[8,4096]{1,0:T(8,128)(2,1)}, u32[]{:S(2)}) copy-start(bf16[8,4096]{1,0:T(8,128)(2,1)} %param.15) | copy-start | bytes 196612
  3.8 1.4 %collective-permute-start = (f32[8]{0:T(128)S(1)}, f32[8]{0:T(128)S(1)}, u32[]{:S(2)}, u32[]{:S(2)}) collective-permute-start(f32[8]{0:T(128)S(1)} %get-tuple-element.13), channel_id=1, source_target_pairs={{0,1},{1,0},{2,3},{3,2},{4,5},{5,4},{6,7},{7,6},{8,9},{9,8},{10,11... | collective-permute-start | bytes 104 | tf_op jit(solution)/shard_map/ppermute | solution.py:18
  4.3 0.7 %copy-start.5 = (s32[8,4]{0,1:T(4,128)S(1)}, s32[8,4]{0,1:T(4,128)}, u32[]{:S(2)}) copy-start(s32[8,4]{0,1:T(4,128)} %param.29) | copy-start | bytes 388
  4.3 0.9 %copy-start.6 = (bf16[8192]{0:T(1024)(128)(2,1)S(1)}, bf16[8192]{0:T(1024)(128)(2,1)}, u32[]{:S(2)}) copy-start(bf16[8192]{0:T(1024)(128)(2,1)} %param.22) | copy-start | bytes 49156
  5.4 16.1 %copy-start.9 = (bf16[32,8192]{1,0:T(8,128)(2,1)S(1)}, bf16[32,8192]{1,0:T(8,128)(2,1)}, u32[]{:S(2)}) copy-start(bf16[32,8192]{1,0:T(8,128)(2,1)} %param.26) | copy-start | bytes 1572868
  20.0 1.4 %collective-permute-start.2 = (bf16[16,4096]{1,0:T(8,128)(2,1)S(1)}, bf16[16,4096]{1,0:T(8,128)(2,1)S(1)}, u32[]{:S(2)}, u32[]{:S(2)}) collective-permute-start(bf16[16,4096]{1,0:T(8,128)(2,1)S(1)} %reshape.62), channel_id=1, source_target_pairs={{0,1},{1,0},{2,3},{3,2},{4,5},{5,4},{6,7},{7,6},{8,9},{9,8},{10,11... | collective-permute-start | bytes 393224 | tf_op jit(solution)/shard_map/ppermute | solution.py:18
  20.1 1.6 %copy-start.10 = (bf16[32,8192]{1,0:T(8,128)(2,1)S(1)}, bf16[32,8192]{1,0:T(8,128)(2,1)}, u32[]{:S(2)}) copy-start(bf16[32,8192]{1,0:T(8,128)(2,1)} %param.27) | copy-start | bytes 1572868
  20.1 3.0 %collective-permute-start.1 = (bf16[8,4096]{1,0:T(8,128)(2,1)S(1)}, bf16[8,4096]{1,0:T(8,128)(2,1)S(1)}, u32[]{:S(2)}, u32[]{:S(2)}) collective-permute-start(bf16[8,4096]{1,0:T(8,128)(2,1)S(1)} %fusion.21), channel_id=1, source_target_pairs={{0,1},{1,0},{2,3},{3,2},{4,5},{5,4},{6,7},{7,6},{8,9},{9,8},{10,11... | collective-permute-start | bytes 196616 | tf_op jit(solution)/shard_map/ppermute | solution.py:18
  21.7 1.1 %copy-start.3 = (bf16[32,8192]{1,0:T(8,128)(2,1)S(1)}, bf16[32,8192]{1,0:T(8,128)(2,1)}, u32[]{:S(2)}) copy-start(bf16[32,8192]{1,0:T(8,128)(2,1)} %param.28) | copy-start | bytes 1572868
  21.9 6.7 %copy-start.1 = (bf16[64,8192]{1,0:T(8,128)(2,1)S(1)}, bf16[64,8192]{1,0:T(8,128)(2,1)}, u32[]{:S(2)}) copy-start(bf16[64,8192]{1,0:T(8,128)(2,1)} %param.23) | copy-start | bytes 3145732
  22.9 1.4 %collective-permute-start.3 = (bf16[8,2,4096]{2,0,1:T(8,128)(2,1)S(1)}, bf16[8,2,4096]{2,0,1:T(8,128)(2,1)S(1)}, u32[]{:S(2)}, u32[]{:S(2)}) collective-permute-start(bf16[8,2,4096]{2,0,1:T(8,128)(2,1)S(1)} %convolution_convert_fusion), channel_id=1, source_target_pairs={{0,1},{1,0},{2,3},{3,2},{4,5},{5,4},{6,7},{7,6},{8,9},{9,8},{10,11... | collective-permute-start | bytes 393224 | tf_op jit(solution)/shard_map/ppermute | solution.py:18
  23.2 5.9 %copy-start.2 = (bf16[64,8192]{1,0:T(8,128)(2,1)S(1)}, bf16[64,8192]{1,0:T(8,128)(2,1)}, u32[]{:S(2)}) copy-start(bf16[64,8192]{1,0:T(8,128)(2,1)} %param.24) | copy-start | bytes 3145732
  25.3 10.9 %all-to-all-start.1 = ((bf16[8,2,4096]{2,1,0:T(2,128)(2,1)}), bf16[8,2,4096]{2,1,0:T(2,128)(2,1)S(1)}, u32[]{:S(2)}, u32[]{:S(2)}) async-start(bf16[8,2,4096]{2,1,0:T(2,128)(2,1)} %copy.31), calls=%async_computation.1 | async-start | bytes 262144 | tf_op jit(solution)/shard_map/all_to_all | solution.py:143
  29.6 6.6 %collective-permute-start.4 = (f32[8,4096]{1,0:T(8,128)S(1)}, f32[8,4096]{1,0:T(8,128)S(1)}, u32[]{:S(2)}, u32[]{:S(2)}) collective-permute-start(f32[8,4096]{1,0:T(8,128)S(1)} %fusion.6), channel_id=1, source_target_pairs={{0,1},{1,0},{2,3},{3,2},{4,5},{5,4},{6,7},{7,6},{8,9},{9,8},{10,11... | collective-permute-start | bytes 393224 | tf_op jit(solution)/shard_map/ppermute | solution.py:18

commit v22 on v21

--- a/solution.py
+++ b/solution.py
@@ -25,7 +25,7 @@
     return jnp.where(myself == 0, low_first, high_first)
 
 
-def attention_rows(query, key_cache, value_cache, key_new, value_new, lengths):
+def attention_rows(query, key_cache, value_cache, key_new, value_new, lengths, residual):
     count = key_cache.shape[0]
     kv_local = key_cache.shape[1]
     slots = key_cache.shape[2]
@@ -38,11 +38,12 @@
     values_all = jnp.concatenate(
         [value_cache, jnp.broadcast_to(value_new[:, :, None, :], copies)], axis=2
     )
-    scores, values_all = lax.optimization_barrier(
+    scores, values_all, residual_wide = lax.optimization_barrier(
         (
             jnp.einsum("rgjd,rgpd->rgjp", queries, keys_all, preferred_element_type=jnp.float32)
             * scale_factor,
             values_all,
+            residual.astype(jnp.float32),
         )
     )
     positions = jnp.arange(slots + 8, dtype=jnp.int32)[None, :]
@@ -55,7 +56,7 @@
     blended = jnp.einsum(
         "rgjp,rgpd->rgjd", weights, values_all, preferred_element_type=jnp.float32
     )
-    return blended.reshape(count, -1)
+    return residual_wide + blended.reshape(count, -1)
 
 
 def swiglu_rows(normed, gate_rows, up_rows, down_rows):
@@ -105,8 +106,9 @@
     cold_down,
     active,
 ):
-    attended = attention_rows(query, key_cache, value_cache, key_new, value_new, lengths)
-    stream = (residual_in.astype(jnp.float32) + attended).astype(jnp.bfloat16)
+    stream = attention_rows(
+        query, key_cache, value_cache, key_new, value_new, lengths, residual_in
+    ).astype(jnp.bfloat16)
     half_width = stream.shape[1]
     myself = lax.axis_index("heads")
     local_wide = stream.astype(jnp.float32)

time: 37.5 us -> 37.3 us (level)
    convert_element_type x0 -> x1, other arithmetic: none -> 0.96 us  [attention_rows(): residual.astype(jnp.float32)]
    concatenate x1, other arithmetic: 0.97 us -> 0.02 us  [attention_rows(): jnp.concatenate([value_cache, jnp.broadcast_to(value_new[:, :, None, :],...]
    broadcast_in_dim x1, local copies, waits for them, and re-layouts: 0.78 us -> 0.01 us  [attention_rows(): jnp.broadcast_to(value_new[:, :, None, :], copies)]
    unnamed x26 -> x28, local copies, waits for them, and re-layouts: 2.3 us -> 2.87 us
where the time goes in v22:
time: 37.3 us; the launch traced here: 36.9 us
  blocking collectives  14.3 us (38%)
  waiting for transfers between devices  8.15 us (22%)
  starting transfers between devices  4.85 us (13%)
  local copies, waits for them, and re-layouts  3.92 us (11%)
  matrix products  3.72 us (10%)
  other arithmetic  1.81 us (5%)
    all_to_all x1, blocking collectives, local(): lax.all_to_all(outgoing, 'rows', split_axis=0, concat_axis=0, tiled=True)  14.3 us
    all_to_all x1, waiting for transfers between devices, local(): lax.all_to_all(owner_sum, 'rows', split_axis=0, concat_axis=0, tiled=True)  6.15 us
    all_to_all x1, starting transfers between devices, local(): lax.all_to_all(owner_sum, 'rows', split_axis=0, concat_axis=0, tiled=True)  3.37 us
    unnamed x28, local copies, waits for them, and re-layouts  2.87 us
    ppermute x5, waiting for transfers between devices, partner(): return lax.ppermute(block, axis, route)  1.99 us
    ppermute x5, starting transfers between devices, partner(): return lax.ppermute(block, axis, route)  1.48 us
    convert_element_type x1, other arithmetic, attention_rows(): residual.astype(jnp.float32)  0.96 us
    dot_general x1, matrix products, collect_rows(): lax.dot_general(selector, returned, (((0,), (0,)), ((), ())), precision=l...  0.89 us
  transfers between devices with their start and end apart: 6, of which 3 were waited for; matrix products, arithmetic and copies ran while one was open for 6% of the time, Pallas kernels for 0%

profile of v22, /device:TPU:0, one launch (start us, length us, event | category | flops | bytes accessed | tf_op | source)
XLA Modules:
  0.0 36.9 jit_solution(8872684488173911127)
XLA Ops:
  0.0 0.0 copy-start
  0.0 0.0 copy-start.4
  0.0 0.0 copy-start.7
  0.0 1.0 %convert_element_type.57 = f32[8,4096]{1,0:T(8,128)S(1)} convert(bf16[8,4096]{1,0:T(8,128)(2,1)} %param.15) | non-fusion elementwise | flops 32768 | bytes 196608 | tf_op jit(solution)/shard_map/convert_element_type | solution.py:46
  1.0 0.0 copy-done.7
  1.0 0.0 copy-done.4
  1.0 0.0 copy-start.8
  1.0 0.0 copy-start.12
  1.1 0.0 copy-start.13
  1.1 0.6 %copy-done.8 = bf16[8,2,128]{2,1,0:T(2,128)(2,1)S(1)} copy-done((bf16[8,2,128]{2,1,0:T(2,128)(2,1)S(1)}, bf16[8,2,128]{2,1,0:T(2,128)(2,1)}, u32[]{:S(2)}) %copy-start.8) | copy-done | bytes 4120
  1.7 0.2 copy-done.12
  2.0 0.0 copy-done.13
  2.0 0.0 copy-start.9
  2.0 0.2 fusion.4
  2.2 0.5 %copy-done.9 = s32[8]{0:T(128)S(1)} copy-done((s32[8]{0:T(128)S(1)}, s32[8]{0:T(128)}, u32[]{:S(2)}) %copy-start.9) | copy-done | bytes 56
  2.6 0.1 fusion.38
  2.7 0.2 fusion.54
  2.9 0.5 %fusion.24 = f32[8,2,16,128]{3,2,1,0:T(8,128)S(1)} fusion(bf16[8,2,40,128]{3,2,1,0:T(8,128)(2,1)S(1)} %pad_maximum_fusion, f32[8,2,16]{2,1,0:T(2,128)S(1)} %fusion.54, f32[8,2,16,40]{3,2,1,0:T(8,128)S(1)} %fusion.4, pred[8,40]{1,0:T(8,128)(4,1)S(1)} %fusion.38), kind=kOutput, calls=%fused_computation.37 | convolution fusion | flops 2672935 | bytes 337216 | tf_op jit(solution)/shard_map/rgjp,rgpd->rgjd/dot_general | solution.py:56
  3.4 0.2 fusion.19
  3.6 0.5 %collective-permute-start = (f32[8]{0:T(128)S(1)}, f32[8]{0:T(128)S(1)}, u32[]{:S(2)}, u32[]{:S(2)}) collective-permute-start(f32[8]{0:T(128)S(1)} %get-tuple-element.15), channel_id=1, source_target_pairs={{0,1},{1,0},{2,3},{3,2},{4,5},{5,4},{6,7},{7,6},{8,9},{9,8},{10,11... | collective-permute-start | bytes 104 | tf_op jit(solution)/shard_map/ppermute | solution.py:18
  4.1 0.0 copy-start.5
  4.1 0.0 copy-start.6
  4.1 0.7 %copy-done.5 = s32[8,4]{0,1:T(4,128)S(1)} copy-done((s32[8,4]{0,1:T(4,128)S(1)}, s32[8,4]{0,1:T(4,128)}, u32[]{:S(2)}) %copy-start.5) | copy-done | bytes 152
  4.8 0.2 reduce_window_sum.11
  5.0 0.0 copy-done.6
  5.0 0.0 collective-permute-done
  5.1 0.1 fusion.21
  5.2 0.0 copy-start.10
  5.2 0.2 convolution_convert_fusion.1
  5.3 0.1 copy.28
  5.5 14.3 %all_to_all.10 = bf16[8,2,4096]{2,1,0:T(2,128)(2,1)S(1)} all-to-all(bf16[8,2,4096]{2,1,0:T(2,128)(2,1)S(1)} %copy.28), channel_id=1, replica_groups=mesh['groups'=2,'rows'=8,'heads'=2] {'rows'}, dimensions={0} | all-to-all | bytes 262144 | tf_op jit(solution)/shard_map/all_to_all | solution.py:137
  19.7 0.1 reshape.62
  19.8 0.1 collective-permute-start.2
  19.9 0.0 copy-start.11
  19.9 0.5 %collective-permute-start.1 = (bf16[8,4096]{1,0:T(8,128)(2,1)S(1)}, bf16[8,4096]{1,0:T(8,128)(2,1)S(1)}, u32[]{:S(2)}, u32[]{:S(2)}) collective-permute-start(bf16[8,4096]{1,0:T(8,128)(2,1)S(1)} %fusion.21), channel_id=1, source_target_pairs={{0,1},{1,0},{2,3},{3,2},{4,5},{5,4},{6,7},{7,6},{8,9},{9,8},{10,11... | collective-permute-start | bytes 196616 | tf_op jit(solution)/shard_map/ppermute | solution.py:18
  20.4 0.8 %collective-permute-done.2 = bf16[16,4096]{1,0:T(8,128)(2,1)S(1)} collective-permute-done((bf16[16,4096]{1,0:T(8,128)(2,1)S(1)}, bf16[16,4096]{1,0:T(8,128)(2,1)S(1)}, u32[]{:S(2)}, u32[]{:S(2)}) %collective-permute-start.2) | collective-permute-done | bytes 131104 | tf_op jit(solution)/shard_map/ppermute | solution.py:18
  21.2 0.0 copy-done.10
  21.2 0.2 fusion.31
  21.5 0.0 copy-done.11
  21.5 0.0 copy-start.3
  21.5 0.3 multiply_convert_fusion
  21.7 0.0 copy-start.1
  21.7 0.8 %copy-done.3 = bf16[32,8192]{1,0:T(8,128)(2,1)S(1)} copy-done((bf16[32,8192]{1,0:T(8,128)(2,1)S(1)}, bf16[32,8192]{1,0:T(8,128)(2,1)}, u32[]{:S(2)}) %copy-start.3) | copy-done | bytes 524312
  22.5 0.2 convolution_convert_fusion
  22.7 0.2 collective-permute-start.3
  22.9 0.0 collective-permute-done.1
  22.9 0.0 copy-start.2
  23.0 1.2 %collective-permute-done.3 = bf16[8,2,4096]{2,0,1:T(8,128)(2,1)S(1)} collective-permute-done((bf16[8,2,4096]{2,0,1:T(8,128)(2,1)S(1)}, bf16[8,2,4096]{2,0,1:T(8,128)(2,1)S(1)}, u32[]{:S(2)}, u32[]{:S(2)}) %collective-permute-start.3) | collective-permute-done | bytes 131104 | tf_op jit(solution)/shard_map/ppermute | solution.py:18
  24.1 0.2 add_convert_fusion
  24.3 0.8 %copy.31 = bf16[8,2,4096]{2,1,0:T(2,128)(2,1)} copy(bf16[8,2,4096]{2,0,1:T(8,128)(2,1)S(1)} %add_convert_fusion) | data formatting | bytes 262144 | tf_op jit(solution)/shard_map/optimization_barrier | solution.py:144
  25.1 3.4 %all-to-all-start.1 = ((bf16[8,2,4096]{2,1,0:T(2,128)(2,1)}), bf16[8,2,4096]{2,1,0:T(2,128)(2,1)S(1)}, u32[]{:S(2)}, u32[]{:S(2)}) async-start(bf16[8,2,4096]{2,1,0:T(2,128)(2,1)} %copy.31), calls=%async_computation.1 | async-start | bytes 262144 | tf_op jit(solution)/shard_map/all_to_all | solution.py:145
  28.5 0.0 copy-done.1
  28.5 0.4 %fusion.55 = f32[8,64]{1,0:T(8,128)S(1)} fusion(bf16[8,8192]{1,0:T(8,128)(2,1)S(1)} %maximum_select_fusion.1, bf16[64,8192]{1,0:T(8,128)(2,1)S(1)} %copy-done.1), kind=kOutput, calls=%fused_computation.69 | convolution fusion | flops 8388608 | bytes 1181696 | tf_op jit(solution)/shard_map/rd,nd->rn/dot_general | solution.py:70
  28.8 0.0 copy-done.2
  28.8 0.4 %fusion.5 = bf16[8,64]{1,0:T(8,128)(2,1)S(1)} fusion(bf16[8,8192]{1,0:T(8,128)(2,1)S(1)} %maximum_select_fusion.1, bf16[64,8192]{1,0:T(8,128)(2,1)S(1)} %copy-done.2, f32[8,64]{1,0:T(8,128)S(1)} %fusion.55), kind=kOutput, calls=%fused_computation.10 | convolution fusion | flops 8391680 | bytes 1182720 | tf_op jit(solution)/shard_map/rd,nd->rn/dot_general | solution.py:71
  29.2 0.0 copy-done
  29.2 0.2 fusion.6
  29.4 0.2 collective-permute-start.4
  29.6 0.2 convolution_add_fusion
  29.8 6.2 %all-to-all-done.1 = bf16[8,2,4096]{2,1,0:T(2,128)(2,1)S(1)} async-done(((bf16[8,2,4096]{2,1,0:T(2,128)(2,1)}), bf16[8,2,4096]{2,1,0:T(2,128)(2,1)S(1)}, u32[]{:S(2)}, u32[]{:S(2)}) %all-to-all-start.1) | async-done | bytes 131104 | tf_op jit(solution)/shard_map/all_to_all | solution.py:145
  36.0 0.1 reshape.64
  36.0 0.0 collective-permute-done.4
  36.0 0.9 %add_convert_fusion.1 = bf16[8,4096]{1,0:T(8,128)(2,1)} fusion(f32[8,4096]{1,0:T(8,128)S(1)} %convolution_add_fusion, f32[8,4096]{1,0:T(8,128)S(1)} %collective-permute-done.4, f32[16,8]{1,0:T(8,128)S(1)} %bitcast.39, bf16[16,4096]{1,0:T(8,128)(2,1)S(1)} %reshape.64), kind=kOutput, calls=%fused_computation.33 | convolution fusion | flops 6389760 | bytes 459264 | tf_op jit(solution)/shard_map/dot_general | solution.py:83
  (12 shorter events, 0.1 us)
Async XLA Ops:
  0.0 29.2 %copy-start = (bf16[64,8192]{1,0:T(8,128)(2,1)S(1)}, bf16[64,8192]{1,0:T(8,128)(2,1)}, u32[]{:S(2)}) copy-start(bf16[64,8192]{1,0:T(8,128)(2,1)} %param.25) | copy-start | bytes 3145732
  0.0 1.0 %copy-start.4 = (bf16[8,2,32,128]{3,2,1,0:T(8,128)(2,1)S(1)}, bf16[8,2,32,128]{3,2,1,0:T(8,128)(2,1)}, u32[]{:S(2)}) copy-start(bf16[8,2,32,128]{3,2,1,0:T(8,128)(2,1)} %param.18) | copy-start | bytes 393220
  0.0 1.0 %copy-start.7 = (bf16[8,2,128]{2,1,0:T(2,128)(2,1)S(1)}, bf16[8,2,128]{2,1,0:T(2,128)(2,1)}, u32[]{:S(2)}) copy-start(bf16[8,2,128]{2,1,0:T(2,128)(2,1)} %param.20) | copy-start | bytes 12292
  1.0 0.7 %copy-start.8 = (bf16[8,2,128]{2,1,0:T(2,128)(2,1)S(1)}, bf16[8,2,128]{2,1,0:T(2,128)(2,1)}, u32[]{:S(2)}) copy-start(bf16[8,2,128]{2,1,0:T(2,128)(2,1)} %param.19) | copy-start | bytes 12292
  1.0 0.9 %copy-start.12 = (bf16[8,2,32,128]{3,2,1,0:T(8,128)(2,1)S(1)}, bf16[8,2,32,128]{3,2,1,0:T(8,128)(2,1)}, u32[]{:S(2)}) copy-start(bf16[8,2,32,128]{3,2,1,0:T(8,128)(2,1)} %param.17) | copy-start | bytes 393220
  1.1 0.9 %copy-start.13 = (bf16[8,4096]{1,0:T(8,128)(2,1)S(1)}, bf16[8,4096]{1,0:T(8,128)(2,1)}, u32[]{:S(2)}) copy-start(bf16[8,4096]{1,0:T(8,128)(2,1)} %param.16) | copy-start | bytes 196612
  2.0 0.7 %copy-start.9 = (s32[8]{0:T(128)S(1)}, s32[8]{0:T(128)}, u32[]{:S(2)}) copy-start(s32[8]{0:T(128)} %param.21) | copy-start | bytes 100
  3.6 1.4 %collective-permute-start = (f32[8]{0:T(128)S(1)}, f32[8]{0:T(128)S(1)}, u32[]{:S(2)}, u32[]{:S(2)}) collective-permute-start(f32[8]{0:T(128)S(1)} %get-tuple-element.15), channel_id=1, source_target_pairs={{0,1},{1,0},{2,3},{3,2},{4,5},{5,4},{6,7},{7,6},{8,9},{9,8},{10,11... | collective-permute-start | bytes 104 | tf_op jit(solution)/shard_map/ppermute | solution.py:18
  4.1 0.7 %copy-start.5 = (s32[8,4]{0,1:T(4,128)S(1)}, s32[8,4]{0,1:T(4,128)}, u32[]{:S(2)}) copy-start(s32[8,4]{0,1:T(4,128)} %param.29) | copy-start | bytes 388
  4.1 0.9 %copy-start.6 = (bf16[8192]{0:T(1024)(128)(2,1)S(1)}, bf16[8192]{0:T(1024)(128)(2,1)}, u32[]{:S(2)}) copy-start(bf16[8192]{0:T(1024)(128)(2,1)} %param.22) | copy-start | bytes 49156
  5.2 16.1 %copy-start.10 = (bf16[32,8192]{1,0:T(8,128)(2,1)S(1)}, bf16[32,8192]{1,0:T(8,128)(2,1)}, u32[]{:S(2)}) copy-start(bf16[32,8192]{1,0:T(8,128)(2,1)} %param.26) | copy-start | bytes 1572868
  19.8 1.4 %collective-permute-start.2 = (bf16[16,4096]{1,0:T(8,128)(2,1)S(1)}, bf16[16,4096]{1,0:T(8,128)(2,1)S(1)}, u32[]{:S(2)}, u32[]{:S(2)}) collective-permute-start(bf16[16,4096]{1,0:T(8,128)(2,1)S(1)} %reshape.62), channel_id=1, source_target_pairs={{0,1},{1,0},{2,3},{3,2},{4,5},{5,4},{6,7},{7,6},{8,9},{9,8},{10,11... | collective-permute-start | bytes 393224 | tf_op jit(solution)/shard_map/ppermute | solution.py:18
  19.9 1.6 %copy-start.11 = (bf16[32,8192]{1,0:T(8,128)(2,1)S(1)}, bf16[32,8192]{1,0:T(8,128)(2,1)}, u32[]{:S(2)}) copy-start(bf16[32,8192]{1,0:T(8,128)(2,1)} %param.27) | copy-start | bytes 1572868
  19.9 3.0 %collective-permute-start.1 = (bf16[8,4096]{1,0:T(8,128)(2,1)S(1)}, bf16[8,4096]{1,0:T(8,128)(2,1)S(1)}, u32[]{:S(2)}, u32[]{:S(2)}) collective-permute-start(bf16[8,4096]{1,0:T(8,128)(2,1)S(1)} %fusion.21), channel_id=1, source_target_pairs={{0,1},{1,0},{2,3},{3,2},{4,5},{5,4},{6,7},{7,6},{8,9},{9,8},{10,11... | collective-permute-start | bytes 196616 | tf_op jit(solution)/shard_map/ppermute | solution.py:18
  21.5 1.1 %copy-start.3 = (bf16[32,8192]{1,0:T(8,128)(2,1)S(1)}, bf16[32,8192]{1,0:T(8,128)(2,1)}, u32[]{:S(2)}) copy-start(bf16[32,8192]{1,0:T(8,128)(2,1)} %param.28) | copy-start | bytes 1572868
  21.7 6.7 %copy-start.1 = (bf16[64,8192]{1,0:T(8,128)(2,1)S(1)}, bf16[64,8192]{1,0:T(8,128)(2,1)}, u32[]{:S(2)}) copy-start(bf16[64,8192]{1,0:T(8,128)(2,1)} %param.23) | copy-start | bytes 3145732
  22.7 1.4 %collective-permute-start.3 = (bf16[8,2,4096]{2,0,1:T(8,128)(2,1)S(1)}, bf16[8,2,4096]{2,0,1:T(8,128)(2,1)S(1)}, u32[]{:S(2)}, u32[]{:S(2)}) collective-permute-start(bf16[8,2,4096]{2,0,1:T(8,128)(2,1)S(1)} %convolution_convert_fusion), channel_id=1, source_target_pairs={{0,1},{1,0},{2,3},{3,2},{4,5},{5,4},{6,7},{7,6},{8,9},{9,8},{10,11... | collective-permute-start | bytes 393224 | tf_op jit(solution)/shard_map/ppermute | solution.py:18
  22.9 5.9 %copy-start.2 = (bf16[64,8192]{1,0:T(8,128)(2,1)S(1)}, bf16[64,8192]{1,0:T(8,128)(2,1)}, u32[]{:S(2)}) copy-start(bf16[64,8192]{1,0:T(8,128)(2,1)} %param.24) | copy-start | bytes 3145732
  25.1 10.9 %all-to-all-start.1 = ((bf16[8,2,4096]{2,1,0:T(2,128)(2,1)}), bf16[8,2,4096]{2,1,0:T(2,128)(2,1)S(1)}, u32[]{:S(2)}, u32[]{:S(2)}) async-start(bf16[8,2,4096]{2,1,0:T(2,128)(2,1)} %copy.31), calls=%async_computation.1 | async-start | bytes 262144 | tf_op jit(solution)/shard_map/all_to_all | solution.py:145
  29.4 6.6 %collective-permute-start.4 = (f32[8,4096]{1,0:T(8,128)S(1)}, f32[8,4096]{1,0:T(8,128)S(1)}, u32[]{:S(2)}, u32[]{:S(2)}) collective-permute-start(f32[8,4096]{1,0:T(8,128)S(1)} %fusion.6), channel_id=1, source_target_pairs={{0,1},{1,0},{2,3},{3,2},{4,5},{5,4},{6,7},{7,6},{8,9},{9,8},{10,11... | collective-permute-start | bytes 393224 | tf_op jit(solution)/shard_map/ppermute | solution.py:18

commit v23 on v22

--- a/solution.py
+++ b/solution.py
@@ -38,16 +38,18 @@
     values_all = jnp.concatenate(
         [value_cache, jnp.broadcast_to(value_new[:, :, None, :], copies)], axis=2
     )
-    scores, values_all, residual_wide = lax.optimization_barrier(
+    positions = jnp.arange(slots + 8, dtype=jnp.int32)[None, :]
+    visible = (positions < lengths[:, None]) | (positions == slots)
+    scores, values_all, residual_wide, visible = lax.optimization_barrier(
         (
             jnp.einsum("rgjd,rgpd->rgjp", queries, keys_all, preferred_element_type=jnp.float32)
             * scale_factor,
             values_all,
             residual.astype(jnp.float32),
+            visible,
         )
     )
-    positions = jnp.arange(slots + 8, dtype=jnp.int32)[None, :]
-    visible = ((positions < lengths[:, None]) | (positions == slots))[:, None, None, :]
+    visible = visible[:, None, None, :]
     scores = jnp.where(visible, scores, -1e30)
     highest = jnp.max(scores, axis=-1)
     expons = jnp.where(visible, jnp.exp(scores - highest[..., None]), 0.0)

time: 37.3 us -> 36.8 us (0.987)
  local copies, waits for them, and re-layouts: 3.92 us -> 3.4 us
    unnamed x28, local copies, waits for them, and re-layouts: 2.87 us -> 2.34 us
where the time goes in v23:
time: 36.8 us; the launch traced here: 36.4 us
  blocking collectives  14.3 us (39%)
  waiting for transfers between devices  8.15 us (22%)
  starting transfers between devices  4.85 us (13%)
  matrix products  3.72 us (10%)
  local copies, waits for them, and re-layouts  3.4 us (9%)
  other arithmetic  1.82 us (5%)
    all_to_all x1, blocking collectives, local(): lax.all_to_all(outgoing, 'rows', split_axis=0, concat_axis=0, tiled=True)  14.3 us
    all_to_all x1, waiting for transfers between devices, local(): lax.all_to_all(owner_sum, 'rows', split_axis=0, concat_axis=0, tiled=True)  6.15 us
    all_to_all x1, starting transfers between devices, local(): lax.all_to_all(owner_sum, 'rows', split_axis=0, concat_axis=0, tiled=True)  3.37 us
    unnamed x28, local copies, waits for them, and re-layouts  2.34 us
    ppermute x5, waiting for transfers between devices, partner(): return lax.ppermute(block, axis, route)  1.99 us
    ppermute x5, starting transfers between devices, partner(): return lax.ppermute(block, axis, route)  1.48 us
    convert_element_type x1, other arithmetic, attention_rows(): residual.astype(jnp.float32)  0.96 us
    dot_general x1, matrix products, collect_rows(): lax.dot_general(selector, returned, (((0,), (0,)), ((), ())), precision=l...  0.89 us
  transfers between devices with their start and end apart: 6, of which 3 were waited for; matrix products, arithmetic and copies ran while one was open for 6% of the time, Pallas kernels for 0%

profile of v23, /device:TPU:0, one launch (start us, length us, event | category | flops | bytes accessed | tf_op | source)
XLA Modules:
  0.0 36.4 jit_solution(17894288206026013212)
XLA Ops:
  0.0 0.0 copy-start
  0.0 0.0 copy-start.4
  0.0 0.0 copy-start.7
  0.0 1.0 %convert_element_type.57 = f32[8,4096]{1,0:T(8,128)S(1)} convert(bf16[8,4096]{1,0:T(8,128)(2,1)} %param.15) | non-fusion elementwise | flops 32768 | bytes 196608 | tf_op jit(solution)/shard_map/convert_element_type | solution.py:48
  1.0 0.0 copy-done.7
  1.0 0.0 copy-done.4
  1.0 0.0 copy-start.9
  1.0 0.0 copy-start.8
  1.1 0.0 copy-start.12
  1.1 0.0 copy-start.13
  1.1 0.6 %copy-done.9 = s32[8]{0:T(128)S(1)} copy-done((s32[8]{0:T(128)S(1)}, s32[8]{0:T(128)}, u32[]{:S(2)}) %copy-start.9) | copy-done | bytes 56
  1.7 0.1 fusion.38
  1.8 0.0 copy-done.8
  1.8 0.2 copy-done.12
  2.0 0.0 copy-done.13
  2.0 0.2 fusion.4
  2.2 0.2 fusion.54
  2.4 0.5 %fusion.24 = f32[8,2,16,128]{3,2,1,0:T(8,128)S(1)} fusion(bf16[8,2,40,128]{3,2,1,0:T(8,128)(2,1)S(1)} %pad_maximum_fusion, f32[8,2,16]{2,1,0:T(2,128)S(1)} %fusion.54, f32[8,2,16,40]{3,2,1,0:T(8,128)S(1)} %fusion.4, pred[8,40]{1,0:T(8,128)(4,1)S(1)} %fusion.38), kind=kOutput, calls=%fused_computation.37 | convolution fusion | flops 2672935 | bytes 337216 | tf_op jit(solution)/shard_map/rgjp,rgpd->rgjd/dot_general | solution.py:58
  2.9 0.2 fusion.19
  3.1 0.5 %collective-permute-start = (f32[8]{0:T(128)S(1)}, f32[8]{0:T(128)S(1)}, u32[]{:S(2)}, u32[]{:S(2)}) collective-permute-start(f32[8]{0:T(128)S(1)} %get-tuple-element.17), channel_id=1, source_target_pairs={{0,1},{1,0},{2,3},{3,2},{4,5},{5,4},{6,7},{7,6},{8,9},{9,8},{10,11... | collective-permute-start | bytes 104 | tf_op jit(solution)/shard_map/ppermute | solution.py:18
  3.6 0.0 copy-start.5
  3.6 0.0 copy-start.6
  3.6 0.7 %copy-done.5 = s32[8,4]{0,1:T(4,128)S(1)} copy-done((s32[8,4]{0,1:T(4,128)S(1)}, s32[8,4]{0,1:T(4,128)}, u32[]{:S(2)}) %copy-start.5) | copy-done | bytes 152
  4.3 0.2 reduce_window_sum.11
  4.5 0.0 copy-done.6
  4.5 0.0 collective-permute-done
  4.6 0.1 fusion.21
  4.7 0.0 copy-start.10
  4.7 0.2 convolution_convert_fusion.1
  4.8 0.1 copy.28
  5.0 14.3 %all_to_all.10 = bf16[8,2,4096]{2,1,0:T(2,128)(2,1)S(1)} all-to-all(bf16[8,2,4096]{2,1,0:T(2,128)(2,1)S(1)} %copy.28), channel_id=1, replica_groups=mesh['groups'=2,'rows'=8,'heads'=2] {'rows'}, dimensions={0} | all-to-all | bytes 262144 | tf_op jit(solution)/shard_map/all_to_all | solution.py:139
  19.2 0.1 reshape.35
  19.3 0.1 collective-permute-start.2
  19.4 0.0 copy-start.11
  19.4 0.5 %collective-permute-start.1 = (bf16[8,4096]{1,0:T(8,128)(2,1)S(1)}, bf16[8,4096]{1,0:T(8,128)(2,1)S(1)}, u32[]{:S(2)}, u32[]{:S(2)}) collective-permute-start(bf16[8,4096]{1,0:T(8,128)(2,1)S(1)} %fusion.21), channel_id=1, source_target_pairs={{0,1},{1,0},{2,3},{3,2},{4,5},{5,4},{6,7},{7,6},{8,9},{9,8},{10,11... | collective-permute-start | bytes 196616 | tf_op jit(solution)/shard_map/ppermute | solution.py:18
  19.9 0.8 %collective-permute-done.2 = bf16[16,4096]{1,0:T(8,128)(2,1)S(1)} collective-permute-done((bf16[16,4096]{1,0:T(8,128)(2,1)S(1)}, bf16[16,4096]{1,0:T(8,128)(2,1)S(1)}, u32[]{:S(2)}, u32[]{:S(2)}) %collective-permute-start.2) | collective-permute-done | bytes 131104 | tf_op jit(solution)/shard_map/ppermute | solution.py:18
  20.7 0.0 copy-done.10
  20.7 0.2 fusion.31
  21.0 0.0 copy-done.11
  21.0 0.0 copy-start.3
  21.0 0.3 multiply_convert_fusion
  21.2 0.0 copy-start.1
  21.2 0.8 %copy-done.3 = bf16[32,8192]{1,0:T(8,128)(2,1)S(1)} copy-done((bf16[32,8192]{1,0:T(8,128)(2,1)S(1)}, bf16[32,8192]{1,0:T(8,128)(2,1)}, u32[]{:S(2)}) %copy-start.3) | copy-done | bytes 524312
  22.0 0.2 convolution_convert_fusion
  22.2 0.2 collective-permute-start.3
  22.4 0.0 collective-permute-done.1
  22.4 0.0 copy-start.2
  22.5 1.2 %collective-permute-done.3 = bf16[8,2,4096]{2,0,1:T(8,128)(2,1)S(1)} collective-permute-done((bf16[8,2,4096]{2,0,1:T(8,128)(2,1)S(1)}, bf16[8,2,4096]{2,0,1:T(8,128)(2,1)S(1)}, u32[]{:S(2)}, u32[]{:S(2)}) %collective-permute-start.3) | collective-permute-done | bytes 131104 | tf_op jit(solution)/shard_map/ppermute | solution.py:18
  23.6 0.2 add_convert_fusion
  23.8 0.8 %copy.31 = bf16[8,2,4096]{2,1,0:T(2,128)(2,1)} copy(bf16[8,2,4096]{2,0,1:T(8,128)(2,1)S(1)} %add_convert_fusion) | data formatting | bytes 262144 | tf_op jit(solution)/shard_map/optimization_barrier | solution.py:146
  24.6 3.4 %all-to-all-start.1 = ((bf16[8,2,4096]{2,1,0:T(2,128)(2,1)}), bf16[8,2,4096]{2,1,0:T(2,128)(2,1)S(1)}, u32[]{:S(2)}, u32[]{:S(2)}) async-start(bf16[8,2,4096]{2,1,0:T(2,128)(2,1)} %copy.31), calls=%async_computation.1 | async-start | bytes 262144 | tf_op jit(solution)/shard_map/all_to_all | solution.py:147
  27.9 0.0 copy-done.1
  28.0 0.4 %fusion.55 = f32[8,64]{1,0:T(8,128)S(1)} fusion(bf16[8,8192]{1,0:T(8,128)(2,1)S(1)} %maximum_select_fusion.1, bf16[64,8192]{1,0:T(8,128)(2,1)S(1)} %copy-done.1), kind=kOutput, calls=%fused_computation.69 | convolution fusion | flops 8388608 | bytes 1181696 | tf_op jit(solution)/shard_map/rd,nd->rn/dot_general | solution.py:72
  28.3 0.0 copy-done.2
  28.3 0.4 %fusion.5 = bf16[8,64]{1,0:T(8,128)(2,1)S(1)} fusion(bf16[8,8192]{1,0:T(8,128)(2,1)S(1)} %maximum_select_fusion.1, bf16[64,8192]{1,0:T(8,128)(2,1)S(1)} %copy-done.2, f32[8,64]{1,0:T(8,128)S(1)} %fusion.55), kind=kOutput, calls=%fused_computation.10 | convolution fusion | flops 8391680 | bytes 1182720 | tf_op jit(solution)/shard_map/rd,nd->rn/dot_general | solution.py:73
  28.7 0.0 copy-done
  28.7 0.2 fusion.6
  28.9 0.2 collective-permute-start.4
  29.1 0.2 convolution_add_fusion
  29.3 6.2 %all-to-all-done.1 = bf16[8,2,4096]{2,1,0:T(2,128)(2,1)S(1)} async-done(((bf16[8,2,4096]{2,1,0:T(2,128)(2,1)}), bf16[8,2,4096]{2,1,0:T(2,128)(2,1)S(1)}, u32[]{:S(2)}, u32[]{:S(2)}) %all-to-all-start.1) | async-done | bytes 131104 | tf_op jit(solution)/shard_map/all_to_all | solution.py:147
  35.5 0.1 reshape.37
  35.5 0.0 collective-permute-done.4
  35.5 0.9 %add_convert_fusion.1 = bf16[8,4096]{1,0:T(8,128)(2,1)} fusion(f32[8,4096]{1,0:T(8,128)S(1)} %convolution_add_fusion, f32[8,4096]{1,0:T(8,128)S(1)} %collective-permute-done.4, f32[16,8]{1,0:T(8,128)S(1)} %bitcast.39, bf16[16,4096]{1,0:T(8,128)(2,1)S(1)} %reshape.37), kind=kOutput, calls=%fused_computation.33 | convolution fusion | flops 6389760 | bytes 459264 | tf_op jit(solution)/shard_map/dot_general | solution.py:85
  (12 shorter events, 0.1 us)
Async XLA Ops:
  0.0 28.7 %copy-start = (bf16[64,8192]{1,0:T(8,128)(2,1)S(1)}, bf16[64,8192]{1,0:T(8,128)(2,1)}, u32[]{:S(2)}) copy-start(bf16[64,8192]{1,0:T(8,128)(2,1)} %param.25) | copy-start | bytes 3145732
  0.0 1.0 %copy-start.4 = (bf16[8,2,32,128]{3,2,1,0:T(8,128)(2,1)S(1)}, bf16[8,2,32,128]{3,2,1,0:T(8,128)(2,1)}, u32[]{:S(2)}) copy-start(bf16[8,2,32,128]{3,2,1,0:T(8,128)(2,1)} %param.18) | copy-start | bytes 393220
  0.0 1.0 %copy-start.7 = (bf16[8,2,128]{2,1,0:T(2,128)(2,1)S(1)}, bf16[8,2,128]{2,1,0:T(2,128)(2,1)}, u32[]{:S(2)}) copy-start(bf16[8,2,128]{2,1,0:T(2,128)(2,1)} %param.20) | copy-start | bytes 12292
  1.0 0.7 %copy-start.9 = (s32[8]{0:T(128)S(1)}, s32[8]{0:T(128)}, u32[]{:S(2)}) copy-start(s32[8]{0:T(128)} %param.21) | copy-start | bytes 100
  1.0 0.7 %copy-start.8 = (bf16[8,2,128]{2,1,0:T(2,128)(2,1)S(1)}, bf16[8,2,128]{2,1,0:T(2,128)(2,1)}, u32[]{:S(2)}) copy-start(bf16[8,2,128]{2,1,0:T(2,128)(2,1)} %param.19) | copy-start | bytes 12292
  1.1 0.9 %copy-start.12 = (bf16[8,2,32,128]{3,2,1,0:T(8,128)(2,1)S(1)}, bf16[8,2,32,128]{3,2,1,0:T(8,128)(2,1)}, u32[]{:S(2)}) copy-start(bf16[8,2,32,128]{3,2,1,0:T(8,128)(2,1)} %param.17) | copy-start | bytes 393220
  1.1 0.9 %copy-start.13 = (bf16[8,4096]{1,0:T(8,128)(2,1)S(1)}, bf16[8,4096]{1,0:T(8,128)(2,1)}, u32[]{:S(2)}) copy-start(bf16[8,4096]{1,0:T(8,128)(2,1)} %param.16) | copy-start | bytes 196612
  3.1 1.4 %collective-permute-start = (f32[8]{0:T(128)S(1)}, f32[8]{0:T(128)S(1)}, u32[]{:S(2)}, u32[]{:S(2)}) collective-permute-start(f32[8]{0:T(128)S(1)} %get-tuple-element.17), channel_id=1, source_target_pairs={{0,1},{1,0},{2,3},{3,2},{4,5},{5,4},{6,7},{7,6},{8,9},{9,8},{10,11... | collective-permute-start | bytes 104 | tf_op jit(solution)/shard_map/ppermute | solution.py:18
  3.6 0.7 %copy-start.5 = (s32[8,4]{0,1:T(4,128)S(1)}, s32[8,4]{0,1:T(4,128)}, u32[]{:S(2)}) copy-start(s32[8,4]{0,1:T(4,128)} %param.29) | copy-start | bytes 388
  3.6 0.9 %copy-start.6 = (bf16[8192]{0:T(1024)(128)(2,1)S(1)}, bf16[8192]{0:T(1024)(128)(2,1)}, u32[]{:S(2)}) copy-start(bf16[8192]{0:T(1024)(128)(2,1)} %param.22) | copy-start | bytes 49156
  4.7 16.1 %copy-start.10 = (bf16[32,8192]{1,0:T(8,128)(2,1)S(1)}, bf16[32,8192]{1,0:T(8,128)(2,1)}, u32[]{:S(2)}) copy-start(bf16[32,8192]{1,0:T(8,128)(2,1)} %param.26) | copy-start | bytes 1572868
  19.3 1.4 %collective-permute-start.2 = (bf16[16,4096]{1,0:T(8,128)(2,1)S(1)}, bf16[16,4096]{1,0:T(8,128)(2,1)S(1)}, u32[]{:S(2)}, u32[]{:S(2)}) collective-permute-start(bf16[16,4096]{1,0:T(8,128)(2,1)S(1)} %reshape.35), channel_id=1, source_target_pairs={{0,1},{1,0},{2,3},{3,2},{4,5},{5,4},{6,7},{7,6},{8,9},{9,8},{10,11... | collective-permute-start | bytes 393224 | tf_op jit(solution)/shard_map/ppermute | solution.py:18
  19.4 1.6 %copy-start.11 = (bf16[32,8192]{1,0:T(8,128)(2,1)S(1)}, bf16[32,8192]{1,0:T(8,128)(2,1)}, u32[]{:S(2)}) copy-start(bf16[32,8192]{1,0:T(8,128)(2,1)} %param.27) | copy-start | bytes 1572868
  19.4 3.0 %collective-permute-start.1 = (bf16[8,4096]{1,0:T(8,128)(2,1)S(1)}, bf16[8,4096]{1,0:T(8,128)(2,1)S(1)}, u32[]{:S(2)}, u32[]{:S(2)}) collective-permute-start(bf16[8,4096]{1,0:T(8,128)(2,1)S(1)} %fusion.21), channel_id=1, source_target_pairs={{0,1},{1,0},{2,3},{3,2},{4,5},{5,4},{6,7},{7,6},{8,9},{9,8},{10,11... | collective-permute-start | bytes 196616 | tf_op jit(solution)/shard_map/ppermute | solution.py:18
  21.0 1.1 %copy-start.3 = (bf16[32,8192]{1,0:T(8,128)(2,1)S(1)}, bf16[32,8192]{1,0:T(8,128)(2,1)}, u32[]{:S(2)}) copy-start(bf16[32,8192]{1,0:T(8,128)(2,1)} %param.28) | copy-start | bytes 1572868
  21.2 6.7 %copy-start.1 = (bf16[64,8192]{1,0:T(8,128)(2,1)S(1)}, bf16[64,8192]{1,0:T(8,128)(2,1)}, u32[]{:S(2)}) copy-start(bf16[64,8192]{1,0:T(8,128)(2,1)} %param.23) | copy-start | bytes 3145732
  22.2 1.4 %collective-permute-start.3 = (bf16[8,2,4096]{2,0,1:T(8,128)(2,1)S(1)}, bf16[8,2,4096]{2,0,1:T(8,128)(2,1)S(1)}, u32[]{:S(2)}, u32[]{:S(2)}) collective-permute-start(bf16[8,2,4096]{2,0,1:T(8,128)(2,1)S(1)} %convolution_convert_fusion), channel_id=1, source_target_pairs={{0,1},{1,0},{2,3},{3,2},{4,5},{5,4},{6,7},{7,6},{8,9},{9,8},{10,11... | collective-permute-start | bytes 393224 | tf_op jit(solution)/shard_map/ppermute | solution.py:18
  22.4 5.9 %copy-start.2 = (bf16[64,8192]{1,0:T(8,128)(2,1)S(1)}, bf16[64,8192]{1,0:T(8,128)(2,1)}, u32[]{:S(2)}) copy-start(bf16[64,8192]{1,0:T(8,128)(2,1)} %param.24) | copy-start | bytes 3145732
  24.6 10.9 %all-to-all-start.1 = ((bf16[8,2,4096]{2,1,0:T(2,128)(2,1)}), bf16[8,2,4096]{2,1,0:T(2,128)(2,1)S(1)}, u32[]{:S(2)}, u32[]{:S(2)}) async-start(bf16[8,2,4096]{2,1,0:T(2,128)(2,1)} %copy.31), calls=%async_computation.1 | async-start | bytes 262144 | tf_op jit(solution)/shard_map/all_to_all | solution.py:147
  28.9 6.6 %collective-permute-start.4 = (f32[8,4096]{1,0:T(8,128)S(1)}, f32[8,4096]{1,0:T(8,128)S(1)}, u32[]{:S(2)}, u32[]{:S(2)}) collective-permute-start(f32[8,4096]{1,0:T(8,128)S(1)} %fusion.6), channel_id=1, source_target_pairs={{0,1},{1,0},{2,3},{3,2},{4,5},{5,4},{6,7},{7,6},{8,9},{9,8},{10,11... | collective-permute-start | bytes 393224 | tf_op jit(solution)/shard_map/ppermute | solution.py:18
